TPU v7x, 128 devices: a whole 4x4x4 slice. The times are simulated.
128 devices in a mesh: section: 8 (over z, core), ctx: 16 (over y, x).
Axes of the slice: x: 4, y: 4, z: 4, core: 2. Of those that a mesh axis runs over, the one named last changes fastest.
Arguments:
- previous: bfloat16 [8, 2048, 8192], P('section', 'ctx'), may hold values from -6 to 6
- fresh: bfloat16 [2048, 8192], P('ctx'), may hold values from -6 to 6
- dt_raw: float32 [8, 2048, 128], P('section', 'ctx'), may hold values from -3 to 4100
- dt_bias: float32 [8, 128], P('section'), may hold values from -0.5 to 0.5
- a_log: float32 [8, 128], P('section'), may hold values from -12 to -2
- b_in: bfloat16 [8, 2048, 1024], P('section', 'ctx'), may hold values from -0.5 to 0.5
- c_in: bfloat16 [8, 2048, 1024], P('section', 'ctx'), may hold values from -6 to 6
- skip_d: float32 [8, 128], P('section'), may hold values from 0.5 to 1.5
- norm_gain: bfloat16 [8, 8192], P('section'), may hold values from 0.099609375 to 1.8984375
- queries: bfloat16 [8, 2048, 8192], P('section', 'ctx'), may hold values from -12 to 12
- keys: bfloat16 [8, 2048, 1024], P('section', 'ctx'), may hold values from -12 to 12
- values: bfloat16 [8, 2048, 1024], P('section', 'ctx'), may hold values from -6 to 6
- doc_ids: int32 [8, 2048], P('section'), may hold values from 0 to 7, never falling along the last dimension, each value on 1 to 512 neighbouring positions
Outputs:
- section_out: bfloat16 [8, 2048, 8192], P('section', 'ctx')
Inputs may be any that keep to these rules, and one draw needn't show every extreme that they name: `doc_ids`: each row never falls; every document covers 1 to 512 positions and one covers exactly 512.
All inputs are finite; a program needn't handle non-finite values.
Results may differ from a plain program's by a relative error of at most 0.0085.
Values may be sent and summed in bfloat16 or wider, within the bound.
No kernel may reach another device: no remote copies, remote signals or barrier semaphores. Data moves between devices by JAX's collectives and lax.ppermute only.
A program may use at most 256 MiB of HBM per device.

v0:
```python
import math

import jax
import jax.numpy as jnp
from jax import lax
from jax.sharding import PartitionSpec as P

HEAD_A = 128
STATE = 128
GROUPS = 8


norm_eps = 1e-05


def entering(value, axis, join, neutral):
    count, mine = (lax.axis_size(axis), lax.axis_index(axis))
    pieces = jax.tree.map(lambda part: lax.all_gather(part, axis), value)
    running = jax.tree.map(
        lambda part, zero: jnp.full_like(part, 0) + jnp.asarray(zero, part.dtype), value, neutral
    )

    def lap(position, running):
        longer = join(running, jax.tree.map(lambda part: part[position], pieces))
        return jax.tree.map(lambda new, old: jnp.where(position < mine, new, old), longer, running)

    return lax.fori_loop(0, count - 1, lap, running)


def shifted(value, axis, by):
    peers = lax.axis_size(axis)
    pairs = [(i, i + by) for i in range(peers) if 0 <= i + by < peers]
    return lax.ppermute(value, axis, pairs)


def chain_combine(earlier, later):
    return (earlier[0] * later[0], later[0][:, None, None] * earlier[1] + later[1])


def mixer_block(
    stream, dt_row, bias_row, alog_row, b_row, c_row, skip_row, gain_row, own_ids, prev_last
):
    tok_rows, model_width = stream.shape
    mamba_heads = dt_row.shape[1]
    head_dim = model_width // mamba_heads
    per_group = mamba_heads // GROUPS
    head_input = stream.reshape(tok_rows, mamba_heads, head_dim)
    step_size = jax.nn.softplus(dt_row + bias_row[None, :])
    log_cum = jnp.cumsum(-step_size * jnp.exp(alog_row)[None, :], axis=0)
    b_groups = b_row.reshape(tok_rows, GROUPS, STATE)
    c_groups = c_row.reshape(tok_rows, GROUPS, STATE)
    rows_at = jnp.arange(tok_rows)
    same_doc = (own_ids[:, None] == own_ids[None, :]) & (rows_at[:, None] >= rows_at[None, :])
    log_gaps = jnp.where(same_doc[:, :, None], log_cum[:, None, :] - log_cum[None, :, :], 0.0)
    decay_mask = jnp.where(same_doc[:, :, None], jnp.exp(log_gaps), 0.0)
    inner_cb = jnp.einsum("ign,jgn->ijg", c_groups, b_groups, preferred_element_type=jnp.float32)
    inner_cb = jnp.repeat(inner_cb, per_group, axis=2)
    intra_w = (decay_mask * inner_cb * step_size[None, :, :]).astype(jnp.bfloat16)
    local_out = jnp.einsum("ijh,jhp->ihp", intra_w, head_input, preferred_element_type=jnp.float32)
    last_id = own_ids[-1]
    end_scale = (
        jnp.exp(log_cum[-1][None, :] - log_cum)
        * step_size
        * (own_ids == last_id).astype(jnp.float32)[:, None]
    )
    end_w = (
        end_scale[:, :, None] * jnp.repeat(b_groups, per_group, axis=1).astype(jnp.float32)
    ).astype(jnp.bfloat16)
    block_state = jnp.einsum("thn,thp->hpn", end_w, head_input, preferred_element_type=jnp.float32)
    edge_match = (own_ids[0] == prev_last).astype(jnp.float32)
    block_gain = jnp.exp(log_cum[-1]) * (own_ids[0] == last_id).astype(jnp.float32) * edge_match
    identity = (jnp.ones_like(block_gain), jnp.zeros_like(block_state))
    carried = entering((block_gain, block_state), "ctx", chain_combine, identity)
    state_bf = carried[1].astype(jnp.bfloat16)
    edge_valid = (own_ids == prev_last).astype(jnp.float32)
    carried_out = jnp.einsum(
        "tgn,gkpn->tgkp",
        c_groups,
        state_bf.reshape(GROUPS, per_group, head_dim, STATE),
        preferred_element_type=jnp.float32,
    ).reshape(tok_rows, mamba_heads, head_dim)
    carried_out = carried_out * (jnp.exp(log_cum) * edge_valid[:, None])[:, :, None]
    mixer_out = local_out + carried_out + skip_row[None, :, None] * head_input.astype(jnp.float32)
    flat_out = mixer_out.reshape(tok_rows, model_width)
    inv_rms = lax.rsqrt(jnp.mean(flat_out * flat_out, axis=1, keepdims=True) + norm_eps)
    return (
        stream.astype(jnp.float32) + flat_out * inv_rms * gain_row.astype(jnp.float32)[None, :]
    ).astype(jnp.bfloat16)


def masked_softmax(logits, allowed):
    logits = jnp.where(allowed, logits, -jnp.inf)
    row_max = jnp.max(logits, axis=2, keepdims=True)
    exp_terms = jnp.exp(logits - row_max)
    return (exp_terms / jnp.sum(exp_terms, axis=2, keepdims=True)).astype(jnp.bfloat16)


def attend_heads(query_row, key_row, value_row, all_ids):
    tok_rows, model_width = query_row.shape
    ctx_size = lax.axis_size("ctx")
    total_len = tok_rows * ctx_size
    kv_heads = key_row.shape[1] // HEAD_A
    per_dev = model_width // HEAD_A // ctx_size
    query_split = query_row.reshape(tok_rows, ctx_size, per_dev * HEAD_A)
    key_split = jnp.repeat(
        key_row.reshape(tok_rows, kv_heads, HEAD_A), ctx_size // kv_heads, axis=1
    )
    value_split = jnp.repeat(
        value_row.reshape(tok_rows, kv_heads, HEAD_A), ctx_size // kv_heads, axis=1
    )
    query_all, key_all, value_all = (
        lax.all_to_all(query_split, "ctx", split_axis=1, concat_axis=0, tiled=True),
        lax.all_to_all(key_split, "ctx", split_axis=1, concat_axis=0, tiled=True),
        lax.all_to_all(value_split, "ctx", split_axis=1, concat_axis=0, tiled=True),
    )
    query_heads = query_all.reshape(total_len, per_dev, HEAD_A)
    key_full = key_all.reshape(total_len, HEAD_A)
    value_full = value_all.reshape(total_len, HEAD_A)
    block_rows = min(512, total_len)
    key_at = jnp.arange(total_len)
    inv_sqrt = 1.0 / math.sqrt(HEAD_A)

    def one_block(index):
        query_at = index * block_rows + jnp.arange(block_rows)
        query_block = lax.dynamic_slice_in_dim(query_heads, index * block_rows, block_rows)
        query_ids = lax.dynamic_slice_in_dim(all_ids, index * block_rows, block_rows)
        allowed = (query_ids[:, None] == all_ids[None, :]) & (query_at[:, None] >= key_at[None, :])
        logits = (
            jnp.einsum("igd,jd->igj", query_block, key_full, preferred_element_type=jnp.float32)
            * inv_sqrt
        )
        probs = masked_softmax(logits, allowed[:, None, :])
        return jnp.einsum(
            "igj,jd->igd", probs, value_full, preferred_element_type=jnp.float32
        ).astype(jnp.bfloat16)

    block_outs = lax.map(one_block, jnp.arange(total_len // block_rows))
    head_major = block_outs.reshape(total_len, 1, per_dev * HEAD_A)
    returned = lax.all_to_all(head_major, "ctx", split_axis=0, concat_axis=1, tiled=True)
    return returned.reshape(tok_rows, model_width)


def attend_part(query_row, key_row, value_row, all_ids):
    return attend_heads(query_row, key_row, value_row, all_ids)


def body(
    previous,
    fresh,
    dt_raw,
    dt_bias,
    a_log,
    b_in,
    c_in,
    skip_d,
    norm_gain,
    queries,
    keys,
    values,
    doc_ids,
):
    tok_rows = fresh.shape[0]
    handed = shifted(previous[0], "section", 1)
    stream = jnp.where(lax.axis_index("section") == 0, fresh, handed)
    all_ids = doc_ids[0]
    first_row = lax.axis_index("ctx") * tok_rows
    own_ids = lax.dynamic_slice_in_dim(all_ids, first_row, tok_rows)
    before = lax.dynamic_slice_in_dim(all_ids, jnp.maximum(first_row - 1, 0), 1)[0]
    prev_last = jnp.where(first_row > 0, before, -1)
    mixed = mixer_block(
        stream,
        dt_raw[0],
        dt_bias[0],
        a_log[0],
        b_in[0],
        c_in[0],
        skip_d[0],
        norm_gain[0],
        own_ids,
        prev_last,
    )
    attended = attend_part(queries[0], keys[0], values[0], all_ids)
    return (mixed.astype(jnp.float32) + attended.astype(jnp.float32)).astype(jnp.bfloat16)[None]


def solution(mesh):
    in_specs = (
        P("section", "ctx", None),
        P("ctx", None),
        P("section", "ctx", None),
        P("section", None),
        P("section", None),
        P("section", "ctx", None),
        P("section", "ctx", None),
        P("section", None),
        P("section", None),
        P("section", "ctx", None),
        P("section", "ctx", None),
        P("section", "ctx", None),
        P("section", None),
    )
    out_specs = P("section", "ctx", None)
    return jax.shard_map(body, mesh=mesh, in_specs=in_specs, out_specs=out_specs, check_vma=False)
```

profile of v0, /device:TPU:32, one launch (start us, length us, event | category | flops | bytes accessed | tf_op | source)
XLA Modules:
  0.0 577.5 jit_solution(1548500493419480628)
XLA Ops:
  25.5 12.9 %collective-permute-done = bf16[128,8192]{0,1:T(8,128)(2,1)} collective-permute-done((bf16[128,8192]{0,1:T(8,128)(2,1)}, bf16[128,8192]{0,1:T(8,128)(2,1)}, u32[]{:S(2)}, u32[]{:S(2)}) %collective-permute-start) | collective-permute-done | bytes 2097184 | tf_op jit(solution)/shard_map/ppermute | solution.py:33
  46.7 7.0 %all-to-all-start.1 = ((bf16[128,16,128]{2,0,1:T(8,128)(2,1)}), bf16[128,16,128]{2,0,1:T(8,128)(2,1)S(1)}, u32[]{:S(2)}, u32[]{:S(2)}) async-start(bf16[128,16,128]{2,0,1:T(8,128)(2,1)} %bitcast.29), calls=%async_computation.1 | async-start | bytes 1048576 | tf_op jit(solution)/shard_map/all_to_all | solution.py:113
  56.2 8.8 %all-to-all-done.1 = bf16[128,16,128]{2,0,1:T(8,128)(2,1)S(1)} async-done(((bf16[128,16,128]{2,0,1:T(8,128)(2,1)}), bf16[128,16,128]{2,0,1:T(8,128)(2,1)S(1)}, u32[]{:S(2)}, u32[]{:S(2)}) %all-to-all-start.1) | async-done | bytes 524320 | tf_op jit(solution)/shard_map/all_to_all | solution.py:113
  68.9 51.3 %all-to-all-done = bf16[128,16,512]{0,2,1:T(8,128)(2,1)S(1)} async-done(((bf16[128,16,512]{0,2,1:T(8,128)(2,1)}), bf16[128,16,512]{0,2,1:T(8,128)(2,1)S(1)}, u32[]{:S(2)}, u32[]{:S(2)}) %all-to-all-start) | async-done | bytes 2097184 | tf_op jit(solution)/shard_map/all_to_all | solution.py:112
  132.6 10.2 %all-to-all-done.2 = bf16[128,16,128]{2,0,1:T(8,128)(2,1)} async-done(((bf16[128,16,128]{2,0,1:T(8,128)(2,1)}), bf16[128,16,128]{2,0,1:T(8,128)(2,1)}, u32[]{:S(2)}, u32[]{:S(2)}) %all-to-all-start.2) | async-done | bytes 524320 | tf_op jit(solution)/shard_map/all_to_all | solution.py:114
  142.9 93.2 %while.25 = (s32[]{:T(128)}, bf16[4,512,4,128]{3,2,1,0:T(4,128)(2,1)S(1)}, s32[4]{0:T(128)S(1)}, s32[2048]{0:T(1024)S(1)}, s32[1,2048]{1,0:T(1,128)S(1)}, /*inde...) while((s32[]{:T(128)}, ...), condition=%wide.region_7.8_spmd.clone, body=%wide.region_4.7_spmd.clone.sunk | while | flops 2176059904 | bytes 38832316 | solution.py:137
  145.4 11.1 %fusion.74 = (f32[512,4]{0,1:T(4,128)S(1)}, f32[512,4,2048]{2,0,1:T(8,128)}) fusion(pred[512,2048]{1,0:T(8,128)(4,1)S(1)} %fusion.73, bf16[2048,128]{1,0:T(8,128)(2,1)} %get-tuple-element.360, bf16[2048,4,128]{0,2,1:T(8,128)(2,1)} %get-tuple-element.359, s32[]{:T(128)S(6)} %select_n.105), kind=kOutput, calls=%fused_computation.70.clone.1 | convolution fusion | flops 1090521088 | bytes 18882564 | tf_op jit(solution)/shard_map/while/body/eval_jaxpr/sub | solution.py:94
  156.5 8.2 %fusion.75 = bf16[1,512,4,128]{3,1,2,0:T(8,128)(2,1)S(1)} fusion(f32[512,4,2048]{2,0,1:T(8,128)} %get-tuple-element.323, f32[512,4]{0,1:T(4,128)S(1)} %get-tuple-element.324, bf16[2048,128]{1,0:T(8,128)(2,1)} %get-tuple-element.361), kind=kOutput, calls=%fused_computation.14.clone.1 | convolution fusion | flops 1082392576 | bytes 17833984 | tf_op jit(solution)/shard_map/while/body/eval_jaxpr/igj,jd->igd/dot_general | solution.py:133
  167.7 14.3 %fusion.74 = (f32[512,4]{0,1:T(4,128)S(1)}, f32[512,4,2048]{2,0,1:T(8,128)}) fusion(pred[512,2048]{1,0:T(8,128)(4,1)S(1)} %fusion.73, bf16[2048,128]{1,0:T(8,128)(2,1)} %get-tuple-element.360, bf16[2048,4,128]{0,2,1:T(8,128)(2,1)} %get-tuple-element.359, s32[]{:T(128)S(6)} %select_n.105), kind=kOutput, calls=%fused_computation.70.clone.1 | convolution fusion | flops 1090521088 | bytes 18882564 | tf_op jit(solution)/shard_map/while/body/eval_jaxpr/sub | solution.py:94
  182.0 8.2 %fusion.75 = bf16[1,512,4,128]{3,1,2,0:T(8,128)(2,1)S(1)} fusion(f32[512,4,2048]{2,0,1:T(8,128)} %get-tuple-element.323, f32[512,4]{0,1:T(4,128)S(1)} %get-tuple-element.324, bf16[2048,128]{1,0:T(8,128)(2,1)} %get-tuple-element.361), kind=kOutput, calls=%fused_computation.14.clone.1 | convolution fusion | flops 1082392576 | bytes 17833984 | tf_op jit(solution)/shard_map/while/body/eval_jaxpr/igj,jd->igd/dot_general | solution.py:133
  193.2 11.1 %fusion.74 = (f32[512,4]{0,1:T(4,128)S(1)}, f32[512,4,2048]{2,0,1:T(8,128)}) fusion(pred[512,2048]{1,0:T(8,128)(4,1)S(1)} %fusion.73, bf16[2048,128]{1,0:T(8,128)(2,1)} %get-tuple-element.360, bf16[2048,4,128]{0,2,1:T(8,128)(2,1)} %get-tuple-element.359, s32[]{:T(128)S(6)} %select_n.105), kind=kOutput, calls=%fused_computation.70.clone.1 | convolution fusion | flops 1090521088 | bytes 18882564 | tf_op jit(solution)/shard_map/while/body/eval_jaxpr/sub | solution.py:94
  204.3 8.6 %fusion.75 = bf16[1,512,4,128]{3,1,2,0:T(8,128)(2,1)S(1)} fusion(f32[512,4,2048]{2,0,1:T(8,128)} %get-tuple-element.323, f32[512,4]{0,1:T(4,128)S(1)} %get-tuple-element.324, bf16[2048,128]{1,0:T(8,128)(2,1)} %get-tuple-element.361), kind=kOutput, calls=%fused_computation.14.clone.1 | convolution fusion | flops 1082392576 | bytes 17833984 | tf_op jit(solution)/shard_map/while/body/eval_jaxpr/igj,jd->igd/dot_general | solution.py:133
  216.0 11.1 %fusion.74 = (f32[512,4]{0,1:T(4,128)S(1)}, f32[512,4,2048]{2,0,1:T(8,128)}) fusion(pred[512,2048]{1,0:T(8,128)(4,1)S(1)} %fusion.73, bf16[2048,128]{1,0:T(8,128)(2,1)} %get-tuple-element.360, bf16[2048,4,128]{0,2,1:T(8,128)(2,1)} %get-tuple-element.359, s32[]{:T(128)S(6)} %select_n.105), kind=kOutput, calls=%fused_computation.70.clone.1 | convolution fusion | flops 1090521088 | bytes 18882564 | tf_op jit(solution)/shard_map/while/body/eval_jaxpr/sub | solution.py:94
  227.0 8.6 %fusion.75 = bf16[1,512,4,128]{3,1,2,0:T(8,128)(2,1)S(1)} fusion(f32[512,4,2048]{2,0,1:T(8,128)} %get-tuple-element.323, f32[512,4]{0,1:T(4,128)S(1)} %get-tuple-element.324, bf16[2048,128]{1,0:T(8,128)(2,1)} %get-tuple-element.361), kind=kOutput, calls=%fused_computation.14.clone.1 | convolution fusion | flops 1082392576 | bytes 17833984 | tf_op jit(solution)/shard_map/while/body/eval_jaxpr/igj,jd->igd/dot_general | solution.py:133
  236.1 6.2 %reshape.281 = bf16[2048,1,512]{2,1,0:T(2,128)(2,1)} reshape(bf16[4,512,4,128]{3,2,1,0:T(4,128)(2,1)S(1)} %get-tuple-element.147) | data formatting | bytes 4194304 | tf_op jit(solution)/shard_map/reshape | solution.py:138
  242.9 14.1 %reduce.1 = bf16[2048,512]{1,0:T(8,128)(2,1)S(1)} reduce(bf16[2048,1,512]{2,1,0:T(2,128)(2,1)} %reshape.281, bf16[]{:T(256)} %broadcast.141), dimensions={1}, to_apply=%reshape.281.reduce_sub_computation | reduce | bytes 4194306 | tf_op jit(solution)/shard_map/reshape | solution.py:138
  271.2 55.1 %all-gather.1 = f32[16,1,128]{2,1,0:T(1,128)S(1)} all-gather(f32[1,1,128]{2,1,0:T(1,128)S(1)} %copy-done.24), channel_id=1, replica_groups=mesh['section'=8,'ctx'=16] {'ctx'}, dimensions={0}, use_global_device_ids=true | all-gather | bytes 8704 | tf_op jit(solution)/shard_map/all_gather | solution.py:18
  326.4 6.8 %reshape.283 = bf16[2048,1,512]{2,1,0:T(2,128)(2,1)} reshape(bf16[16,2,32768]{2,1,0:T(2,128)(2,1)S(1)} %all-to-all-done.3) | data formatting | bytes 4194304
  344.2 121.8 %all-gather.4.cloned.1.call-done = f32[2048,64,128]{2,1,0:T(8,128)} async-done(((f32[128,64,128]{2,1,0:T(8,128)}), f32[2048,64,128]{2,1,0:T(8,128)}) %all-gather.4.cloned.1.call-update) | async-done | bytes 67108880 | tf_op jit(solution)/shard_map/all_gather | solution.py:18
  466.0 89.7 %while.26 = (s32[]{:T(128)}, f32[128,64,128]{2,1,0:T(8,128)}, s32[]{:T(128)}, f32[16,128]{1,0:T(8,128)S(1)}, f32[16,128,64,128]{3,2,1,0:T(8,128)}, /*index=5*/s32[]{:T(128)}, s32[]{:T(128)}) while((s32[]{:T(128)}, f32[128,64,128]{2,1,0:T(8,128)}, s32[]{:T(128)}, f32[16,128]{1,0:T(8,128)S(1)}, f32[16,128,64,128]{3,2,1,0:T(8,128)}, ...), condition=%wide.region_2.3_spmd.clone, body=%wide.region_1.2_spmd.clone.sunk | while | flops 4194308 | bytes 12584553 | solution.py:27
  470.8 6.1 %fusion.76 = f32[128,64,128]{2,1,0:T(8,128)} fusion(f32[16,128,64,128]{3,2,1,0:T(8,128)} %get-tuple-element.384, s32[]{:T(128)} %get-tuple-element.373, f32[128,64,128]{2,1,0:T(8,128)} %get-tuple-element.374, f32[128]{0:T(128)S(1)} %dynamic-slice_bitcast_fusion.2, pred[]{:T(512)S(6)} %compare.3, pred[]{:T(512)S(6)} %lt.39), kind=kLoop, calls=%fused_computation.28.clone.1 | loop fusion | flops 4194304 | bytes 12583430 | tf_op jit(solution)/shard_map/while/body/eval_jaxpr/jit(_where)/select_n | solution.py:25
  476.9 6.1 %fusion.76 = f32[128,64,128]{2,1,0:T(8,128)} fusion(f32[16,128,64,128]{3,2,1,0:T(8,128)} %get-tuple-element.384, s32[]{:T(128)} %get-tuple-element.373, f32[128,64,128]{2,1,0:T(8,128)} %get-tuple-element.374, f32[128]{0:T(128)S(1)} %dynamic-slice_bitcast_fusion.2, pred[]{:T(512)S(6)} %compare.3, pred[]{:T(512)S(6)} %lt.39), kind=kLoop, calls=%fused_computation.28.clone.1 | loop fusion | flops 4194304 | bytes 12583430 | tf_op jit(solution)/shard_map/while/body/eval_jaxpr/jit(_where)/select_n | solution.py:25
  482.9 6.1 %fusion.76 = f32[128,64,128]{2,1,0:T(8,128)} fusion(f32[16,128,64,128]{3,2,1,0:T(8,128)} %get-tuple-element.384, s32[]{:T(128)} %get-tuple-element.373, f32[128,64,128]{2,1,0:T(8,128)} %get-tuple-element.374, f32[128]{0:T(128)S(1)} %dynamic-slice_bitcast_fusion.2, pred[]{:T(512)S(6)} %compare.3, pred[]{:T(512)S(6)} %lt.39), kind=kLoop, calls=%fused_computation.28.clone.1 | loop fusion | flops 4194304 | bytes 12583430 | tf_op jit(solution)/shard_map/while/body/eval_jaxpr/jit(_where)/select_n | solution.py:25
  501.1 6.1 %fusion.76 = f32[128,64,128]{2,1,0:T(8,128)} fusion(f32[16,128,64,128]{3,2,1,0:T(8,128)} %get-tuple-element.384, s32[]{:T(128)} %get-tuple-element.373, f32[128,64,128]{2,1,0:T(8,128)} %get-tuple-element.374, f32[128]{0:T(128)S(1)} %dynamic-slice_bitcast_fusion.2, pred[]{:T(512)S(6)} %compare.3, pred[]{:T(512)S(6)} %lt.39), kind=kLoop, calls=%fused_computation.28.clone.1 | loop fusion | flops 4194304 | bytes 12583430 | tf_op jit(solution)/shard_map/while/body/eval_jaxpr/jit(_where)/select_n | solution.py:25
  (158 shorter events, 158.3 us)
Async XLA Ops:
  6.5 6.1 %copy-start.13 = (s32[1,2048]{1,0:T(1,128)S(1)}, s32[1,2048]{1,0:T(1,128)}, u32[]{:S(2)}) copy-start(s32[1,2048]{1,0:T(1,128)} %param.29) | copy-start | bytes 24580
  6.5 10.1 %copy-start.26 = (f32[1,128]{1,0:T(1,128)S(1)}, f32[1,128]{1,0:T(1,128)}, u32[]{:S(2)}) copy-start(f32[1,128]{1,0:T(1,128)} %param.21) | copy-start | bytes 1540
  6.5 10.1 %copy-start.22 = (f32[1,128]{1,0:T(1,128)S(1)}, f32[1,128]{1,0:T(1,128)}, u32[]{:S(2)}) copy-start(f32[1,128]{1,0:T(1,128)} %param.20) | copy-start | bytes 1540
  6.5 10.1 %copy-start.10 = (f32[1,128,128]{2,1,0:T(8,128)S(1)}, f32[1,128,128]{2,1,0:T(8,128)}, u32[]{:S(2)}) copy-start(f32[1,128,128]{2,1,0:T(8,128)} %param.19) | copy-start | bytes 196612
  6.5 12.3 %copy-start.14 = (bf16[1,128,1024]{2,1,0:T(8,128)(2,1)S(1)}, bf16[1,128,1024]{2,1,0:T(8,128)(2,1)}, u32[]{:S(2)}) copy-start(bf16[1,128,1024]{2,1,0:T(8,128)(2,1)} %param.22) | copy-start | bytes 786436
  6.5 459.5 %all-gather.4.cloned.1.call-start = ((), (), s32[]{:S(2)}) async-start(), calls=%async_computation.4 | async-start | bytes 71303168 | tf_op jit(solution)/shard_map/all_gather | solution.py:18
  10.8 27.7 %collective-permute-start = (bf16[128,8192]{0,1:T(8,128)(2,1)}, bf16[128,8192]{0,1:T(8,128)(2,1)}, u32[]{:S(2)}, u32[]{:S(2)}) collective-permute-start(bf16[128,8192]{0,1:T(8,128)(2,1)} %bitcast), channel_id=1, source_target_pairs={{0,16},{16,32},{32,48},{48,64},{64,80},{80,96},{96,112},{1,17},{17... | collective-permute-start | bytes 6291464 | tf_op jit(solution)/shard_map/ppermute | solution.py:33
  14.0 11.5 %copy-start.20 = (s32[1,128]{1,0:T(1,128)}, s32[1,128]{1,0:T(1,128)S(1)}, u32[]{:S(2)}) copy-start(s32[1,128]{1,0:T(1,128)S(1)} %get-tuple-element.235) | copy-start | bytes 1540
  44.8 9.0 %copy-start.7 = (bf16[1,128,8192]{2,1,0:T(8,128)(2,1)S(1)}, bf16[1,128,8192]{2,1,0:T(8,128)(2,1)}, u32[]{:S(2)}) copy-start(bf16[1,128,8192]{2,1,0:T(8,128)(2,1)} %param.26) | copy-start | bytes 6291460
  46.7 18.3 %all-to-all-start.1 = ((bf16[128,16,128]{2,0,1:T(8,128)(2,1)}), bf16[128,16,128]{2,0,1:T(8,128)(2,1)S(1)}, u32[]{:S(2)}, u32[]{:S(2)}) async-start(bf16[128,16,128]{2,0,1:T(8,128)(2,1)} %bitcast.29), calls=%async_computation.1 | async-start | bytes 1048576 | tf_op jit(solution)/shard_map/all_to_all | solution.py:113
  53.8 15.0 %copy-start.16 = (bf16[1,128,1024]{2,1,0:T(8,128)(2,1)S(1)}, bf16[1,128,1024]{2,1,0:T(8,128)(2,1)}, u32[]{:S(2)}) copy-start(bf16[1,128,1024]{2,1,0:T(8,128)(2,1)} %param.28) | copy-start | bytes 786436
  65.0 55.1 %all-to-all-start = ((bf16[128,16,512]{0,2,1:T(8,128)(2,1)}), bf16[128,16,512]{0,2,1:T(8,128)(2,1)S(1)}, u32[]{:S(2)}, u32[]{:S(2)}) async-start(bf16[128,16,512]{0,2,1:T(8,128)(2,1)} %bitcast.158), calls=%async_computation | async-start | bytes 4194304 | tf_op jit(solution)/shard_map/all_to_all | solution.py:112
  121.1 21.8 %all-to-all-start.2 = ((bf16[128,16,128]{2,0,1:T(8,128)(2,1)}), bf16[128,16,128]{2,0,1:T(8,128)(2,1)}, u32[]{:S(2)}, u32[]{:S(2)}) async-start(bf16[128,16,128]{2,0,1:T(8,128)(2,1)} %bitcast.33), calls=%async_computation.2 | async-start | bytes 1048576 | tf_op jit(solution)/shard_map/all_to_all | solution.py:114
  128.3 14.6 %copy-start.6 = (bf16[4,512,4,128]{3,2,1,0:T(4,128)(2,1)S(1)}, bf16[4,512,4,128]{3,2,1,0:T(4,128)(2,1)}, u32[]{:S(2)}) copy-start(bf16[4,512,4,128]{3,2,1,0:T(4,128)(2,1)} %custom-call.1) | copy-start | bytes 6291460
  257.0 7.2 %copy-start.9 = (f32[128,128]{1,0:T(8,128)S(1)}, f32[128,128]{1,0:T(8,128)}, u32[]{:S(2)}) copy-start(f32[128,128]{1,0:T(8,128)} %copy-done.8) | copy-start | bytes 196612
  257.0 7.3 %copy-start.17 = (bf16[1,128,1024]{2,1,0:T(8,128)(2,1)S(1)}, bf16[1,128,1024]{2,1,0:T(8,128)(2,1)}, u32[]{:S(2)}) copy-start(bf16[1,128,1024]{2,1,0:T(8,128)(2,1)} %param.23) | copy-start | bytes 786436
  257.0 7.4 %copy-start.18 = (f32[128,128]{1,0:T(8,128)S(1)}, f32[128,128]{1,0:T(8,128)}, u32[]{:S(2)}) copy-start(f32[128,128]{1,0:T(8,128)} %get-tuple-element.238) | copy-start | bytes 196612
  257.0 7.4 %copy-start.5 = (bf16[16,8,8,128]{3,2,1,0:T(8,128)(2,1)S(1)}, bf16[16,8,8,128]{3,2,1,0:T(8,128)(2,1)}, u32[]{:S(2)}) copy-start(bf16[16,8,8,128]{3,2,1,0:T(8,128)(2,1)} %copy-done.4) | copy-start | bytes 786436
  259.8 7.1 %copy-start.11 = (f32[1,128,128]{2,1,0:T(8,128)S(1)}, f32[1,128,128]{2,1,0:T(8,128)}, u32[]{:S(2)}) copy-start(f32[1,128,128]{2,1,0:T(8,128)} %param.19) | copy-start | bytes 196612
  259.8 7.1 %copy-start.23 = (f32[1,128]{1,0:T(1,128)S(1)}, f32[1,128]{1,0:T(1,128)}, u32[]{:S(2)}) copy-start(f32[1,128]{1,0:T(1,128)} %param.20) | copy-start | bytes 1540
  259.8 7.3 %copy-start.19 = (bf16[1,8192]{1,0:T(2,128)(2,1)S(1)}, bf16[1,8192]{1,0:T(2,128)(2,1)}, u32[]{:S(2)}) copy-start(bf16[1,8192]{1,0:T(2,128)(2,1)} %param.25) | copy-start | bytes 49156
  259.8 7.3 %copy-start.21 = (s32[1,128]{1,0:T(1,128)S(1)}, s32[1,128]{1,0:T(1,128)}, u32[]{:S(2)}) copy-start(s32[1,128]{1,0:T(1,128)} %copy-done.20) | copy-start | bytes 1540
  259.8 66.6 %all-to-all-start.3 = ((bf16[16,2,32768]{2,1,0:T(2,128)(2,1)}), bf16[16,2,32768]{2,1,0:T(2,128)(2,1)S(1)}, u32[]{:S(2)}, u32[]{:S(2)}) async-start(bf16[16,2,32768]{2,1,0:T(2,128)(2,1)} %reshape.282), calls=%async_computation.3 | async-start | bytes 4194304 | tf_op jit(solution)/shard_map/all_to_all | solution.py:139
  264.2 7.1 %copy-start.24 = (f32[1,1,128]{2,1,0:T(1,128)S(1)}, f32[1,1,128]{2,1,0:T(1,128)}, u32[]{:S(2)}) copy-start(f32[1,1,128]{2,1,0:T(1,128)} %get-tuple-element.241) | copy-start | bytes 1540
  (9 other events, 19.9 us)
Sparse Core Ops, SparseCore 0:
  44.9 421.0 all-gather.3
where the time goes:
time: 580 us; the launch traced here: 577 us
  waiting for transfers between devices  205 us (35%)
  other arithmetic  128 us (22%)
  matrix products  89.3 us (15%)
  local copies, waits for them, and re-layouts  59.3 us (10%)
  blocking collectives  55.1 us (10%)
  starting transfers between devices  21.5 us (4%)
  between operations  16.6 us (3%)
    all_gather x1, waiting for transfers between devices, entering(): pieces = jax.tree.map(lambda part: lax.all_gather(part, axis), value)  122 us
    select_n x15, other arithmetic, lap(): jnp.where(position < mine, new, old)  89.6 us
    all_gather x1, blocking collectives, entering(): pieces = jax.tree.map(lambda part: lax.all_gather(part, axis), value)  55.1 us
    all_to_all x1, waiting for transfers between devices, attend_heads(): lax.all_to_all(query_split, 'ctx', split_axis=1, concat_axis=0, tiled=True)  51.3 us
    sub x4, matrix products, masked_softmax(): exp_terms = jnp.exp(logits - row_max)  47.6 us
    dot_general x4, matrix products, one_block(): jnp.einsum('igj,jd->igd', probs, value_full, preferred_element_type=jnp.f...  33.7 us
    unnamed x63, local copies, waits for them, and re-layouts  24.7 us
    reshape x1, other arithmetic, attend_heads(): head_major = block_outs.reshape(total_len, 1, per_dev * HEAD_A)  14.1 us
  transfers between devices with their start and end apart: 6, of which 5 were waited for; matrix products, arithmetic and copies ran while one was open for 28% of the time, Pallas kernels for 0%

commit v1 on v0

v1 whole, which is shorter than its diff:
```python
import math

import jax
import jax.numpy as jnp
from jax import lax
from jax.sharding import PartitionSpec as P

HEAD_A = 128
STATE = 128
GROUPS = 8
BLOCK = 128
MOST_DOC = 512
Q_BLOCK = 256


norm_eps = 1e-05


def shifted(value, axis, by):
    peers = lax.axis_size(axis)
    pairs = [(i, i + by) for i in range(peers) if 0 <= i + by < peers]
    return lax.ppermute(value, axis, pairs)


def to_heads(row, chunks):
    tok_rows = row.shape[0]
    width = row.shape[1] // chunks
    moved = lax.all_to_all(row.reshape(tok_rows, chunks, width), "ctx", split_axis=1, concat_axis=0, tiled=True)
    return moved.reshape(tok_rows * chunks, width)


def mixer_heads(x_h, dt_h, bias_h, alog_h, b_g, c_g, skip_h, all_ids):
    total, heads, head_dim = x_h.shape
    nblk = total // BLOCK
    step = jax.nn.softplus(dt_h + bias_h[None, :])
    log_rate = -step * jnp.exp(alog_h)[None, :]
    log_cum = jnp.cumsum(log_rate.reshape(nblk, BLOCK, heads), axis=1)
    lc = log_cum.transpose(0, 2, 1)
    st = step.reshape(nblk, BLOCK, heads).transpose(0, 2, 1)
    ids = all_ids.reshape(nblk, BLOCK)
    xb = x_h.reshape(nblk, BLOCK, heads, head_dim)
    bb = b_g.reshape(nblk, BLOCK, STATE)
    cb_in = c_g.reshape(nblk, BLOCK, STATE)
    rows_at = jnp.arange(BLOCK)
    same_doc = (ids[:, :, None] == ids[:, None, :]) & (rows_at[:, None] >= rows_at[None, :])[None]
    inner_cb = jnp.einsum("bin,bjn->bij", cb_in, bb, preferred_element_type=jnp.float32)
    decay = jnp.where(same_doc[:, None], jnp.exp(lc[:, :, :, None] - lc[:, :, None, :]), 0.0)
    intra_w = (decay * inner_cb[:, None] * st[:, :, None, :]).astype(jnp.bfloat16)
    local_out = jnp.einsum("bhij,bjhp->bihp", intra_w, xb, preferred_element_type=jnp.float32)
    last_id = ids[:, -1]
    end_scale = (
        jnp.exp(lc[:, :, -1:] - lc) * st * (ids == last_id[:, None]).astype(jnp.float32)[:, None, :]
    )
    end_w = (end_scale[:, :, :, None] * bb.astype(jnp.float32)[:, None]).astype(jnp.bfloat16)
    block_state = jnp.einsum("bhjn,bjhp->bhpn", end_w, xb, preferred_element_type=jnp.float32)
    prev_last = jnp.concatenate([jnp.full((1,), -1, ids.dtype), last_id[:-1]])
    edge_match = (ids[:, 0] == prev_last).astype(jnp.float32)
    block_gain = jnp.exp(lc[:, :, -1]) * (ids[:, 0] == last_id).astype(jnp.float32)[:, None]
    block_gain = block_gain * edge_match[:, None]
    carries = [jnp.zeros_like(block_state[0])]
    for b in range(nblk - 1):
        carries.append(block_gain[b][:, None, None] * carries[-1] + block_state[b])
    carry_bf = jnp.stack(carries).astype(jnp.bfloat16)
    carried = jnp.einsum("bin,bhpn->bihp", cb_in, carry_bf, preferred_element_type=jnp.float32)
    edge_valid = (ids == prev_last[:, None]).astype(jnp.float32)
    scale = jnp.exp(log_cum) * edge_valid[:, :, None]
    carried = carried * scale[:, :, :, None]
    mixer_out = local_out + carried + skip_h[None, None, :, None] * xb.astype(jnp.float32)
    return mixer_out.reshape(total, heads * head_dim)


def attend_heads(q_h, k_h, v_h, all_ids):
    total, qpd, _ = q_h.shape
    inv_sqrt = 1.0 / math.sqrt(HEAD_A)
    q_blk = min(Q_BLOCK, total)
    window = min(q_blk + MOST_DOC, total)
    outs = []
    for i in range(total // q_blk):
        q0 = i * q_blk
        k0 = max(0, min(q0 + q_blk - window, total - window))
        qb = q_h[q0:q0 + q_blk]
        kb = k_h[k0:k0 + window]
        vb = v_h[k0:k0 + window]
        q_at = q0 + jnp.arange(q_blk)
        k_at = k0 + jnp.arange(window)
        allowed = (all_ids[q0:q0 + q_blk][:, None] == all_ids[k0:k0 + window][None, :]) & (
            q_at[:, None] >= k_at[None, :]
        )
        logits = jnp.einsum("igd,jd->igj", qb, kb, preferred_element_type=jnp.float32) * inv_sqrt
        logits = jnp.where(allowed[:, None, :], logits, -jnp.inf)
        row_max = jnp.max(logits, axis=2, keepdims=True)
        exp_terms = jnp.exp(logits - row_max)
        probs = (exp_terms / jnp.sum(exp_terms, axis=2, keepdims=True)).astype(jnp.bfloat16)
        outs.append(
            jnp.einsum("igj,jd->igd", probs, vb, preferred_element_type=jnp.float32).astype(jnp.bfloat16)
        )
    return jnp.concatenate(outs, axis=0).reshape(total, qpd * HEAD_A)


def body(
    previous,
    fresh,
    dt_raw,
    dt_bias,
    a_log,
    b_in,
    c_in,
    skip_d,
    norm_gain,
    queries,
    keys,
    values,
    doc_ids,
):
    tok_rows, width = fresh.shape
    nctx = lax.axis_size("ctx")
    me = lax.axis_index("ctx")
    total = tok_rows * nctx
    part = width // nctx
    mamba_heads = dt_raw.shape[2]
    heads_dev = mamba_heads // nctx
    head_dim = width // mamba_heads
    kv_heads = keys.shape[2] // HEAD_A
    qpd = part // HEAD_A

    q_h = to_heads(queries[0], nctx).reshape(total, qpd, HEAD_A)
    kvbc = jnp.stack(
        [
            keys[0].reshape(tok_rows, kv_heads, HEAD_A),
            values[0].reshape(tok_rows, kv_heads, HEAD_A),
            b_in[0].reshape(tok_rows, GROUPS, STATE),
            c_in[0].reshape(tok_rows, GROUPS, STATE),
        ],
        axis=2,
    )
    kvbc = jnp.repeat(kvbc, nctx // kv_heads, axis=1).reshape(tok_rows, nctx * 4 * HEAD_A)
    kvbc_h = to_heads(kvbc, nctx).reshape(total, 4, HEAD_A)
    k_h, v_h, b_g, c_g = kvbc_h[:, 0], kvbc_h[:, 1], kvbc_h[:, 2], kvbc_h[:, 3]
    dt_h = to_heads(dt_raw[0], nctx)

    handed = shifted(previous[0], "section", 1)
    stream = jnp.where(lax.axis_index("section") == 0, fresh, handed)
    x_h = to_heads(stream, nctx)

    all_ids = doc_ids[0]
    bias_h = lax.dynamic_slice_in_dim(dt_bias[0], me * heads_dev, heads_dev)
    alog_h = lax.dynamic_slice_in_dim(a_log[0], me * heads_dev, heads_dev)
    skip_h = lax.dynamic_slice_in_dim(skip_d[0], me * heads_dev, heads_dev)
    gain_h = lax.dynamic_slice_in_dim(norm_gain[0], me * part, part)

    attended = attend_heads(q_h, k_h, v_h, all_ids)

    mixer_out = mixer_heads(
        x_h.reshape(total, heads_dev, head_dim), dt_h, bias_h, alog_h, b_g, c_g, skip_h, all_ids
    )
    sq_part = jnp.sum(mixer_out * mixer_out, axis=1, keepdims=True)
    mean_sq = lax.psum(sq_part, "ctx") / width
    inv_rms = lax.rsqrt(mean_sq + norm_eps)
    mixed = (
        x_h.astype(jnp.float32) + mixer_out * inv_rms * gain_h.astype(jnp.float32)[None, :]
    ).astype(jnp.bfloat16)
    out_h = (mixed.astype(jnp.float32) + attended.astype(jnp.float32)).astype(jnp.bfloat16)
    returned = lax.all_to_all(
        out_h.reshape(total, 1, part), "ctx", split_axis=0, concat_axis=1, tiled=True
    )
    return returned.reshape(tok_rows, width)[None]


def solution(mesh):
    in_specs = (
        P("section", "ctx", None),
        P("ctx", None),
        P("section", "ctx", None),
        P("section", None),
        P("section", None),
        P("section", "ctx", None),
        P("section", "ctx", None),
        P("section", None),
        P("section", None),
        P("section", "ctx", None),
        P("section", "ctx", None),
        P("section", "ctx", None),
        P("section", None),
    )
    out_specs = P("section", "ctx", None)
    return jax.shard_map(body, mesh=mesh, in_specs=in_specs, out_specs=out_specs, check_vma=False)
```

time: 580 us -> 349 us (0.60)
  waiting for transfers between devices: 205 us -> 43 us
  other arithmetic: 128 us -> 41.4 us
  local copies, waits for them, and re-layouts: 59.3 us -> 101 us
  matrix products: 89.3 us -> 70.6 us
  between operations: 16.6 us -> 0.74 us
  blocking collectives: 55.1 us -> 61.2 us
    all_gather x1 -> x0, waiting for transfers between devices: 122 us -> none  [entering(): pieces = jax.tree.map(lambda part: lax.all_gather(part, axis), value)]
    select_n x15 -> x0, other arithmetic: 89.6 us -> none  [lap(): jnp.where(position < mine, new, old)]
    all_gather x1 -> x0, blocking collectives: 55.1 us -> none  [entering(): pieces = jax.tree.map(lambda part: lax.all_gather(part, axis), value)]
    psum x0 -> x1, blocking collectives: none -> 36.8 us  [body(): mean_sq = lax.psum(sq_part, 'ctx') / width]
    all_to_all x4, waiting for transfers between devices: 70.3 us -> 43 us  [to_heads(): lax.all_to_all(row.reshape(tok_rows, chunks, width), 'ctx', split_axis=1,...]
    all_to_all x0 -> x1, blocking collectives: none -> 24.5 us  [body(): lax.all_to_all(out_h.reshape(total, 1, part), 'ctx', split_axis=0, concat...]
    slice x1 -> x18, local copies, waits for them, and re-layouts: 0.59 us -> 17.8 us  [the longest x9 12.8 us: attend_heads(): qb = q_h[q0:q0 + q_blk]]
    reshape x1 -> x0, other arithmetic: 14.1 us -> none  [attend_heads(): head_major = block_outs.reshape(total_len, 1, per_dev * HEAD_A)]
  transfers between devices with their start and end apart: 6 -> 5, of which waited for: 5 -> 3; matrix products, arithmetic and copies ran while one was open for 28% -> 37% of each run, Pallas kernels for 0% -> 0%
where the time goes in v1:
time: 349 us; the launch traced here: 343 us
  local copies, waits for them, and re-layouts  101 us (29%)
  matrix products  70.6 us (20%)
  blocking collectives  61.2 us (18%)
  waiting for transfers between devices  43 us (12%)
  other arithmetic  41.4 us (12%)
  starting transfers between devices  24.4 us (7%)
    all_to_all x4, waiting for transfers between devices, to_heads(): lax.all_to_all(row.reshape(tok_rows, chunks, width), 'ctx', split_axis=1,...  43 us
    psum x1, blocking collectives, body(): mean_sq = lax.psum(sq_part, 'ctx') / width  36.8 us
    sub x8, matrix products, attend_heads(): exp_terms = jnp.exp(logits - row_max)  33.9 us
    unnamed x106, local copies, waits for them, and re-layouts  28.5 us
    all_to_all x1, blocking collectives, body(): lax.all_to_all(out_h.reshape(total, 1, part), 'ctx', split_axis=0, concat...  24.5 us
    all_to_all x4, starting transfers between devices, to_heads(): lax.all_to_all(row.reshape(tok_rows, chunks, width), 'ctx', split_axis=1,...  22.5 us
    dot_general x8, matrix products, attend_heads(): jnp.einsum('igj,jd->igd', probs, vb, preferred_element_type=jnp.float32)  22.1 us
    reshape x2, local copies, waits for them, and re-layouts, mixer_heads(): return mixer_out.reshape(total, heads * head_dim)  14.4 us
  transfers between devices with their start and end apart: 5, of which 3 were waited for; matrix products, arithmetic and copies ran while one was open for 37% of the time, Pallas kernels for 0%

profile of v1, /device:TPU:32, one launch (start us, length us, event | category | flops | bytes accessed | tf_op | source)
XLA Modules:
  0.0 342.8 jit_solution(9871857477045259311)
XLA Ops:
  1.7 7.0 %all-to-all-start.1 = ((f32[128,16,8]{0,2,1:T(8,128)}), f32[128,16,8]{0,2,1:T(8,128)S(1)}, u32[]{:S(2)}, u32[]{:S(2)}) async-start(f32[128,16,8]{0,2,1:T(8,128)} %bitcast.8), calls=%async_computation.1 | async-start | bytes 131072 | tf_op jit(solution)/shard_map/all_to_all | solution.py:28
  19.1 7.2 %all-to-all-start.2 = ((bf16[128,16,512]{0,2,1:T(8,128)(2,1)}), bf16[128,16,512]{0,2,1:T(8,128)(2,1)S(1)}, u32[]{:S(2)}, u32[]{:S(2)}) async-start(bf16[128,16,512]{0,2,1:T(8,128)(2,1)} %bitcast.366), calls=%async_computation.2 | async-start | bytes 4194304 | tf_op jit(solution)/shard_map/all_to_all | solution.py:28
  37.5 22.9 %all-to-all-done.2 = bf16[128,16,512]{0,2,1:T(8,128)(2,1)S(1)} async-done(((bf16[128,16,512]{0,2,1:T(8,128)(2,1)}), bf16[128,16,512]{0,2,1:T(8,128)(2,1)S(1)}, u32[]{:S(2)}, u32[]{:S(2)}) %all-to-all-start.2) | async-done | bytes 2097184 | tf_op jit(solution)/shard_map/all_to_all | solution.py:28
  60.4 4.4 %all-to-all-start.3 = ((bf16[128,16,512]{2,0,1:T(8,128)(2,1)}), bf16[128,16,512]{2,0,1:T(8,128)(2,1)}, u32[]{:S(2)}, u32[]{:S(2)}) async-start(bf16[128,16,512]{2,0,1:T(8,128)(2,1)} %copy.368), calls=%async_computation.3 | async-start | bytes 4194304 | tf_op jit(solution)/shard_map/all_to_all | solution.py:28
  78.4 4.3 %copy.358 = bf16[16,128,1,512]{1,0,3,2:T(8,128)(2,1)} copy(bf16[16,128,1,512]{1,3,0,2:T(8,128)(2,1)} %bitcast.365) | data formatting | bytes 4194304 | tf_op jit(solution)/shard_map/all_to_all | solution.py:28
  82.7 4.2 %reshape_reshape.4 = bf16[2048,4,128]{0,2,1:T(8,128)(2,1)} reshape(bf16[16,128,1,512]{1,0,3,2:T(8,128)(2,1)} %copy.358) | data formatting | bytes 4194304 | tf_op jit(solution)/shard_map/reshape;reshape | solution.py:137
  89.0 10.7 %all-to-all-done.3 = bf16[128,16,512]{2,0,1:T(8,128)(2,1)} async-done(((bf16[128,16,512]{2,0,1:T(8,128)(2,1)}), bf16[128,16,512]{2,0,1:T(8,128)(2,1)}, u32[]{:S(2)}, u32[]{:S(2)}) %all-to-all-start.3) | async-done | bytes 2097184 | tf_op jit(solution)/shard_map/all_to_all | solution.py:28
  118.9 4.4 %fusion.188 = (f32[256,4]{0,1:T(4,128)}, f32[256,4,768]{0,2,1:T(8,128)}) fusion(pred[256,768]{0,1:T(8,128)(4,1)} %get-tuple-element.67, bf16[256,4,128]{2,1,0:T(4,128)(2,1)S(1)} %copy-done.18, bf16[2048,4,128]{0,2,1:T(8,128)(2,1)} %reshape_reshape.4), kind=kOutput, calls=%fused_computation.279 | convolution fusion | flops 204473088 | bytes 3805184 | tf_op jit(solution)/shard_map/sub | solution.py:92
  123.3 4.6 %fusion.193 = (f32[256,4]{0,1:T(4,128)}, f32[256,4,768]{0,2,1:T(8,128)}) fusion(pred[256,768]{0,1:T(8,128)(4,1)} %get-tuple-element.66, bf16[256,4,128]{2,1,0:T(4,128)(2,1)} %slice.360, bf16[2048,4,128]{0,2,1:T(8,128)(2,1)} %reshape_reshape.4), kind=kOutput, calls=%fused_computation.280 | convolution fusion | flops 204473088 | bytes 3805184 | tf_op jit(solution)/shard_map/sub | solution.py:92
  127.9 4.4 %fusion.198 = (f32[256,4]{0,1:T(4,128)}, f32[256,4,768]{0,2,1:T(8,128)}) fusion(pred[256,768]{0,1:T(8,128)(4,1)} %compare_and_fusion.5, bf16[256,4,128]{2,1,0:T(4,128)(2,1)S(1)} %copy-done.17, bf16[2048,4,128]{0,2,1:T(8,128)(2,1)} %reshape_reshape.4), kind=kOutput, calls=%fused_computation.281 | convolution fusion | flops 204473088 | bytes 3805184 | tf_op jit(solution)/shard_map/sub | solution.py:92
  132.3 4.5 %fusion.203 = (f32[256,4]{0,1:T(4,128)}, f32[256,4,768]{0,2,1:T(8,128)}) fusion(pred[256,768]{0,1:T(8,128)(4,1)} %get-tuple-element.90, bf16[256,4,128]{2,1,0:T(4,128)(2,1)} %slice.374, bf16[2048,4,128]{0,2,1:T(8,128)(2,1)} %reshape_reshape.4), kind=kOutput, calls=%fused_computation.282 | convolution fusion | flops 204473088 | bytes 3805184 | tf_op jit(solution)/shard_map/sub | solution.py:92
  140.7 4.4 %fusion.213 = (f32[256,4]{0,1:T(4,128)}, f32[256,4,768]{0,2,1:T(8,128)}) fusion(pred[256,768]{0,1:T(8,128)(4,1)} %get-tuple-element.88, bf16[256,4,128]{2,1,0:T(4,128)(2,1)S(1)} %slice.390, bf16[2048,4,128]{0,2,1:T(8,128)(2,1)} %reshape_reshape.4), kind=kOutput, calls=%fused_computation.284 | convolution fusion | flops 204473088 | bytes 3805184 | tf_op jit(solution)/shard_map/sub | solution.py:92
  183.2 5.4 %copy.397 = f32[2048,1,512]{2,0,1:T(8,128)} copy(f32[2048,1,512]{0,2,1:T(8,128)} %bitcast.362) | data formatting | bytes 8388608 | tf_op jit(solution)/shard_map/convert_element_type | solution.py:162
  190.0 9.5 %all-to-all-done = bf16[128,16,512]{0,2,1:T(8,128)(2,1)S(1)} async-done(((bf16[128,16,512]{0,2,1:T(8,128)(2,1)}), bf16[128,16,512]{0,2,1:T(8,128)(2,1)S(1)}, u32[]{:S(2)}, u32[]{:S(2)}) %all-to-all-start) | async-done | bytes 2097184 | tf_op jit(solution)/shard_map/all_to_all | solution.py:28
  199.5 6.5 %fusion.9 = f32[16,8,64,128]{3,2,1,0:T(8,128)S(1)} fusion(bf16[16,128,8,64]{1,3,2,0:T(8,128)(2,1)S(1)} %bitcast.360, f32[16,128,128]{2,1,0:T(8,128)} %convert_element_type.149, f32[16,8,128]{2,1,0:T(8,128)S(1)} %get-tuple-element.42), kind=kOutput, calls=%fused_computation.11 | convolution fusion | flops 272629760 | bytes 7405568 | tf_op jit(solution)/shard_map/bhjn,bjhp->bhpn/dot_general | solution.py:55
  223.9 6.0 %multiply_reduce_fusion = (f32[16,128]{1,0:T(8,128)S(1)}, f32[16,128,8,64]{1,3,2,0:T(8,128)}) fusion(bf16[16,128,8,64]{1,3,2,0:T(8,128)(2,1)S(1)} %bitcast.361, f32[8]{0:T(128)S(1)} %copy-done.37, f32[16,128,8,64]{1,3,2,0:T(8,128)S(1)} %fusion.225, f32[16,128,8]{1,2,0:T(8,128)S(1)} %copy-done.20, f32[16,8,128]{2,1,0:T(8,128)S(1)} %copy-done.21, ...), kind=kOutput, calls=%fused_computation.17 | convolution fusion | flops 286259200 | bytes 12001312 | tf_op jit(solution)/shard_map/bhij,bjhp->bihp/dot_general | solution.py:49
  230.0 6.9 %copy.411 = f32[16,128,8,64]{3,2,1,0:T(8,128)} copy(f32[16,128,8,64]{1,3,2,0:T(8,128)} %get-tuple-element.86) | data formatting | bytes 8388608 | tf_op jit(solution)/shard_map/reshape | solution.py:69
  236.9 7.5 %reshape.754 = f32[2048,1,512]{2,0,1:T(8,128)} reshape(f32[16,128,8,64]{3,2,1,0:T(8,128)} %copy.411) | data formatting | bytes 8388608 | tf_op jit(solution)/shard_map/reshape | solution.py:69
  244.4 36.8 %psum.7 = f32[2048,1]{0,1:T(1,128)S(1)} all-reduce(f32[2048,1]{0,1:T(1,128)S(1)} %bitcast.392), channel_id=1, replica_groups=mesh['section'=8,'ctx'=16] {'ctx'}, use_global_device_ids=true, to_apply=%region_2.3 | all-reduce | flops 2048 | bytes 16384 | tf_op jit(solution)/shard_map/psum | solution.py:157
  283.5 5.3 %copy.353 = f32[16,128,1,512]{3,1,0,2:T(8,128)} copy(f32[16,128,1,512]{1,3,0,2:T(8,128)} %bitcast_convert_fusion) | data formatting | bytes 8388608 | tf_op jit(solution)/shard_map/convert_element_type | solution.py:160
  288.9 5.3 %add_convert_fusion = bf16[2048,1,512]{2,0,1:T(8,128)(2,1)S(1)} fusion(f32[2048,1,512]{2,0,1:T(8,128)} %copy.397, f32[2048,1,512]{2,0,1:T(8,128)} %reshape.754, f32[16,128,1,512]{3,1,0,2:T(8,128)} %copy.353, f32[512]{0:T(512)S(1)} %bitcast.391, f32[2048]{0:T(1024)S(1)} %bitcast.389), kind=kLoop, calls=%fused_computation.16 | loop fusion | flops 7340032 | bytes 14690304 | tf_op jit(solution)/shard_map/convert_element_type | solution.py:162
  297.8 4.5 %reshape.780 = bf16[16,2,32768]{2,1,0:T(2,128)(2,1)} reshape(bf16[2048,512]{1,0:T(8,128)(2,1)} %reduce.51) | data formatting | bytes 4194304
  302.3 24.5 %all_to_all.75 = bf16[16,2,32768]{2,1,0:T(2,128)(2,1)S(1)} all-to-all(bf16[16,2,32768]{2,1,0:T(2,128)(2,1)} %reshape.780), channel_id=1, replica_groups=mesh['section'=8,'ctx'=16] {'ctx'}, dimensions={0} | all-to-all | bytes 4194304 | tf_op jit(solution)/shard_map/all_to_all | solution.py:163
  326.8 6.8 %reshape.781 = bf16[2048,1,512]{2,1,0:T(2,128)(2,1)} reshape(bf16[16,2,32768]{2,1,0:T(2,128)(2,1)S(1)} %all_to_all.75) | data formatting | bytes 4194304
  (201 shorter events, 134.0 us)
Async XLA Ops:
  0.0 64.8 %copy-start = (f32[1,128]{1,0:T(1,128)S(1)}, f32[1,128]{1,0:T(1,128)}, u32[]{:S(2)}) copy-start(f32[1,128]{1,0:T(1,128)} %param.20) | copy-start | bytes 1540
  0.0 14.7 %copy-start.9 = (s32[1,2048]{1,0:T(1,128)S(1)}, s32[1,2048]{1,0:T(1,128)}, u32[]{:S(2)}) copy-start(s32[1,2048]{1,0:T(1,128)} %param.25) | copy-start | bytes 24580
  0.0 15.2 %copy-start.11 = (bf16[1,128,1024]{2,1,0:T(8,128)(2,1)S(1)}, bf16[1,128,1024]{2,1,0:T(8,128)(2,1)}, u32[]{:S(2)}) copy-start(bf16[1,128,1024]{2,1,0:T(8,128)(2,1)} %param.23) | copy-start | bytes 786436
  0.0 15.3 %copy-start.12 = (bf16[1,128,1024]{2,1,0:T(8,128)(2,1)S(1)}, bf16[1,128,1024]{2,1,0:T(8,128)(2,1)}, u32[]{:S(2)}) copy-start(bf16[1,128,1024]{2,1,0:T(8,128)(2,1)} %param.24) | copy-start | bytes 786436
  0.0 15.4 %copy-start.13 = (bf16[1,128,1024]{2,1,0:T(8,128)(2,1)S(1)}, bf16[1,128,1024]{2,1,0:T(8,128)(2,1)}, u32[]{:S(2)}) copy-start(bf16[1,128,1024]{2,1,0:T(8,128)(2,1)} %param.18) | copy-start | bytes 786436
  0.0 15.4 %copy-start.14 = (bf16[1,128,1024]{2,1,0:T(8,128)(2,1)S(1)}, bf16[1,128,1024]{2,1,0:T(8,128)(2,1)}, u32[]{:S(2)}) copy-start(bf16[1,128,1024]{2,1,0:T(8,128)(2,1)} %param.19) | copy-start | bytes 786436
  1.7 15.5 %all-to-all-start.1 = ((f32[128,16,8]{0,2,1:T(8,128)}), f32[128,16,8]{0,2,1:T(8,128)S(1)}, u32[]{:S(2)}, u32[]{:S(2)}) async-start(f32[128,16,8]{0,2,1:T(8,128)} %bitcast.8), calls=%async_computation.1 | async-start | bytes 131072 | tf_op jit(solution)/shard_map/all_to_all | solution.py:28
  12.8 147.3 %collective-permute-start = (bf16[128,8192]{0,1:T(8,128)(2,1)}, bf16[128,8192]{0,1:T(8,128)(2,1)}, u32[]{:S(2)}, u32[]{:S(2)}) collective-permute-start(bf16[128,8192]{0,1:T(8,128)(2,1)} %bitcast), channel_id=1, source_target_pairs={{0,16},{16,32},{32,48},{48,64},{64,80},{80,96},{96,112},{1,17},{17... | collective-permute-start | bytes 6291464 | tf_op jit(solution)/shard_map/ppermute | solution.py:22
  19.1 41.3 %all-to-all-start.2 = ((bf16[128,16,512]{0,2,1:T(8,128)(2,1)}), bf16[128,16,512]{0,2,1:T(8,128)(2,1)S(1)}, u32[]{:S(2)}, u32[]{:S(2)}) async-start(bf16[128,16,512]{0,2,1:T(8,128)(2,1)} %bitcast.366), calls=%async_computation.2 | async-start | bytes 4194304 | tf_op jit(solution)/shard_map/all_to_all | solution.py:28
  60.4 39.3 %all-to-all-start.3 = ((bf16[128,16,512]{2,0,1:T(8,128)(2,1)}), bf16[128,16,512]{2,0,1:T(8,128)(2,1)}, u32[]{:S(2)}, u32[]{:S(2)}) async-start(bf16[128,16,512]{2,0,1:T(8,128)(2,1)} %copy.368), calls=%async_computation.3 | async-start | bytes 4194304 | tf_op jit(solution)/shard_map/all_to_all | solution.py:28
  163.3 36.2 %all-to-all-start = ((bf16[128,16,512]{0,2,1:T(8,128)(2,1)}), bf16[128,16,512]{0,2,1:T(8,128)(2,1)S(1)}, u32[]{:S(2)}, u32[]{:S(2)}) async-start(bf16[128,16,512]{0,2,1:T(8,128)(2,1)} %bitcast.363), calls=%async_computation | async-start | bytes 4194304 | tf_op jit(solution)/shard_map/all_to_all | solution.py:28
  199.5 6.5 %copy-start.7 = (bf16[16,8,64,128]{3,2,1,0:T(8,128)(2,1)S(1)}, bf16[16,8,64,128]{3,2,1,0:T(8,128)(2,1)}, u32[]{:S(2)}) copy-start(bf16[16,8,64,128]{3,2,1,0:T(8,128)(2,1)} %broadcast_dynamic-update-slice_fusion) | copy-start | bytes 6291460
  199.5 6.7 %copy-start.33 = (f32[8]{0:T(128)S(1)}, f32[8]{0:T(128)}, u32[]{:S(2)}) copy-start(f32[8]{0:T(128)} %get-tuple-element.26) | copy-start | bytes 100
  199.5 8.4 %copy-start.26 = (f32[8]{0:T(128)S(1)}, f32[8]{0:T(128)}, u32[]{:S(2)}) copy-start(f32[8]{0:T(128)} %get-tuple-element.25) | copy-start | bytes 100
  199.5 9.5 %copy-start.32 = (f32[8]{0:T(128)S(1)}, f32[8]{0:T(128)}, u32[]{:S(2)}) copy-start(f32[8]{0:T(128)} %get-tuple-element.24) | copy-start | bytes 100
  206.0 6.5 %copy-start.24 = (f32[8]{0:T(128)S(1)}, f32[8]{0:T(128)}, u32[]{:S(2)}) copy-start(f32[8]{0:T(128)} %get-tuple-element.21) | copy-start | bytes 100
  206.0 7.5 %copy-start.30 = (f32[8]{0:T(128)S(1)}, f32[8]{0:T(128)}, u32[]{:S(2)}) copy-start(f32[8]{0:T(128)} %get-tuple-element.20) | copy-start | bytes 100
  206.2 8.6 %copy-start.23 = (f32[8]{0:T(128)S(1)}, f32[8]{0:T(128)}, u32[]{:S(2)}) copy-start(f32[8]{0:T(128)} %get-tuple-element.19) | copy-start | bytes 100
  206.3 9.5 %copy-start.29 = (f32[8]{0:T(128)S(1)}, f32[8]{0:T(128)}, u32[]{:S(2)}) copy-start(f32[8]{0:T(128)} %get-tuple-element.18) | copy-start | bytes 100
  209.0 8.0 %copy-start.22 = (f32[8]{0:T(128)S(1)}, f32[8]{0:T(128)}, u32[]{:S(2)}) copy-start(f32[8]{0:T(128)} %get-tuple-element.17) | copy-start | bytes 100
  210.2 7.9 %copy-start.28 = (f32[8]{0:T(128)S(1)}, f32[8]{0:T(128)}, u32[]{:S(2)}) copy-start(f32[8]{0:T(128)} %get-tuple-element.16) | copy-start | bytes 100
  212.5 7.9 %copy-start.27 = (f32[8]{0:T(128)S(1)}, f32[8]{0:T(128)}, u32[]{:S(2)}) copy-start(f32[8]{0:T(128)} %get-tuple-element.14) | copy-start | bytes 100
  213.6 8.0 %copy-start.34 = (f32[8]{0:T(128)S(1)}, f32[8]{0:T(128)}, u32[]{:S(2)}) copy-start(f32[8]{0:T(128)} %get-tuple-element.13) | copy-start | bytes 100
  336.3 6.5 %copy-start.1 = (f32[1,128]{1,0:T(1,128)S(1)}, f32[1,128]{1,0:T(1,128)}, u32[]{:S(2)}) copy-start(f32[1,128]{1,0:T(1,128)} %param.20) | copy-start | bytes 1540
  (28 other events, 89.6 us)

commit v2 on v1

--- a/solution.py
+++ b/solution.py
@@ -25,8 +25,16 @@
 def to_heads(row, chunks):
     tok_rows = row.shape[0]
     width = row.shape[1] // chunks
-    moved = lax.all_to_all(row.reshape(tok_rows, chunks, width), "ctx", split_axis=1, concat_axis=0, tiled=True)
+    lead = row.reshape(tok_rows, chunks, width).transpose(1, 0, 2)
+    moved = lax.all_to_all(lead, "ctx", split_axis=0, concat_axis=0, tiled=True)
     return moved.reshape(tok_rows * chunks, width)
+
+
+def to_rows(block, chunks):
+    total, width = block.shape
+    tok_rows = total // chunks
+    moved = lax.all_to_all(block.reshape(chunks, tok_rows, width), "ctx", split_axis=0, concat_axis=0, tiled=True)
+    return moved.transpose(1, 0, 2).reshape(tok_rows, chunks * width)
 
 
 def mixer_heads(x_h, dt_h, bias_h, alog_h, b_g, c_g, skip_h, all_ids):
@@ -153,17 +161,17 @@
     mixer_out = mixer_heads(
         x_h.reshape(total, heads_dev, head_dim), dt_h, bias_h, alog_h, b_g, c_g, skip_h, all_ids
     )
-    sq_part = jnp.sum(mixer_out * mixer_out, axis=1, keepdims=True)
-    mean_sq = lax.psum(sq_part, "ctx") / width
+    sq_part = jnp.sum(mixer_out * mixer_out, axis=1)
+    sq_all = lax.all_to_all(
+        jnp.broadcast_to(sq_part[None], (nctx, total)), "ctx", split_axis=0, concat_axis=0, tiled=True
+    )
+    mean_sq = (jnp.sum(sq_all, axis=0) / width)[:, None]
     inv_rms = lax.rsqrt(mean_sq + norm_eps)
     mixed = (
         x_h.astype(jnp.float32) + mixer_out * inv_rms * gain_h.astype(jnp.float32)[None, :]
     ).astype(jnp.bfloat16)
     out_h = (mixed.astype(jnp.float32) + attended.astype(jnp.float32)).astype(jnp.bfloat16)
-    returned = lax.all_to_all(
-        out_h.reshape(total, 1, part), "ctx", split_axis=0, concat_axis=1, tiled=True
-    )
-    return returned.reshape(tok_rows, width)[None]
+    return to_rows(out_h, nctx)[None]
 
 
 def solution(mesh):

time: 349 us -> 295 us (0.85); the launches traced: 343 us -> 293 us
  local copies, waits for them, and re-layouts: 101 us -> 57.2 us
  blocking collectives: 61.2 us -> 34.7 us
  waiting for transfers between devices: 43 us -> 67.2 us
  other arithmetic: 41.4 us -> 36.1 us
    psum x1 -> x0, blocking collectives: 36.8 us -> none  [body(): mean_sq = lax.psum(sq_part, 'ctx') / width]
    all_to_all x4 -> x5, waiting for transfers between devices: 43 us -> 67.2 us  [the longest x4 67.1 us: to_heads(): moved = lax.all_to_all(lead, 'ctx', split_axis=0, concat_axis=0, tiled=True)]
    reshape x2 -> x0, local copies, waits for them, and re-layouts: 14.4 us -> none  [mixer_heads(): return mixer_out.reshape(total, heads * head_dim)]
    unnamed x106 -> x96, local copies, waits for them, and re-layouts: 28.5 us -> 17.2 us
    all_to_all x1, blocking collectives: 24.5 us -> 34.7 us  [to_rows(): lax.all_to_all(block.reshape(chunks, tok_rows, width), 'ctx', split_axis=...]
    convert_element_type x2 -> x0, local copies, waits for them, and re-layouts: 5.94 us -> none  [the longest x1 5.35 us: body(): x_h.astype(jnp.float32)]
    convert_element_type x2 -> x1, local copies, waits for them, and re-layouts: 9.57 us -> 4.2 us  [body(): attended.astype(jnp.float32)]
    convert_element_type x2 -> x1, other arithmetic: 8.31 us -> 5.42 us  [body(): (mixed.astype(jnp.float32) + attended.astype(jnp.float32)).astype(jnp.bfl...]
  transfers between devices with their start and end apart: 5 -> 6, of which waited for: 3 -> 4; matrix products, arithmetic and copies ran while one was open for 37% -> 40% of each run, Pallas kernels for 0% -> 0%
where the time goes in v2:
time: 295 us; the launch traced here: 293 us
  matrix products  72.1 us (24%)
  waiting for transfers between devices  67.2 us (23%)
  local copies, waits for them, and re-layouts  57.2 us (19%)
  other arithmetic  36.1 us (12%)
  blocking collectives  34.7 us (12%)
  starting transfers between devices  25.3 us (9%)
    all_to_all x4, waiting for transfers between devices, to_heads(): moved = lax.all_to_all(lead, 'ctx', split_axis=0, concat_axis=0, tiled=True)  67.1 us
    sub x8, matrix products, attend_heads(): exp_terms = jnp.exp(logits - row_max)  35.3 us
    all_to_all x1, blocking collectives, to_rows(): lax.all_to_all(block.reshape(chunks, tok_rows, width), 'ctx', split_axis=...  34.7 us
    dot_general x8, matrix products, attend_heads(): jnp.einsum('igj,jd->igd', probs, vb, preferred_element_type=jnp.float32)  22.1 us
    all_to_all x4, starting transfers between devices, to_heads(): moved = lax.all_to_all(lead, 'ctx', split_axis=0, concat_axis=0, tiled=True)  19.9 us
    unnamed x96, local copies, waits for them, and re-layouts  17.2 us
    unnamed x14, other arithmetic  13.7 us
    slice x9, local copies, waits for them, and re-layouts, attend_heads(): qb = q_h[q0:q0 + q_blk]  9.38 us
  transfers between devices with their start and end apart: 6, of which 4 were waited for; matrix products, arithmetic and copies ran while one was open for 40% of the time, Pallas kernels for 0%

profile of v2, /device:TPU:32, one launch (start us, length us, event | category | flops | bytes accessed | tf_op | source)
XLA Modules:
  0.0 293.3 jit_solution(9441015023637919633)
XLA Ops:
  0.0 4.2 %copy.434 = bf16[1,128,8192]{1,2,0:T(8,128)(2,1)} copy(bf16[1,128,8192]{2,1,0:T(8,128)(2,1)} %param.13) | data formatting | bytes 4194304 | tf_op args[0]
  6.9 7.0 %all-to-all-start.1 = ((f32[16,128,8]{1,2,0:T(8,128)}), f32[16,128,8]{1,2,0:T(8,128)S(1)}, u32[]{:S(2)}, u32[]{:S(2)}) async-start(f32[16,128,8]{1,2,0:T(8,128)} %bitcast.6), calls=%async_computation.1 | async-start | bytes 131072 | tf_op jit(solution)/shard_map/all_to_all | solution.py:29
  21.6 4.7 %all-to-all-start.4 = ((bf16[16,128,512]{2,1,0:T(8,128)(2,1)}), bf16[16,128,512]{2,1,0:T(8,128)(2,1)}, u32[]{:S(2)}, u32[]{:S(2)}) async-start(bf16[16,128,512]{2,1,0:T(8,128)(2,1)} %bitcast.316), calls=%async_computation.4 | async-start | bytes 4194304 | tf_op jit(solution)/shard_map/all_to_all | solution.py:29
  36.2 25.4 %all-to-all-done.4 = bf16[16,128,512]{2,1,0:T(8,128)(2,1)} async-done(((bf16[16,128,512]{2,1,0:T(8,128)(2,1)}), bf16[16,128,512]{2,1,0:T(8,128)(2,1)}, u32[]{:S(2)}, u32[]{:S(2)}) %all-to-all-start.4) | async-done | bytes 2097184 | tf_op jit(solution)/shard_map/all_to_all | solution.py:29
  63.4 4.4 %all-to-all-start.2 = ((bf16[16,128,512]{1,2,0:T(8,128)(2,1)}), bf16[16,128,512]{1,2,0:T(8,128)(2,1)}, u32[]{:S(2)}, u32[]{:S(2)}) async-start(bf16[16,128,512]{1,2,0:T(8,128)(2,1)} %bitcast.322), calls=%async_computation.2 | async-start | bytes 4194304 | tf_op jit(solution)/shard_map/all_to_all | solution.py:29
  82.8 18.8 %all-to-all-done.2 = bf16[16,128,512]{1,2,0:T(8,128)(2,1)} async-done(((bf16[16,128,512]{1,2,0:T(8,128)(2,1)}), bf16[16,128,512]{1,2,0:T(8,128)(2,1)}, u32[]{:S(2)}, u32[]{:S(2)}) %all-to-all-start.2) | async-done | bytes 2097184 | tf_op jit(solution)/shard_map/all_to_all | solution.py:29
  101.6 4.3 %copy.440 = bf16[16,128,512]{1,0,2:T(8,128)(2,1)} copy(bf16[16,128,512]{1,2,0:T(8,128)(2,1)} %all-to-all-done.2) | data formatting | bytes 4194304 | tf_op jit(solution)/shard_map/all_to_all | solution.py:29
  105.9 4.2 %reshape_reshape.4 = bf16[2048,4,128]{0,2,1:T(8,128)(2,1)} reshape(bf16[16,128,512]{1,0,2:T(8,128)(2,1)} %copy.440) | data formatting | bytes 4194304 | tf_op jit(solution)/shard_map/reshape;reshape | solution.py:145
  117.3 4.5 %fusion.186 = (f32[256,4]{0,1:T(4,128)}, f32[256,4,768]{0,2,1:T(8,128)}) fusion(pred[256,768]{0,1:T(8,128)(4,1)} %get-tuple-element.68, bf16[256,4,128]{2,1,0:T(4,128)(2,1)} %slice.352, bf16[2048,4,128]{0,2,1:T(8,128)(2,1)} %reshape_reshape.4), kind=kOutput, calls=%fused_computation.280 | convolution fusion | flops 204473088 | bytes 3805184 | tf_op jit(solution)/shard_map/sub | solution.py:100
  121.8 4.5 %fusion.191 = (f32[256,4]{0,1:T(4,128)}, f32[256,4,768]{0,2,1:T(8,128)}) fusion(pred[256,768]{0,1:T(8,128)(4,1)} %get-tuple-element.67, bf16[256,4,128]{2,1,0:T(4,128)(2,1)} %slice.357, bf16[2048,4,128]{0,2,1:T(8,128)(2,1)} %reshape_reshape.4), kind=kOutput, calls=%fused_computation.281 | convolution fusion | flops 204473088 | bytes 3805184 | tf_op jit(solution)/shard_map/sub | solution.py:100
  126.3 4.5 %fusion.196 = (f32[256,4]{0,1:T(4,128)}, f32[256,4,768]{0,2,1:T(8,128)}) fusion(pred[256,768]{0,1:T(8,128)(4,1)} %get-tuple-element.66, bf16[256,4,128]{2,1,0:T(4,128)(2,1)} %slice.360, bf16[2048,4,128]{0,2,1:T(8,128)(2,1)} %reshape_reshape.4), kind=kOutput, calls=%fused_computation.282 | convolution fusion | flops 204473088 | bytes 3805184 | tf_op jit(solution)/shard_map/sub | solution.py:100
  130.8 4.0 %fusion.201 = (f32[256,4]{0,1:T(4,128)S(1)}, f32[256,4,768]{0,2,1:T(8,128)}) fusion(pred[256,768]{0,1:T(8,128)(4,1)} %compare_and_fusion.5, bf16[256,4,128]{2,1,0:T(4,128)(2,1)} %slice.366, bf16[2048,4,128]{0,2,1:T(8,128)(2,1)} %reshape_reshape.4), kind=kOutput, calls=%fused_computation.283 | convolution fusion | flops 204473088 | bytes 3805184 | tf_op jit(solution)/shard_map/sub | solution.py:100
  134.8 4.5 %fusion.206 = (f32[256,4]{0,1:T(4,128)}, f32[256,4,768]{0,2,1:T(8,128)}) fusion(pred[256,768]{0,1:T(8,128)(4,1)} %get-tuple-element.90, bf16[256,4,128]{2,1,0:T(4,128)(2,1)} %slice.374, bf16[2048,4,128]{0,2,1:T(8,128)(2,1)} %reshape_reshape.4), kind=kOutput, calls=%fused_computation.284 | convolution fusion | flops 204473088 | bytes 3805184 | tf_op jit(solution)/shard_map/sub | solution.py:100
  139.3 4.5 %fusion.211 = (f32[256,4]{0,1:T(4,128)}, f32[256,4,768]{0,2,1:T(8,128)}) fusion(pred[256,768]{0,1:T(8,128)(4,1)} %get-tuple-element.89, bf16[256,4,128]{2,1,0:T(4,128)(2,1)S(1)} %slice.382, bf16[2048,4,128]{0,2,1:T(8,128)(2,1)} %reshape_reshape.4), kind=kOutput, calls=%fused_computation.285 | convolution fusion | flops 204473088 | bytes 3805184 | tf_op jit(solution)/shard_map/sub | solution.py:100
  143.7 4.4 %fusion.216 = (f32[256,4]{0,1:T(4,128)}, f32[256,4,768]{0,2,1:T(8,128)}) fusion(pred[256,768]{0,1:T(8,128)(4,1)} %get-tuple-element.88, bf16[256,4,128]{2,1,0:T(4,128)(2,1)S(1)} %slice.390, bf16[2048,4,128]{0,2,1:T(8,128)(2,1)} %reshape_reshape.4), kind=kOutput, calls=%fused_computation.286 | convolution fusion | flops 204473088 | bytes 3805184 | tf_op jit(solution)/shard_map/sub | solution.py:100
  152.4 4.4 %fusion.221 = (f32[256,4]{0,1:T(4,128)}, f32[256,4,768]{0,2,1:T(8,128)}) fusion(pred[256,768]{0,1:T(8,128)(4,1)} %get-tuple-element.87, bf16[256,4,128]{2,1,0:T(4,128)(2,1)S(1)} %slice.398, bf16[2048,4,128]{0,2,1:T(8,128)(2,1)} %reshape_reshape.4), kind=kOutput, calls=%fused_computation.287 | convolution fusion | flops 204473088 | bytes 3805184 | tf_op jit(solution)/shard_map/sub | solution.py:100
  168.4 3.7 %all-to-all-start = ((bf16[16,128,512]{1,2,0:T(8,128)(2,1)}), bf16[16,128,512]{1,2,0:T(8,128)(2,1)S(1)}, u32[]{:S(2)}, u32[]{:S(2)}) async-start(bf16[16,128,512]{1,2,0:T(8,128)(2,1)} %bitcast.321), calls=%async_computation | async-start | bytes 4194304 | tf_op jit(solution)/shard_map/all_to_all | solution.py:29
  182.7 20.4 %all-to-all-done = bf16[16,128,512]{1,2,0:T(8,128)(2,1)S(1)} async-done(((bf16[16,128,512]{1,2,0:T(8,128)(2,1)}), bf16[16,128,512]{1,2,0:T(8,128)(2,1)S(1)}, u32[]{:S(2)}, u32[]{:S(2)}) %all-to-all-start) | async-done | bytes 2097184 | tf_op jit(solution)/shard_map/all_to_all | solution.py:29
  203.0 6.5 %fusion.9 = f32[16,8,64,128]{3,2,1,0:T(8,128)S(1)} fusion(bf16[16,128,8,64]{1,3,2,0:T(8,128)(2,1)S(1)} %bitcast.317, f32[16,128,128]{2,1,0:T(8,128)} %convert_element_type.111, f32[16,8,128]{2,1,0:T(8,128)S(1)} %get-tuple-element.42), kind=kOutput, calls=%fused_computation.11 | convolution fusion | flops 272629760 | bytes 7405568 | tf_op jit(solution)/shard_map/bhjn,bjhp->bhpn/dot_general | solution.py:63
  227.4 6.0 %multiply_reduce_fusion = (f32[16,128]{1,0:T(8,128)S(1)}, f32[16,128,8,64]{1,3,2,0:T(8,128)}) fusion(bf16[16,128,8,64]{1,3,2,0:T(8,128)(2,1)S(1)} %bitcast.318, f32[8]{0:T(128)S(1)} %copy-done.30, f32[16,128,8,64]{1,3,2,0:T(8,128)S(1)} %fusion.228, f32[16,128,8]{1,2,0:T(8,128)S(1)} %copy-done.12, f32[16,8,128]{2,1,0:T(8,128)S(1)} %copy-done.13, ...), kind=kOutput, calls=%fused_computation.20 | convolution fusion | flops 286259200 | bytes 12001312 | tf_op jit(solution)/shard_map/bhij,bjhp->bihp/dot_general | solution.py:57
  241.0 4.2 %copy.477 = f32[2048,4,128]{0,2,1:T(8,128)} copy(bf16[2048,4,128]{2,0,1:T(8,128)(2,1)} %fusion.78) | data formatting | bytes 6291456 | tf_op jit(solution)/shard_map/convert_element_type | solution.py:173
  245.2 5.1 %copy.508 = f32[64,8,16,128]{3,2,1,0:T(8,128)} copy(f32[64,8,16,128]{3,1,2,0:T(8,128)} %bitcast.320) | data formatting | bytes 8388608
  250.3 5.4 %fusion.14 = bf16[16,128,512]{1,2,0:T(8,128)(2,1)S(1)} fusion(f32[16,128,512]{1,0,2:T(8,128)} %bitcast.319, f32[16,128,8,64]{1,3,2,0:T(8,128)} %get-tuple-element.86, bf16[16,128,512]{1,2,0:T(8,128)(2,1)S(1)} %all-to-all-done, f32[512]{0:T(512)S(1)} %bitcast.347, f32[16,128]{1,0:T(8,128)S(1)} %rsqrt_bitcast_fusion), kind=kLoop, calls=%fused_computation.19 | loop fusion | flops 8388608 | bytes 12593152 | tf_op jit(solution)/shard_map/convert_element_type | solution.py:173
  255.8 34.7 %all_to_all.31 = bf16[16,128,512]{1,2,0:T(8,128)(2,1)S(1)} all-to-all(bf16[16,128,512]{1,2,0:T(8,128)(2,1)S(1)} %fusion.14), channel_id=1, replica_groups=mesh['section'=8,'ctx'=16] {'ctx'}, dimensions={0} | all-to-all | bytes 4194304 | tf_op jit(solution)/shard_map/all_to_all | solution.py:36
  (186 shorter events, 98.2 us)
Async XLA Ops:
  0.0 67.8 %copy-start = (f32[1,128]{1,0:T(1,128)S(1)}, f32[1,128]{1,0:T(1,128)}, u32[]{:S(2)}) copy-start(f32[1,128]{1,0:T(1,128)} %param.20) | copy-start | bytes 1540
  0.0 14.0 %copy-start.6 = (s32[1,2048]{1,0:T(1,128)S(1)}, s32[1,2048]{1,0:T(1,128)}, u32[]{:S(2)}) copy-start(s32[1,2048]{1,0:T(1,128)} %param.25) | copy-start | bytes 24580
  0.0 14.4 %copy-start.4 = (bf16[1,128,8192]{2,1,0:T(8,128)(2,1)S(1)}, bf16[1,128,8192]{2,1,0:T(8,128)(2,1)}, u32[]{:S(2)}) copy-start(bf16[1,128,8192]{2,1,0:T(8,128)(2,1)} %param.22) | copy-start | bytes 6291460
  4.3 161.0 %collective-permute-start = (bf16[128,8192]{0,1:T(8,128)(2,1)}, bf16[128,8192]{0,1:T(8,128)(2,1)}, u32[]{:S(2)}, u32[]{:S(2)}) collective-permute-start(bf16[128,8192]{0,1:T(8,128)(2,1)} %bitcast.330), channel_id=1, source_target_pairs={{0,16},{16,32},{32,48},{48,64},{64,80},{80,96},{96,112},{1,17},{17... | collective-permute-start | bytes 6291464 | tf_op jit(solution)/shard_map/ppermute | solution.py:22
  6.9 14.7 %all-to-all-start.1 = ((f32[16,128,8]{1,2,0:T(8,128)}), f32[16,128,8]{1,2,0:T(8,128)S(1)}, u32[]{:S(2)}, u32[]{:S(2)}) async-start(f32[16,128,8]{1,2,0:T(8,128)} %bitcast.6), calls=%async_computation.1 | async-start | bytes 131072 | tf_op jit(solution)/shard_map/all_to_all | solution.py:29
  18.9 7.4 %copy-start.28 = (f32[1,128]{1,0:T(1,128)S(1)}, f32[1,128]{1,0:T(1,128)}, u32[]{:S(2)}) copy-start(f32[1,128]{1,0:T(1,128)} %param.16) | copy-start | bytes 1540
  18.9 7.5 %copy-start.29 = (f32[1,128]{1,0:T(1,128)S(1)}, f32[1,128]{1,0:T(1,128)}, u32[]{:S(2)}) copy-start(f32[1,128]{1,0:T(1,128)} %param.17) | copy-start | bytes 1540
  21.6 39.9 %all-to-all-start.4 = ((bf16[16,128,512]{2,1,0:T(8,128)(2,1)}), bf16[16,128,512]{2,1,0:T(8,128)(2,1)}, u32[]{:S(2)}, u32[]{:S(2)}) async-start(bf16[16,128,512]{2,1,0:T(8,128)(2,1)} %bitcast.316), calls=%async_computation.4 | async-start | bytes 4194304 | tf_op jit(solution)/shard_map/all_to_all | solution.py:29
  63.4 38.3 %all-to-all-start.2 = ((bf16[16,128,512]{1,2,0:T(8,128)(2,1)}), bf16[16,128,512]{1,2,0:T(8,128)(2,1)}, u32[]{:S(2)}, u32[]{:S(2)}) async-start(bf16[16,128,512]{1,2,0:T(8,128)(2,1)} %bitcast.322), calls=%async_computation.2 | async-start | bytes 4194304 | tf_op jit(solution)/shard_map/all_to_all | solution.py:29
  168.4 34.7 %all-to-all-start = ((bf16[16,128,512]{1,2,0:T(8,128)(2,1)}), bf16[16,128,512]{1,2,0:T(8,128)(2,1)S(1)}, u32[]{:S(2)}, u32[]{:S(2)}) async-start(bf16[16,128,512]{1,2,0:T(8,128)(2,1)} %bitcast.321), calls=%async_computation | async-start | bytes 4194304 | tf_op jit(solution)/shard_map/all_to_all | solution.py:29
  203.0 6.5 %copy-start.3 = (bf16[16,8,64,128]{3,2,1,0:T(8,128)(2,1)S(1)}, bf16[16,8,64,128]{3,2,1,0:T(8,128)(2,1)}, u32[]{:S(2)}) copy-start(bf16[16,8,64,128]{3,2,1,0:T(8,128)(2,1)} %broadcast_dynamic-update-slice_fusion) | copy-start | bytes 6291460
  203.0 6.7 %copy-start.26 = (f32[8]{0:T(128)S(1)}, f32[8]{0:T(128)}, u32[]{:S(2)}) copy-start(f32[8]{0:T(128)} %get-tuple-element.26) | copy-start | bytes 100
  203.0 8.4 %copy-start.19 = (f32[8]{0:T(128)S(1)}, f32[8]{0:T(128)}, u32[]{:S(2)}) copy-start(f32[8]{0:T(128)} %get-tuple-element.25) | copy-start | bytes 100
  203.0 9.5 %copy-start.25 = (f32[8]{0:T(128)S(1)}, f32[8]{0:T(128)}, u32[]{:S(2)}) copy-start(f32[8]{0:T(128)} %get-tuple-element.24) | copy-start | bytes 100
  209.6 7.5 %copy-start.23 = (f32[8]{0:T(128)S(1)}, f32[8]{0:T(128)}, u32[]{:S(2)}) copy-start(f32[8]{0:T(128)} %get-tuple-element.20) | copy-start | bytes 100
  209.7 8.6 %copy-start.16 = (f32[8]{0:T(128)S(1)}, f32[8]{0:T(128)}, u32[]{:S(2)}) copy-start(f32[8]{0:T(128)} %get-tuple-element.19) | copy-start | bytes 100
  209.8 9.5 %copy-start.22 = (f32[8]{0:T(128)S(1)}, f32[8]{0:T(128)}, u32[]{:S(2)}) copy-start(f32[8]{0:T(128)} %get-tuple-element.18) | copy-start | bytes 100
  212.5 8.0 %copy-start.15 = (f32[8]{0:T(128)S(1)}, f32[8]{0:T(128)}, u32[]{:S(2)}) copy-start(f32[8]{0:T(128)} %get-tuple-element.17) | copy-start | bytes 100
  213.7 7.9 %copy-start.21 = (f32[8]{0:T(128)S(1)}, f32[8]{0:T(128)}, u32[]{:S(2)}) copy-start(f32[8]{0:T(128)} %get-tuple-element.16) | copy-start | bytes 100
  216.0 7.9 %copy-start.20 = (f32[8]{0:T(128)S(1)}, f32[8]{0:T(128)}, u32[]{:S(2)}) copy-start(f32[8]{0:T(128)} %get-tuple-element.14) | copy-start | bytes 100
  217.1 8.0 %copy-start.27 = (f32[8]{0:T(128)S(1)}, f32[8]{0:T(128)}, u32[]{:S(2)}) copy-start(f32[8]{0:T(128)} %get-tuple-element.13) | copy-start | bytes 100
  227.4 10.3 %copy-start.36 = (f32[256,4]{0,1:T(4,128)S(1)}, f32[256,4]{0,1:T(4,128)}, u32[]{:S(2)}) copy-start(f32[256,4]{0,1:T(4,128)} %get-tuple-element.83) | copy-start | bytes 12292
  234.2 16.0 %all-to-all-start.3 = ((f32[16,1,2048]{2,1,0:T(1,128)}), f32[16,1,2048]{2,1,0:T(1,128)S(1)}, u32[]{:S(2)}, u32[]{:S(2)}) async-start(f32[16,1,2048]{2,1,0:T(1,128)} %broadcast_in_dim.75), calls=%async_computation.3 | async-start | bytes 262144 | tf_op jit(solution)/shard_map/all_to_all | solution.py:165
  255.8 37.6 %copy-start.1 = (f32[1,128]{1,0:T(1,128)S(1)}, f32[1,128]{1,0:T(1,128)}, u32[]{:S(2)}) copy-start(f32[1,128]{1,0:T(1,128)} %param.20) | copy-start | bytes 1540
  (25 other events, 73.3 us)

commit v3 on v2

--- a/solution.py
+++ b/solution.py
@@ -3,6 +3,7 @@
 import jax
 import jax.numpy as jnp
 from jax import lax
+from jax.experimental import pallas as pl
 from jax.sharding import PartitionSpec as P
 
 HEAD_A = 128
@@ -77,32 +78,48 @@
     return mixer_out.reshape(total, heads * head_dim)
 
 
-def attend_heads(q_h, k_h, v_h, all_ids):
-    total, qpd, _ = q_h.shape
-    inv_sqrt = 1.0 / math.sqrt(HEAD_A)
+def attend_heads(q_h, k_h, v_h, all_ids, interpret=False):
+    total, q_width = q_h.shape
+    groups = q_width // HEAD_A
     q_blk = min(Q_BLOCK, total)
     window = min(q_blk + MOST_DOC, total)
-    outs = []
-    for i in range(total // q_blk):
-        q0 = i * q_blk
-        k0 = max(0, min(q0 + q_blk - window, total - window))
-        qb = q_h[q0:q0 + q_blk]
-        kb = k_h[k0:k0 + window]
-        vb = v_h[k0:k0 + window]
-        q_at = q0 + jnp.arange(q_blk)
-        k_at = k0 + jnp.arange(window)
-        allowed = (all_ids[q0:q0 + q_blk][:, None] == all_ids[k0:k0 + window][None, :]) & (
-            q_at[:, None] >= k_at[None, :]
-        )
-        logits = jnp.einsum("igd,jd->igj", qb, kb, preferred_element_type=jnp.float32) * inv_sqrt
-        logits = jnp.where(allowed[:, None, :], logits, -jnp.inf)
-        row_max = jnp.max(logits, axis=2, keepdims=True)
-        exp_terms = jnp.exp(logits - row_max)
-        probs = (exp_terms / jnp.sum(exp_terms, axis=2, keepdims=True)).astype(jnp.bfloat16)
-        outs.append(
-            jnp.einsum("igj,jd->igd", probs, vb, preferred_element_type=jnp.float32).astype(jnp.bfloat16)
-        )
-    return jnp.concatenate(outs, axis=0).reshape(total, qpd * HEAD_A)
+    inv_sqrt = 1.0 / math.sqrt(HEAD_A)
+
+    def kernel(q_ref, k_ref, v_ref, ic_ref, ir_ref, o_ref):
+        q0 = pl.multiple_of(pl.program_id(0) * q_blk, q_blk)
+        k0 = pl.multiple_of(jnp.clip(q0 + q_blk - window, 0, total - window), q_blk)
+        kb = k_ref[pl.ds(k0, window), :]
+        vb = v_ref[pl.ds(k0, window), :]
+        qid = ic_ref[pl.ds(q0, q_blk), :]
+        kid = ir_ref[:, pl.ds(k0, window)]
+        q_at = q0 + lax.broadcasted_iota(jnp.int32, (q_blk, window), 0)
+        k_at = k0 + lax.broadcasted_iota(jnp.int32, (q_blk, window), 1)
+        allowed = (qid == kid) & (q_at >= k_at)
+        for g in range(groups):
+            cols = slice(g * HEAD_A, (g + 1) * HEAD_A)
+            logits = lax.dot_general(
+                q_ref[:, cols], kb, (((1,), (1,)), ((), ())), preferred_element_type=jnp.float32
+            ) * inv_sqrt
+            logits = jnp.where(allowed, logits, -jnp.inf)
+            row_max = jnp.max(logits, axis=1, keepdims=True)
+            exp_terms = jnp.exp(logits - row_max)
+            probs = (exp_terms / jnp.sum(exp_terms, axis=1, keepdims=True)).astype(jnp.bfloat16)
+            o_ref[:, cols] = jnp.dot(probs, vb, preferred_element_type=jnp.float32).astype(o_ref.dtype)
+
+    return pl.pallas_call(
+        kernel,
+        grid=(total // q_blk,),
+        in_specs=[
+            pl.BlockSpec((q_blk, q_width), lambda i: (i, 0)),
+            pl.BlockSpec((total, HEAD_A), lambda i: (0, 0)),
+            pl.BlockSpec((total, HEAD_A), lambda i: (0, 0)),
+            pl.BlockSpec((total, 1), lambda i: (0, 0)),
+            pl.BlockSpec((1, total), lambda i: (0, 0)),
+        ],
+        out_specs=pl.BlockSpec((q_blk, q_width), lambda i: (i, 0)),
+        out_shape=jax.ShapeDtypeStruct((total, q_width), jnp.bfloat16),
+        interpret=interpret,
+    )(q_h, k_h, v_h, all_ids.reshape(total, 1), all_ids.reshape(1, total))
 
 
 def body(
@@ -131,7 +148,7 @@
     kv_heads = keys.shape[2] // HEAD_A
     qpd = part // HEAD_A
 
-    q_h = to_heads(queries[0], nctx).reshape(total, qpd, HEAD_A)
+    q_h = to_heads(queries[0], nctx)
     kvbc = jnp.stack(
         [
             keys[0].reshape(tok_rows, kv_heads, HEAD_A),

time: 295 us -> 233 us (0.79)
  matrix products: 72.1 us -> 15.5 us
  waiting for transfers between devices: 67.2 us -> 36.9 us
  Pallas kernels: 0 us -> 21.7 us
  other arithmetic: 36.1 us -> 27.8 us
  starting transfers between devices: 25.3 us -> 31.5 us
  local copies, waits for them, and re-layouts: 57.2 us -> 62.5 us
    sub x8 -> x0, matrix products: 35.3 us -> none  [attend_heads(): exp_terms = jnp.exp(logits - row_max)]
    all_to_all x4, waiting for transfers between devices: 67.1 us -> 36.9 us  [to_heads(): moved = lax.all_to_all(lead, 'ctx', split_axis=0, concat_axis=0, tiled=True)]
    dot_general x8 -> x0, matrix products: 22.1 us -> none  [attend_heads(): jnp.einsum('igj,jd->igd', probs, vb, preferred_element_type=jnp.float32)]
    pallas_call x0 -> x1, Pallas kernels: none -> 21.7 us  [attend_heads(): pl.pallas_call(kernel, grid=(total // q_blk,), in_specs=[pl.BlockSpec((q_...]
    reshape x0 -> x3, local copies, waits for them, and re-layouts: none -> 16 us  [the longest x2 14.4 us: mixer_heads(): return mixer_out.reshape(total, heads * head_dim)]
    slice x11 -> x0, local copies, waits for them, and re-layouts: 9.4 us -> none  [the longest x9 9.38 us: attend_heads(): qb = q_h[q0:q0 + q_blk]]
    and x4 -> x0, other arithmetic: 4.89 us -> none  [attend_heads(): (all_ids[q0:q0 + q_blk][:, None] == all_ids[k0:k0 + window][None, :]) & (...]
    unnamed x96 -> x41, local copies, waits for them, and re-layouts: 17.2 us -> 12.4 us
  transfers between devices with their start and end apart: 6 -> 6, of which waited for: 4 -> 3; matrix products, arithmetic and copies ran while one was open for 40% -> 40% of each run, Pallas kernels for 0% -> 9%
where the time goes in v3:
time: 233 us; the launch traced here: 231 us
  local copies, waits for them, and re-layouts  62.5 us (27%)
  waiting for transfers between devices  36.9 us (16%)
  blocking collectives  35 us (15%)
  starting transfers between devices  31.5 us (14%)
  other arithmetic  27.8 us (12%)
  Pallas kernels  21.7 us (9%)
  matrix products  15.5 us (7%)
    all_to_all x4, waiting for transfers between devices, to_heads(): moved = lax.all_to_all(lead, 'ctx', split_axis=0, concat_axis=0, tiled=True)  36.9 us
    all_to_all x1, blocking collectives, to_rows(): lax.all_to_all(block.reshape(chunks, tok_rows, width), 'ctx', split_axis=...  35 us
    all_to_all x4, starting transfers between devices, to_heads(): moved = lax.all_to_all(lead, 'ctx', split_axis=0, concat_axis=0, tiled=True)  22.5 us
    pallas_call x1, Pallas kernels, attend_heads(): pl.pallas_call(kernel, grid=(total // q_blk,), in_specs=[pl.BlockSpec((q_...  21.7 us
    reshape x2, local copies, waits for them, and re-layouts, mixer_heads(): return mixer_out.reshape(total, heads * head_dim)  14.4 us
    unnamed x14, other arithmetic  13.8 us
    unnamed x41, local copies, waits for them, and re-layouts  12.4 us
    all_to_all x1, starting transfers between devices, body(): lax.all_to_all(jnp.broadcast_to(sq_part[None], (nctx, total)), 'ctx', spl...  6.91 us
  transfers between devices with their start and end apart: 6, of which 3 were waited for; matrix products, arithmetic and copies ran while one was open for 40% of the time, Pallas kernels for 9%

profile of v3, /device:TPU:32, one launch (start us, length us, event | category | flops | bytes accessed | tf_op | source)
XLA Modules:
  0.0 231.4 jit_solution(17382155389816591389)
XLA Ops:
  0.0 2.0 collective-permute-start
  3.6 7.0 %all-to-all-start.1 = ((f32[16,128,8]{1,2,0:T(8,128)}), f32[16,128,8]{1,2,0:T(8,128)S(1)}, u32[]{:S(2)}, u32[]{:S(2)}) async-start(f32[16,128,8]{1,2,0:T(8,128)} %bitcast.6), calls=%async_computation.1 | async-start | bytes 131072 | tf_op jit(solution)/shard_map/all_to_all | solution.py:30
  20.2 7.2 %all-to-all-start.2 = ((bf16[16,128,512]{1,2,0:T(8,128)(2,1)}), bf16[16,128,512]{1,2,0:T(8,128)(2,1)}, u32[]{:S(2)}, u32[]{:S(2)}) async-start(bf16[16,128,512]{1,2,0:T(8,128)(2,1)} %bitcast.99), calls=%async_computation.2 | async-start | bytes 4194304 | tf_op jit(solution)/shard_map/all_to_all | solution.py:30
  28.1 2.4 %copy.238 = bf16[16,8,16,512]{3,2,1,0:T(8,128)(2,1)S(1)} copy(bf16[16,8,16,512]{3,1,2,0:T(8,128)(2,1)} %bitcast.108) | data formatting | bytes 4194304
  30.5 2.5 %copy.242 = bf16[128,16,512]{2,0,1:T(8,128)(2,1)} copy(bf16[128,16,512]{2,1,0:T(8,128)(2,1)S(1)} %bitcast.101) | data formatting | bytes 4194304 | tf_op jit(solution)/shard_map/reshape;squeeze | solution.py:29
  36.4 26.1 %all-to-all-done.2 = bf16[16,128,512]{1,2,0:T(8,128)(2,1)} async-done(((bf16[16,128,512]{1,2,0:T(8,128)(2,1)}), bf16[16,128,512]{1,2,0:T(8,128)(2,1)}, u32[]{:S(2)}, u32[]{:S(2)}) %all-to-all-start.2) | async-done | bytes 2097184 | tf_op jit(solution)/shard_map/all_to_all | solution.py:30
  62.6 3.7 %all-to-all-start = ((bf16[16,128,512]{2,1,0:T(8,128)(2,1)}), bf16[16,128,512]{2,1,0:T(8,128)(2,1)S(1)}, u32[]{:S(2)}, u32[]{:S(2)}) async-start(bf16[16,128,512]{2,1,0:T(8,128)(2,1)} %bitcast.98), calls=%async_computation | async-start | bytes 4194304 | tf_op jit(solution)/shard_map/all_to_all | solution.py:30
  74.0 4.3 %copy.211 = bf16[16,128,512]{1,0,2:T(8,128)(2,1)} copy(bf16[16,128,512]{1,2,0:T(8,128)(2,1)} %all-to-all-done.2) | data formatting | bytes 4194304 | tf_op jit(solution)/shard_map/all_to_all | solution.py:30
  78.3 4.2 %reshape_reshape.3 = bf16[2048,4,128]{0,2,1:T(8,128)(2,1)} reshape(bf16[16,128,512]{1,0,2:T(8,128)(2,1)} %copy.211) | data formatting | bytes 4194304 | tf_op jit(solution)/shard_map/reshape;reshape | solution.py:162
  82.5 2.8 %fusion.25 = (bf16[2048,1,128]{0,2,1:T(8,128)(2,1)S(1)}, bf16[2048,1,128]{0,2,1:T(8,128)(2,1)}, bf16[2048,1,128]{0,2,1:T(8,128)(2,1)}, bf16[2048,1,128]{0,2,1:T(8,128)(2,1)}) fusion(bf16[2048,4,128]{0,2,1:T(8,128)(2,1)} %reshape_reshape.3), kind=kLoop, calls=%fused_computation.98 | loop fusion | bytes 4194304 | tf_op jit(solution)/shard_map/slice | solution.py:163
  89.4 10.7 %all-to-all-done = bf16[16,128,512]{2,1,0:T(8,128)(2,1)S(1)} async-done(((bf16[16,128,512]{2,1,0:T(8,128)(2,1)}), bf16[16,128,512]{2,1,0:T(8,128)(2,1)S(1)}, u32[]{:S(2)}, u32[]{:S(2)}) %all-to-all-start) | async-done | bytes 2097184 | tf_op jit(solution)/shard_map/all_to_all | solution.py:30
  100.1 4.6 %all-to-all-start.4 = ((bf16[16,128,512]{2,1,0:T(8,128)(2,1)}), bf16[16,128,512]{2,1,0:T(8,128)(2,1)}, u32[]{:S(2)}, u32[]{:S(2)}) async-start(bf16[16,128,512]{2,1,0:T(8,128)(2,1)} %bitcast.97), calls=%async_computation.4 | async-start | bytes 4194304 | tf_op jit(solution)/shard_map/all_to_all | solution.py:30
  104.7 2.4 %copy.206 = bf16[16,128,512]{1,2,0:T(8,128)(2,1)} copy(bf16[16,128,512]{2,1,0:T(8,128)(2,1)S(1)} %all-to-all-done) | data formatting | bytes 4194304 | tf_op jit(solution)/shard_map/all_to_all | solution.py:30
  107.1 4.9 %fusion.1 = f32[16,8,64,128]{3,2,1,0:T(8,128)S(1)} fusion(bf16[16,128,8,64]{1,3,2,0:T(8,128)(2,1)} %bitcast.92, f32[16,128,128]{2,1,0:T(8,128)} %convert_element_type.59, f32[16,8,128]{2,1,0:T(8,128)S(1)} %get-tuple-element.36), kind=kOutput, calls=%fused_computation.3 | convolution fusion | flops 272629760 | bytes 7405568 | tf_op jit(solution)/shard_map/bhjn,bjhp->bhpn/dot_general | solution.py:64
  128.7 6.0 %fusion = f32[16,8,64,128]{3,2,1,0:T(8,128)S(1)} fusion(bf16[16,128,8,64]{1,3,2,0:T(8,128)(2,1)S(1)} %bitcast.93, f32[16,8,128]{2,1,0:T(8,128)S(1)} %get-tuple-element.37, f32[16,128,128]{2,1,0:T(8,128)S(1)} %copy-done.8, f32[16,8,128]{2,1,0:T(8,128)S(1)} %bitcast.120, pred[16,128,128]{2,1,0:T(8,128)(4,1)S(1)} %copy-done.10), kind=kOutput, calls=%fused_computation.2 | convolution fusion | flops 278921216 | bytes 7733248 | tf_op jit(solution)/shard_map/bhij,bjhp->bihp/dot_general | solution.py:58
  134.8 3.1 %multiply_reduce_fusion = (f32[16,128]{1,0:T(8,128)S(1)}, f32[16,128,8,64]{1,3,2,0:T(8,128)}) fusion(bf16[16,128,8,64]{1,3,2,0:T(8,128)(2,1)S(1)} %bitcast.94, f32[8]{0:T(128)S(1)} %copy-done.13, f32[16,128,8]{1,2,0:T(8,128)S(1)} %copy.217, bf16[16,128,128,1]{2,1,3,0:T(8,128)(2,1)S(1)} %bitcast.103, bf16[16,8,64,128]{3,2,1,0:T(8,128)(2,1)S(1)} %fusion.15, ...), kind=kOutput, calls=%fused_computation.9 | convolution fusion | flops 275773440 | bytes 13180960 | tf_op jit(solution)/shard_map/bin,bhpn->bihp/dot_general | solution.py:73
  138.6 6.9 %all-to-all-start.3 = ((f32[16,1,2048]{2,1,0:T(1,128)}), f32[16,1,2048]{2,1,0:T(1,128)S(1)}, u32[]{:S(2)}, u32[]{:S(2)}) async-start(f32[16,1,2048]{2,1,0:T(1,128)} %broadcast_in_dim.25), calls=%async_computation.3 | async-start | bytes 262144 | tf_op jit(solution)/shard_map/all_to_all | solution.py:182
  149.6 21.7 %shard_map.127 = bf16[2048,512]{1,0:T(8,128)(2,1)} custom-call(bf16[2048,512]{1,0:T(8,128)(2,1)} %bitcast.24.q_ref, bf16[2048,128]{1,0:T(8,128)(2,1)} %bitcast.106, bf16[2048,128]{1,0:T(8,128)(2,1)} %bitcast.107, s32[2048,1]{1,0:T(8,128)} %copy.224.ic_ref, s32[1,2048]{1,0:T(1,128)} %ir_ref.1), custom_call_target="tpu_custom_call" | custom-call | tf_op jit(solution)/shard_map/pallas_call | solution.py:109
  171.4 6.9 %copy.228 = f32[16,128,8,64]{3,2,1,0:T(8,128)} copy(f32[16,128,8,64]{1,3,2,0:T(8,128)} %get-tuple-element.47) | data formatting | bytes 8388608 | tf_op jit(solution)/shard_map/reshape | solution.py:78
  178.3 7.5 %reshape.156 = f32[2048,512]{1,0:T(8,128)} reshape(f32[16,128,8,64]{3,2,1,0:T(8,128)} %copy.228) | data formatting | bytes 8388608 | tf_op jit(solution)/shard_map/reshape | solution.py:78
  185.9 3.8 %add_convert_fusion = bf16[2048,512]{1,0:T(8,128)(2,1)S(1)} fusion(bf16[2048,512]{1,0:T(8,128)(2,1)} %shard_map.127, f32[2048,512]{1,0:T(8,128)} %reshape.156, bf16[16,128,512]{2,1,0:T(8,128)(2,1)S(1)} %all-to-all-done, f32[512]{0:T(512)S(1)} %bitcast.127, f32[2048]{0:T(1024)S(1)} %add_rsqrt_fusion), kind=kLoop, calls=%fused_computation.8 | loop fusion | flops 9437184 | bytes 10496000 | tf_op jit(solution)/shard_map/convert_element_type | solution.py:190
  189.7 35.0 %all_to_all.31 = bf16[16,128,512]{2,1,0:T(8,128)(2,1)S(1)} all-to-all(bf16[16,128,512]{2,1,0:T(8,128)(2,1)S(1)} %bitcast.95), channel_id=1, replica_groups=mesh['section'=8,'ctx'=16] {'ctx'}, dimensions={0} | all-to-all | bytes 4194304 | tf_op jit(solution)/shard_map/all_to_all | solution.py:37
  224.7 2.5 %copy.225 = bf16[128,16,512]{2,1,0:T(8,128)(2,1)} copy(bf16[128,16,512]{2,0,1:T(8,128)(2,1)S(1)} %bitcast.100) | data formatting | bytes 4194304 | tf_op jit(solution)/shard_map/transpose | solution.py:38
  227.2 4.2 %broadcast_in_dim_reshape.3 = bf16[1,128,8192]{2,1,0:T(8,128)(2,1)} reshape(bf16[128,16,512]{2,1,0:T(8,128)(2,1)} %copy.225) | data formatting | bytes 4194304 | tf_op jit(solution)/shard_map/broadcast_in_dim;reshape | solution.py:191
  (95 shorter events, 48.5 us)
Async XLA Ops:
  0.0 27.3 %copy-start = (f32[1,128]{1,0:T(1,128)S(1)}, f32[1,128]{1,0:T(1,128)}, u32[]{:S(2)}) copy-start(f32[1,128]{1,0:T(1,128)} %param.20) | copy-start | bytes 1540
  0.0 33.0 %collective-permute-start = (bf16[128,8192]{1,0:T(8,128)(2,1)}, bf16[128,8192]{1,0:T(8,128)(2,1)}, u32[]{:S(2)}, u32[]{:S(2)}) collective-permute-start(bf16[128,8192]{1,0:T(8,128)(2,1)} %bitcast.128), channel_id=1, source_target_pairs={{0,16},{16,32},{32,48},{48,64},{64,80},{80,96},{96,112},{1,17},{17... | collective-permute-start | bytes 6291464 | tf_op jit(solution)/shard_map/ppermute | solution.py:23
  3.6 14.7 %all-to-all-start.1 = ((f32[16,128,8]{1,2,0:T(8,128)}), f32[16,128,8]{1,2,0:T(8,128)S(1)}, u32[]{:S(2)}, u32[]{:S(2)}) async-start(f32[16,128,8]{1,2,0:T(8,128)} %bitcast.6), calls=%async_computation.1 | async-start | bytes 131072 | tf_op jit(solution)/shard_map/all_to_all | solution.py:30
  14.7 1.0 copy-start.9
  14.7 3.5 %copy-start.14 = (f32[1,128]{1,0:T(1,128)S(1)}, f32[1,128]{1,0:T(1,128)}, u32[]{:S(2)}) copy-start(f32[1,128]{1,0:T(1,128)} %param.16) | copy-start | bytes 1540
  14.7 3.4 %copy-start.15 = (f32[1,128]{1,0:T(1,128)S(1)}, f32[1,128]{1,0:T(1,128)}, u32[]{:S(2)}) copy-start(f32[1,128]{1,0:T(1,128)} %param.17) | copy-start | bytes 1540
  20.2 42.4 %all-to-all-start.2 = ((bf16[16,128,512]{1,2,0:T(8,128)(2,1)}), bf16[16,128,512]{1,2,0:T(8,128)(2,1)}, u32[]{:S(2)}, u32[]{:S(2)}) async-start(bf16[16,128,512]{1,2,0:T(8,128)(2,1)} %bitcast.99), calls=%async_computation.2 | async-start | bytes 4194304 | tf_op jit(solution)/shard_map/all_to_all | solution.py:30
  30.5 2.5 %copy-start.5 = (bf16[128,8192]{1,0:T(8,128)(2,1)S(1)}, bf16[128,8192]{1,0:T(8,128)(2,1)}, u32[]{:S(2)}) copy-start(bf16[128,8192]{1,0:T(8,128)(2,1)} %param.14) | copy-start | bytes 6291460
  62.6 37.5 %all-to-all-start = ((bf16[16,128,512]{2,1,0:T(8,128)(2,1)}), bf16[16,128,512]{2,1,0:T(8,128)(2,1)S(1)}, u32[]{:S(2)}, u32[]{:S(2)}) async-start(bf16[16,128,512]{2,1,0:T(8,128)(2,1)} %bitcast.98), calls=%async_computation | async-start | bytes 4194304 | tf_op jit(solution)/shard_map/all_to_all | solution.py:30
  100.1 37.8 %all-to-all-start.4 = ((bf16[16,128,512]{2,1,0:T(8,128)(2,1)}), bf16[16,128,512]{2,1,0:T(8,128)(2,1)}, u32[]{:S(2)}, u32[]{:S(2)}) async-start(bf16[16,128,512]{2,1,0:T(8,128)(2,1)} %bitcast.97), calls=%async_computation.4 | async-start | bytes 4194304 | tf_op jit(solution)/shard_map/all_to_all | solution.py:30
  107.1 4.9 %copy-start.4 = (bf16[16,8,64,128]{3,2,1,0:T(8,128)(2,1)S(1)}, bf16[16,8,64,128]{3,2,1,0:T(8,128)(2,1)}, u32[]{:S(2)}) copy-start(bf16[16,8,64,128]{3,2,1,0:T(8,128)(2,1)} %broadcast_dynamic-update-slice_fusion) | copy-start | bytes 6291460
  107.1 5.0 %copy-start.11 = (f32[8]{0:T(128)S(1)}, f32[8]{0:T(128)}, u32[]{:S(2)}) copy-start(f32[8]{0:T(128)} %get-tuple-element.20) | copy-start | bytes 100
  112.0 1.9 copy-start.2
  122.9 4.7 %copy-start.12 = (f32[8]{0:T(128)S(1)}, f32[8]{0:T(128)}, u32[]{:S(2)}) copy-start(f32[8]{0:T(128)} %get-tuple-element.7) | copy-start | bytes 100
  122.9 5.7 %copy-start.3 = (bf16[16,128,512]{1,2,0:T(8,128)(2,1)S(1)}, bf16[16,128,512]{1,2,0:T(8,128)(2,1)}, u32[]{:S(2)}) copy-start(bf16[16,128,512]{1,2,0:T(8,128)(2,1)} %copy.206) | copy-start | bytes 6291460
  123.0 5.7 %copy-start.8 = (f32[16,128,128]{2,1,0:T(8,128)S(1)}, f32[16,128,128]{2,1,0:T(8,128)}, u32[]{:S(2)}) copy-start(f32[16,128,128]{2,1,0:T(8,128)} %fusion.27) | copy-start | bytes 3145732
  123.0 5.7 %copy-start.10 = (pred[16,128,128]{2,1,0:T(8,128)(4,1)S(1)}, pred[16,128,128]{2,1,0:T(8,128)(4,1)}, u32[]{:S(2)}) copy-start(pred[16,128,128]{2,1,0:T(8,128)(4,1)} %compare_and_fusion) | copy-start | bytes 786436
  128.7 6.0 %copy-start.13 = (f32[8]{0:T(128)S(1)}, f32[8]{0:T(128)}, u32[]{:S(2)}) copy-start(f32[8]{0:T(128)} %fusion.22) | copy-start | bytes 100
  134.8 12.8 %copy-start.7 = (bf16[2048,1,128]{0,2,1:T(8,128)(2,1)S(1)}, bf16[2048,1,128]{0,2,1:T(8,128)(2,1)}, u32[]{:S(2)}) copy-start(bf16[2048,1,128]{0,2,1:T(8,128)(2,1)} %get-tuple-element.39) | copy-start | bytes 1572868
  137.9 10.7 %copy-start.6 = (bf16[2048,1,128]{0,2,1:T(8,128)(2,1)S(1)}, bf16[2048,1,128]{0,2,1:T(8,128)(2,1)}, u32[]{:S(2)}) copy-start(bf16[2048,1,128]{0,2,1:T(8,128)(2,1)} %get-tuple-element.40) | copy-start | bytes 1572868
  138.6 47.2 %all-to-all-start.3 = ((f32[16,1,2048]{2,1,0:T(1,128)}), f32[16,1,2048]{2,1,0:T(1,128)S(1)}, u32[]{:S(2)}, u32[]{:S(2)}) async-start(f32[16,1,2048]{2,1,0:T(1,128)} %broadcast_in_dim.25), calls=%async_computation.3 | async-start | bytes 262144 | tf_op jit(solution)/shard_map/all_to_all | solution.py:182
  224.7 6.7 %copy-start.1 = (f32[1,128]{1,0:T(1,128)S(1)}, f32[1,128]{1,0:T(1,128)}, u32[]{:S(2)}) copy-start(f32[1,128]{1,0:T(1,128)} %param.20) | copy-start | bytes 1540

commit v4 on v3

--- a/solution.py
+++ b/solution.py
@@ -4,6 +4,7 @@
 import jax.numpy as jnp
 from jax import lax
 from jax.experimental import pallas as pl
+from jax.experimental.pallas import tpu as pltpu
 from jax.sharding import PartitionSpec as P
 
 HEAD_A = 128
@@ -38,44 +39,100 @@
     return moved.transpose(1, 0, 2).reshape(tok_rows, chunks * width)
 
 
-def mixer_heads(x_h, dt_h, bias_h, alog_h, b_g, c_g, skip_h, all_ids):
-    total, heads, head_dim = x_h.shape
+def mixer_heads(x_h, dt_h, bias_h, alog_h, b_g, c_g, skip_h, all_ids, interpret=False):
+    total, x_width = x_h.shape
+    heads = dt_h.shape[1]
+    head_dim = x_width // heads
     nblk = total // BLOCK
     step = jax.nn.softplus(dt_h + bias_h[None, :])
     log_rate = -step * jnp.exp(alog_h)[None, :]
     log_cum = jnp.cumsum(log_rate.reshape(nblk, BLOCK, heads), axis=1)
-    lc = log_cum.transpose(0, 2, 1)
-    st = step.reshape(nblk, BLOCK, heads).transpose(0, 2, 1)
+    st = step.reshape(nblk, BLOCK, heads)
     ids = all_ids.reshape(nblk, BLOCK)
-    xb = x_h.reshape(nblk, BLOCK, heads, head_dim)
-    bb = b_g.reshape(nblk, BLOCK, STATE)
-    cb_in = c_g.reshape(nblk, BLOCK, STATE)
-    rows_at = jnp.arange(BLOCK)
-    same_doc = (ids[:, :, None] == ids[:, None, :]) & (rows_at[:, None] >= rows_at[None, :])[None]
-    inner_cb = jnp.einsum("bin,bjn->bij", cb_in, bb, preferred_element_type=jnp.float32)
-    decay = jnp.where(same_doc[:, None], jnp.exp(lc[:, :, :, None] - lc[:, :, None, :]), 0.0)
-    intra_w = (decay * inner_cb[:, None] * st[:, :, None, :]).astype(jnp.bfloat16)
-    local_out = jnp.einsum("bhij,bjhp->bihp", intra_w, xb, preferred_element_type=jnp.float32)
     last_id = ids[:, -1]
+    prev_last = jnp.concatenate([jnp.full((1,), -1, ids.dtype), last_id[:-1]])
+    edge_valid = (ids == prev_last[:, None]).astype(jnp.float32)
+    carry_scale = jnp.exp(log_cum) * edge_valid[:, :, None]
     end_scale = (
-        jnp.exp(lc[:, :, -1:] - lc) * st * (ids == last_id[:, None]).astype(jnp.float32)[:, None, :]
-    )
-    end_w = (end_scale[:, :, :, None] * bb.astype(jnp.float32)[:, None]).astype(jnp.bfloat16)
-    block_state = jnp.einsum("bhjn,bjhp->bhpn", end_w, xb, preferred_element_type=jnp.float32)
-    prev_last = jnp.concatenate([jnp.full((1,), -1, ids.dtype), last_id[:-1]])
+        jnp.exp(log_cum[:, -1:, :] - log_cum) * st * (ids == last_id[:, None]).astype(jnp.float32)[:, :, None]
+    )
     edge_match = (ids[:, 0] == prev_last).astype(jnp.float32)
-    block_gain = jnp.exp(lc[:, :, -1]) * (ids[:, 0] == last_id).astype(jnp.float32)[:, None]
+    block_gain = jnp.exp(log_cum[:, -1, :]) * (ids[:, 0] == last_id).astype(jnp.float32)[:, None]
     block_gain = block_gain * edge_match[:, None]
-    carries = [jnp.zeros_like(block_state[0])]
-    for b in range(nblk - 1):
-        carries.append(block_gain[b][:, None, None] * carries[-1] + block_state[b])
-    carry_bf = jnp.stack(carries).astype(jnp.bfloat16)
-    carried = jnp.einsum("bin,bhpn->bihp", cb_in, carry_bf, preferred_element_type=jnp.float32)
-    edge_valid = (ids == prev_last[:, None]).astype(jnp.float32)
-    scale = jnp.exp(log_cum) * edge_valid[:, :, None]
-    carried = carried * scale[:, :, :, None]
-    mixer_out = local_out + carried + skip_h[None, None, :, None] * xb.astype(jnp.float32)
-    return mixer_out.reshape(total, heads * head_dim)
+    gain_rows = jnp.broadcast_to(block_gain[:, :, None], (nblk, heads, STATE))
+    lc_rows = log_cum.transpose(0, 2, 1)
+    st_rows = st.transpose(0, 2, 1)
+    x_t = x_h.T
+
+    def kernel(x_ref, xt_ref, b_ref, c_ref, lcc_ref, lcr_ref, str_ref, csc_ref, esc_ref, gain_ref,
+               idc_ref, idr_ref, skip_ref, o_ref, sq_ref, carry_ref):
+        @pl.when(pl.program_id(0) == 0)
+        def _():
+            carry_ref[...] = jnp.zeros(carry_ref.shape, carry_ref.dtype)
+
+        b_blk = b_ref[...]
+        c_blk = c_ref[...]
+        inner_cb = lax.dot_general(c_blk, b_blk, (((1,), (1,)), ((), ())), preferred_element_type=jnp.float32)
+        rows_at = lax.broadcasted_iota(jnp.int32, (BLOCK, BLOCK), 0)
+        cols_at = lax.broadcasted_iota(jnp.int32, (BLOCK, BLOCK), 1)
+        same_doc = (idc_ref[...] == idr_ref[0]) & (rows_at >= cols_at)
+        b_f32 = b_blk.astype(jnp.float32)
+        sq = jnp.zeros((BLOCK, 1), jnp.float32)
+        for h in range(heads):
+            cols = slice(h * head_dim, (h + 1) * head_dim)
+            lc_c = lcc_ref[0, :, h:h + 1]
+            lc_r = lcr_ref[0, h:h + 1, :]
+            decay = jnp.where(same_doc, jnp.exp(lc_c - lc_r), 0.0)
+            intra_w = (decay * inner_cb * str_ref[0, h:h + 1, :]).astype(jnp.bfloat16)
+            xh = x_ref[:, cols]
+            local = jnp.dot(intra_w, xh, preferred_element_type=jnp.float32)
+            state_bf = carry_ref[h].astype(jnp.bfloat16)
+            carried = lax.dot_general(
+                c_blk, state_bf, (((1,), (1,)), ((), ())), preferred_element_type=jnp.float32
+            )
+            carried = carried * csc_ref[0, :, h:h + 1]
+            out = local + carried + skip_ref[h] * xh.astype(jnp.float32)
+            o_ref[:, cols] = out
+            sq = sq + jnp.sum(out * out, axis=1, keepdims=True)
+            end_w = (esc_ref[0, :, h:h + 1] * b_f32).astype(jnp.bfloat16)
+            block_state = jnp.dot(xt_ref[cols, :], end_w, preferred_element_type=jnp.float32)
+            carry_ref[h] = gain_ref[0, h:h + 1, :] * carry_ref[h] + block_state
+        sq_ref[...] = sq
+
+    per_block = lambda shape: pl.BlockSpec((1,) + shape, lambda i: (i, 0, 0))
+    return pl.pallas_call(
+        kernel,
+        grid=(nblk,),
+        in_specs=[
+            pl.BlockSpec((BLOCK, x_width), lambda i: (i, 0)),
+            pl.BlockSpec((x_width, BLOCK), lambda i: (0, i)),
+            pl.BlockSpec((BLOCK, STATE), lambda i: (i, 0)),
+            pl.BlockSpec((BLOCK, STATE), lambda i: (i, 0)),
+            per_block((BLOCK, heads)),
+            per_block((heads, BLOCK)),
+            per_block((heads, BLOCK)),
+            per_block((BLOCK, heads)),
+            per_block((BLOCK, heads)),
+            per_block((heads, STATE)),
+            pl.BlockSpec((BLOCK, 1), lambda i: (i, 0)),
+            per_block((1, BLOCK)),
+            pl.BlockSpec(memory_space=pltpu.SMEM),
+        ],
+        out_specs=[
+            pl.BlockSpec((BLOCK, x_width), lambda i: (i, 0)),
+            pl.BlockSpec((BLOCK, 1), lambda i: (i, 0)),
+        ],
+        out_shape=[
+            jax.ShapeDtypeStruct((total, x_width), jnp.float32),
+            jax.ShapeDtypeStruct((total, 1), jnp.float32),
+        ],
+        scratch_shapes=[pltpu.VMEM((heads, head_dim, STATE), jnp.float32)],
+        compiler_params=pltpu.CompilerParams(dimension_semantics=("arbitrary",)),
+        interpret=interpret,
+    )(
+        x_h, x_t, b_g, c_g, log_cum, lc_rows, st_rows, carry_scale, end_scale, gain_rows,
+        all_ids.reshape(total, 1), ids.reshape(nblk, 1, BLOCK), skip_h,
+    )
 
 
 def attend_heads(q_h, k_h, v_h, all_ids, interpret=False):
@@ -175,10 +232,8 @@
 
     attended = attend_heads(q_h, k_h, v_h, all_ids)
 
-    mixer_out = mixer_heads(
-        x_h.reshape(total, heads_dev, head_dim), dt_h, bias_h, alog_h, b_g, c_g, skip_h, all_ids
-    )
-    sq_part = jnp.sum(mixer_out * mixer_out, axis=1)
+    mixer_out, sq_part = mixer_heads(x_h, dt_h, bias_h, alog_h, b_g, c_g, skip_h, all_ids)
+    sq_part = sq_part[:, 0]
     sq_all = lax.all_to_all(
         jnp.broadcast_to(sq_part[None], (nctx, total)), "ctx", split_axis=0, concat_axis=0, tiled=True
     )

time: 233 us -> 244 us (1.047)
  Pallas kernels: 21.7 us -> 56.4 us
  waiting for transfers between devices: 36.9 us -> 58.6 us
  matrix products: 15.5 us -> 0 us
  local copies, waits for them, and re-layouts: 62.5 us -> 47.3 us
  other arithmetic: 27.8 us -> 16.5 us
  starting transfers between devices: 31.5 us -> 28.8 us
    pallas_call x0 -> x1, Pallas kernels: none -> 34.4 us  [mixer_heads(): pl.pallas_call(kernel, grid=(nblk,), in_specs=[pl.BlockSpec((BLOCK, x_wid...]
    all_to_all x4, waiting for transfers between devices: 36.9 us -> 55.5 us  [to_heads(): moved = lax.all_to_all(lead, 'ctx', split_axis=0, concat_axis=0, tiled=True)]
    dot_general x4 -> x0, matrix products: 15.5 us -> none  [the longest x1 6.02 us: mixer_heads(): jnp.einsum('bhij,bjhp->bihp', intra_w, xb, preferred_element_type=jnp.flo...]
    reshape x2 -> x0, local copies, waits for them, and re-layouts: 14.4 us -> none  [mixer_heads(): return mixer_out.reshape(total, heads * head_dim)]
    unnamed x14 -> x0, other arithmetic: 13.8 us -> none
    transpose x0 -> x2, local copies, waits for them, and re-layouts: none -> 4.64 us  [the longest x1 2.49 us: mixer_heads(): x_t = x_h.T]
    unnamed x41 -> x33, local copies, waits for them, and re-layouts: 12.4 us -> 16.4 us
    all_to_all x2, local copies, waits for them, and re-layouts: 6.72 us -> 2.99 us  [to_heads(): moved = lax.all_to_all(lead, 'ctx', split_axis=0, concat_axis=0, tiled=True)]
  transfers between devices with their start and end apart: 6 -> 6, of which waited for: 3 -> 4; matrix products, arithmetic and copies ran while one was open for 40% -> 22% of each run, Pallas kernels for 9% -> 23%
where the time goes in v4:
time: 244 us; the launch traced here: 243 us
  waiting for transfers between devices  58.6 us (24%)
  Pallas kernels  56.4 us (23%)
  local copies, waits for them, and re-layouts  47.3 us (19%)
  blocking collectives  35 us (14%)
  starting transfers between devices  28.8 us (12%)
  other arithmetic  16.5 us (7%)
    all_to_all x4, waiting for transfers between devices, to_heads(): moved = lax.all_to_all(lead, 'ctx', split_axis=0, concat_axis=0, tiled=True)  55.5 us
    all_to_all x1, blocking collectives, to_rows(): lax.all_to_all(block.reshape(chunks, tok_rows, width), 'ctx', split_axis=...  35 us
    pallas_call x1, Pallas kernels, mixer_heads(): pl.pallas_call(kernel, grid=(nblk,), in_specs=[pl.BlockSpec((BLOCK, x_wid...  34.4 us
    pallas_call x1, Pallas kernels, attend_heads(): pl.pallas_call(kernel, grid=(total // q_blk,), in_specs=[pl.BlockSpec((q_...  21.9 us
    all_to_all x4, starting transfers between devices, to_heads(): moved = lax.all_to_all(lead, 'ctx', split_axis=0, concat_axis=0, tiled=True)  19.9 us
    unnamed x33, local copies, waits for them, and re-layouts  16.4 us
    all_to_all x1, starting transfers between devices, body(): lax.all_to_all(jnp.broadcast_to(sq_part[None], (nctx, total)), 'ctx', spl...  6.91 us
  transfers between devices with their start and end apart: 6, of which 4 were waited for; matrix products, arithmetic and copies ran while one was open for 22% of the time, Pallas kernels for 23%

profile of v4, /device:TPU:32, one launch (start us, length us, event | category | flops | bytes accessed | tf_op | source)
XLA Modules:
  0.0 242.9 jit_solution(10552519115017606572)
XLA Ops:
  0.0 2.0 collective-permute-start
  3.6 7.0 %all-to-all-start.2 = ((f32[16,128,8]{1,2,0:T(8,128)}), f32[16,128,8]{1,2,0:T(8,128)S(1)}, u32[]{:S(2)}, u32[]{:S(2)}) async-start(f32[16,128,8]{1,2,0:T(8,128)} %bitcast.9), calls=%async_computation.2 | async-start | bytes 131072 | tf_op jit(solution)/shard_map/all_to_all | solution.py:31
  15.6 2.7 %all-to-all-done.2 = f32[16,128,8]{1,2,0:T(8,128)S(1)} async-done(((f32[16,128,8]{1,2,0:T(8,128)}), f32[16,128,8]{1,2,0:T(8,128)S(1)}, u32[]{:S(2)}, u32[]{:S(2)}) %all-to-all-start.2) | async-done | bytes 65568 | tf_op jit(solution)/shard_map/all_to_all | solution.py:31
  20.2 4.5 %all-to-all-start.1 = ((bf16[16,128,512]{1,2,0:T(8,128)(2,1)}), bf16[16,128,512]{1,2,0:T(8,128)(2,1)S(1)}, u32[]{:S(2)}, u32[]{:S(2)}) async-start(bf16[16,128,512]{1,2,0:T(8,128)(2,1)} %bitcast.86), calls=%async_computation.1 | async-start | bytes 4194304 | tf_op jit(solution)/shard_map/all_to_all | solution.py:31
  24.7 3.1 %collective-permute-done = bf16[128,8192]{1,0:T(8,128)(2,1)} collective-permute-done((bf16[128,8192]{1,0:T(8,128)(2,1)}, bf16[128,8192]{1,0:T(8,128)(2,1)}, u32[]{:S(2)}, u32[]{:S(2)}) %collective-permute-start) | collective-permute-done | bytes 2097184 | tf_op jit(solution)/shard_map/ppermute | solution.py:24
  31.1 28.7 %all-to-all-done.1 = bf16[16,128,512]{1,2,0:T(8,128)(2,1)S(1)} async-done(((bf16[16,128,512]{1,2,0:T(8,128)(2,1)}), bf16[16,128,512]{1,2,0:T(8,128)(2,1)S(1)}, u32[]{:S(2)}, u32[]{:S(2)}) %all-to-all-start.1) | async-done | bytes 2097184 | tf_op jit(solution)/shard_map/all_to_all | solution.py:31
  61.2 3.7 %all-to-all-start = ((bf16[16,128,512]{2,1,0:T(8,128)(2,1)}), bf16[16,128,512]{2,1,0:T(8,128)(2,1)S(1)}, u32[]{:S(2)}, u32[]{:S(2)}) async-start(bf16[16,128,512]{2,1,0:T(8,128)(2,1)} %bitcast.85), calls=%async_computation | async-start | bytes 4194304 | tf_op jit(solution)/shard_map/all_to_all | solution.py:31
  66.7 2.4 copy.179
  69.1 2.5 %copy.185 = bf16[128,16,512]{2,0,1:T(8,128)(2,1)} copy(bf16[128,16,512]{2,1,0:T(8,128)(2,1)S(1)} %bitcast.88) | data formatting | bytes 4194304 | tf_op jit(solution)/shard_map/reshape;squeeze | solution.py:30
  74.6 24.1 %all-to-all-done = bf16[16,128,512]{2,1,0:T(8,128)(2,1)S(1)} async-done(((bf16[16,128,512]{2,1,0:T(8,128)(2,1)}), bf16[16,128,512]{2,1,0:T(8,128)(2,1)S(1)}, u32[]{:S(2)}, u32[]{:S(2)}) %all-to-all-start) | async-done | bytes 2097184 | tf_op jit(solution)/shard_map/all_to_all | solution.py:31
  98.7 4.6 %all-to-all-start.4 = ((bf16[16,128,512]{2,1,0:T(8,128)(2,1)}), bf16[16,128,512]{2,1,0:T(8,128)(2,1)}, u32[]{:S(2)}, u32[]{:S(2)}) async-start(bf16[16,128,512]{2,1,0:T(8,128)(2,1)} %bitcast.84), calls=%async_computation.4 | async-start | bytes 4194304 | tf_op jit(solution)/shard_map/all_to_all | solution.py:31
  107.4 3.3 %multiply_multiply_fusion = (f32[16,128,8]{2,1,0:T(8,128)}, f32[16,8,128]{1,2,0:T(8,128)}) fusion(f32[16,128,8]{2,1,0:T(8,128)S(1)} %copy.151, f32[16,128]{1,0:T(8,128)S(1)} %get-tuple-element.21, f32[16,128,8]{2,1,0:T(8,128)} %copy-done.3, f32[8]{0:T(128)S(1)} %get-tuple-element.25), kind=kLoop, calls=%fused_computation.9 | loop fusion | flops 147456 | bytes 270368 | tf_op jit(solution)/shard_map/mul | solution.py:57
  110.6 2.2 copy.157.str_ref
  115.2 2.7 %copy.137 = bf16[16,128,512]{1,0,2:T(8,128)(2,1)} copy(bf16[16,128,512]{1,2,0:T(8,128)(2,1)S(1)} %copy-done.5) | data formatting | bytes 4194304 | tf_op jit(solution)/shard_map/all_to_all | solution.py:31
  117.9 4.2 %reshape_reshape.3 = bf16[2048,4,128]{0,2,1:T(8,128)(2,1)} reshape(bf16[16,128,512]{1,0,2:T(8,128)(2,1)} %copy.137) | data formatting | bytes 4194304 | tf_op jit(solution)/shard_map/reshape;reshape | solution.py:219
  122.1 2.7 %fusion.11 = (bf16[2048,1,128]{0,2,1:T(8,128)(2,1)}, bf16[2048,1,128]{0,2,1:T(8,128)(2,1)S(1)}, bf16[2048,1,128]{0,2,1:T(8,128)(2,1)}, bf16[2048,1,128]{0,2,1:T(8,128)(2,1)S(1)}) fusion(bf16[2048,4,128]{0,2,1:T(8,128)(2,1)} %reshape_reshape.3), kind=kLoop, calls=%fused_computation.34 | loop fusion | bytes 4194304 | tf_op jit(solution)/shard_map/slice | solution.py:220
  126.8 2.0 copy.168
  128.9 2.5 %copy.155.xt_ref = bf16[512,2048]{1,0:T(8,128)(2,1)} copy(bf16[512,2048]{0,1:T(8,128)(2,1)S(1)} %bitcast.80) | data formatting | bytes 4194304 | tf_op jit(solution)/shard_map/transpose | solution.py:65
  132.1 34.4 %shard_map.127 = (f32[2048,512]{1,0:T(8,128)}, f32[2048,1]{1,0:T(8,128)}) custom-call(bf16[2048,512]{1,0:T(8,128)(2,1)} %bitcast.81, bf16[512,2048]{1,0:T(8,128)(2,1)} %copy.155.xt_ref, bf16[2048,128]{1,0:T(8,128)(2,1)} %bitcast.89, bf16[2048,128]{1,0:T(8,128)(2,1)} %bitcast.90, f32[16,128,8]{2,1,0:T(8,128)} %copy.156.lcc_ref, f32[16,8,128]{2,1,0:T(8,128)} %bitcast.98, ...), custom_call_target="tpu_custom_call" | custom-call | tf_op jit(solution)/shard_map/pallas_call | solution.py:103
  168.8 6.9 %all-to-all-start.3 = ((f32[16,1,2048]{2,1,0:T(1,128)}), f32[16,1,2048]{2,1,0:T(1,128)S(1)}, u32[]{:S(2)}, u32[]{:S(2)}) async-start(f32[16,1,2048]{2,1,0:T(1,128)} %broadcast_in_dim.11), calls=%async_computation.3 | async-start | bytes 262144 | tf_op jit(solution)/shard_map/all_to_all | solution.py:237
  178.5 21.9 %shard_map.128 = bf16[2048,512]{1,0:T(8,128)(2,1)} custom-call(bf16[2048,512]{1,0:T(8,128)(2,1)} %bitcast.26.q_ref, bf16[2048,128]{1,0:T(8,128)(2,1)} %bitcast.91, bf16[2048,128]{1,0:T(8,128)(2,1)} %bitcast.92, s32[2048,1]{1,0:T(8,128)} %copy.158.idc_ref.ic_ref, s32[1,2048]{1,0:T(1,128)} %ir_ref.1), custom_call_target="tpu_custom_call" | custom-call | tf_op jit(solution)/shard_map/pallas_call | solution.py:166
  200.5 3.8 %add_convert_fusion = bf16[2048,512]{1,0:T(8,128)(2,1)S(1)} fusion(bf16[2048,512]{1,0:T(8,128)(2,1)} %shard_map.128, f32[2048,512]{1,0:T(8,128)} %get-tuple-element.7, f32[512]{0:T(512)S(1)} %bitcast.108, f32[2048]{0:T(1024)S(1)} %add_rsqrt_fusion, bf16[16,128,512]{2,1,0:T(8,128)(2,1)S(1)} %copy-done.2), kind=kLoop, calls=%fused_computation | loop fusion | flops 9437184 | bytes 10496000 | tf_op jit(solution)/shard_map/convert_element_type | solution.py:245
  204.3 35.0 %all_to_all.31 = bf16[16,128,512]{2,1,0:T(8,128)(2,1)S(1)} all-to-all(bf16[16,128,512]{2,1,0:T(8,128)(2,1)S(1)} %bitcast.82), channel_id=1, replica_groups=mesh['section'=8,'ctx'=16] {'ctx'}, dimensions={0} | all-to-all | bytes 4194304 | tf_op jit(solution)/shard_map/all_to_all | solution.py:38
  240.5 2.3 broadcast_in_dim_reshape.3
  (66 shorter events, 33.2 us)
Async XLA Ops:
  0.0 71.7 %copy-start = (f32[1,128]{1,0:T(1,128)S(1)}, f32[1,128]{1,0:T(1,128)}, u32[]{:S(2)}) copy-start(f32[1,128]{1,0:T(1,128)} %param.20) | copy-start | bytes 1540
  0.0 27.8 %collective-permute-start = (bf16[128,8192]{1,0:T(8,128)(2,1)}, bf16[128,8192]{1,0:T(8,128)(2,1)}, u32[]{:S(2)}, u32[]{:S(2)}) collective-permute-start(bf16[128,8192]{1,0:T(8,128)(2,1)} %bitcast.111), channel_id=1, source_target_pairs={{0,16},{16,32},{32,48},{48,64},{64,80},{80,96},{96,112},{1,17},{17... | collective-permute-start | bytes 6291464 | tf_op jit(solution)/shard_map/ppermute | solution.py:24
  3.6 14.7 %all-to-all-start.2 = ((f32[16,128,8]{1,2,0:T(8,128)}), f32[16,128,8]{1,2,0:T(8,128)S(1)}, u32[]{:S(2)}, u32[]{:S(2)}) async-start(f32[16,128,8]{1,2,0:T(8,128)} %bitcast.9), calls=%async_computation.2 | async-start | bytes 131072 | tf_op jit(solution)/shard_map/all_to_all | solution.py:31
  20.2 39.7 %all-to-all-start.1 = ((bf16[16,128,512]{1,2,0:T(8,128)(2,1)}), bf16[16,128,512]{1,2,0:T(8,128)(2,1)S(1)}, u32[]{:S(2)}, u32[]{:S(2)}) async-start(bf16[16,128,512]{1,2,0:T(8,128)(2,1)} %bitcast.86), calls=%async_computation.1 | async-start | bytes 4194304 | tf_op jit(solution)/shard_map/all_to_all | solution.py:31
  59.8 1.3 copy-start.4
  59.8 5.1 %copy-start.7 = (s32[1,2048]{1,0:T(1,128)S(1)}, s32[1,2048]{1,0:T(1,128)}, u32[]{:S(2)}) copy-start(s32[1,2048]{1,0:T(1,128)} %ir_ref.1) | copy-start | bytes 24580
  61.2 37.5 %all-to-all-start = ((bf16[16,128,512]{2,1,0:T(8,128)(2,1)}), bf16[16,128,512]{2,1,0:T(8,128)(2,1)S(1)}, u32[]{:S(2)}, u32[]{:S(2)}) async-start(bf16[16,128,512]{2,1,0:T(8,128)(2,1)} %bitcast.85), calls=%async_computation | async-start | bytes 4194304 | tf_op jit(solution)/shard_map/all_to_all | solution.py:31
  69.1 3.3 %copy-start.8 = (f32[1,128]{1,0:T(1,128)S(1)}, f32[1,128]{1,0:T(1,128)}, u32[]{:S(2)}) copy-start(f32[1,128]{1,0:T(1,128)} %param.16) | copy-start | bytes 1540
  69.1 3.2 %copy-start.9 = (f32[1,128]{1,0:T(1,128)S(1)}, f32[1,128]{1,0:T(1,128)}, u32[]{:S(2)}) copy-start(f32[1,128]{1,0:T(1,128)} %param.17) | copy-start | bytes 1540
  72.9 25.8 %copy-start.3 = (f32[16,128,8]{2,1,0:T(8,128)}, f32[16,128,8]{2,1,0:T(8,128)S(1)}, u32[]{:S(2)}) copy-start(f32[16,128,8]{2,1,0:T(8,128)S(1)} %copy.141) | copy-start | bytes 196612
  98.7 30.2 %copy-start.1 = (bf16[16,128,512]{2,1,0:T(8,128)(2,1)}, bf16[16,128,512]{2,1,0:T(8,128)(2,1)S(1)}, u32[]{:S(2)}) copy-start(bf16[16,128,512]{2,1,0:T(8,128)(2,1)S(1)} %all-to-all-done) | copy-start | bytes 6291460
  98.7 69.4 %all-to-all-start.4 = ((bf16[16,128,512]{2,1,0:T(8,128)(2,1)}), bf16[16,128,512]{2,1,0:T(8,128)(2,1)}, u32[]{:S(2)}, u32[]{:S(2)}) async-start(bf16[16,128,512]{2,1,0:T(8,128)(2,1)} %bitcast.84), calls=%async_computation.4 | async-start | bytes 4194304 | tf_op jit(solution)/shard_map/all_to_all | solution.py:31
  105.6 5.0 %copy-start.6 = (f32[16,128,8]{1,2,0:T(8,128)}, f32[16,128,8]{1,2,0:T(8,128)S(1)}, u32[]{:S(2)}) copy-start(f32[16,128,8]{1,2,0:T(8,128)S(1)} %copy.144) | copy-start | bytes 196612
  113.3 2.0 copy-start.5
  168.8 31.6 %all-to-all-start.3 = ((f32[16,1,2048]{2,1,0:T(1,128)}), f32[16,1,2048]{2,1,0:T(1,128)S(1)}, u32[]{:S(2)}, u32[]{:S(2)}) async-start(f32[16,1,2048]{2,1,0:T(1,128)} %broadcast_in_dim.11), calls=%async_computation.3 | async-start | bytes 262144 | tf_op jit(solution)/shard_map/all_to_all | solution.py:237
  178.5 22.0 %copy-start.2 = (bf16[16,128,512]{2,1,0:T(8,128)(2,1)S(1)}, bf16[16,128,512]{2,1,0:T(8,128)(2,1)}, u32[]{:S(2)}) copy-start(bf16[16,128,512]{2,1,0:T(8,128)(2,1)} %copy-done.1) | copy-start | bytes 6291460

commit v5 on v4

--- a/solution.py
+++ b/solution.py
@@ -135,24 +135,21 @@
     )
 
 
-def attend_heads(q_h, k_h, v_h, all_ids, interpret=False):
-    total, q_width = q_h.shape
-    groups = q_width // HEAD_A
-    q_blk = min(Q_BLOCK, total)
-    window = min(q_blk + MOST_DOC, total)
+def attend_rows(q_row, kv_win, ids_q, ids_k, interpret=False):
+    tok_rows, q_width = q_row.shape
+    window = kv_win.shape[0]
+    kv_heads = kv_win.shape[1] // (2 * HEAD_A)
+    group = q_width // HEAD_A // kv_heads
+    lead = window - tok_rows
     inv_sqrt = 1.0 / math.sqrt(HEAD_A)
 
-    def kernel(q_ref, k_ref, v_ref, ic_ref, ir_ref, o_ref):
-        q0 = pl.multiple_of(pl.program_id(0) * q_blk, q_blk)
-        k0 = pl.multiple_of(jnp.clip(q0 + q_blk - window, 0, total - window), q_blk)
-        kb = k_ref[pl.ds(k0, window), :]
-        vb = v_ref[pl.ds(k0, window), :]
-        qid = ic_ref[pl.ds(q0, q_blk), :]
-        kid = ir_ref[:, pl.ds(k0, window)]
-        q_at = q0 + lax.broadcasted_iota(jnp.int32, (q_blk, window), 0)
-        k_at = k0 + lax.broadcasted_iota(jnp.int32, (q_blk, window), 1)
-        allowed = (qid == kid) & (q_at >= k_at)
-        for g in range(groups):
+    def kernel(q_ref, k_ref, v_ref, iq_ref, ik_ref, o_ref):
+        q_at = lead + lax.broadcasted_iota(jnp.int32, (tok_rows, window), 0)
+        k_at = lax.broadcasted_iota(jnp.int32, (tok_rows, window), 1)
+        allowed = (iq_ref[...] == ik_ref[...]) & (q_at >= k_at)
+        kb = k_ref[...]
+        vb = v_ref[...]
+        for g in range(group):
             cols = slice(g * HEAD_A, (g + 1) * HEAD_A)
             logits = lax.dot_general(
                 q_ref[:, cols], kb, (((1,), (1,)), ((), ())), preferred_element_type=jnp.float32
@@ -165,18 +162,18 @@
 
     return pl.pallas_call(
         kernel,
-        grid=(total // q_blk,),
+        grid=(kv_heads,),
         in_specs=[
-            pl.BlockSpec((q_blk, q_width), lambda i: (i, 0)),
-            pl.BlockSpec((total, HEAD_A), lambda i: (0, 0)),
-            pl.BlockSpec((total, HEAD_A), lambda i: (0, 0)),
-            pl.BlockSpec((total, 1), lambda i: (0, 0)),
-            pl.BlockSpec((1, total), lambda i: (0, 0)),
-        ],
-        out_specs=pl.BlockSpec((q_blk, q_width), lambda i: (i, 0)),
-        out_shape=jax.ShapeDtypeStruct((total, q_width), jnp.bfloat16),
+            pl.BlockSpec((tok_rows, group * HEAD_A), lambda i: (0, i)),
+            pl.BlockSpec((window, HEAD_A), lambda i: (0, i)),
+            pl.BlockSpec((window, HEAD_A), lambda i: (0, kv_heads + i)),
+            pl.BlockSpec((tok_rows, 1), lambda i: (0, 0)),
+            pl.BlockSpec((1, window), lambda i: (0, 0)),
+        ],
+        out_specs=pl.BlockSpec((tok_rows, group * HEAD_A), lambda i: (0, i)),
+        out_shape=jax.ShapeDtypeStruct((tok_rows, q_width), jnp.bfloat16),
         interpret=interpret,
-    )(q_h, k_h, v_h, all_ids.reshape(total, 1), all_ids.reshape(1, total))
+    )(q_row, kv_win, kv_win, ids_q, ids_k)
 
 
 def body(
@@ -205,45 +202,44 @@
     kv_heads = keys.shape[2] // HEAD_A
     qpd = part // HEAD_A
 
-    q_h = to_heads(queries[0], nctx)
-    kvbc = jnp.stack(
-        [
-            keys[0].reshape(tok_rows, kv_heads, HEAD_A),
-            values[0].reshape(tok_rows, kv_heads, HEAD_A),
-            b_in[0].reshape(tok_rows, GROUPS, STATE),
-            c_in[0].reshape(tok_rows, GROUPS, STATE),
-        ],
-        axis=2,
-    )
-    kvbc = jnp.repeat(kvbc, nctx // kv_heads, axis=1).reshape(tok_rows, nctx * 4 * HEAD_A)
-    kvbc_h = to_heads(kvbc, nctx).reshape(total, 4, HEAD_A)
-    k_h, v_h, b_g, c_g = kvbc_h[:, 0], kvbc_h[:, 1], kvbc_h[:, 2], kvbc_h[:, 3]
+    rep = nctx // kv_heads
+    bc = jnp.stack(
+        [b_in[0].reshape(tok_rows, GROUPS, STATE), c_in[0].reshape(tok_rows, GROUPS, STATE)], axis=2
+    )
+    bc_h = to_heads(jnp.repeat(bc, rep, axis=1).reshape(tok_rows, nctx * 2 * STATE), nctx)
+    b_g, c_g = bc_h[:, :STATE], bc_h[:, STATE:]
     dt_h = to_heads(dt_raw[0], nctx)
 
     handed = shifted(previous[0], "section", 1)
     stream = jnp.where(lax.axis_index("section") == 0, fresh, handed)
     x_h = to_heads(stream, nctx)
 
+    halo = -(-MOST_DOC // tok_rows)
+    kv_row = jnp.concatenate([keys[0], values[0]], axis=1)
+    kv_win = jnp.concatenate([shifted(kv_row, "ctx", by) for by in range(halo, 0, -1)] + [kv_row], axis=0)
     all_ids = doc_ids[0]
+    lead = halo * tok_rows
+    padded_ids = jnp.concatenate([jnp.full((lead,), -1, all_ids.dtype), all_ids])
+    ids_k = lax.dynamic_slice_in_dim(padded_ids, me * tok_rows, lead + tok_rows)
+    ids_q = lax.dynamic_slice_in_dim(all_ids, me * tok_rows, tok_rows)
+    attended = attend_rows(queries[0], kv_win, ids_q.reshape(tok_rows, 1), ids_k.reshape(1, lead + tok_rows))
+
     bias_h = lax.dynamic_slice_in_dim(dt_bias[0], me * heads_dev, heads_dev)
     alog_h = lax.dynamic_slice_in_dim(a_log[0], me * heads_dev, heads_dev)
     skip_h = lax.dynamic_slice_in_dim(skip_d[0], me * heads_dev, heads_dev)
     gain_h = lax.dynamic_slice_in_dim(norm_gain[0], me * part, part)
 
-    attended = attend_heads(q_h, k_h, v_h, all_ids)
-
     mixer_out, sq_part = mixer_heads(x_h, dt_h, bias_h, alog_h, b_g, c_g, skip_h, all_ids)
-    sq_part = sq_part[:, 0]
     sq_all = lax.all_to_all(
-        jnp.broadcast_to(sq_part[None], (nctx, total)), "ctx", split_axis=0, concat_axis=0, tiled=True
+        jnp.broadcast_to(sq_part[:, 0][None], (nctx, total)), "ctx", split_axis=0, concat_axis=0, tiled=True
     )
     mean_sq = (jnp.sum(sq_all, axis=0) / width)[:, None]
     inv_rms = lax.rsqrt(mean_sq + norm_eps)
     mixed = (
         x_h.astype(jnp.float32) + mixer_out * inv_rms * gain_h.astype(jnp.float32)[None, :]
     ).astype(jnp.bfloat16)
-    out_h = (mixed.astype(jnp.float32) + attended.astype(jnp.float32)).astype(jnp.bfloat16)
-    return to_rows(out_h, nctx)[None]
+    mixed_rows = to_rows(mixed, nctx)
+    return (mixed_rows.astype(jnp.float32) + attended.astype(jnp.float32)).astype(jnp.bfloat16)[None]
 
 
 def solution(mesh):

time: 244 us -> 264 us (1.082)
  blocking collectives: 35 us -> 0 us
  waiting for transfers between devices: 58.6 us -> 84.3 us
  starting transfers between devices: 28.8 us -> 45.7 us
  Pallas kernels: 56.4 us -> 63.1 us
  other arithmetic: 16.5 us -> 21.7 us
    ppermute x1 -> x5, waiting for transfers between devices: 3.11 us -> 47.8 us  [shifted(): return lax.ppermute(value, axis, pairs)]
    all_to_all x1 -> x0, blocking collectives: 35 us -> none  [to_rows(): lax.all_to_all(block.reshape(chunks, tok_rows, width), 'ctx', split_axis=...]
    all_to_all x4 -> x3, waiting for transfers between devices: 55.5 us -> 34.7 us  [to_heads(): moved = lax.all_to_all(lead, 'ctx', split_axis=0, concat_axis=0, tiled=True)]
    ppermute x1 -> x5, starting transfers between devices: 2.04 us -> 18.4 us  [shifted(): return lax.ppermute(value, axis, pairs)]
    reshape x1 -> x5, local copies, waits for them, and re-layouts: 1.53 us -> 9.22 us  [the longest x1 3.94 us: to_rows(): block.reshape(chunks, tok_rows, width)]
    another operation x3 -> x1, local copies, waits for them, and re-layouts: 7.33 us -> 0.54 us  [body(): jnp.stack([b_in[0].reshape(tok_rows, GROUPS, STATE), c_in[0].reshape(tok_...]
    pallas_call x1, Pallas kernels: 21.9 us -> 28.7 us  [attend_rows(): pl.pallas_call(kernel, grid=(kv_heads,), in_specs=[pl.BlockSpec((tok_rows...]
    unnamed x33 -> x34, local copies, waits for them, and re-layouts: 16.4 us -> 10.8 us
  transfers between devices with their start and end apart: 6 -> 10, of which waited for: 4 -> 4; matrix products, arithmetic and copies ran while one was open for 22% -> 17% of each run, Pallas kernels for 23% -> 11%
where the time goes in v5:
time: 264 us; the launch traced here: 261 us
  waiting for transfers between devices  84.3 us (32%)
  Pallas kernels  63.1 us (24%)
  local copies, waits for them, and re-layouts  46.4 us (18%)
  starting transfers between devices  45.7 us (17%)
  other arithmetic  21.7 us (8%)
    ppermute x5, waiting for transfers between devices, shifted(): return lax.ppermute(value, axis, pairs)  47.8 us
    all_to_all x3, waiting for transfers between devices, to_heads(): moved = lax.all_to_all(lead, 'ctx', split_axis=0, concat_axis=0, tiled=True)  34.7 us
    pallas_call x1, Pallas kernels, mixer_heads(): pl.pallas_call(kernel, grid=(nblk,), in_specs=[pl.BlockSpec((BLOCK, x_wid...  34.4 us
    pallas_call x1, Pallas kernels, attend_rows(): pl.pallas_call(kernel, grid=(kv_heads,), in_specs=[pl.BlockSpec((tok_rows...  28.7 us
    ppermute x5, starting transfers between devices, shifted(): return lax.ppermute(value, axis, pairs)  18.4 us
    all_to_all x3, starting transfers between devices, to_heads(): moved = lax.all_to_all(lead, 'ctx', split_axis=0, concat_axis=0, tiled=True)  18 us
    unnamed x34, local copies, waits for them, and re-layouts  10.8 us
    all_to_all x1, starting transfers between devices, to_rows(): lax.all_to_all(block.reshape(chunks, tok_rows, width), 'ctx', split_axis=...  5.6 us
  transfers between devices with their start and end apart: 10, of which 4 were waited for; matrix products, arithmetic and copies ran while one was open for 17% of the time, Pallas kernels for 11%

profile of v5, /device:TPU:32, one launch (start us, length us, event | category | flops | bytes accessed | tf_op | source)
XLA Modules:
  0.0 261.5 jit_solution(6395261989081945531)
XLA Ops:
  3.6 7.0 %all-to-all-start.2 = ((f32[16,128,8]{1,2,0:T(8,128)}), f32[16,128,8]{1,2,0:T(8,128)S(1)}, u32[]{:S(2)}, u32[]{:S(2)}) async-start(f32[16,128,8]{1,2,0:T(8,128)} %bitcast.7), calls=%async_computation.2 | async-start | bytes 131072 | tf_op jit(solution)/shard_map/all_to_all | solution.py:31
  19.8 7.3 %all-to-all-start.1 = ((bf16[16,128,256]{2,1,0:T(8,128)(2,1)}), bf16[16,128,256]{2,1,0:T(8,128)(2,1)}, u32[]{:S(2)}, u32[]{:S(2)}) async-start(bf16[16,128,256]{2,1,0:T(8,128)(2,1)} %bitcast.4), calls=%async_computation.1 | async-start | bytes 2097152 | tf_op jit(solution)/shard_map/all_to_all | solution.py:31
  30.8 2.4 copy.123
  33.3 14.6 %all-to-all-done.1 = bf16[16,128,256]{2,1,0:T(8,128)(2,1)} async-done(((bf16[16,128,256]{2,1,0:T(8,128)(2,1)}), bf16[16,128,256]{2,1,0:T(8,128)(2,1)}, u32[]{:S(2)}, u32[]{:S(2)}) %all-to-all-start.1) | async-done | bytes 1048608 | tf_op jit(solution)/shard_map/all_to_all | solution.py:31
  47.9 3.7 %all-to-all-start = ((bf16[16,128,512]{1,2,0:T(8,128)(2,1)}), bf16[16,128,512]{1,2,0:T(8,128)(2,1)S(1)}, u32[]{:S(2)}, u32[]{:S(2)}) async-start(bf16[16,128,512]{1,2,0:T(8,128)(2,1)} %bitcast.75), calls=%async_computation | async-start | bytes 4194304 | tf_op jit(solution)/shard_map/all_to_all | solution.py:31
  55.7 3.3 %multiply_multiply_fusion = (f32[16,128,8]{2,1,0:T(8,128)}, f32[16,8,128]{1,2,0:T(8,128)}) fusion(f32[16,128,8]{2,1,0:T(8,128)S(1)} %copy.137, f32[16,128]{1,0:T(8,128)S(1)} %get-tuple-element.21, f32[16,128,8]{2,1,0:T(8,128)} %copy-done.3, f32[8]{0:T(128)S(1)} %get-tuple-element.25), kind=kLoop, calls=%fused_computation.9 | loop fusion | flops 147456 | bytes 270368 | tf_op jit(solution)/shard_map/mul | solution.py:57
  59.0 2.2 copy.143.str_ref
  63.0 2.3 fusion.15
  65.3 20.1 %all-to-all-done = bf16[16,128,512]{1,2,0:T(8,128)(2,1)S(1)} async-done(((bf16[16,128,512]{1,2,0:T(8,128)(2,1)}), bf16[16,128,512]{1,2,0:T(8,128)(2,1)S(1)}, u32[]{:S(2)}, u32[]{:S(2)}) %all-to-all-start) | async-done | bytes 2097184 | tf_op jit(solution)/shard_map/all_to_all | solution.py:31
  85.4 2.6 fusion.13
  87.9 3.9 %copy.141.x_ref = bf16[2048,512]{1,0:T(8,128)(2,1)} copy(bf16[2048,512]{0,1:T(8,128)(2,1)} %get-tuple-element.10) | data formatting | bytes 4194304 | tf_op jit(solution)/shard_map/reshape | solution.py:32
  92.6 34.4 %shard_map.127 = (f32[2048,512]{1,0:T(8,128)}, f32[2048,1]{1,0:T(8,128)}) custom-call(bf16[2048,512]{1,0:T(8,128)(2,1)} %copy.141.x_ref, bf16[512,2048]{1,0:T(8,128)(2,1)} %get-tuple-element.9.xt_ref, bf16[2048,128]{1,0:T(8,128)(2,1)} %get-tuple-element.16.b_ref, bf16[2048,128]{1,0:T(8,128)(2,1)} %get-tuple-element.15.c_ref, f32[16,128,8]{2,1,0:T(8,128)} %copy.142.lcc_ref, ...), custom_call_target="tpu_custom_call" | custom-call | tf_op jit(solution)/shard_map/pallas_call | solution.py:103
  129.3 3.7 %all-to-all-start.3 = ((f32[16,1,2048]{2,1,0:T(1,128)}), f32[16,1,2048]{2,1,0:T(1,128)S(1)}, u32[]{:S(2)}, u32[]{:S(2)}) async-start(f32[16,1,2048]{2,1,0:T(1,128)} %broadcast_in_dim.13), calls=%async_computation.3 | async-start | bytes 262144 | tf_op jit(solution)/shard_map/all_to_all | solution.py:233
  133.7 5.5 %copy.146 = f32[2048,512]{0,1:T(8,128)} copy(f32[2048,512]{1,0:T(8,128)} %get-tuple-element.7) | data formatting | bytes 8388608 | tf_op jit(solution)/shard_map/pallas_call | solution.py:103
  141.1 4.3 %add_convert_fusion.1 = bf16[2048,512]{0,1:T(8,128)(2,1)} fusion(f32[2048,512]{0,1:T(8,128)} %copy.146, f32[512]{0:T(512)S(1)} %bitcast.92, f32[2048]{0:T(1024)S(1)} %add_rsqrt_fusion, bf16[16,128,512]{1,2,0:T(8,128)(2,1)S(1)} %all-to-all-done), kind=kLoop, calls=%fused_computation.2 | loop fusion | flops 5242880 | bytes 8398848 | tf_op jit(solution)/shard_map/convert_element_type | solution.py:240
  145.3 3.9 %copy.151 = bf16[2048,512]{1,0:T(8,128)(2,1)} copy(bf16[2048,512]{0,1:T(8,128)(2,1)} %add_convert_fusion.1) | data formatting | bytes 4194304 | tf_op jit(solution)/shard_map/reshape | solution.py:38
  149.3 5.6 %all-to-all-start.4 = ((bf16[16,128,512]{2,1,0:T(8,128)(2,1)}), bf16[16,128,512]{2,1,0:T(8,128)(2,1)}, u32[]{:S(2)}, u32[]{:S(2)}) async-start(bf16[16,128,512]{2,1,0:T(8,128)(2,1)} %bitcast.23), calls=%async_computation.4 | async-start | bytes 4194304 | tf_op jit(solution)/shard_map/all_to_all | solution.py:38
  155.7 4.6 %collective-permute-start.1 = (bf16[128,2048]{1,0:T(8,128)(2,1)}, bf16[128,2048]{1,0:T(8,128)(2,1)}, u32[]{:S(2)}, u32[]{:S(2)}) collective-permute-start(bf16[128,2048]{1,0:T(8,128)(2,1)} %pad_maximum_fusion.1), channel_id=1, source_target_pairs={{0,4},{1,5},{2,6},{3,7},{4,8},{5,9},{6,10},{7,11},{8,12},{9,13},{1... | collective-permute-start | bytes 1572872 | tf_op jit(solution)/shard_map/ppermute | solution.py:24
  160.3 5.4 %collective-permute-start.2 = (bf16[128,2048]{1,0:T(8,128)(2,1)}, bf16[128,2048]{1,0:T(8,128)(2,1)}, u32[]{:S(2)}, u32[]{:S(2)}) collective-permute-start(bf16[128,2048]{1,0:T(8,128)(2,1)} %pad_maximum_fusion.1), channel_id=1, source_target_pairs={{0,3},{1,4},{2,5},{3,6},{4,7},{5,8},{6,9},{7,10},{8,11},{9,12},{10... | collective-permute-start | bytes 1572872 | tf_op jit(solution)/shard_map/ppermute | solution.py:24
  165.7 3.7 %collective-permute-start.3 = (bf16[128,2048]{1,0:T(8,128)(2,1)}, bf16[128,2048]{1,0:T(8,128)(2,1)}, u32[]{:S(2)}, u32[]{:S(2)}) collective-permute-start(bf16[128,2048]{1,0:T(8,128)(2,1)} %pad_maximum_fusion.1), channel_id=1, source_target_pairs={{0,2},{1,3},{2,4},{3,5},{4,6},{5,7},{6,8},{7,9},{8,10},{9,11},{10,... | collective-permute-start | bytes 1572872 | tf_op jit(solution)/shard_map/ppermute | solution.py:24
  169.4 2.7 %collective-permute-start.4 = (bf16[128,2048]{1,0:T(8,128)(2,1)}, bf16[128,2048]{1,0:T(8,128)(2,1)}, u32[]{:S(2)}, u32[]{:S(2)}) collective-permute-start(bf16[128,2048]{1,0:T(8,128)(2,1)} %pad_maximum_fusion.1), channel_id=1, source_target_pairs={{0,1},{1,2},{2,3},{3,4},{4,5},{5,6},{6,7},{7,8},{8,9},{9,10},{10,1... | collective-permute-start | bytes 1572872 | tf_op jit(solution)/shard_map/ppermute | solution.py:24
  173.6 47.8 %collective-permute-done.1 = bf16[128,2048]{1,0:T(8,128)(2,1)} collective-permute-done((bf16[128,2048]{1,0:T(8,128)(2,1)}, bf16[128,2048]{1,0:T(8,128)(2,1)}, u32[]{:S(2)}, u32[]{:S(2)}) %collective-permute-start.1) | collective-permute-done | bytes 524320 | tf_op jit(solution)/shard_map/ppermute | solution.py:24
  227.3 28.7 %shard_map.128 = bf16[128,8192]{1,0:T(8,128)(2,1)} custom-call(bf16[128,8192]{1,0:T(8,128)(2,1)} %bitcast.76, bf16[640,2048]{1,0:T(8,128)(2,1)} %copy-done.2, bf16[640,2048]{1,0:T(8,128)(2,1)} %copy-done.2, s32[128,1]{1,0:T(8,128)} %copy.149.iq_ref, s32[1,640]{1,0:T(1,128)} %reshape.154.ik_ref), custom_call_target="tpu_custom_call" | custom-call | tf_op jit(solution)/shard_map/pallas_call | solution.py:163
  255.9 2.1 convert_bitcast_fusion
  (82 shorter events, 39.4 us)
Async XLA Ops:
  0.0 19.1 %copy-start = (f32[1,128]{1,0:T(1,128)S(1)}, f32[1,128]{1,0:T(1,128)}, u32[]{:S(2)}) copy-start(f32[1,128]{1,0:T(1,128)} %param.20) | copy-start | bytes 1540
  0.0 29.0 %collective-permute-start = (bf16[128,8192]{1,0:T(8,128)(2,1)}, bf16[128,8192]{1,0:T(8,128)(2,1)}, u32[]{:S(2)}, u32[]{:S(2)}) collective-permute-start(bf16[128,8192]{1,0:T(8,128)(2,1)} %bitcast.95), channel_id=1, source_target_pairs={{0,16},{16,32},{32,48},{48,64},{64,80},{80,96},{96,112},{1,17},{17... | collective-permute-start | bytes 6291464 | tf_op jit(solution)/shard_map/ppermute | solution.py:24
  3.6 16.1 %all-to-all-start.2 = ((f32[16,128,8]{1,2,0:T(8,128)}), f32[16,128,8]{1,2,0:T(8,128)S(1)}, u32[]{:S(2)}, u32[]{:S(2)}) async-start(f32[16,128,8]{1,2,0:T(8,128)} %bitcast.7), calls=%async_computation.2 | async-start | bytes 131072 | tf_op jit(solution)/shard_map/all_to_all | solution.py:31
  14.6 2.9 %copy-start.8 = (s32[1,2048]{1,0:T(1,128)S(1)}, s32[1,2048]{1,0:T(1,128)}, u32[]{:S(2)}) copy-start(s32[1,2048]{1,0:T(1,128)} %param.25) | copy-start | bytes 24580
  15.2 3.8 %copy-start.10 = (f32[1,128]{1,0:T(1,128)S(1)}, f32[1,128]{1,0:T(1,128)}, u32[]{:S(2)}) copy-start(f32[1,128]{1,0:T(1,128)} %param.16) | copy-start | bytes 1540
  15.2 3.7 %copy-start.11 = (f32[1,128]{1,0:T(1,128)S(1)}, f32[1,128]{1,0:T(1,128)}, u32[]{:S(2)}) copy-start(f32[1,128]{1,0:T(1,128)} %param.17) | copy-start | bytes 1540
  19.8 28.1 %all-to-all-start.1 = ((bf16[16,128,256]{2,1,0:T(8,128)(2,1)}), bf16[16,128,256]{2,1,0:T(8,128)(2,1)}, u32[]{:S(2)}, u32[]{:S(2)}) async-start(bf16[16,128,256]{2,1,0:T(8,128)(2,1)} %bitcast.4), calls=%async_computation.1 | async-start | bytes 2097152 | tf_op jit(solution)/shard_map/all_to_all | solution.py:31
  27.4 3.5 %copy-start.3 = (f32[16,128,8]{2,1,0:T(8,128)}, f32[16,128,8]{2,1,0:T(8,128)S(1)}, u32[]{:S(2)}) copy-start(f32[16,128,8]{2,1,0:T(8,128)S(1)} %copy.127) | copy-start | bytes 196612
  47.9 37.5 %all-to-all-start = ((bf16[16,128,512]{1,2,0:T(8,128)(2,1)}), bf16[16,128,512]{1,2,0:T(8,128)(2,1)S(1)}, u32[]{:S(2)}, u32[]{:S(2)}) async-start(bf16[16,128,512]{1,2,0:T(8,128)(2,1)} %bitcast.75), calls=%async_computation | async-start | bytes 4194304 | tf_op jit(solution)/shard_map/all_to_all | solution.py:31
  53.9 5.1 %copy-start.7 = (f32[16,128,8]{1,2,0:T(8,128)}, f32[16,128,8]{1,2,0:T(8,128)S(1)}, u32[]{:S(2)}) copy-start(f32[16,128,8]{1,2,0:T(8,128)S(1)} %copy.130) | copy-start | bytes 196612
  129.3 11.7 %all-to-all-start.3 = ((f32[16,1,2048]{2,1,0:T(1,128)}), f32[16,1,2048]{2,1,0:T(1,128)S(1)}, u32[]{:S(2)}, u32[]{:S(2)}) async-start(f32[16,1,2048]{2,1,0:T(1,128)} %broadcast_in_dim.13), calls=%async_computation.3 | async-start | bytes 262144 | tf_op jit(solution)/shard_map/all_to_all | solution.py:233
  149.3 5.6 %copy-start.5 = (bf16[1,128,1024]{2,1,0:T(8,128)(2,1)S(1)}, bf16[1,128,1024]{2,1,0:T(8,128)(2,1)}, u32[]{:S(2)}) copy-start(bf16[1,128,1024]{2,1,0:T(8,128)(2,1)} %param.24) | copy-start | bytes 786436
  149.3 5.6 %copy-start.6 = (bf16[1,128,1024]{2,1,0:T(8,128)(2,1)S(1)}, bf16[1,128,1024]{2,1,0:T(8,128)(2,1)}, u32[]{:S(2)}) copy-start(bf16[1,128,1024]{2,1,0:T(8,128)(2,1)} %param.23) | copy-start | bytes 786436
  149.3 22.8 %copy-start.9 = (s32[1,2048]{1,0:T(1,128)S(1)}, s32[1,2048]{1,0:T(1,128)}, u32[]{:S(2)}) copy-start(s32[1,2048]{1,0:T(1,128)} %param.25) | copy-start | bytes 24580
  149.3 106.7 %all-to-all-start.4 = ((bf16[16,128,512]{2,1,0:T(8,128)(2,1)}), bf16[16,128,512]{2,1,0:T(8,128)(2,1)}, u32[]{:S(2)}, u32[]{:S(2)}) async-start(bf16[16,128,512]{2,1,0:T(8,128)(2,1)} %bitcast.23), calls=%async_computation.4 | async-start | bytes 4194304 | tf_op jit(solution)/shard_map/all_to_all | solution.py:38
  155.7 65.6 %collective-permute-start.1 = (bf16[128,2048]{1,0:T(8,128)(2,1)}, bf16[128,2048]{1,0:T(8,128)(2,1)}, u32[]{:S(2)}, u32[]{:S(2)}) collective-permute-start(bf16[128,2048]{1,0:T(8,128)(2,1)} %pad_maximum_fusion.1), channel_id=1, source_target_pairs={{0,4},{1,5},{2,6},{3,7},{4,8},{5,9},{6,10},{7,11},{8,12},{9,13},{1... | collective-permute-start | bytes 1572872 | tf_op jit(solution)/shard_map/ppermute | solution.py:24
  160.3 62.1 %collective-permute-start.2 = (bf16[128,2048]{1,0:T(8,128)(2,1)}, bf16[128,2048]{1,0:T(8,128)(2,1)}, u32[]{:S(2)}, u32[]{:S(2)}) collective-permute-start(bf16[128,2048]{1,0:T(8,128)(2,1)} %pad_maximum_fusion.1), channel_id=1, source_target_pairs={{0,3},{1,4},{2,5},{3,6},{4,7},{5,8},{6,9},{7,10},{8,11},{9,12},{10... | collective-permute-start | bytes 1572872 | tf_op jit(solution)/shard_map/ppermute | solution.py:24
  165.7 57.8 %collective-permute-start.3 = (bf16[128,2048]{1,0:T(8,128)(2,1)}, bf16[128,2048]{1,0:T(8,128)(2,1)}, u32[]{:S(2)}, u32[]{:S(2)}) collective-permute-start(bf16[128,2048]{1,0:T(8,128)(2,1)} %pad_maximum_fusion.1), channel_id=1, source_target_pairs={{0,2},{1,3},{2,4},{3,5},{4,6},{5,7},{6,8},{7,9},{8,10},{9,11},{10,... | collective-permute-start | bytes 1572872 | tf_op jit(solution)/shard_map/ppermute | solution.py:24
  169.4 55.2 %collective-permute-start.4 = (bf16[128,2048]{1,0:T(8,128)(2,1)}, bf16[128,2048]{1,0:T(8,128)(2,1)}, u32[]{:S(2)}, u32[]{:S(2)}) collective-permute-start(bf16[128,2048]{1,0:T(8,128)(2,1)} %pad_maximum_fusion.1), channel_id=1, source_target_pairs={{0,1},{1,2},{2,3},{3,4},{4,5},{5,6},{6,7},{7,8},{8,9},{9,10},{10,1... | collective-permute-start | bytes 1572872 | tf_op jit(solution)/shard_map/ppermute | solution.py:24
  225.7 1.5 copy-start.2
  258.1 1.6 copy-start.4
  258.6 2.9 %copy-start.1 = (f32[1,128]{1,0:T(1,128)S(1)}, f32[1,128]{1,0:T(1,128)}, u32[]{:S(2)}) copy-start(f32[1,128]{1,0:T(1,128)} %param.20) | copy-start | bytes 1540

commit v6 on v5

--- a/solution.py
+++ b/solution.py
@@ -217,6 +217,7 @@
     halo = -(-MOST_DOC // tok_rows)
     kv_row = jnp.concatenate([keys[0], values[0]], axis=1)
     kv_win = jnp.concatenate([shifted(kv_row, "ctx", by) for by in range(halo, 0, -1)] + [kv_row], axis=0)
+    kv_win, x_h = lax.optimization_barrier((kv_win, x_h))
     all_ids = doc_ids[0]
     lead = halo * tok_rows
     padded_ids = jnp.concatenate([jnp.full((lead,), -1, all_ids.dtype), all_ids])

time: 264 us -> 216 us (0.82)
  waiting for transfers between devices: 84.3 us -> 45.9 us
  starting transfers between devices: 45.7 us -> 40.2 us
  other arithmetic: 21.7 us -> 18.7 us
    ppermute x5, waiting for transfers between devices: 47.8 us -> 0.01 us  [shifted(): return lax.ppermute(value, axis, pairs)]
    all_to_all x3, waiting for transfers between devices: 34.7 us -> 44.4 us  [to_heads(): moved = lax.all_to_all(lead, 'ctx', split_axis=0, concat_axis=0, tiled=True)]
    all_to_all x3, starting transfers between devices: 18 us -> 12.3 us  [to_heads(): moved = lax.all_to_all(lead, 'ctx', split_axis=0, concat_axis=0, tiled=True)]
    unnamed x34 -> x40, local copies, waits for them, and re-layouts: 10.8 us -> 12.6 us
  transfers between devices with their start and end apart: 10 -> 10, of which waited for: 4 -> 4; matrix products, arithmetic and copies ran while one was open for 17% -> 20% of each run, Pallas kernels for 11% -> 13%
where the time goes in v6:
time: 216 us; the launch traced here: 214 us
  Pallas kernels  63.1 us (29%)
  waiting for transfers between devices  45.9 us (21%)
  local copies, waits for them, and re-layouts  45.8 us (21%)
  starting transfers between devices  40.2 us (19%)
  other arithmetic  18.7 us (9%)
    all_to_all x3, waiting for transfers between devices, to_heads(): moved = lax.all_to_all(lead, 'ctx', split_axis=0, concat_axis=0, tiled=True)  44.4 us
    pallas_call x1, Pallas kernels, mixer_heads(): pl.pallas_call(kernel, grid=(nblk,), in_specs=[pl.BlockSpec((BLOCK, x_wid...  34.4 us
    pallas_call x1, Pallas kernels, attend_rows(): pl.pallas_call(kernel, grid=(kv_heads,), in_specs=[pl.BlockSpec((tok_rows...  28.7 us
    ppermute x5, starting transfers between devices, shifted(): return lax.ppermute(value, axis, pairs)  18.6 us
    unnamed x40, local copies, waits for them, and re-layouts  12.6 us
    all_to_all x3, starting transfers between devices, to_heads(): moved = lax.all_to_all(lead, 'ctx', split_axis=0, concat_axis=0, tiled=True)  12.3 us
    all_to_all x1, starting transfers between devices, to_rows(): lax.all_to_all(block.reshape(chunks, tok_rows, width), 'ctx', split_axis=...  5.6 us
    pallas_call x1, local copies, waits for them, and re-layouts, mixer_heads(): pl.pallas_call(kernel, grid=(nblk,), in_specs=[pl.BlockSpec((BLOCK, x_wid...  5.57 us
  transfers between devices with their start and end apart: 10, of which 4 were waited for; matrix products, arithmetic and copies ran while one was open for 20% of the time, Pallas kernels for 13%

profile of v6, /device:TPU:32, one launch (start us, length us, event | category | flops | bytes accessed | tf_op | source)
XLA Modules:
  0.0 214.0 jit_solution(8475825918701082500)
XLA Ops:
  1.9 4.2 %collective-permute-start.3 = (bf16[128,2048]{1,0:T(8,128)(2,1)}, bf16[128,2048]{1,0:T(8,128)(2,1)}, u32[]{:S(2)}, u32[]{:S(2)}) collective-permute-start(bf16[128,2048]{1,0:T(8,128)(2,1)} %pad_maximum_fusion), channel_id=1, source_target_pairs={{0,1},{1,2},{2,3},{3,4},{4,5},{5,6},{6,7},{7,8},{8,9},{9,10},{10,1... | collective-permute-start | bytes 1572872 | tf_op jit(solution)/shard_map/ppermute | solution.py:24
  6.1 4.7 %collective-permute-start.2 = (bf16[128,2048]{1,0:T(8,128)(2,1)}, bf16[128,2048]{1,0:T(8,128)(2,1)}, u32[]{:S(2)}, u32[]{:S(2)}) collective-permute-start(bf16[128,2048]{1,0:T(8,128)(2,1)} %pad_maximum_fusion), channel_id=1, source_target_pairs={{0,2},{1,3},{2,4},{3,5},{4,6},{5,7},{6,8},{7,9},{8,10},{9,11},{10,... | collective-permute-start | bytes 1572872 | tf_op jit(solution)/shard_map/ppermute | solution.py:24
  10.8 4.4 %collective-permute-start.1 = (bf16[128,2048]{1,0:T(8,128)(2,1)}, bf16[128,2048]{1,0:T(8,128)(2,1)}, u32[]{:S(2)}, u32[]{:S(2)}) collective-permute-start(bf16[128,2048]{1,0:T(8,128)(2,1)} %pad_maximum_fusion), channel_id=1, source_target_pairs={{0,3},{1,4},{2,5},{3,6},{4,7},{5,8},{6,9},{7,10},{8,11},{9,12},{10... | collective-permute-start | bytes 1572872 | tf_op jit(solution)/shard_map/ppermute | solution.py:24
  15.2 3.4 %collective-permute-start = (bf16[128,2048]{1,0:T(8,128)(2,1)}, bf16[128,2048]{1,0:T(8,128)(2,1)}, u32[]{:S(2)}, u32[]{:S(2)}) collective-permute-start(bf16[128,2048]{1,0:T(8,128)(2,1)} %pad_maximum_fusion), channel_id=1, source_target_pairs={{0,4},{1,5},{2,6},{3,7},{4,8},{5,9},{6,10},{7,11},{8,12},{9,13},{1... | collective-permute-start | bytes 1572872 | tf_op jit(solution)/shard_map/ppermute | solution.py:24
  20.2 3.5 %all-to-all-start.2 = ((f32[16,128,8]{1,2,0:T(8,128)}), f32[16,128,8]{1,2,0:T(8,128)S(1)}, u32[]{:S(2)}, u32[]{:S(2)}) async-start(f32[16,128,8]{1,2,0:T(8,128)} %bitcast.9), calls=%async_computation.2 | async-start | bytes 131072 | tf_op jit(solution)/shard_map/all_to_all | solution.py:31
  23.7 1.9 collective-permute-start.4
  34.7 22.0 %all-to-all-done.2 = f32[16,128,8]{1,2,0:T(8,128)S(1)} async-done(((f32[16,128,8]{1,2,0:T(8,128)}), f32[16,128,8]{1,2,0:T(8,128)S(1)}, u32[]{:S(2)}, u32[]{:S(2)}) %all-to-all-start.2) | async-done | bytes 65568 | tf_op jit(solution)/shard_map/all_to_all | solution.py:31
  56.6 4.3 %all-to-all-start.1 = ((bf16[16,128,256]{2,1,0:T(8,128)(2,1)}), bf16[16,128,256]{2,1,0:T(8,128)(2,1)}, u32[]{:S(2)}, u32[]{:S(2)}) async-start(bf16[16,128,256]{2,1,0:T(8,128)(2,1)} %bitcast.6), calls=%async_computation.1 | async-start | bytes 2097152 | tf_op jit(solution)/shard_map/all_to_all | solution.py:31
  64.8 2.0 multiply_multiply_fusion
  68.7 2.4 %copy.123 = bf16[128,8192]{0,1:T(8,128)(2,1)} copy(bf16[128,8192]{1,0:T(8,128)(2,1)S(1)} %broadcast_select_fusion) | data formatting | bytes 4194304 | tf_op jit(solution)/shard_map/jit(_where)/select_n | solution.py:214
  71.1 7.7 %all-to-all-done.1 = bf16[16,128,256]{2,1,0:T(8,128)(2,1)} async-done(((bf16[16,128,256]{2,1,0:T(8,128)(2,1)}), bf16[16,128,256]{2,1,0:T(8,128)(2,1)}, u32[]{:S(2)}, u32[]{:S(2)}) %all-to-all-start.1) | async-done | bytes 1048608 | tf_op jit(solution)/shard_map/all_to_all | solution.py:31
  78.8 4.4 %all-to-all-start = ((bf16[16,128,512]{1,2,0:T(8,128)(2,1)}), bf16[16,128,512]{1,2,0:T(8,128)(2,1)}, u32[]{:S(2)}, u32[]{:S(2)}) async-start(bf16[16,128,512]{1,2,0:T(8,128)(2,1)} %bitcast.69), calls=%async_computation | async-start | bytes 4194304 | tf_op jit(solution)/shard_map/all_to_all | solution.py:31
  87.0 2.0 constant_dynamic-update-slice_fusion.4
  92.8 1.9 constant_dynamic-update-slice_fusion.1
  95.5 2.3 %fusion.14 = (bf16[2048,128]{1,0:T(8,128)(2,1)}, bf16[2048,128]{1,0:T(8,128)(2,1)}) fusion(bf16[2048,256]{1,0:T(8,128)(2,1)} %bitcast.7), kind=kLoop, calls=%fused_computation.45 | loop fusion | bytes 2097152 | tf_op jit(solution)/shard_map/slice | solution.py:210
  97.8 14.8 %all-to-all-done = bf16[16,128,512]{1,2,0:T(8,128)(2,1)} async-done(((bf16[16,128,512]{1,2,0:T(8,128)(2,1)}), bf16[16,128,512]{1,2,0:T(8,128)(2,1)}, u32[]{:S(2)}, u32[]{:S(2)}) %all-to-all-start) | async-done | bytes 2097184 | tf_op jit(solution)/shard_map/all_to_all | solution.py:31
  114.5 2.6 %copy.141.x_ref = bf16[2048,512]{1,0:T(8,128)(2,1)} copy(bf16[2048,512]{0,1:T(8,128)(2,1)S(1)} %copy_bitcast_fusion) | data formatting | bytes 4194304 | tf_op jit(solution)/shard_map/optimization_barrier | solution.py:220
  117.8 34.4 %shard_map.127 = (f32[2048,512]{1,0:T(8,128)}, f32[2048,1]{1,0:T(8,128)}) custom-call(bf16[2048,512]{1,0:T(8,128)(2,1)} %copy.141.x_ref, bf16[512,2048]{1,0:T(8,128)(2,1)} %bitcast.67, bf16[2048,128]{1,0:T(8,128)(2,1)} %get-tuple-element.18.b_ref, bf16[2048,128]{1,0:T(8,128)(2,1)} %get-tuple-element.17.c_ref, f32[16,128,8]{2,1,0:T(8,128)} %copy.142.lcc_ref, ...), custom_call_target="tpu_custom_call" | custom-call | tf_op jit(solution)/shard_map/pallas_call | solution.py:103
  154.6 3.7 %all-to-all-start.3 = ((f32[16,1,2048]{2,1,0:T(1,128)}), f32[16,1,2048]{2,1,0:T(1,128)S(1)}, u32[]{:S(2)}, u32[]{:S(2)}) async-start(f32[16,1,2048]{2,1,0:T(1,128)} %broadcast_in_dim.13), calls=%async_computation.3 | async-start | bytes 262144 | tf_op jit(solution)/shard_map/all_to_all | solution.py:234
  159.0 5.6 %copy.146 = f32[2048,512]{0,1:T(8,128)} copy(f32[2048,512]{1,0:T(8,128)} %get-tuple-element.10) | data formatting | bytes 8388608 | tf_op jit(solution)/shard_map/pallas_call | solution.py:103
  166.2 4.3 %add_convert_fusion.1 = bf16[2048,512]{0,1:T(8,128)(2,1)} fusion(f32[2048,512]{0,1:T(8,128)} %copy.146, bf16[2048,512]{0,1:T(8,128)(2,1)S(1)} %copy-done.3, f32[512]{0:T(512)S(1)} %bitcast.87, f32[2048]{0:T(1024)S(1)} %add_rsqrt_fusion), kind=kLoop, calls=%fused_computation.2 | loop fusion | flops 5242880 | bytes 8398848 | tf_op jit(solution)/shard_map/convert_element_type | solution.py:241
  170.4 3.9 %copy.151 = bf16[2048,512]{1,0:T(8,128)(2,1)} copy(bf16[2048,512]{0,1:T(8,128)(2,1)} %add_convert_fusion.1) | data formatting | bytes 4194304 | tf_op jit(solution)/shard_map/reshape | solution.py:38
  174.3 5.6 %all-to-all-start.4 = ((bf16[16,128,512]{2,1,0:T(8,128)(2,1)}), bf16[16,128,512]{2,1,0:T(8,128)(2,1)S(1)}, u32[]{:S(2)}, u32[]{:S(2)}) async-start(bf16[16,128,512]{2,1,0:T(8,128)(2,1)} %bitcast.70), calls=%async_computation.4 | async-start | bytes 4194304 | tf_op jit(solution)/shard_map/all_to_all | solution.py:38
  181.4 28.7 %shard_map.128 = bf16[128,8192]{1,0:T(8,128)(2,1)} custom-call(bf16[128,8192]{1,0:T(8,128)(2,1)} %bitcast.71, bf16[640,2048]{1,0:T(8,128)(2,1)} %constant_dynamic-update-slice_fusion.k_ref.v_ref, bf16[640,2048]{1,0:T(8,128)(2,1)} %constant_dynamic-update-slice_fusion.k_ref.v_ref, s32[128,1]{1,0:T(8,128)} %copy.149.iq_ref, s32[1,640]{1,0:T(1,128)} %reshape.154.ik_ref), custom_call_target="tpu_custom_call" | custom-call | tf_op jit(solution)/shard_map/pallas_call | solution.py:163
  (88 shorter events, 39.0 us)
Async XLA Ops:
  0.0 34.1 %copy-start = (f32[1,128]{1,0:T(1,128)S(1)}, f32[1,128]{1,0:T(1,128)}, u32[]{:S(2)}) copy-start(f32[1,128]{1,0:T(1,128)} %param.20) | copy-start | bytes 1540
  1.9 90.9 %collective-permute-start.3 = (bf16[128,2048]{1,0:T(8,128)(2,1)}, bf16[128,2048]{1,0:T(8,128)(2,1)}, u32[]{:S(2)}, u32[]{:S(2)}) collective-permute-start(bf16[128,2048]{1,0:T(8,128)(2,1)} %pad_maximum_fusion), channel_id=1, source_target_pairs={{0,1},{1,2},{2,3},{3,4},{4,5},{5,6},{6,7},{7,8},{8,9},{9,10},{10,1... | collective-permute-start | bytes 1572872 | tf_op jit(solution)/shard_map/ppermute | solution.py:24
  6.1 84.8 %collective-permute-start.2 = (bf16[128,2048]{1,0:T(8,128)(2,1)}, bf16[128,2048]{1,0:T(8,128)(2,1)}, u32[]{:S(2)}, u32[]{:S(2)}) collective-permute-start(bf16[128,2048]{1,0:T(8,128)(2,1)} %pad_maximum_fusion), channel_id=1, source_target_pairs={{0,2},{1,3},{2,4},{3,5},{4,6},{5,7},{6,8},{7,9},{8,10},{9,11},{10,... | collective-permute-start | bytes 1572872 | tf_op jit(solution)/shard_map/ppermute | solution.py:24
  10.8 78.2 %collective-permute-start.1 = (bf16[128,2048]{1,0:T(8,128)(2,1)}, bf16[128,2048]{1,0:T(8,128)(2,1)}, u32[]{:S(2)}, u32[]{:S(2)}) collective-permute-start(bf16[128,2048]{1,0:T(8,128)(2,1)} %pad_maximum_fusion), channel_id=1, source_target_pairs={{0,3},{1,4},{2,5},{3,6},{4,7},{5,8},{6,9},{7,10},{8,11},{9,12},{10... | collective-permute-start | bytes 1572872 | tf_op jit(solution)/shard_map/ppermute | solution.py:24
  15.2 71.8 %collective-permute-start = (bf16[128,2048]{1,0:T(8,128)(2,1)}, bf16[128,2048]{1,0:T(8,128)(2,1)}, u32[]{:S(2)}, u32[]{:S(2)}) collective-permute-start(bf16[128,2048]{1,0:T(8,128)(2,1)} %pad_maximum_fusion), channel_id=1, source_target_pairs={{0,4},{1,5},{2,6},{3,7},{4,8},{5,9},{6,10},{7,11},{8,12},{9,13},{1... | collective-permute-start | bytes 1572872 | tf_op jit(solution)/shard_map/ppermute | solution.py:24
  20.2 36.5 %all-to-all-start.2 = ((f32[16,128,8]{1,2,0:T(8,128)}), f32[16,128,8]{1,2,0:T(8,128)S(1)}, u32[]{:S(2)}, u32[]{:S(2)}) async-start(f32[16,128,8]{1,2,0:T(8,128)} %bitcast.9), calls=%async_computation.2 | async-start | bytes 131072 | tf_op jit(solution)/shard_map/all_to_all | solution.py:31
  23.7 43.1 %collective-permute-start.4 = (bf16[128,8192]{1,0:T(8,128)(2,1)}, bf16[128,8192]{1,0:T(8,128)(2,1)}, u32[]{:S(2)}, u32[]{:S(2)}) collective-permute-start(bf16[128,8192]{1,0:T(8,128)(2,1)} %bitcast.90), channel_id=1, source_target_pairs={{0,16},{16,32},{32,48},{48,64},{64,80},{80,96},{96,112},{1,17},{17... | collective-permute-start | bytes 6291464 | tf_op jit(solution)/shard_map/ppermute | solution.py:24
  29.5 2.9 %copy-start.11 = (s32[1,2048]{1,0:T(1,128)S(1)}, s32[1,2048]{1,0:T(1,128)}, u32[]{:S(2)}) copy-start(s32[1,2048]{1,0:T(1,128)} %param.25) | copy-start | bytes 24580
  30.1 3.8 %copy-start.13 = (f32[1,128]{1,0:T(1,128)S(1)}, f32[1,128]{1,0:T(1,128)}, u32[]{:S(2)}) copy-start(f32[1,128]{1,0:T(1,128)} %param.16) | copy-start | bytes 1540
  30.1 3.8 %copy-start.14 = (f32[1,128]{1,0:T(1,128)S(1)}, f32[1,128]{1,0:T(1,128)}, u32[]{:S(2)}) copy-start(f32[1,128]{1,0:T(1,128)} %param.17) | copy-start | bytes 1540
  56.6 22.1 %all-to-all-start.1 = ((bf16[16,128,256]{2,1,0:T(8,128)(2,1)}), bf16[16,128,256]{2,1,0:T(8,128)(2,1)}, u32[]{:S(2)}, u32[]{:S(2)}) async-start(bf16[16,128,256]{2,1,0:T(8,128)(2,1)} %bitcast.6), calls=%async_computation.1 | async-start | bytes 2097152 | tf_op jit(solution)/shard_map/all_to_all | solution.py:31
  63.0 3.8 %copy-start.10 = (f32[16,128,8]{1,2,0:T(8,128)}, f32[16,128,8]{1,2,0:T(8,128)S(1)}, u32[]{:S(2)}) copy-start(f32[16,128,8]{1,2,0:T(8,128)S(1)} %copy.130) | copy-start | bytes 196612
  64.8 2.0 copy-start.7
  71.1 12.1 %copy-start.6 = (f32[16,128,8]{2,1,0:T(8,128)S(1)}, f32[16,128,8]{2,1,0:T(8,128)}, u32[]{:S(2)}) copy-start(f32[16,128,8]{2,1,0:T(8,128)} %copy.133) | copy-start | bytes 196612
  78.8 33.8 %all-to-all-start = ((bf16[16,128,512]{1,2,0:T(8,128)(2,1)}), bf16[16,128,512]{1,2,0:T(8,128)(2,1)}, u32[]{:S(2)}, u32[]{:S(2)}) async-start(bf16[16,128,512]{1,2,0:T(8,128)(2,1)} %bitcast.69), calls=%async_computation | async-start | bytes 4194304 | tf_op jit(solution)/shard_map/all_to_all | solution.py:31
  83.2 2.9 %copy-start.5 = (f32[16,8,128]{1,2,0:T(8,128)S(1)}, f32[16,8,128]{1,2,0:T(8,128)}, u32[]{:S(2)}) copy-start(f32[16,8,128]{1,2,0:T(8,128)} %get-tuple-element.14) | copy-start | bytes 196612
  86.1 8.6 %copy-start.8 = (bf16[1,128,1024]{2,1,0:T(8,128)(2,1)S(1)}, bf16[1,128,1024]{2,1,0:T(8,128)(2,1)}, u32[]{:S(2)}) copy-start(bf16[1,128,1024]{2,1,0:T(8,128)(2,1)} %param.24) | copy-start | bytes 786436
  86.1 8.6 %copy-start.9 = (bf16[1,128,1024]{2,1,0:T(8,128)(2,1)S(1)}, bf16[1,128,1024]{2,1,0:T(8,128)(2,1)}, u32[]{:S(2)}) copy-start(bf16[1,128,1024]{2,1,0:T(8,128)(2,1)} %param.23) | copy-start | bytes 786436
  114.5 3.4 %copy-start.2 = (bf16[2048,512]{0,1:T(8,128)(2,1)}, bf16[2048,512]{0,1:T(8,128)(2,1)S(1)}, u32[]{:S(2)}) copy-start(bf16[2048,512]{0,1:T(8,128)(2,1)S(1)} %copy_bitcast_fusion) | copy-start | bytes 6291460
  154.6 11.5 %all-to-all-start.3 = ((f32[16,1,2048]{2,1,0:T(1,128)}), f32[16,1,2048]{2,1,0:T(1,128)S(1)}, u32[]{:S(2)}, u32[]{:S(2)}) async-start(f32[16,1,2048]{2,1,0:T(1,128)} %broadcast_in_dim.13), calls=%async_computation.3 | async-start | bytes 262144 | tf_op jit(solution)/shard_map/all_to_all | solution.py:234
  159.0 7.2 %copy-start.3 = (bf16[2048,512]{0,1:T(8,128)(2,1)S(1)}, bf16[2048,512]{0,1:T(8,128)(2,1)}, u32[]{:S(2)}) copy-start(bf16[2048,512]{0,1:T(8,128)(2,1)} %copy-done.2) | copy-start | bytes 6291460
  174.3 5.6 %copy-start.12 = (s32[1,2048]{1,0:T(1,128)S(1)}, s32[1,2048]{1,0:T(1,128)}, u32[]{:S(2)}) copy-start(s32[1,2048]{1,0:T(1,128)} %param.25) | copy-start | bytes 24580
  174.3 35.7 %all-to-all-start.4 = ((bf16[16,128,512]{2,1,0:T(8,128)(2,1)}), bf16[16,128,512]{2,1,0:T(8,128)(2,1)S(1)}, u32[]{:S(2)}, u32[]{:S(2)}) async-start(bf16[16,128,512]{2,1,0:T(8,128)(2,1)} %bitcast.70), calls=%async_computation.4 | async-start | bytes 4194304 | tf_op jit(solution)/shard_map/all_to_all | solution.py:38
  211.1 2.9 %copy-start.1 = (f32[1,128]{1,0:T(1,128)S(1)}, f32[1,128]{1,0:T(1,128)}, u32[]{:S(2)}) copy-start(f32[1,128]{1,0:T(1,128)} %param.20) | copy-start | bytes 1540
  (1 other events, 1.6 us)

commit v7 on v5

--- a/solution.py
+++ b/solution.py
@@ -216,13 +216,13 @@
 
     halo = -(-MOST_DOC // tok_rows)
     kv_row = jnp.concatenate([keys[0], values[0]], axis=1)
+    kv_row, x_h = lax.optimization_barrier((kv_row, x_h))
     kv_win = jnp.concatenate([shifted(kv_row, "ctx", by) for by in range(halo, 0, -1)] + [kv_row], axis=0)
     all_ids = doc_ids[0]
     lead = halo * tok_rows
     padded_ids = jnp.concatenate([jnp.full((lead,), -1, all_ids.dtype), all_ids])
     ids_k = lax.dynamic_slice_in_dim(padded_ids, me * tok_rows, lead + tok_rows)
     ids_q = lax.dynamic_slice_in_dim(all_ids, me * tok_rows, tok_rows)
-    attended = attend_rows(queries[0], kv_win, ids_q.reshape(tok_rows, 1), ids_k.reshape(1, lead + tok_rows))
 
     bias_h = lax.dynamic_slice_in_dim(dt_bias[0], me * heads_dev, heads_dev)
     alog_h = lax.dynamic_slice_in_dim(a_log[0], me * heads_dev, heads_dev)
@@ -230,6 +230,8 @@
     gain_h = lax.dynamic_slice_in_dim(norm_gain[0], me * part, part)
 
     mixer_out, sq_part = mixer_heads(x_h, dt_h, bias_h, alog_h, b_g, c_g, skip_h, all_ids)
+    kv_win, mixer_out, sq_part = lax.optimization_barrier((kv_win, mixer_out, sq_part))
+    attended = attend_rows(queries[0], kv_win, ids_q.reshape(tok_rows, 1), ids_k.reshape(1, lead + tok_rows))
     sq_all = lax.all_to_all(
         jnp.broadcast_to(sq_part[:, 0][None], (nctx, total)), "ctx", split_axis=0, concat_axis=0, tiled=True
     )

time: 264 us -> 224 us (0.85)
  the two profiles are of different devices: /device:TPU:32 before, /device:TPU:1 now
where the time goes in v7:
time: 224 us; the launch traced here: 222 us
  Pallas kernels  63.1 us (28%)
  local copies, waits for them, and re-layouts  49 us (22%)
  waiting for transfers between devices  48.3 us (22%)
  starting transfers between devices  46 us (21%)
  other arithmetic  15.4 us (7%)
    all_to_all x3, waiting for transfers between devices, to_heads(): moved = lax.all_to_all(lead, 'ctx', split_axis=0, concat_axis=0, tiled=True)  35.6 us
    pallas_call x1, Pallas kernels, mixer_heads(): pl.pallas_call(kernel, grid=(nblk,), in_specs=[pl.BlockSpec((BLOCK, x_wid...  34.4 us
    pallas_call x1, Pallas kernels, attend_rows(): pl.pallas_call(kernel, grid=(kv_heads,), in_specs=[pl.BlockSpec((tok_rows...  28.7 us
    ppermute x5, starting transfers between devices, shifted(): return lax.ppermute(value, axis, pairs)  19.6 us
    all_to_all x3, starting transfers between devices, to_heads(): moved = lax.all_to_all(lead, 'ctx', split_axis=0, concat_axis=0, tiled=True)  18 us
    unnamed x38, local copies, waits for them, and re-layouts  12.6 us
    ppermute x5, waiting for transfers between devices, shifted(): return lax.ppermute(value, axis, pairs)  10.9 us
    optimization_barrier x1, local copies, waits for them, and re-layouts, body(): lax.optimization_barrier((kv_win, mixer_out, sq_part))  5.56 us
  transfers between devices with their start and end apart: 10, of which 4 were waited for; matrix products, arithmetic and copies ran while one was open for 21% of the time, Pallas kernels for 28%

profile of v7, /device:TPU:1, one launch (start us, length us, event | category | flops | bytes accessed | tf_op | source)
XLA Modules:
  0.0 222.2 jit_solution(11413725398250218692)
XLA Ops:
  0.0 5.0 %collective-permute-start = (bf16[128,8192]{1,0:T(8,128)(2,1)}, bf16[128,8192]{1,0:T(8,128)(2,1)}, u32[]{:S(2)}, u32[]{:S(2)}) collective-permute-start(bf16[128,8192]{1,0:T(8,128)(2,1)} %bitcast.89), channel_id=1, source_target_pairs={{0,16},{16,32},{32,48},{48,64},{64,80},{80,96},{96,112},{1,17},{17... | collective-permute-start | bytes 6291464 | tf_op jit(solution)/shard_map/ppermute | solution.py:24
  6.6 6.8 %all-to-all-start.2 = ((f32[16,128,8]{1,2,0:T(8,128)}), f32[16,128,8]{1,2,0:T(8,128)S(1)}, u32[]{:S(2)}, u32[]{:S(2)}) async-start(f32[16,128,8]{1,2,0:T(8,128)} %bitcast.9), calls=%async_computation.2 | async-start | bytes 131072 | tf_op jit(solution)/shard_map/all_to_all | solution.py:31
  17.5 10.9 %collective-permute-done = bf16[128,8192]{1,0:T(8,128)(2,1)} collective-permute-done((bf16[128,8192]{1,0:T(8,128)(2,1)}, bf16[128,8192]{1,0:T(8,128)(2,1)}, u32[]{:S(2)}, u32[]{:S(2)}) %collective-permute-start) | collective-permute-done | bytes 2097184 | tf_op jit(solution)/shard_map/ppermute | solution.py:24
  30.1 2.4 %copy.123 = bf16[128,8192]{0,1:T(8,128)(2,1)} copy(bf16[128,8192]{1,0:T(8,128)(2,1)S(1)} %broadcast_select_fusion) | data formatting | bytes 4194304 | tf_op jit(solution)/shard_map/jit(_where)/select_n | solution.py:214
  32.6 6.8 %all-to-all-start = ((bf16[16,128,512]{1,2,0:T(8,128)(2,1)}), bf16[16,128,512]{1,2,0:T(8,128)(2,1)}, u32[]{:S(2)}, u32[]{:S(2)}) async-start(bf16[16,128,512]{1,2,0:T(8,128)(2,1)} %bitcast.69), calls=%async_computation | async-start | bytes 4194304 | tf_op jit(solution)/shard_map/all_to_all | solution.py:31
  49.3 2.0 multiply_multiply_fusion
  51.2 9.5 %all-to-all-done = bf16[16,128,512]{1,2,0:T(8,128)(2,1)} async-done(((bf16[16,128,512]{1,2,0:T(8,128)(2,1)}), bf16[16,128,512]{1,2,0:T(8,128)(2,1)}, u32[]{:S(2)}, u32[]{:S(2)}) %all-to-all-start) | async-done | bytes 2097184 | tf_op jit(solution)/shard_map/all_to_all | solution.py:31
  60.7 4.4 %all-to-all-start.1 = ((bf16[16,128,256]{2,1,0:T(8,128)(2,1)}), bf16[16,128,256]{2,1,0:T(8,128)(2,1)}, u32[]{:S(2)}, u32[]{:S(2)}) async-start(bf16[16,128,256]{2,1,0:T(8,128)(2,1)} %bitcast.71), calls=%async_computation.1 | async-start | bytes 2097152 | tf_op jit(solution)/shard_map/all_to_all | solution.py:31
  68.4 4.0 %collective-permute-start.1 = (bf16[128,2048]{1,0:T(8,128)(2,1)}, bf16[128,2048]{1,0:T(8,128)(2,1)}, u32[]{:S(2)}, u32[]{:S(2)}) collective-permute-start(bf16[128,2048]{1,0:T(8,128)(2,1)} %pad_maximum_fusion), channel_id=1, source_target_pairs={{0,4},{1,5},{2,6},{3,7},{4,8},{5,9},{6,10},{7,11},{8,12},{9,13},{1... | collective-permute-start | bytes 1572872 | tf_op jit(solution)/shard_map/ppermute | solution.py:24
  73.7 2.1 copy.143.str_ref
  75.9 5.1 %collective-permute-start.2 = (bf16[128,2048]{1,0:T(8,128)(2,1)}, bf16[128,2048]{1,0:T(8,128)(2,1)}, u32[]{:S(2)}, u32[]{:S(2)}) collective-permute-start(bf16[128,2048]{1,0:T(8,128)(2,1)} %pad_maximum_fusion), channel_id=1, source_target_pairs={{0,3},{1,4},{2,5},{3,6},{4,7},{5,8},{6,9},{7,10},{8,11},{9,12},{10... | collective-permute-start | bytes 1572872 | tf_op jit(solution)/shard_map/ppermute | solution.py:24
  81.0 3.4 %collective-permute-start.3 = (bf16[128,2048]{1,0:T(8,128)(2,1)}, bf16[128,2048]{1,0:T(8,128)(2,1)}, u32[]{:S(2)}, u32[]{:S(2)}) collective-permute-start(bf16[128,2048]{1,0:T(8,128)(2,1)} %pad_maximum_fusion), channel_id=1, source_target_pairs={{0,2},{1,3},{2,4},{3,5},{4,6},{5,7},{6,8},{7,9},{8,10},{9,11},{10,... | collective-permute-start | bytes 1572872 | tf_op jit(solution)/shard_map/ppermute | solution.py:24
  84.4 26.2 %all-to-all-done.1 = bf16[16,128,256]{2,1,0:T(8,128)(2,1)} async-done(((bf16[16,128,256]{2,1,0:T(8,128)(2,1)}), bf16[16,128,256]{2,1,0:T(8,128)(2,1)}, u32[]{:S(2)}, u32[]{:S(2)}) %all-to-all-start.1) | async-done | bytes 1048608 | tf_op jit(solution)/shard_map/all_to_all | solution.py:31
  110.6 2.3 %fusion.14 = (bf16[2048,128]{1,0:T(8,128)(2,1)}, bf16[2048,128]{1,0:T(8,128)(2,1)}) fusion(bf16[2048,256]{1,0:T(8,128)(2,1)} %bitcast.7), kind=kLoop, calls=%fused_computation.45 | loop fusion | bytes 2097152 | tf_op jit(solution)/shard_map/slice | solution.py:210
  112.9 2.1 collective-permute-start.4
  115.0 2.5 %copy.141.x_ref = bf16[2048,512]{1,0:T(8,128)(2,1)} copy(bf16[2048,512]{0,1:T(8,128)(2,1)S(1)} %copy_bitcast_fusion) | data formatting | bytes 4194304 | tf_op jit(solution)/shard_map/optimization_barrier | solution.py:219
  118.2 34.4 %shard_map.127 = (f32[2048,512]{1,0:T(8,128)}, f32[2048,1]{1,0:T(8,128)}) custom-call(bf16[2048,512]{1,0:T(8,128)(2,1)} %copy.141.x_ref, bf16[512,2048]{1,0:T(8,128)(2,1)} %bitcast.67, bf16[2048,128]{1,0:T(8,128)(2,1)} %get-tuple-element.24.b_ref, bf16[2048,128]{1,0:T(8,128)(2,1)} %get-tuple-element.23.c_ref, f32[16,128,8]{2,1,0:T(8,128)} %copy.142.lcc_ref, ...), custom_call_target="tpu_custom_call" | custom-call | tf_op jit(solution)/shard_map/pallas_call | solution.py:103
  152.6 2.0 constant_dynamic-update-slice_fusion.4
  163.3 3.7 %all-to-all-start.3 = ((f32[16,1,2048]{2,1,0:T(1,128)}), f32[16,1,2048]{2,1,0:T(1,128)S(1)}, u32[]{:S(2)}, u32[]{:S(2)}) async-start(f32[16,1,2048]{2,1,0:T(1,128)} %broadcast_in_dim.13), calls=%async_computation.3 | async-start | bytes 262144 | tf_op jit(solution)/shard_map/all_to_all | solution.py:235
  167.7 5.6 %copy.146 = f32[2048,512]{0,1:T(8,128)} copy(f32[2048,512]{1,0:T(8,128)} %get-tuple-element.16) | data formatting | bytes 8388608 | tf_op jit(solution)/shard_map/optimization_barrier | solution.py:233
  175.1 4.3 %add_convert_fusion.1 = bf16[2048,512]{0,1:T(8,128)(2,1)} fusion(f32[2048,512]{0,1:T(8,128)} %copy.146, bf16[2048,512]{0,1:T(8,128)(2,1)S(1)} %copy-done.3, f32[512]{0:T(512)S(1)} %bitcast.86, f32[2048]{0:T(1024)S(1)} %add_rsqrt_fusion), kind=kLoop, calls=%fused_computation.2 | loop fusion | flops 5242880 | bytes 8398848 | tf_op jit(solution)/shard_map/convert_element_type | solution.py:242
  179.4 3.9 %copy.151 = bf16[2048,512]{1,0:T(8,128)(2,1)} copy(bf16[2048,512]{0,1:T(8,128)(2,1)} %add_convert_fusion.1) | data formatting | bytes 4194304 | tf_op jit(solution)/shard_map/reshape | solution.py:38
  183.3 4.8 %all-to-all-start.4 = ((bf16[16,128,512]{2,1,0:T(8,128)(2,1)}), bf16[16,128,512]{2,1,0:T(8,128)(2,1)S(1)}, u32[]{:S(2)}, u32[]{:S(2)}) async-start(bf16[16,128,512]{2,1,0:T(8,128)(2,1)} %bitcast.70), calls=%async_computation.4 | async-start | bytes 4194304 | tf_op jit(solution)/shard_map/all_to_all | solution.py:38
  189.5 28.7 %shard_map.128 = bf16[128,8192]{1,0:T(8,128)(2,1)} custom-call(bf16[128,8192]{1,0:T(8,128)(2,1)} %bitcast.72, bf16[640,2048]{1,0:T(8,128)(2,1)} %constant_dynamic-update-slice_fusion.k_ref.v_ref, bf16[640,2048]{1,0:T(8,128)(2,1)} %constant_dynamic-update-slice_fusion.k_ref.v_ref, s32[128,1]{1,0:T(8,128)} %copy.149.iq_ref, s32[1,640]{1,0:T(1,128)} %reshape.154.ik_ref), custom_call_target="tpu_custom_call" | custom-call | tf_op jit(solution)/shard_map/pallas_call | solution.py:163
  (86 shorter events, 39.1 us)
Async XLA Ops:
  0.0 39.4 %copy-start = (f32[1,128]{1,0:T(1,128)S(1)}, f32[1,128]{1,0:T(1,128)}, u32[]{:S(2)}) copy-start(f32[1,128]{1,0:T(1,128)} %param.20) | copy-start | bytes 1540
  0.0 28.3 %collective-permute-start = (bf16[128,8192]{1,0:T(8,128)(2,1)}, bf16[128,8192]{1,0:T(8,128)(2,1)}, u32[]{:S(2)}, u32[]{:S(2)}) collective-permute-start(bf16[128,8192]{1,0:T(8,128)(2,1)} %bitcast.89), channel_id=1, source_target_pairs={{0,16},{16,32},{32,48},{48,64},{64,80},{80,96},{96,112},{1,17},{17... | collective-permute-start | bytes 6291464 | tf_op jit(solution)/shard_map/ppermute | solution.py:24
  6.6 26.0 %all-to-all-start.2 = ((f32[16,128,8]{1,2,0:T(8,128)}), f32[16,128,8]{1,2,0:T(8,128)S(1)}, u32[]{:S(2)}, u32[]{:S(2)}) async-start(f32[16,128,8]{1,2,0:T(8,128)} %bitcast.9), calls=%async_computation.2 | async-start | bytes 131072 | tf_op jit(solution)/shard_map/all_to_all | solution.py:31
  32.6 28.1 %all-to-all-start = ((bf16[16,128,512]{1,2,0:T(8,128)(2,1)}), bf16[16,128,512]{1,2,0:T(8,128)(2,1)}, u32[]{:S(2)}, u32[]{:S(2)}) async-start(bf16[16,128,512]{1,2,0:T(8,128)(2,1)} %bitcast.69), calls=%async_computation | async-start | bytes 4194304 | tf_op jit(solution)/shard_map/all_to_all | solution.py:31
  39.4 3.6 %copy-start.8 = (s32[1,2048]{1,0:T(1,128)S(1)}, s32[1,2048]{1,0:T(1,128)}, u32[]{:S(2)}) copy-start(s32[1,2048]{1,0:T(1,128)} %param.25) | copy-start | bytes 24580
  40.6 3.8 %copy-start.12 = (f32[1,128]{1,0:T(1,128)S(1)}, f32[1,128]{1,0:T(1,128)}, u32[]{:S(2)}) copy-start(f32[1,128]{1,0:T(1,128)} %param.16) | copy-start | bytes 1540
  40.6 3.8 %copy-start.13 = (f32[1,128]{1,0:T(1,128)S(1)}, f32[1,128]{1,0:T(1,128)}, u32[]{:S(2)}) copy-start(f32[1,128]{1,0:T(1,128)} %param.17) | copy-start | bytes 1540
  40.6 3.9 %copy-start.10 = (bf16[1,128,1024]{2,1,0:T(8,128)(2,1)S(1)}, bf16[1,128,1024]{2,1,0:T(8,128)(2,1)}, u32[]{:S(2)}) copy-start(bf16[1,128,1024]{2,1,0:T(8,128)(2,1)} %param.24) | copy-start | bytes 786436
  40.6 3.9 %copy-start.11 = (bf16[1,128,1024]{2,1,0:T(8,128)(2,1)S(1)}, bf16[1,128,1024]{2,1,0:T(8,128)(2,1)}, u32[]{:S(2)}) copy-start(bf16[1,128,1024]{2,1,0:T(8,128)(2,1)} %param.23) | copy-start | bytes 786436
  47.4 3.8 %copy-start.7 = (f32[16,128,8]{1,2,0:T(8,128)}, f32[16,128,8]{1,2,0:T(8,128)S(1)}, u32[]{:S(2)}) copy-start(f32[16,128,8]{1,2,0:T(8,128)S(1)} %copy.130) | copy-start | bytes 196612
  51.2 13.9 %copy-start.5 = (f32[16,128,8]{2,1,0:T(8,128)S(1)}, f32[16,128,8]{2,1,0:T(8,128)}, u32[]{:S(2)}) copy-start(f32[16,128,8]{2,1,0:T(8,128)} %copy.133) | copy-start | bytes 196612
  60.7 49.9 %all-to-all-start.1 = ((bf16[16,128,256]{2,1,0:T(8,128)(2,1)}), bf16[16,128,256]{2,1,0:T(8,128)(2,1)}, u32[]{:S(2)}, u32[]{:S(2)}) async-start(bf16[16,128,256]{2,1,0:T(8,128)(2,1)} %bitcast.71), calls=%async_computation.1 | async-start | bytes 2097152 | tf_op jit(solution)/shard_map/all_to_all | solution.py:31
  68.4 46.6 %copy-start.2 = (bf16[2048,512]{0,1:T(8,128)(2,1)}, bf16[2048,512]{0,1:T(8,128)(2,1)S(1)}, u32[]{:S(2)}) copy-start(bf16[2048,512]{0,1:T(8,128)(2,1)S(1)} %copy_bitcast_fusion) | copy-start | bytes 6291460
  68.4 84.2 %collective-permute-start.1 = (bf16[128,2048]{1,0:T(8,128)(2,1)}, bf16[128,2048]{1,0:T(8,128)(2,1)}, u32[]{:S(2)}, u32[]{:S(2)}) collective-permute-start(bf16[128,2048]{1,0:T(8,128)(2,1)} %pad_maximum_fusion), channel_id=1, source_target_pairs={{0,4},{1,5},{2,6},{3,7},{4,8},{5,9},{6,10},{7,11},{8,12},{9,13},{1... | collective-permute-start | bytes 1572872 | tf_op jit(solution)/shard_map/ppermute | solution.py:24
  75.9 78.7 %collective-permute-start.2 = (bf16[128,2048]{1,0:T(8,128)(2,1)}, bf16[128,2048]{1,0:T(8,128)(2,1)}, u32[]{:S(2)}, u32[]{:S(2)}) collective-permute-start(bf16[128,2048]{1,0:T(8,128)(2,1)} %pad_maximum_fusion), channel_id=1, source_target_pairs={{0,3},{1,4},{2,5},{3,6},{4,7},{5,8},{6,9},{7,10},{8,11},{9,12},{10... | collective-permute-start | bytes 1572872 | tf_op jit(solution)/shard_map/ppermute | solution.py:24
  81.0 75.5 %collective-permute-start.3 = (bf16[128,2048]{1,0:T(8,128)(2,1)}, bf16[128,2048]{1,0:T(8,128)(2,1)}, u32[]{:S(2)}, u32[]{:S(2)}) collective-permute-start(bf16[128,2048]{1,0:T(8,128)(2,1)} %pad_maximum_fusion), channel_id=1, source_target_pairs={{0,2},{1,3},{2,4},{3,5},{4,6},{5,7},{6,8},{7,9},{8,10},{9,11},{10,... | collective-permute-start | bytes 1572872 | tf_op jit(solution)/shard_map/ppermute | solution.py:24
  112.9 45.5 %collective-permute-start.4 = (bf16[128,2048]{1,0:T(8,128)(2,1)}, bf16[128,2048]{1,0:T(8,128)(2,1)}, u32[]{:S(2)}, u32[]{:S(2)}) collective-permute-start(bf16[128,2048]{1,0:T(8,128)(2,1)} %pad_maximum_fusion), channel_id=1, source_target_pairs={{0,1},{1,2},{2,3},{3,4},{4,5},{5,6},{6,7},{7,8},{8,9},{9,10},{10,1... | collective-permute-start | bytes 1572872 | tf_op jit(solution)/shard_map/ppermute | solution.py:24
  152.6 9.6 %copy-start.6 = (f32[2048,1]{1,0:T(8,128)S(1)}, f32[2048,1]{1,0:T(8,128)}, u32[]{:S(2)}) copy-start(f32[2048,1]{1,0:T(8,128)} %get-tuple-element.17) | copy-start | bytes 24580
  163.3 11.7 %all-to-all-start.3 = ((f32[16,1,2048]{2,1,0:T(1,128)}), f32[16,1,2048]{2,1,0:T(1,128)S(1)}, u32[]{:S(2)}, u32[]{:S(2)}) async-start(f32[16,1,2048]{2,1,0:T(1,128)} %broadcast_in_dim.13), calls=%async_computation.3 | async-start | bytes 262144 | tf_op jit(solution)/shard_map/all_to_all | solution.py:235
  167.7 7.5 %copy-start.3 = (bf16[2048,512]{0,1:T(8,128)(2,1)S(1)}, bf16[2048,512]{0,1:T(8,128)(2,1)}, u32[]{:S(2)}) copy-start(bf16[2048,512]{0,1:T(8,128)(2,1)} %copy-done.2) | copy-start | bytes 6291460
  183.3 4.8 %copy-start.9 = (s32[1,2048]{1,0:T(1,128)S(1)}, s32[1,2048]{1,0:T(1,128)}, u32[]{:S(2)}) copy-start(s32[1,2048]{1,0:T(1,128)} %param.25) | copy-start | bytes 24580
  183.3 34.9 %all-to-all-start.4 = ((bf16[16,128,512]{2,1,0:T(8,128)(2,1)}), bf16[16,128,512]{2,1,0:T(8,128)(2,1)S(1)}, u32[]{:S(2)}, u32[]{:S(2)}) async-start(bf16[16,128,512]{2,1,0:T(8,128)(2,1)} %bitcast.70), calls=%async_computation.4 | async-start | bytes 4194304 | tf_op jit(solution)/shard_map/all_to_all | solution.py:38
  218.8 1.6 copy-start.4
  219.3 2.9 %copy-start.1 = (f32[1,128]{1,0:T(1,128)S(1)}, f32[1,128]{1,0:T(1,128)}, u32[]{:S(2)}) copy-start(f32[1,128]{1,0:T(1,128)} %param.20) | copy-start | bytes 1540

commit v8 on v7

--- a/solution.py
+++ b/solution.py
@@ -59,12 +59,11 @@
     edge_match = (ids[:, 0] == prev_last).astype(jnp.float32)
     block_gain = jnp.exp(log_cum[:, -1, :]) * (ids[:, 0] == last_id).astype(jnp.float32)[:, None]
     block_gain = block_gain * edge_match[:, None]
-    gain_rows = jnp.broadcast_to(block_gain[:, :, None], (nblk, heads, STATE))
+    gain_rows = jnp.broadcast_to(block_gain[:, :, None], (nblk, heads, head_dim))
     lc_rows = log_cum.transpose(0, 2, 1)
     st_rows = st.transpose(0, 2, 1)
-    x_t = x_h.T
-
-    def kernel(x_ref, xt_ref, b_ref, c_ref, lcc_ref, lcr_ref, str_ref, csc_ref, esc_ref, gain_ref,
+
+    def kernel(x_ref, b_ref, c_ref, lcc_ref, lcr_ref, str_ref, csc_ref, esc_ref, gain_ref,
                idc_ref, idr_ref, skip_ref, o_ref, sq_ref, carry_ref):
         @pl.when(pl.program_id(0) == 0)
         def _():
@@ -87,15 +86,13 @@
             xh = x_ref[:, cols]
             local = jnp.dot(intra_w, xh, preferred_element_type=jnp.float32)
             state_bf = carry_ref[h].astype(jnp.bfloat16)
-            carried = lax.dot_general(
-                c_blk, state_bf, (((1,), (1,)), ((), ())), preferred_element_type=jnp.float32
-            )
+            carried = jnp.dot(c_blk, state_bf, preferred_element_type=jnp.float32)
             carried = carried * csc_ref[0, :, h:h + 1]
             out = local + carried + skip_ref[h] * xh.astype(jnp.float32)
             o_ref[:, cols] = out
             sq = sq + jnp.sum(out * out, axis=1, keepdims=True)
-            end_w = (esc_ref[0, :, h:h + 1] * b_f32).astype(jnp.bfloat16)
-            block_state = jnp.dot(xt_ref[cols, :], end_w, preferred_element_type=jnp.float32)
+            end_w_t = (esc_ref[0, :, h:h + 1] * b_f32).T.astype(jnp.bfloat16)
+            block_state = jnp.dot(end_w_t, xh, preferred_element_type=jnp.float32)
             carry_ref[h] = gain_ref[0, h:h + 1, :] * carry_ref[h] + block_state
         sq_ref[...] = sq
 
@@ -105,7 +102,6 @@
         grid=(nblk,),
         in_specs=[
             pl.BlockSpec((BLOCK, x_width), lambda i: (i, 0)),
-            pl.BlockSpec((x_width, BLOCK), lambda i: (0, i)),
             pl.BlockSpec((BLOCK, STATE), lambda i: (i, 0)),
             pl.BlockSpec((BLOCK, STATE), lambda i: (i, 0)),
             per_block((BLOCK, heads)),
@@ -113,7 +109,7 @@
             per_block((heads, BLOCK)),
             per_block((BLOCK, heads)),
             per_block((BLOCK, heads)),
-            per_block((heads, STATE)),
+            per_block((heads, head_dim)),
             pl.BlockSpec((BLOCK, 1), lambda i: (i, 0)),
             per_block((1, BLOCK)),
             pl.BlockSpec(memory_space=pltpu.SMEM),
@@ -126,11 +122,11 @@
             jax.ShapeDtypeStruct((total, x_width), jnp.float32),
             jax.ShapeDtypeStruct((total, 1), jnp.float32),
         ],
-        scratch_shapes=[pltpu.VMEM((heads, head_dim, STATE), jnp.float32)],
+        scratch_shapes=[pltpu.VMEM((heads, STATE, head_dim), jnp.float32)],
         compiler_params=pltpu.CompilerParams(dimension_semantics=("arbitrary",)),
         interpret=interpret,
     )(
-        x_h, x_t, b_g, c_g, log_cum, lc_rows, st_rows, carry_scale, end_scale, gain_rows,
+        x_h, b_g, c_g, log_cum, lc_rows, st_rows, carry_scale, end_scale, gain_rows,
         all_ids.reshape(total, 1), ids.reshape(nblk, 1, BLOCK), skip_h,
     )
 

time: 224 us -> 219 us (0.978)
  the two profiles are of different devices: /device:TPU:1 before, /device:TPU:98 now
where the time goes in v8:
time: 219 us; the launch traced here: 218 us
  Pallas kernels  74.5 us (34%)
  starting transfers between devices  62.3 us (28%)
  waiting for transfers between devices  35.2 us (16%)
  local copies, waits for them, and re-layouts  29.7 us (14%)
  other arithmetic  15.8 us (7%)
    pallas_call x1, Pallas kernels, mixer_heads(): pl.pallas_call(kernel, grid=(nblk,), in_specs=[pl.BlockSpec((BLOCK, x_wid...  45.8 us
    pallas_call x1, Pallas kernels, attend_rows(): pl.pallas_call(kernel, grid=(kv_heads,), in_specs=[pl.BlockSpec((tok_rows...  28.7 us
    all_to_all x3, starting transfers between devices, to_heads(): moved = lax.all_to_all(lead, 'ctx', split_axis=0, concat_axis=0, tiled=True)  20.9 us
    all_to_all x1, starting transfers between devices, body(): lax.all_to_all(jnp.broadcast_to(sq_part[:, 0][None], (nctx, total)), 'ctx...  19.5 us
    ppermute x5, starting transfers between devices, shifted(): return lax.ppermute(value, axis, pairs)  16.8 us
    ppermute x5, waiting for transfers between devices, shifted(): return lax.ppermute(value, axis, pairs)  16.6 us
    all_to_all x3, waiting for transfers between devices, to_heads(): moved = lax.all_to_all(lead, 'ctx', split_axis=0, concat_axis=0, tiled=True)  12.5 us
    unnamed x42, local copies, waits for them, and re-layouts  9.69 us
  transfers between devices with their start and end apart: 10, of which 3 were waited for; matrix products, arithmetic and copies ran while one was open for 14% of the time, Pallas kernels for 34%

profile of v8, /device:TPU:98, one launch (start us, length us, event | category | flops | bytes accessed | tf_op | source)
XLA Modules:
  0.0 217.8 jit_solution(3113975538581084395)
XLA Ops:
  0.0 2.0 collective-permute-start
  3.6 7.5 %all-to-all-start.2 = ((f32[16,128,8]{1,2,0:T(8,128)}), f32[16,128,8]{1,2,0:T(8,128)S(1)}, u32[]{:S(2)}, u32[]{:S(2)}) async-start(f32[16,128,8]{1,2,0:T(8,128)} %bitcast.8), calls=%async_computation.2 | async-start | bytes 131072 | tf_op jit(solution)/shard_map/all_to_all | solution.py:31
  11.1 16.6 %collective-permute-done = bf16[128,8192]{1,0:T(8,128)(2,1)S(1)} collective-permute-done((bf16[128,8192]{1,0:T(8,128)(2,1)}, bf16[128,8192]{1,0:T(8,128)(2,1)S(1)}, u32[]{:S(2)}, u32[]{:S(2)}) %collective-permute-start) | collective-permute-done | bytes 2097184 | tf_op jit(solution)/shard_map/ppermute | solution.py:24
  29.6 7.6 %all-to-all-start = ((bf16[16,128,512]{2,1,0:T(8,128)(2,1)}), bf16[16,128,512]{2,1,0:T(8,128)(2,1)S(1)}, u32[]{:S(2)}, u32[]{:S(2)}) async-start(bf16[16,128,512]{2,1,0:T(8,128)(2,1)} %bitcast.70), calls=%async_computation | async-start | bytes 4194304 | tf_op jit(solution)/shard_map/all_to_all | solution.py:31
  43.1 1.8 pad_maximum_fusion
  47.9 12.5 %all-to-all-done = bf16[16,128,512]{2,1,0:T(8,128)(2,1)S(1)} async-done(((bf16[16,128,512]{2,1,0:T(8,128)(2,1)}), bf16[16,128,512]{2,1,0:T(8,128)(2,1)S(1)}, u32[]{:S(2)}, u32[]{:S(2)}) %all-to-all-start) | async-done | bytes 2097184 | tf_op jit(solution)/shard_map/all_to_all | solution.py:31
  60.5 5.8 %all-to-all-start.1 = ((bf16[16,128,256]{2,1,0:T(8,128)(2,1)}), bf16[16,128,256]{2,1,0:T(8,128)(2,1)}, u32[]{:S(2)}, u32[]{:S(2)}) async-start(bf16[16,128,256]{2,1,0:T(8,128)(2,1)} %bitcast.72), calls=%async_computation.1 | async-start | bytes 2097152 | tf_op jit(solution)/shard_map/all_to_all | solution.py:31
  69.2 2.8 %broadcast_multiply_fusion.csc_ref = f32[16,128,8]{2,1,0:T(8,128)} fusion(f32[16,128,8]{2,1,0:T(8,128)} %copy.116, f32[16,128]{1,0:T(8,128)S(1)} %get-tuple-element.30), kind=kLoop, calls=%fused_computation.13 | loop fusion | flops 16384 | bytes 139264 | tf_op jit(solution)/shard_map/mul | solution.py:55
  71.9 1.6 multiply_multiply_fusion
  73.6 3.4 %collective-permute-start.1 = (bf16[128,2048]{1,0:T(8,128)(2,1)}, bf16[128,2048]{1,0:T(8,128)(2,1)S(1)}, u32[]{:S(2)}, u32[]{:S(2)}) collective-permute-start(bf16[128,2048]{1,0:T(8,128)(2,1)} %pad_maximum_fusion), channel_id=1, source_target_pairs={{0,4},{1,5},{2,6},{3,7},{4,8},{5,9},{6,10},{7,11},{8,12},{9,13},{1... | collective-permute-start | bytes 1572872 | tf_op jit(solution)/shard_map/ppermute | solution.py:24
  79.3 3.4 %collective-permute-start.2 = (bf16[128,2048]{1,0:T(8,128)(2,1)}, bf16[128,2048]{1,0:T(8,128)(2,1)S(1)}, u32[]{:S(2)}, u32[]{:S(2)}) collective-permute-start(bf16[128,2048]{1,0:T(8,128)(2,1)} %pad_maximum_fusion), channel_id=1, source_target_pairs={{0,3},{1,4},{2,5},{3,6},{4,7},{5,8},{6,9},{7,10},{8,11},{9,12},{10... | collective-permute-start | bytes 1572872 | tf_op jit(solution)/shard_map/ppermute | solution.py:24
  82.7 5.0 %collective-permute-start.3 = (bf16[128,2048]{1,0:T(8,128)(2,1)}, bf16[128,2048]{1,0:T(8,128)(2,1)}, u32[]{:S(2)}, u32[]{:S(2)}) collective-permute-start(bf16[128,2048]{1,0:T(8,128)(2,1)} %pad_maximum_fusion), channel_id=1, source_target_pairs={{0,2},{1,3},{2,4},{3,5},{4,6},{5,7},{6,8},{7,9},{8,10},{9,11},{10,... | collective-permute-start | bytes 1572872 | tf_op jit(solution)/shard_map/ppermute | solution.py:24
  87.7 2.3 %fusion.14 = (bf16[2048,128]{1,0:T(8,128)(2,1)}, bf16[2048,128]{1,0:T(8,128)(2,1)}) fusion(bf16[2048,256]{1,0:T(8,128)(2,1)} %bitcast.6), kind=kLoop, calls=%fused_computation.45 | loop fusion | bytes 2097152 | tf_op jit(solution)/shard_map/slice | solution.py:206
  90.0 2.9 %collective-permute-start.4 = (bf16[128,2048]{1,0:T(8,128)(2,1)}, bf16[128,2048]{1,0:T(8,128)(2,1)}, u32[]{:S(2)}, u32[]{:S(2)}) collective-permute-start(bf16[128,2048]{1,0:T(8,128)(2,1)} %pad_maximum_fusion), channel_id=1, source_target_pairs={{0,1},{1,2},{2,3},{3,4},{4,5},{5,6},{6,7},{7,8},{8,9},{9,10},{10,1... | collective-permute-start | bytes 1572872 | tf_op jit(solution)/shard_map/ppermute | solution.py:24
  93.6 45.8 %shard_map.127 = (f32[2048,512]{1,0:T(8,128)}, f32[2048,1]{1,0:T(8,128)}) custom-call(bf16[2048,512]{1,0:T(8,128)(2,1)} %bitcast.66, bf16[2048,128]{1,0:T(8,128)(2,1)} %get-tuple-element.24.b_ref, bf16[2048,128]{1,0:T(8,128)(2,1)} %get-tuple-element.23.c_ref, f32[16,128,8]{2,1,0:T(8,128)} %copy.124.lcc_ref, f32[16,8,128]{2,1,0:T(8,128)} %bitcast.76, ...), custom_call_target="tpu_custom_call" | custom-call | tf_op jit(solution)/shard_map/pallas_call | solution.py:100
  141.2 2.0 constant_dynamic-update-slice_fusion.2
  143.2 1.9 constant_dynamic-update-slice_fusion.1
  145.1 1.9 constant_dynamic-update-slice_fusion.k_ref.v_ref
  148.1 19.5 %all-to-all-start.3 = ((f32[16,1,2048]{2,1,0:T(1,128)}), f32[16,1,2048]{2,1,0:T(1,128)S(1)}, u32[]{:S(2)}, u32[]{:S(2)}) async-start(f32[16,1,2048]{2,1,0:T(1,128)} %broadcast_in_dim.13), calls=%async_computation.3 | async-start | bytes 262144 | tf_op jit(solution)/shard_map/all_to_all | solution.py:231
  168.2 6.0 %all-to-all-done.3 = f32[16,1,2048]{2,1,0:T(1,128)S(1)} async-done(((f32[16,1,2048]{2,1,0:T(1,128)}), f32[16,1,2048]{2,1,0:T(1,128)S(1)}, u32[]{:S(2)}, u32[]{:S(2)}) %all-to-all-start.3) | async-done | bytes 131104 | tf_op jit(solution)/shard_map/all_to_all | solution.py:231
  174.4 4.2 %add_convert_fusion.1 = bf16[2048,512]{1,0:T(8,128)(2,1)} fusion(f32[2048,512]{1,0:T(8,128)} %get-tuple-element.16, bf16[2048,512]{1,0:T(8,128)(2,1)S(1)} %bitcast.67, f32[512]{0:T(512)S(1)} %bitcast.87, f32[2048]{0:T(1024)S(1)} %add_rsqrt_fusion), kind=kLoop, calls=%fused_computation.2 | loop fusion | flops 5242880 | bytes 8398848 | tf_op jit(solution)/shard_map/convert_element_type | solution.py:238
  178.6 5.1 %all-to-all-start.4 = ((bf16[16,128,512]{2,1,0:T(8,128)(2,1)}), bf16[16,128,512]{2,1,0:T(8,128)(2,1)S(1)}, u32[]{:S(2)}, u32[]{:S(2)}) async-start(bf16[16,128,512]{2,1,0:T(8,128)(2,1)} %bitcast.71), calls=%async_computation.4 | async-start | bytes 4194304 | tf_op jit(solution)/shard_map/all_to_all | solution.py:38
  185.1 28.7 %shard_map.128 = bf16[128,8192]{1,0:T(8,128)(2,1)} custom-call(bf16[128,8192]{1,0:T(8,128)(2,1)} %bitcast.73, bf16[640,2048]{1,0:T(8,128)(2,1)} %constant_dynamic-update-slice_fusion.k_ref.v_ref, bf16[640,2048]{1,0:T(8,128)(2,1)} %constant_dynamic-update-slice_fusion.k_ref.v_ref, s32[128,1]{1,0:T(8,128)} %copy.129.iq_ref, s32[1,640]{1,0:T(1,128)} %reshape.154.ik_ref), custom_call_target="tpu_custom_call" | custom-call | tf_op jit(solution)/shard_map/pallas_call | solution.py:159
  216.0 1.8 fusion
  (86 shorter events, 25.3 us)
Async XLA Ops:
  0.0 42.2 %copy-start = (f32[1,128]{1,0:T(1,128)S(1)}, f32[1,128]{1,0:T(1,128)}, u32[]{:S(2)}) copy-start(f32[1,128]{1,0:T(1,128)} %param.20) | copy-start | bytes 1540
  0.0 27.7 %collective-permute-start = (bf16[128,8192]{1,0:T(8,128)(2,1)}, bf16[128,8192]{1,0:T(8,128)(2,1)S(1)}, u32[]{:S(2)}, u32[]{:S(2)}) collective-permute-start(bf16[128,8192]{1,0:T(8,128)(2,1)} %bitcast.90), channel_id=1, source_target_pairs={{0,16},{16,32},{32,48},{48,64},{64,80},{80,96},{96,112},{1,17},{17... | collective-permute-start | bytes 6291464 | tf_op jit(solution)/shard_map/ppermute | solution.py:24
  3.6 26.0 %all-to-all-start.2 = ((f32[16,128,8]{1,2,0:T(8,128)}), f32[16,128,8]{1,2,0:T(8,128)S(1)}, u32[]{:S(2)}, u32[]{:S(2)}) async-start(f32[16,128,8]{1,2,0:T(8,128)} %bitcast.8), calls=%async_computation.2 | async-start | bytes 131072 | tf_op jit(solution)/shard_map/all_to_all | solution.py:31
  29.6 7.6 %copy-start.9 = (s32[1,2048]{1,0:T(1,128)S(1)}, s32[1,2048]{1,0:T(1,128)}, u32[]{:S(2)}) copy-start(s32[1,2048]{1,0:T(1,128)} %param.25) | copy-start | bytes 24580
  29.6 8.0 %copy-start.11 = (bf16[1,128,1024]{2,1,0:T(8,128)(2,1)S(1)}, bf16[1,128,1024]{2,1,0:T(8,128)(2,1)}, u32[]{:S(2)}) copy-start(bf16[1,128,1024]{2,1,0:T(8,128)(2,1)} %param.18) | copy-start | bytes 786436
  29.6 8.1 %copy-start.12 = (bf16[1,128,1024]{2,1,0:T(8,128)(2,1)S(1)}, bf16[1,128,1024]{2,1,0:T(8,128)(2,1)}, u32[]{:S(2)}) copy-start(bf16[1,128,1024]{2,1,0:T(8,128)(2,1)} %param.19) | copy-start | bytes 786436
  29.6 30.9 %all-to-all-start = ((bf16[16,128,512]{2,1,0:T(8,128)(2,1)}), bf16[16,128,512]{2,1,0:T(8,128)(2,1)S(1)}, u32[]{:S(2)}, u32[]{:S(2)}) async-start(bf16[16,128,512]{2,1,0:T(8,128)(2,1)} %bitcast.70), calls=%async_computation | async-start | bytes 4194304 | tf_op jit(solution)/shard_map/all_to_all | solution.py:31
  38.3 4.5 %copy-start.14 = (f32[1,128]{1,0:T(1,128)S(1)}, f32[1,128]{1,0:T(1,128)}, u32[]{:S(2)}) copy-start(f32[1,128]{1,0:T(1,128)} %param.16) | copy-start | bytes 1540
  38.4 4.5 %copy-start.15 = (f32[1,128]{1,0:T(1,128)S(1)}, f32[1,128]{1,0:T(1,128)}, u32[]{:S(2)}) copy-start(f32[1,128]{1,0:T(1,128)} %param.17) | copy-start | bytes 1540
  38.4 4.7 %copy-start.13 = (bf16[1,128,1024]{2,1,0:T(8,128)(2,1)S(1)}, bf16[1,128,1024]{2,1,0:T(8,128)(2,1)}, u32[]{:S(2)}) copy-start(bf16[1,128,1024]{2,1,0:T(8,128)(2,1)} %param.24) | copy-start | bytes 786436
  47.9 24.0 %copy-start.8 = (f32[16,128,8]{1,2,0:T(8,128)}, f32[16,128,8]{1,2,0:T(8,128)S(1)}, u32[]{:S(2)}) copy-start(f32[16,128,8]{1,2,0:T(8,128)S(1)} %copy.113) | copy-start | bytes 196612
  60.5 11.5 %copy-start.1 = (bf16[16,128,512]{2,1,0:T(8,128)(2,1)}, bf16[16,128,512]{2,1,0:T(8,128)(2,1)S(1)}, u32[]{:S(2)}) copy-start(bf16[16,128,512]{2,1,0:T(8,128)(2,1)S(1)} %all-to-all-done) | copy-start | bytes 6291460
  60.5 27.3 %all-to-all-start.1 = ((bf16[16,128,256]{2,1,0:T(8,128)(2,1)}), bf16[16,128,256]{2,1,0:T(8,128)(2,1)}, u32[]{:S(2)}, u32[]{:S(2)}) async-start(bf16[16,128,256]{2,1,0:T(8,128)(2,1)} %bitcast.72), calls=%async_computation.1 | async-start | bytes 2097152 | tf_op jit(solution)/shard_map/all_to_all | solution.py:31
  69.1 2.8 %copy-start.4 = (f32[16,128,8]{2,1,0:T(8,128)S(1)}, f32[16,128,8]{2,1,0:T(8,128)}, u32[]{:S(2)}) copy-start(f32[16,128,8]{2,1,0:T(8,128)} %copy-done.3) | copy-start | bytes 196612
  69.2 2.8 %copy-start.6 = (f32[16,128,8]{2,1,0:T(8,128)S(1)}, f32[16,128,8]{2,1,0:T(8,128)}, u32[]{:S(2)}) copy-start(f32[16,128,8]{2,1,0:T(8,128)} %copy.120) | copy-start | bytes 196612
  73.6 65.9 %collective-permute-start.1 = (bf16[128,2048]{1,0:T(8,128)(2,1)}, bf16[128,2048]{1,0:T(8,128)(2,1)S(1)}, u32[]{:S(2)}, u32[]{:S(2)}) collective-permute-start(bf16[128,2048]{1,0:T(8,128)(2,1)} %pad_maximum_fusion), channel_id=1, source_target_pairs={{0,4},{1,5},{2,6},{3,7},{4,8},{5,9},{6,10},{7,11},{8,12},{9,13},{1... | collective-permute-start | bytes 1572872 | tf_op jit(solution)/shard_map/ppermute | solution.py:24
  79.3 61.0 %collective-permute-start.2 = (bf16[128,2048]{1,0:T(8,128)(2,1)}, bf16[128,2048]{1,0:T(8,128)(2,1)S(1)}, u32[]{:S(2)}, u32[]{:S(2)}) collective-permute-start(bf16[128,2048]{1,0:T(8,128)(2,1)} %pad_maximum_fusion), channel_id=1, source_target_pairs={{0,3},{1,4},{2,5},{3,6},{4,7},{5,8},{6,9},{7,10},{8,11},{9,12},{10... | collective-permute-start | bytes 1572872 | tf_op jit(solution)/shard_map/ppermute | solution.py:24
  82.7 58.5 %collective-permute-start.3 = (bf16[128,2048]{1,0:T(8,128)(2,1)}, bf16[128,2048]{1,0:T(8,128)(2,1)}, u32[]{:S(2)}, u32[]{:S(2)}) collective-permute-start(bf16[128,2048]{1,0:T(8,128)(2,1)} %pad_maximum_fusion), channel_id=1, source_target_pairs={{0,2},{1,3},{2,4},{3,5},{4,6},{5,7},{6,8},{7,9},{8,10},{9,11},{10,... | collective-permute-start | bytes 1572872 | tf_op jit(solution)/shard_map/ppermute | solution.py:24
  90.0 53.2 %collective-permute-start.4 = (bf16[128,2048]{1,0:T(8,128)(2,1)}, bf16[128,2048]{1,0:T(8,128)(2,1)}, u32[]{:S(2)}, u32[]{:S(2)}) collective-permute-start(bf16[128,2048]{1,0:T(8,128)(2,1)} %pad_maximum_fusion), channel_id=1, source_target_pairs={{0,1},{1,2},{2,3},{3,4},{4,5},{5,6},{6,7},{7,8},{8,9},{9,10},{10,1... | collective-permute-start | bytes 1572872 | tf_op jit(solution)/shard_map/ppermute | solution.py:24
  139.4 7.6 %copy-start.7 = (f32[2048,1]{1,0:T(8,128)S(1)}, f32[2048,1]{1,0:T(8,128)}, u32[]{:S(2)}) copy-start(f32[2048,1]{1,0:T(8,128)} %get-tuple-element.17) | copy-start | bytes 24580
  141.2 33.2 %copy-start.2 = (bf16[16,128,512]{2,1,0:T(8,128)(2,1)S(1)}, bf16[16,128,512]{2,1,0:T(8,128)(2,1)}, u32[]{:S(2)}) copy-start(bf16[16,128,512]{2,1,0:T(8,128)(2,1)} %copy-done.1) | copy-start | bytes 6291460
  148.1 26.2 %all-to-all-start.3 = ((f32[16,1,2048]{2,1,0:T(1,128)}), f32[16,1,2048]{2,1,0:T(1,128)S(1)}, u32[]{:S(2)}, u32[]{:S(2)}) async-start(f32[16,1,2048]{2,1,0:T(1,128)} %broadcast_in_dim.13), calls=%async_computation.3 | async-start | bytes 262144 | tf_op jit(solution)/shard_map/all_to_all | solution.py:231
  178.6 5.1 %copy-start.10 = (s32[1,2048]{1,0:T(1,128)S(1)}, s32[1,2048]{1,0:T(1,128)}, u32[]{:S(2)}) copy-start(s32[1,2048]{1,0:T(1,128)} %param.25) | copy-start | bytes 24580
  178.6 35.2 %all-to-all-start.4 = ((bf16[16,128,512]{2,1,0:T(8,128)(2,1)}), bf16[16,128,512]{2,1,0:T(8,128)(2,1)S(1)}, u32[]{:S(2)}, u32[]{:S(2)}) async-start(bf16[16,128,512]{2,1,0:T(8,128)(2,1)} %bitcast.71), calls=%async_computation.4 | async-start | bytes 4194304 | tf_op jit(solution)/shard_map/all_to_all | solution.py:38
  (2 other events, 2.6 us)

commit v9 on v8

--- a/solution.py
+++ b/solution.py
@@ -61,6 +61,8 @@
     block_gain = block_gain * edge_match[:, None]
     gain_rows = jnp.broadcast_to(block_gain[:, :, None], (nblk, heads, head_dim))
     lc_rows = log_cum.transpose(0, 2, 1)
+    end_rows = end_scale.transpose(0, 2, 1)
+    b_t = b_g.T
     st_rows = st.transpose(0, 2, 1)
 
     def kernel(x_ref, b_ref, c_ref, lcc_ref, lcr_ref, str_ref, csc_ref, esc_ref, gain_ref,
@@ -69,13 +71,13 @@
         def _():
             carry_ref[...] = jnp.zeros(carry_ref.shape, carry_ref.dtype)
 
-        b_blk = b_ref[...]
+        b_t_blk = b_ref[...]
         c_blk = c_ref[...]
-        inner_cb = lax.dot_general(c_blk, b_blk, (((1,), (1,)), ((), ())), preferred_element_type=jnp.float32)
+        inner_cb = jnp.dot(c_blk, b_t_blk, preferred_element_type=jnp.float32)
         rows_at = lax.broadcasted_iota(jnp.int32, (BLOCK, BLOCK), 0)
         cols_at = lax.broadcasted_iota(jnp.int32, (BLOCK, BLOCK), 1)
         same_doc = (idc_ref[...] == idr_ref[0]) & (rows_at >= cols_at)
-        b_f32 = b_blk.astype(jnp.float32)
+        b_t_f32 = b_t_blk.astype(jnp.float32)
         sq = jnp.zeros((BLOCK, 1), jnp.float32)
         for h in range(heads):
             cols = slice(h * head_dim, (h + 1) * head_dim)
@@ -91,7 +93,7 @@
             out = local + carried + skip_ref[h] * xh.astype(jnp.float32)
             o_ref[:, cols] = out
             sq = sq + jnp.sum(out * out, axis=1, keepdims=True)
-            end_w_t = (esc_ref[0, :, h:h + 1] * b_f32).T.astype(jnp.bfloat16)
+            end_w_t = (esc_ref[0, h:h + 1, :] * b_t_f32).astype(jnp.bfloat16)
             block_state = jnp.dot(end_w_t, xh, preferred_element_type=jnp.float32)
             carry_ref[h] = gain_ref[0, h:h + 1, :] * carry_ref[h] + block_state
         sq_ref[...] = sq
@@ -102,13 +104,13 @@
         grid=(nblk,),
         in_specs=[
             pl.BlockSpec((BLOCK, x_width), lambda i: (i, 0)),
-            pl.BlockSpec((BLOCK, STATE), lambda i: (i, 0)),
+            pl.BlockSpec((STATE, BLOCK), lambda i: (0, i)),
             pl.BlockSpec((BLOCK, STATE), lambda i: (i, 0)),
             per_block((BLOCK, heads)),
             per_block((heads, BLOCK)),
             per_block((heads, BLOCK)),
             per_block((BLOCK, heads)),
-            per_block((BLOCK, heads)),
+            per_block((heads, BLOCK)),
             per_block((heads, head_dim)),
             pl.BlockSpec((BLOCK, 1), lambda i: (i, 0)),
             per_block((1, BLOCK)),
@@ -126,7 +128,7 @@
         compiler_params=pltpu.CompilerParams(dimension_semantics=("arbitrary",)),
         interpret=interpret,
     )(
-        x_h, b_g, c_g, log_cum, lc_rows, st_rows, carry_scale, end_scale, gain_rows,
+        x_h, b_t, c_g, log_cum, lc_rows, st_rows, carry_scale, end_rows, gain_rows,
         all_ids.reshape(total, 1), ids.reshape(nblk, 1, BLOCK), skip_h,
     )
 

time: 219 us -> 222 us (1.014)
  the two profiles are of different devices: /device:TPU:98 before, /device:TPU:32 now
where the time goes in v9:
time: 222 us; the launch traced here: 221 us
  waiting for transfers between devices  77.2 us (35%)
  Pallas kernels  59.6 us (27%)
  starting transfers between devices  43 us (19%)
  local copies, waits for them, and re-layouts  27.2 us (12%)
  other arithmetic  13.7 us (6%)
    all_to_all x3, waiting for transfers between devices, to_heads(): moved = lax.all_to_all(lead, 'ctx', split_axis=0, concat_axis=0, tiled=True)  52.9 us
    pallas_call x1, Pallas kernels, mixer_heads(): pl.pallas_call(kernel, grid=(nblk,), in_specs=[pl.BlockSpec((BLOCK, x_wid...  30.9 us
    pallas_call x1, Pallas kernels, attend_rows(): pl.pallas_call(kernel, grid=(kv_heads,), in_specs=[pl.BlockSpec((tok_rows...  28.7 us
    all_to_all x3, starting transfers between devices, to_heads(): moved = lax.all_to_all(lead, 'ctx', split_axis=0, concat_axis=0, tiled=True)  18.5 us
    ppermute x5, waiting for transfers between devices, shifted(): return lax.ppermute(value, axis, pairs)  17 us
    ppermute x5, starting transfers between devices, shifted(): return lax.ppermute(value, axis, pairs)  16.9 us
    unnamed x36, local copies, waits for them, and re-layouts  8.66 us
    all_to_all x1, waiting for transfers between devices, body(): lax.all_to_all(jnp.broadcast_to(sq_part[:, 0][None], (nctx, total)), 'ctx...  7.26 us
  transfers between devices with their start and end apart: 10, of which 4 were waited for; matrix products, arithmetic and copies ran while one was open for 13% of the time, Pallas kernels for 27%

profile of v9, /device:TPU:32, one launch (start us, length us, event | category | flops | bytes accessed | tf_op | source)
XLA Modules:
  0.0 221.0 jit_solution(17900129013579217574)
XLA Ops:
  0.0 2.0 collective-permute-start
  2.1 1.6 copy.106
  3.6 7.0 %all-to-all-start.2 = ((f32[16,128,8]{1,2,0:T(8,128)}), f32[16,128,8]{1,2,0:T(8,128)S(1)}, u32[]{:S(2)}, u32[]{:S(2)}) async-start(f32[16,128,8]{1,2,0:T(8,128)} %bitcast.9), calls=%async_computation.2 | async-start | bytes 131072 | tf_op jit(solution)/shard_map/all_to_all | solution.py:31
  10.7 17.0 %collective-permute-done = bf16[128,8192]{1,0:T(8,128)(2,1)S(1)} collective-permute-done((bf16[128,8192]{1,0:T(8,128)(2,1)}, bf16[128,8192]{1,0:T(8,128)(2,1)S(1)}, u32[]{:S(2)}, u32[]{:S(2)}) %collective-permute-start) | collective-permute-done | bytes 2097184 | tf_op jit(solution)/shard_map/ppermute | solution.py:24
  29.6 7.2 %all-to-all-start = ((bf16[16,128,512]{2,1,0:T(8,128)(2,1)}), bf16[16,128,512]{2,1,0:T(8,128)(2,1)S(1)}, u32[]{:S(2)}, u32[]{:S(2)}) async-start(bf16[16,128,512]{2,1,0:T(8,128)(2,1)} %bitcast.75), calls=%async_computation | async-start | bytes 4194304 | tf_op jit(solution)/shard_map/all_to_all | solution.py:31
  42.6 1.8 pad_maximum_fusion
  45.9 22.2 %all-to-all-done = bf16[16,128,512]{2,1,0:T(8,128)(2,1)S(1)} async-done(((bf16[16,128,512]{2,1,0:T(8,128)(2,1)}), bf16[16,128,512]{2,1,0:T(8,128)(2,1)S(1)}, u32[]{:S(2)}, u32[]{:S(2)}) %all-to-all-start) | async-done | bytes 2097184 | tf_op jit(solution)/shard_map/all_to_all | solution.py:31
  68.1 4.3 %all-to-all-start.1 = ((bf16[16,128,256]{2,1,0:T(8,128)(2,1)}), bf16[16,128,256]{2,1,0:T(8,128)(2,1)}, u32[]{:S(2)}, u32[]{:S(2)}) async-start(bf16[16,128,256]{2,1,0:T(8,128)(2,1)} %bitcast.5), calls=%async_computation.1 | async-start | bytes 2097152 | tf_op jit(solution)/shard_map/all_to_all | solution.py:31
  76.8 3.7 %collective-permute-start.1 = (bf16[128,2048]{1,0:T(8,128)(2,1)}, bf16[128,2048]{1,0:T(8,128)(2,1)S(1)}, u32[]{:S(2)}, u32[]{:S(2)}) collective-permute-start(bf16[128,2048]{1,0:T(8,128)(2,1)} %pad_maximum_fusion), channel_id=1, source_target_pairs={{0,4},{1,5},{2,6},{3,7},{4,8},{5,9},{6,10},{7,11},{8,12},{9,13},{1... | collective-permute-start | bytes 1572872 | tf_op jit(solution)/shard_map/ppermute | solution.py:24
  81.9 4.6 %collective-permute-start.2 = (bf16[128,2048]{1,0:T(8,128)(2,1)}, bf16[128,2048]{1,0:T(8,128)(2,1)S(1)}, u32[]{:S(2)}, u32[]{:S(2)}) collective-permute-start(bf16[128,2048]{1,0:T(8,128)(2,1)} %pad_maximum_fusion), channel_id=1, source_target_pairs={{0,3},{1,4},{2,5},{3,6},{4,7},{5,8},{6,9},{7,10},{8,11},{9,12},{10... | collective-permute-start | bytes 1572872 | tf_op jit(solution)/shard_map/ppermute | solution.py:24
  86.5 4.5 %collective-permute-start.3 = (bf16[128,2048]{1,0:T(8,128)(2,1)}, bf16[128,2048]{1,0:T(8,128)(2,1)}, u32[]{:S(2)}, u32[]{:S(2)}) collective-permute-start(bf16[128,2048]{1,0:T(8,128)(2,1)} %pad_maximum_fusion), channel_id=1, source_target_pairs={{0,2},{1,3},{2,4},{3,5},{4,6},{5,7},{6,8},{7,9},{8,10},{9,11},{10,... | collective-permute-start | bytes 1572872 | tf_op jit(solution)/shard_map/ppermute | solution.py:24
  91.0 30.7 %all-to-all-done.1 = bf16[16,128,256]{2,1,0:T(8,128)(2,1)} async-done(((bf16[16,128,256]{2,1,0:T(8,128)(2,1)}), bf16[16,128,256]{2,1,0:T(8,128)(2,1)}, u32[]{:S(2)}, u32[]{:S(2)}) %all-to-all-start.1) | async-done | bytes 1048608 | tf_op jit(solution)/shard_map/all_to_all | solution.py:31
  121.7 2.1 fusion.12
  124.8 2.1 collective-permute-start.4
  127.6 30.9 %shard_map.127 = (f32[2048,512]{1,0:T(8,128)}, f32[2048,1]{1,0:T(8,128)}) custom-call(bf16[2048,512]{1,0:T(8,128)(2,1)} %bitcast.71, bf16[128,2048]{1,0:T(8,128)(2,1)} %copy.118.b_ref, bf16[2048,128]{1,0:T(8,128)(2,1)} %get-tuple-element.21.c_ref, f32[16,128,8]{2,1,0:T(8,128)} %copy.119.lcc_ref, f32[16,8,128]{2,1,0:T(8,128)} %bitcast.80, ...), custom_call_target="tpu_custom_call" | custom-call | tf_op jit(solution)/shard_map/pallas_call | solution.py:102
  160.2 2.0 constant_dynamic-update-slice_fusion.2
  162.2 1.9 constant_dynamic-update-slice_fusion.1
  164.1 1.9 constant_dynamic-update-slice_fusion.k_ref.v_ref
  167.1 3.5 %all-to-all-start.3 = ((f32[16,1,2048]{2,1,0:T(1,128)}), f32[16,1,2048]{2,1,0:T(1,128)S(1)}, u32[]{:S(2)}, u32[]{:S(2)}) async-start(f32[16,1,2048]{2,1,0:T(1,128)} %broadcast_in_dim.13), calls=%async_computation.3 | async-start | bytes 262144 | tf_op jit(solution)/shard_map/all_to_all | solution.py:233
  171.3 7.3 %all-to-all-done.3 = f32[16,1,2048]{2,1,0:T(1,128)S(1)} async-done(((f32[16,1,2048]{2,1,0:T(1,128)}), f32[16,1,2048]{2,1,0:T(1,128)S(1)}, u32[]{:S(2)}, u32[]{:S(2)}) %all-to-all-start.3) | async-done | bytes 131104 | tf_op jit(solution)/shard_map/all_to_all | solution.py:233
  178.7 4.2 %add_convert_fusion.1 = bf16[2048,512]{1,0:T(8,128)(2,1)} fusion(f32[2048,512]{1,0:T(8,128)} %get-tuple-element.16, bf16[2048,512]{1,0:T(8,128)(2,1)S(1)} %bitcast.72, f32[512]{0:T(512)S(1)} %bitcast.91, f32[2048]{0:T(1024)S(1)} %add_rsqrt_fusion), kind=kLoop, calls=%fused_computation.2 | loop fusion | flops 5242880 | bytes 8398848 | tf_op jit(solution)/shard_map/convert_element_type | solution.py:240
  182.9 4.0 %all-to-all-start.4 = ((bf16[16,128,512]{2,1,0:T(8,128)(2,1)}), bf16[16,128,512]{2,1,0:T(8,128)(2,1)S(1)}, u32[]{:S(2)}, u32[]{:S(2)}) async-start(bf16[16,128,512]{2,1,0:T(8,128)(2,1)} %bitcast.76), calls=%async_computation.4 | async-start | bytes 4194304 | tf_op jit(solution)/shard_map/all_to_all | solution.py:38
  188.3 28.7 %shard_map.128 = bf16[128,8192]{1,0:T(8,128)(2,1)} custom-call(bf16[128,8192]{1,0:T(8,128)(2,1)} %bitcast.77, bf16[640,2048]{1,0:T(8,128)(2,1)} %constant_dynamic-update-slice_fusion.k_ref.v_ref, bf16[640,2048]{1,0:T(8,128)(2,1)} %constant_dynamic-update-slice_fusion.k_ref.v_ref, s32[128,1]{1,0:T(8,128)} %copy.123.iq_ref, s32[1,640]{1,0:T(1,128)} %reshape.154.ik_ref), custom_call_target="tpu_custom_call" | custom-call | tf_op jit(solution)/shard_map/pallas_call | solution.py:161
  219.2 1.8 fusion
  (78 shorter events, 23.7 us)
Async XLA Ops:
  0.0 41.7 %copy-start = (f32[1,128]{1,0:T(1,128)S(1)}, f32[1,128]{1,0:T(1,128)}, u32[]{:S(2)}) copy-start(f32[1,128]{1,0:T(1,128)} %param.20) | copy-start | bytes 1540
  0.0 27.7 %collective-permute-start = (bf16[128,8192]{1,0:T(8,128)(2,1)}, bf16[128,8192]{1,0:T(8,128)(2,1)S(1)}, u32[]{:S(2)}, u32[]{:S(2)}) collective-permute-start(bf16[128,8192]{1,0:T(8,128)(2,1)} %bitcast.94), channel_id=1, source_target_pairs={{0,16},{16,32},{32,48},{48,64},{64,80},{80,96},{96,112},{1,17},{17... | collective-permute-start | bytes 6291464 | tf_op jit(solution)/shard_map/ppermute | solution.py:24
  3.6 26.0 %all-to-all-start.2 = ((f32[16,128,8]{1,2,0:T(8,128)}), f32[16,128,8]{1,2,0:T(8,128)S(1)}, u32[]{:S(2)}, u32[]{:S(2)}) async-start(f32[16,128,8]{1,2,0:T(8,128)} %bitcast.9), calls=%async_computation.2 | async-start | bytes 131072 | tf_op jit(solution)/shard_map/all_to_all | solution.py:31
  29.6 7.2 %copy-start.6 = (s32[1,2048]{1,0:T(1,128)S(1)}, s32[1,2048]{1,0:T(1,128)}, u32[]{:S(2)}) copy-start(s32[1,2048]{1,0:T(1,128)} %param.25) | copy-start | bytes 24580
  29.6 7.6 %copy-start.8 = (bf16[1,128,1024]{2,1,0:T(8,128)(2,1)S(1)}, bf16[1,128,1024]{2,1,0:T(8,128)(2,1)}, u32[]{:S(2)}) copy-start(bf16[1,128,1024]{2,1,0:T(8,128)(2,1)} %param.18) | copy-start | bytes 786436
  29.6 7.7 %copy-start.9 = (bf16[1,128,1024]{2,1,0:T(8,128)(2,1)S(1)}, bf16[1,128,1024]{2,1,0:T(8,128)(2,1)}, u32[]{:S(2)}) copy-start(bf16[1,128,1024]{2,1,0:T(8,128)(2,1)} %param.19) | copy-start | bytes 786436
  29.6 38.5 %all-to-all-start = ((bf16[16,128,512]{2,1,0:T(8,128)(2,1)}), bf16[16,128,512]{2,1,0:T(8,128)(2,1)S(1)}, u32[]{:S(2)}, u32[]{:S(2)}) async-start(bf16[16,128,512]{2,1,0:T(8,128)(2,1)} %bitcast.75), calls=%async_computation | async-start | bytes 4194304 | tf_op jit(solution)/shard_map/all_to_all | solution.py:31
  37.9 4.5 %copy-start.11 = (f32[1,128]{1,0:T(1,128)S(1)}, f32[1,128]{1,0:T(1,128)}, u32[]{:S(2)}) copy-start(f32[1,128]{1,0:T(1,128)} %param.16) | copy-start | bytes 1540
  37.9 4.4 %copy-start.12 = (f32[1,128]{1,0:T(1,128)S(1)}, f32[1,128]{1,0:T(1,128)}, u32[]{:S(2)}) copy-start(f32[1,128]{1,0:T(1,128)} %param.17) | copy-start | bytes 1540
  37.9 4.7 %copy-start.10 = (bf16[1,128,1024]{2,1,0:T(8,128)(2,1)S(1)}, bf16[1,128,1024]{2,1,0:T(8,128)(2,1)}, u32[]{:S(2)}) copy-start(bf16[1,128,1024]{2,1,0:T(8,128)(2,1)} %param.24) | copy-start | bytes 786436
  68.1 6.2 %copy-start.1 = (bf16[16,128,512]{2,1,0:T(8,128)(2,1)}, bf16[16,128,512]{2,1,0:T(8,128)(2,1)S(1)}, u32[]{:S(2)}) copy-start(bf16[16,128,512]{2,1,0:T(8,128)(2,1)S(1)} %all-to-all-done) | copy-start | bytes 6291460
  68.1 53.6 %all-to-all-start.1 = ((bf16[16,128,256]{2,1,0:T(8,128)(2,1)}), bf16[16,128,256]{2,1,0:T(8,128)(2,1)}, u32[]{:S(2)}, u32[]{:S(2)}) async-start(bf16[16,128,256]{2,1,0:T(8,128)(2,1)} %bitcast.5), calls=%async_computation.1 | async-start | bytes 2097152 | tf_op jit(solution)/shard_map/all_to_all | solution.py:31
  74.2 7.6 %copy-start.5 = (f32[16,128,8]{1,2,0:T(8,128)}, f32[16,128,8]{1,2,0:T(8,128)S(1)}, u32[]{:S(2)}) copy-start(f32[16,128,8]{1,2,0:T(8,128)S(1)} %copy.108) | copy-start | bytes 196612
  76.8 81.7 %collective-permute-start.1 = (bf16[128,2048]{1,0:T(8,128)(2,1)}, bf16[128,2048]{1,0:T(8,128)(2,1)S(1)}, u32[]{:S(2)}, u32[]{:S(2)}) collective-permute-start(bf16[128,2048]{1,0:T(8,128)(2,1)} %pad_maximum_fusion), channel_id=1, source_target_pairs={{0,4},{1,5},{2,6},{3,7},{4,8},{5,9},{6,10},{7,11},{8,12},{9,13},{1... | collective-permute-start | bytes 1572872 | tf_op jit(solution)/shard_map/ppermute | solution.py:24
  81.9 77.5 %collective-permute-start.2 = (bf16[128,2048]{1,0:T(8,128)(2,1)}, bf16[128,2048]{1,0:T(8,128)(2,1)S(1)}, u32[]{:S(2)}, u32[]{:S(2)}) collective-permute-start(bf16[128,2048]{1,0:T(8,128)(2,1)} %pad_maximum_fusion), channel_id=1, source_target_pairs={{0,3},{1,4},{2,5},{3,6},{4,7},{5,8},{6,9},{7,10},{8,11},{9,12},{10... | collective-permute-start | bytes 1572872 | tf_op jit(solution)/shard_map/ppermute | solution.py:24
  86.5 73.7 %collective-permute-start.3 = (bf16[128,2048]{1,0:T(8,128)(2,1)}, bf16[128,2048]{1,0:T(8,128)(2,1)}, u32[]{:S(2)}, u32[]{:S(2)}) collective-permute-start(bf16[128,2048]{1,0:T(8,128)(2,1)} %pad_maximum_fusion), channel_id=1, source_target_pairs={{0,2},{1,3},{2,4},{3,5},{4,6},{5,7},{6,8},{7,9},{8,10},{9,11},{10,... | collective-permute-start | bytes 1572872 | tf_op jit(solution)/shard_map/ppermute | solution.py:24
  124.8 37.4 %collective-permute-start.4 = (bf16[128,2048]{1,0:T(8,128)(2,1)}, bf16[128,2048]{1,0:T(8,128)(2,1)}, u32[]{:S(2)}, u32[]{:S(2)}) collective-permute-start(bf16[128,2048]{1,0:T(8,128)(2,1)} %pad_maximum_fusion), channel_id=1, source_target_pairs={{0,1},{1,2},{2,3},{3,4},{4,5},{5,6},{6,7},{7,8},{8,9},{9,10},{10,1... | collective-permute-start | bytes 1572872 | tf_op jit(solution)/shard_map/ppermute | solution.py:24
  158.5 7.5 %copy-start.4 = (f32[2048,1]{1,0:T(8,128)S(1)}, f32[2048,1]{1,0:T(8,128)}, u32[]{:S(2)}) copy-start(f32[2048,1]{1,0:T(8,128)} %get-tuple-element.17) | copy-start | bytes 24580
  160.2 18.5 %copy-start.2 = (bf16[16,128,512]{2,1,0:T(8,128)(2,1)S(1)}, bf16[16,128,512]{2,1,0:T(8,128)(2,1)}, u32[]{:S(2)}) copy-start(bf16[16,128,512]{2,1,0:T(8,128)(2,1)} %copy-done.1) | copy-start | bytes 6291460
  167.1 11.5 %all-to-all-start.3 = ((f32[16,1,2048]{2,1,0:T(1,128)}), f32[16,1,2048]{2,1,0:T(1,128)S(1)}, u32[]{:S(2)}, u32[]{:S(2)}) async-start(f32[16,1,2048]{2,1,0:T(1,128)} %broadcast_in_dim.13), calls=%async_computation.3 | async-start | bytes 262144 | tf_op jit(solution)/shard_map/all_to_all | solution.py:233
  182.9 4.0 %copy-start.7 = (s32[1,2048]{1,0:T(1,128)S(1)}, s32[1,2048]{1,0:T(1,128)}, u32[]{:S(2)}) copy-start(s32[1,2048]{1,0:T(1,128)} %param.25) | copy-start | bytes 24580
  182.9 34.2 %all-to-all-start.4 = ((bf16[16,128,512]{2,1,0:T(8,128)(2,1)}), bf16[16,128,512]{2,1,0:T(8,128)(2,1)S(1)}, u32[]{:S(2)}, u32[]{:S(2)}) async-start(bf16[16,128,512]{2,1,0:T(8,128)(2,1)} %bitcast.76), calls=%async_computation.4 | async-start | bytes 4194304 | tf_op jit(solution)/shard_map/all_to_all | solution.py:38
  217.6 1.6 copy-start.3

commit v10 on v9

--- a/solution.py
+++ b/solution.py
@@ -214,8 +214,8 @@
 
     halo = -(-MOST_DOC // tok_rows)
     kv_row = jnp.concatenate([keys[0], values[0]], axis=1)
-    kv_row, x_h = lax.optimization_barrier((kv_row, x_h))
     kv_win = jnp.concatenate([shifted(kv_row, "ctx", by) for by in range(halo, 0, -1)] + [kv_row], axis=0)
+    kv_win, x_h = lax.optimization_barrier((kv_win, x_h))
     all_ids = doc_ids[0]
     lead = halo * tok_rows
     padded_ids = jnp.concatenate([jnp.full((lead,), -1, all_ids.dtype), all_ids])
@@ -228,7 +228,6 @@
     gain_h = lax.dynamic_slice_in_dim(norm_gain[0], me * part, part)
 
     mixer_out, sq_part = mixer_heads(x_h, dt_h, bias_h, alog_h, b_g, c_g, skip_h, all_ids)
-    kv_win, mixer_out, sq_part = lax.optimization_barrier((kv_win, mixer_out, sq_part))
     attended = attend_rows(queries[0], kv_win, ids_q.reshape(tok_rows, 1), ids_k.reshape(1, lead + tok_rows))
     sq_all = lax.all_to_all(
         jnp.broadcast_to(sq_part[:, 0][None], (nctx, total)), "ctx", split_axis=0, concat_axis=0, tiled=True

time: 222 us -> 219 us (0.986)
  waiting for transfers between devices: 77.2 us -> 45.5 us
  other arithmetic: 13.7 us -> 41.1 us
  local copies, waits for them, and re-layouts: 27.2 us -> 31.3 us
  starting transfers between devices: 43 us -> 40.5 us
    another operation x1, other arithmetic: 1.36 us -> 23.3 us  [mixer_heads(): log_cum = jnp.cumsum(log_rate.reshape(nblk, BLOCK, heads), axis=1)]
    ppermute x5, waiting for transfers between devices: 17 us -> 0.01 us  [shifted(): return lax.ppermute(value, axis, pairs)]
    all_to_all x3, waiting for transfers between devices: 52.9 us -> 38.2 us  [to_heads(): moved = lax.all_to_all(lead, 'ctx', split_axis=0, concat_axis=0, tiled=True)]
    unnamed x36 -> x34, local copies, waits for them, and re-layouts: 8.66 us -> 14.1 us
    all_to_all x3, starting transfers between devices: 18.5 us -> 14.3 us  [to_heads(): moved = lax.all_to_all(lead, 'ctx', split_axis=0, concat_axis=0, tiled=True)]
  transfers between devices with their start and end apart: 10 -> 10, of which waited for: 4 -> 3; matrix products, arithmetic and copies ran while one was open for 13% -> 26% of each run, Pallas kernels for 27% -> 13%
where the time goes in v10:
time: 219 us; the launch traced here: 218 us
  Pallas kernels  59.6 us (27%)
  waiting for transfers between devices  45.5 us (21%)
  other arithmetic  41.1 us (19%)
  starting transfers between devices  40.5 us (18%)
  local copies, waits for them, and re-layouts  31.3 us (14%)
    all_to_all x3, waiting for transfers between devices, to_heads(): moved = lax.all_to_all(lead, 'ctx', split_axis=0, concat_axis=0, tiled=True)  38.2 us
    pallas_call x1, Pallas kernels, mixer_heads(): pl.pallas_call(kernel, grid=(nblk,), in_specs=[pl.BlockSpec((BLOCK, x_wid...  30.9 us
    pallas_call x1, Pallas kernels, attend_rows(): pl.pallas_call(kernel, grid=(kv_heads,), in_specs=[pl.BlockSpec((tok_rows...  28.7 us
    another operation x1, other arithmetic, mixer_heads(): log_cum = jnp.cumsum(log_rate.reshape(nblk, BLOCK, heads), axis=1)  23.3 us
    ppermute x5, starting transfers between devices, shifted(): return lax.ppermute(value, axis, pairs)  18.6 us
    all_to_all x3, starting transfers between devices, to_heads(): moved = lax.all_to_all(lead, 'ctx', split_axis=0, concat_axis=0, tiled=True)  14.3 us
    unnamed x34, local copies, waits for them, and re-layouts  14.1 us
    all_to_all x1, waiting for transfers between devices, body(): lax.all_to_all(jnp.broadcast_to(sq_part[:, 0][None], (nctx, total)), 'ctx...  7.26 us
  transfers between devices with their start and end apart: 10, of which 3 were waited for; matrix products, arithmetic and copies ran while one was open for 26% of the time, Pallas kernels for 13%

profile of v10, /device:TPU:32, one launch (start us, length us, event | category | flops | bytes accessed | tf_op | source)
XLA Modules:
  0.0 218.1 jit_solution(3600505268594179266)
XLA Ops:
  0.0 1.9 pad_maximum_fusion
  1.9 4.2 %collective-permute-start.3 = (bf16[128,2048]{1,0:T(8,128)(2,1)}, bf16[128,2048]{1,0:T(8,128)(2,1)}, u32[]{:S(2)}, u32[]{:S(2)}) collective-permute-start(bf16[128,2048]{1,0:T(8,128)(2,1)} %pad_maximum_fusion), channel_id=1, source_target_pairs={{0,1},{1,2},{2,3},{3,4},{4,5},{5,6},{6,7},{7,8},{8,9},{9,10},{10,1... | collective-permute-start | bytes 1572872 | tf_op jit(solution)/shard_map/ppermute | solution.py:24
  6.1 4.6 %collective-permute-start.2 = (bf16[128,2048]{1,0:T(8,128)(2,1)}, bf16[128,2048]{1,0:T(8,128)(2,1)}, u32[]{:S(2)}, u32[]{:S(2)}) collective-permute-start(bf16[128,2048]{1,0:T(8,128)(2,1)} %pad_maximum_fusion), channel_id=1, source_target_pairs={{0,2},{1,3},{2,4},{3,5},{4,6},{5,7},{6,8},{7,9},{8,10},{9,11},{10,... | collective-permute-start | bytes 1572872 | tf_op jit(solution)/shard_map/ppermute | solution.py:24
  10.7 4.4 %collective-permute-start.1 = (bf16[128,2048]{1,0:T(8,128)(2,1)}, bf16[128,2048]{1,0:T(8,128)(2,1)}, u32[]{:S(2)}, u32[]{:S(2)}) collective-permute-start(bf16[128,2048]{1,0:T(8,128)(2,1)} %pad_maximum_fusion), channel_id=1, source_target_pairs={{0,3},{1,4},{2,5},{3,6},{4,7},{5,8},{6,9},{7,10},{8,11},{9,12},{10... | collective-permute-start | bytes 1572872 | tf_op jit(solution)/shard_map/ppermute | solution.py:24
  15.1 3.5 %collective-permute-start = (bf16[128,2048]{1,0:T(8,128)(2,1)}, bf16[128,2048]{1,0:T(8,128)(2,1)}, u32[]{:S(2)}, u32[]{:S(2)}) collective-permute-start(bf16[128,2048]{1,0:T(8,128)(2,1)} %pad_maximum_fusion), channel_id=1, source_target_pairs={{0,4},{1,5},{2,6},{3,7},{4,8},{5,9},{6,10},{7,11},{8,12},{9,13},{1... | collective-permute-start | bytes 1572872 | tf_op jit(solution)/shard_map/ppermute | solution.py:24
  20.1 3.5 %all-to-all-start.2 = ((f32[16,128,8]{1,2,0:T(8,128)}), f32[16,128,8]{1,2,0:T(8,128)S(1)}, u32[]{:S(2)}, u32[]{:S(2)}) async-start(f32[16,128,8]{1,2,0:T(8,128)} %bitcast.9), calls=%async_computation.2 | async-start | bytes 131072 | tf_op jit(solution)/shard_map/all_to_all | solution.py:31
  23.6 1.9 collective-permute-start.4
  34.6 22.0 %all-to-all-done.2 = f32[16,128,8]{1,2,0:T(8,128)S(1)} async-done(((f32[16,128,8]{1,2,0:T(8,128)}), f32[16,128,8]{1,2,0:T(8,128)S(1)}, u32[]{:S(2)}, u32[]{:S(2)}) %all-to-all-start.2) | async-done | bytes 65568 | tf_op jit(solution)/shard_map/all_to_all | solution.py:31
  56.6 3.7 %all-to-all-start.1 = ((bf16[16,128,256]{2,1,0:T(8,128)(2,1)}), bf16[16,128,256]{2,1,0:T(8,128)(2,1)S(1)}, u32[]{:S(2)}, u32[]{:S(2)}) async-start(bf16[16,128,256]{2,1,0:T(8,128)(2,1)} %bitcast.5), calls=%async_computation.1 | async-start | bytes 2097152 | tf_op jit(solution)/shard_map/all_to_all | solution.py:31
  60.9 23.3 %fusion.14 = f32[16,128,8]{2,0,1:T(8,128)S(1)} fusion(f32[16,128,8]{2,0,1:T(8,128)S(1)} %copy.107), kind=kOutput, calls=%fused_computation.45 | output fusion | flops 2080768 | bytes 131072 | tf_op jit(solution)/shard_map/jit(cumsum)/reduce_window_sum | solution.py:49
  86.7 1.8 broadcast_select_fusion
  91.1 7.2 %all-to-all-start = ((bf16[16,128,512]{2,1,0:T(8,128)(2,1)}), bf16[16,128,512]{2,1,0:T(8,128)(2,1)S(1)}, u32[]{:S(2)}, u32[]{:S(2)}) async-start(bf16[16,128,512]{2,1,0:T(8,128)(2,1)} %bitcast.75), calls=%async_computation | async-start | bytes 4194304 | tf_op jit(solution)/shard_map/all_to_all | solution.py:31
  98.3 2.5 %broadcast_multiply_fusion.csc_ref = f32[16,128,8]{2,1,0:T(8,128)} fusion(f32[16,128,8]{2,1,0:T(8,128)} %copy.111, f32[16,128]{1,0:T(8,128)S(1)} %get-tuple-element.23), kind=kLoop, calls=%fused_computation.9 | loop fusion | flops 16384 | bytes 139264 | tf_op jit(solution)/shard_map/mul | solution.py:55
  102.3 2.0 constant_dynamic-update-slice_fusion.4
  104.3 1.9 constant_dynamic-update-slice_fusion.3
  106.2 1.9 constant_dynamic-update-slice_fusion.2
  108.1 1.9 constant_dynamic-update-slice_fusion.1
  112.8 16.2 %all-to-all-done = bf16[16,128,512]{2,1,0:T(8,128)(2,1)S(1)} async-done(((bf16[16,128,512]{2,1,0:T(8,128)(2,1)}), bf16[16,128,512]{2,1,0:T(8,128)(2,1)S(1)}, u32[]{:S(2)}, u32[]{:S(2)}) %all-to-all-start) | async-done | bytes 2097184 | tf_op jit(solution)/shard_map/all_to_all | solution.py:31
  130.3 30.9 %shard_map.127 = (f32[2048,512]{1,0:T(8,128)}, f32[2048,1]{1,0:T(8,128)}) custom-call(bf16[2048,512]{1,0:T(8,128)(2,1)} %bitcast.71, bf16[128,2048]{1,0:T(8,128)(2,1)} %copy.118.b_ref, bf16[2048,128]{1,0:T(8,128)(2,1)} %get-tuple-element.15.c_ref, f32[16,128,8]{2,1,0:T(8,128)} %copy.119.lcc_ref, f32[16,8,128]{2,1,0:T(8,128)} %bitcast.85, ...), custom_call_target="tpu_custom_call" | custom-call | tf_op jit(solution)/shard_map/pallas_call | solution.py:102
  163.5 3.5 %all-to-all-start.3 = ((f32[16,1,2048]{2,1,0:T(1,128)}), f32[16,1,2048]{2,1,0:T(1,128)S(1)}, u32[]{:S(2)}, u32[]{:S(2)}) async-start(f32[16,1,2048]{2,1,0:T(1,128)} %broadcast_in_dim.13), calls=%async_computation.3 | async-start | bytes 262144 | tf_op jit(solution)/shard_map/all_to_all | solution.py:232
  167.7 7.3 %all-to-all-done.3 = f32[16,1,2048]{2,1,0:T(1,128)S(1)} async-done(((f32[16,1,2048]{2,1,0:T(1,128)}), f32[16,1,2048]{2,1,0:T(1,128)S(1)}, u32[]{:S(2)}, u32[]{:S(2)}) %all-to-all-start.3) | async-done | bytes 131104 | tf_op jit(solution)/shard_map/all_to_all | solution.py:232
  175.1 4.9 %add_convert_fusion.1 = bf16[2048,512]{1,0:T(8,128)(2,1)} fusion(f32[2048,512]{1,0:T(8,128)} %get-tuple-element.10, bf16[2048,512]{1,0:T(8,128)(2,1)} %bitcast.72, f32[512]{0:T(512)S(1)} %bitcast.94, f32[2048]{0:T(1024)S(1)} %add_rsqrt_fusion), kind=kLoop, calls=%fused_computation.2 | loop fusion | flops 5242880 | bytes 8398848 | tf_op jit(solution)/shard_map/convert_element_type | solution.py:239
  180.0 4.0 %all-to-all-start.4 = ((bf16[16,128,512]{2,1,0:T(8,128)(2,1)}), bf16[16,128,512]{2,1,0:T(8,128)(2,1)S(1)}, u32[]{:S(2)}, u32[]{:S(2)}) async-start(bf16[16,128,512]{2,1,0:T(8,128)(2,1)} %bitcast.76), calls=%async_computation.4 | async-start | bytes 4194304 | tf_op jit(solution)/shard_map/all_to_all | solution.py:38
  185.5 28.7 %shard_map.128 = bf16[128,8192]{1,0:T(8,128)(2,1)} custom-call(bf16[128,8192]{1,0:T(8,128)(2,1)} %bitcast.78, bf16[640,2048]{1,0:T(8,128)(2,1)} %constant_dynamic-update-slice_fusion.k_ref.v_ref, bf16[640,2048]{1,0:T(8,128)(2,1)} %constant_dynamic-update-slice_fusion.k_ref.v_ref, s32[128,1]{1,0:T(8,128)} %copy.123.iq_ref, s32[1,640]{1,0:T(1,128)} %reshape.154.ik_ref), custom_call_target="tpu_custom_call" | custom-call | tf_op jit(solution)/shard_map/pallas_call | solution.py:161
  (76 shorter events, 30.3 us)
Async XLA Ops:
  0.0 34.1 %copy-start = (f32[1,128]{1,0:T(1,128)S(1)}, f32[1,128]{1,0:T(1,128)}, u32[]{:S(2)}) copy-start(f32[1,128]{1,0:T(1,128)} %param.20) | copy-start | bytes 1540
  1.9 106.3 %collective-permute-start.3 = (bf16[128,2048]{1,0:T(8,128)(2,1)}, bf16[128,2048]{1,0:T(8,128)(2,1)}, u32[]{:S(2)}, u32[]{:S(2)}) collective-permute-start(bf16[128,2048]{1,0:T(8,128)(2,1)} %pad_maximum_fusion), channel_id=1, source_target_pairs={{0,1},{1,2},{2,3},{3,4},{4,5},{5,6},{6,7},{7,8},{8,9},{9,10},{10,1... | collective-permute-start | bytes 1572872 | tf_op jit(solution)/shard_map/ppermute | solution.py:24
  6.1 100.2 %collective-permute-start.2 = (bf16[128,2048]{1,0:T(8,128)(2,1)}, bf16[128,2048]{1,0:T(8,128)(2,1)}, u32[]{:S(2)}, u32[]{:S(2)}) collective-permute-start(bf16[128,2048]{1,0:T(8,128)(2,1)} %pad_maximum_fusion), channel_id=1, source_target_pairs={{0,2},{1,3},{2,4},{3,5},{4,6},{5,7},{6,8},{7,9},{8,10},{9,11},{10,... | collective-permute-start | bytes 1572872 | tf_op jit(solution)/shard_map/ppermute | solution.py:24
  10.7 93.6 %collective-permute-start.1 = (bf16[128,2048]{1,0:T(8,128)(2,1)}, bf16[128,2048]{1,0:T(8,128)(2,1)}, u32[]{:S(2)}, u32[]{:S(2)}) collective-permute-start(bf16[128,2048]{1,0:T(8,128)(2,1)} %pad_maximum_fusion), channel_id=1, source_target_pairs={{0,3},{1,4},{2,5},{3,6},{4,7},{5,8},{6,9},{7,10},{8,11},{9,12},{10... | collective-permute-start | bytes 1572872 | tf_op jit(solution)/shard_map/ppermute | solution.py:24
  15.1 87.3 %collective-permute-start = (bf16[128,2048]{1,0:T(8,128)(2,1)}, bf16[128,2048]{1,0:T(8,128)(2,1)}, u32[]{:S(2)}, u32[]{:S(2)}) collective-permute-start(bf16[128,2048]{1,0:T(8,128)(2,1)} %pad_maximum_fusion), channel_id=1, source_target_pairs={{0,4},{1,5},{2,6},{3,7},{4,8},{5,9},{6,10},{7,11},{8,12},{9,13},{1... | collective-permute-start | bytes 1572872 | tf_op jit(solution)/shard_map/ppermute | solution.py:24
  20.1 36.5 %all-to-all-start.2 = ((f32[16,128,8]{1,2,0:T(8,128)}), f32[16,128,8]{1,2,0:T(8,128)S(1)}, u32[]{:S(2)}, u32[]{:S(2)}) async-start(f32[16,128,8]{1,2,0:T(8,128)} %bitcast.9), calls=%async_computation.2 | async-start | bytes 131072 | tf_op jit(solution)/shard_map/all_to_all | solution.py:31
  23.6 63.1 %collective-permute-start.4 = (bf16[128,8192]{1,0:T(8,128)(2,1)}, bf16[128,8192]{1,0:T(8,128)(2,1)}, u32[]{:S(2)}, u32[]{:S(2)}) collective-permute-start(bf16[128,8192]{1,0:T(8,128)(2,1)} %bitcast.97), channel_id=1, source_target_pairs={{0,16},{16,32},{32,48},{48,64},{64,80},{80,96},{96,112},{1,17},{17... | collective-permute-start | bytes 6291464 | tf_op jit(solution)/shard_map/ppermute | solution.py:24
  29.5 2.9 %copy-start.8 = (s32[1,2048]{1,0:T(1,128)S(1)}, s32[1,2048]{1,0:T(1,128)}, u32[]{:S(2)}) copy-start(s32[1,2048]{1,0:T(1,128)} %param.25) | copy-start | bytes 24580
  30.1 3.8 %copy-start.10 = (f32[1,128]{1,0:T(1,128)S(1)}, f32[1,128]{1,0:T(1,128)}, u32[]{:S(2)}) copy-start(f32[1,128]{1,0:T(1,128)} %param.16) | copy-start | bytes 1540
  30.1 3.8 %copy-start.11 = (f32[1,128]{1,0:T(1,128)S(1)}, f32[1,128]{1,0:T(1,128)}, u32[]{:S(2)}) copy-start(f32[1,128]{1,0:T(1,128)} %param.17) | copy-start | bytes 1540
  56.6 33.5 %all-to-all-start.1 = ((bf16[16,128,256]{2,1,0:T(8,128)(2,1)}), bf16[16,128,256]{2,1,0:T(8,128)(2,1)S(1)}, u32[]{:S(2)}, u32[]{:S(2)}) async-start(bf16[16,128,256]{2,1,0:T(8,128)(2,1)} %bitcast.5), calls=%async_computation.1 | async-start | bytes 2097152 | tf_op jit(solution)/shard_map/all_to_all | solution.py:31
  84.6 3.9 %copy-start.7 = (f32[16,128,8]{1,2,0:T(8,128)}, f32[16,128,8]{1,2,0:T(8,128)S(1)}, u32[]{:S(2)}) copy-start(f32[16,128,8]{1,2,0:T(8,128)S(1)} %copy.108) | copy-start | bytes 196612
  90.1 1.0 copy-start.3
  91.1 37.9 %all-to-all-start = ((bf16[16,128,512]{2,1,0:T(8,128)(2,1)}), bf16[16,128,512]{2,1,0:T(8,128)(2,1)S(1)}, u32[]{:S(2)}, u32[]{:S(2)}) async-start(bf16[16,128,512]{2,1,0:T(8,128)(2,1)} %bitcast.75), calls=%async_computation | async-start | bytes 4194304 | tf_op jit(solution)/shard_map/all_to_all | solution.py:31
  102.3 7.8 %copy-start.5 = (bf16[1,128,1024]{2,1,0:T(8,128)(2,1)S(1)}, bf16[1,128,1024]{2,1,0:T(8,128)(2,1)}, u32[]{:S(2)}) copy-start(bf16[1,128,1024]{2,1,0:T(8,128)(2,1)} %param.24) | copy-start | bytes 786436
  102.3 7.8 %copy-start.6 = (bf16[1,128,1024]{2,1,0:T(8,128)(2,1)S(1)}, bf16[1,128,1024]{2,1,0:T(8,128)(2,1)}, u32[]{:S(2)}) copy-start(bf16[1,128,1024]{2,1,0:T(8,128)(2,1)} %param.23) | copy-start | bytes 786436
  102.3 8.5 %copy-start.4 = (bf16[16,128,256]{2,1,0:T(8,128)(2,1)S(1)}, bf16[16,128,256]{2,1,0:T(8,128)(2,1)}, u32[]{:S(2)}) copy-start(bf16[16,128,256]{2,1,0:T(8,128)(2,1)} %copy-done.3) | copy-start | bytes 3145732
  129.0 1.3 copy-start.1
  163.5 11.5 %all-to-all-start.3 = ((f32[16,1,2048]{2,1,0:T(1,128)}), f32[16,1,2048]{2,1,0:T(1,128)S(1)}, u32[]{:S(2)}, u32[]{:S(2)}) async-start(f32[16,1,2048]{2,1,0:T(1,128)} %broadcast_in_dim.13), calls=%async_computation.3 | async-start | bytes 262144 | tf_op jit(solution)/shard_map/all_to_all | solution.py:232
  180.0 4.0 %copy-start.9 = (s32[1,2048]{1,0:T(1,128)S(1)}, s32[1,2048]{1,0:T(1,128)}, u32[]{:S(2)}) copy-start(s32[1,2048]{1,0:T(1,128)} %param.25) | copy-start | bytes 24580
  180.0 34.2 %all-to-all-start.4 = ((bf16[16,128,512]{2,1,0:T(8,128)(2,1)}), bf16[16,128,512]{2,1,0:T(8,128)(2,1)S(1)}, u32[]{:S(2)}, u32[]{:S(2)}) async-start(bf16[16,128,512]{2,1,0:T(8,128)(2,1)} %bitcast.76), calls=%async_computation.4 | async-start | bytes 4194304 | tf_op jit(solution)/shard_map/all_to_all | solution.py:38
  214.7 1.6 copy-start.2

commit v11 on v10

--- a/solution.py
+++ b/solution.py
@@ -46,7 +46,11 @@
     nblk = total // BLOCK
     step = jax.nn.softplus(dt_h + bias_h[None, :])
     log_rate = -step * jnp.exp(alog_h)[None, :]
-    log_cum = jnp.cumsum(log_rate.reshape(nblk, BLOCK, heads), axis=1)
+    log_cum = log_rate.reshape(nblk, BLOCK, heads)
+    reach = 1
+    while reach < BLOCK:
+        log_cum = log_cum + jnp.pad(log_cum[:, :-reach], ((0, 0), (reach, 0), (0, 0)))
+        reach *= 2
     st = step.reshape(nblk, BLOCK, heads)
     ids = all_ids.reshape(nblk, BLOCK)
     last_id = ids[:, -1]

time: 219 us -> 203 us (0.927)
  other arithmetic: 41.1 us -> 16.7 us
  waiting for transfers between devices: 45.5 us -> 56.7 us
  starting transfers between devices: 40.5 us -> 36.8 us
    another operation x1 -> x0, other arithmetic: 23.3 us -> none  [mixer_heads(): log_cum = jnp.cumsum(log_rate.reshape(nblk, BLOCK, heads), axis=1)]
    all_to_all x3, waiting for transfers between devices: 38.2 us -> 49.5 us  [to_heads(): moved = lax.all_to_all(lead, 'ctx', split_axis=0, concat_axis=0, tiled=True)]
    all_to_all x3, starting transfers between devices: 14.3 us -> 10.9 us  [to_heads(): moved = lax.all_to_all(lead, 'ctx', split_axis=0, concat_axis=0, tiled=True)]
    mul x1, other arithmetic: 2.54 us -> 0.1 us  [mixer_heads(): carry_scale = jnp.exp(log_cum) * edge_valid[:, :, None]]
    unnamed x34 -> x32, local copies, waits for them, and re-layouts: 14.1 us -> 13.1 us
  transfers between devices with their start and end apart: 10 -> 10, of which waited for: 3 -> 4; matrix products, arithmetic and copies ran while one was open for 26% -> 16% of each run, Pallas kernels for 13% -> 14%
where the time goes in v11:
time: 203 us; the launch traced here: 201 us
  Pallas kernels  59.6 us (29%)
  waiting for transfers between devices  56.7 us (28%)
  starting transfers between devices  36.8 us (18%)
  local copies, waits for them, and re-layouts  30.8 us (15%)
  other arithmetic  16.7 us (8%)
    all_to_all x3, waiting for transfers between devices, to_heads(): moved = lax.all_to_all(lead, 'ctx', split_axis=0, concat_axis=0, tiled=True)  49.5 us
    pallas_call x1, Pallas kernels, mixer_heads(): pl.pallas_call(kernel, grid=(nblk,), in_specs=[pl.BlockSpec((BLOCK, x_wid...  30.9 us
    pallas_call x1, Pallas kernels, attend_rows(): pl.pallas_call(kernel, grid=(kv_heads,), in_specs=[pl.BlockSpec((tok_rows...  28.7 us
    ppermute x5, starting transfers between devices, shifted(): return lax.ppermute(value, axis, pairs)  18.6 us
    unnamed x32, local copies, waits for them, and re-layouts  13.1 us
    all_to_all x3, starting transfers between devices, to_heads(): moved = lax.all_to_all(lead, 'ctx', split_axis=0, concat_axis=0, tiled=True)  10.9 us
    all_to_all x1, waiting for transfers between devices, body(): lax.all_to_all(jnp.broadcast_to(sq_part[:, 0][None], (nctx, total)), 'ctx...  7.26 us
    convert_element_type x1, other arithmetic, body(): mixed = (x_h.astype(jnp.float32) + mixer_out * inv_rms * gain_h.astype(jn...  4.87 us
  transfers between devices with their start and end apart: 10, of which 4 were waited for; matrix products, arithmetic and copies ran while one was open for 16% of the time, Pallas kernels for 14%

profile of v11, /device:TPU:32, one launch (start us, length us, event | category | flops | bytes accessed | tf_op | source)
XLA Modules:
  0.0 201.0 jit_solution(1962175973834510149)
XLA Ops:
  0.0 1.9 pad_maximum_fusion
  1.9 4.2 %collective-permute-start.3 = (bf16[128,2048]{1,0:T(8,128)(2,1)}, bf16[128,2048]{1,0:T(8,128)(2,1)}, u32[]{:S(2)}, u32[]{:S(2)}) collective-permute-start(bf16[128,2048]{1,0:T(8,128)(2,1)} %pad_maximum_fusion), channel_id=1, source_target_pairs={{0,1},{1,2},{2,3},{3,4},{4,5},{5,6},{6,7},{7,8},{8,9},{9,10},{10,1... | collective-permute-start | bytes 1572872 | tf_op jit(solution)/shard_map/ppermute | solution.py:24
  6.1 4.7 %collective-permute-start.2 = (bf16[128,2048]{1,0:T(8,128)(2,1)}, bf16[128,2048]{1,0:T(8,128)(2,1)}, u32[]{:S(2)}, u32[]{:S(2)}) collective-permute-start(bf16[128,2048]{1,0:T(8,128)(2,1)} %pad_maximum_fusion), channel_id=1, source_target_pairs={{0,2},{1,3},{2,4},{3,5},{4,6},{5,7},{6,8},{7,9},{8,10},{9,11},{10,... | collective-permute-start | bytes 1572872 | tf_op jit(solution)/shard_map/ppermute | solution.py:24
  10.7 4.4 %collective-permute-start.1 = (bf16[128,2048]{1,0:T(8,128)(2,1)}, bf16[128,2048]{1,0:T(8,128)(2,1)}, u32[]{:S(2)}, u32[]{:S(2)}) collective-permute-start(bf16[128,2048]{1,0:T(8,128)(2,1)} %pad_maximum_fusion), channel_id=1, source_target_pairs={{0,3},{1,4},{2,5},{3,6},{4,7},{5,8},{6,9},{7,10},{8,11},{9,12},{10... | collective-permute-start | bytes 1572872 | tf_op jit(solution)/shard_map/ppermute | solution.py:24
  15.1 3.5 %collective-permute-start = (bf16[128,2048]{1,0:T(8,128)(2,1)}, bf16[128,2048]{1,0:T(8,128)(2,1)}, u32[]{:S(2)}, u32[]{:S(2)}) collective-permute-start(bf16[128,2048]{1,0:T(8,128)(2,1)} %pad_maximum_fusion), channel_id=1, source_target_pairs={{0,4},{1,5},{2,6},{3,7},{4,8},{5,9},{6,10},{7,11},{8,12},{9,13},{1... | collective-permute-start | bytes 1572872 | tf_op jit(solution)/shard_map/ppermute | solution.py:24
  20.1 3.5 %all-to-all-start.2 = ((f32[16,128,8]{1,2,0:T(8,128)}), f32[16,128,8]{1,2,0:T(8,128)S(1)}, u32[]{:S(2)}, u32[]{:S(2)}) async-start(f32[16,128,8]{1,2,0:T(8,128)} %bitcast.9), calls=%async_computation.2 | async-start | bytes 131072 | tf_op jit(solution)/shard_map/all_to_all | solution.py:31
  23.6 1.9 collective-permute-start.4
  35.4 21.2 %all-to-all-done.2 = f32[16,128,8]{1,2,0:T(8,128)S(1)} async-done(((f32[16,128,8]{1,2,0:T(8,128)}), f32[16,128,8]{1,2,0:T(8,128)S(1)}, u32[]{:S(2)}, u32[]{:S(2)}) %all-to-all-start.2) | async-done | bytes 65568 | tf_op jit(solution)/shard_map/all_to_all | solution.py:31
  56.6 3.7 %all-to-all-start.1 = ((bf16[16,128,256]{2,1,0:T(8,128)(2,1)}), bf16[16,128,256]{2,1,0:T(8,128)(2,1)S(1)}, u32[]{:S(2)}, u32[]{:S(2)}) async-start(bf16[16,128,256]{2,1,0:T(8,128)(2,1)} %bitcast.5), calls=%async_computation.1 | async-start | bytes 2097152 | tf_op jit(solution)/shard_map/all_to_all | solution.py:31
  61.3 1.8 broadcast_select_fusion
  64.7 13.3 %all-to-all-done.1 = bf16[16,128,256]{2,1,0:T(8,128)(2,1)S(1)} async-done(((bf16[16,128,256]{2,1,0:T(8,128)(2,1)}), bf16[16,128,256]{2,1,0:T(8,128)(2,1)S(1)}, u32[]{:S(2)}, u32[]{:S(2)}) %all-to-all-start.1) | async-done | bytes 1048608 | tf_op jit(solution)/shard_map/all_to_all | solution.py:31
  78.0 3.7 %all-to-all-start = ((bf16[16,128,512]{2,1,0:T(8,128)(2,1)}), bf16[16,128,512]{2,1,0:T(8,128)(2,1)S(1)}, u32[]{:S(2)}, u32[]{:S(2)}) async-start(bf16[16,128,512]{2,1,0:T(8,128)(2,1)} %bitcast.80), calls=%async_computation | async-start | bytes 4194304 | tf_op jit(solution)/shard_map/all_to_all | solution.py:31
  85.4 1.9 constant_dynamic-update-slice_fusion.4
  87.4 1.9 constant_dynamic-update-slice_fusion.3
  89.3 1.9 constant_dynamic-update-slice_fusion.2
  91.2 1.9 constant_dynamic-update-slice_fusion.1
  95.0 2.0 %copy.82.b_ref = bf16[128,2048]{1,0:T(8,128)(2,1)} copy(bf16[128,2048]{0,1:T(8,128)(2,1)} %get-tuple-element.16) | data formatting | bytes 1048576 | tf_op jit(solution)/shard_map/transpose | solution.py:69
  97.1 15.0 %all-to-all-done = bf16[16,128,512]{2,1,0:T(8,128)(2,1)S(1)} async-done(((bf16[16,128,512]{2,1,0:T(8,128)(2,1)}), bf16[16,128,512]{2,1,0:T(8,128)(2,1)S(1)}, u32[]{:S(2)}, u32[]{:S(2)}) %all-to-all-start) | async-done | bytes 2097184 | tf_op jit(solution)/shard_map/all_to_all | solution.py:31
  113.4 30.9 %shard_map.127 = (f32[2048,512]{1,0:T(8,128)}, f32[2048,1]{1,0:T(8,128)}) custom-call(bf16[2048,512]{1,0:T(8,128)(2,1)} %bitcast.76, bf16[128,2048]{1,0:T(8,128)(2,1)} %copy.82.b_ref, bf16[2048,128]{1,0:T(8,128)(2,1)} %get-tuple-element.15.c_ref, f32[16,128,8]{2,1,0:T(8,128)} %copy.83.lcc_ref, f32[16,8,128]{2,1,0:T(8,128)} %bitcast.84, ...), custom_call_target="tpu_custom_call" | custom-call | tf_op jit(solution)/shard_map/pallas_call | solution.py:106
  146.6 3.5 %all-to-all-start.3 = ((f32[16,1,2048]{2,1,0:T(1,128)}), f32[16,1,2048]{2,1,0:T(1,128)S(1)}, u32[]{:S(2)}, u32[]{:S(2)}) async-start(f32[16,1,2048]{2,1,0:T(1,128)} %broadcast_in_dim.13), calls=%async_computation.3 | async-start | bytes 262144 | tf_op jit(solution)/shard_map/all_to_all | solution.py:236
  150.8 7.3 %all-to-all-done.3 = f32[16,1,2048]{2,1,0:T(1,128)S(1)} async-done(((f32[16,1,2048]{2,1,0:T(1,128)}), f32[16,1,2048]{2,1,0:T(1,128)S(1)}, u32[]{:S(2)}, u32[]{:S(2)}) %all-to-all-start.3) | async-done | bytes 131104 | tf_op jit(solution)/shard_map/all_to_all | solution.py:236
  158.1 4.9 %add_convert_fusion.1 = bf16[2048,512]{1,0:T(8,128)(2,1)} fusion(f32[2048,512]{1,0:T(8,128)} %get-tuple-element.10, bf16[2048,512]{1,0:T(8,128)(2,1)} %bitcast.77, f32[512]{0:T(512)S(1)} %bitcast.107, f32[2048]{0:T(1024)S(1)} %add_rsqrt_fusion), kind=kLoop, calls=%fused_computation.2 | loop fusion | flops 5242880 | bytes 8398848 | tf_op jit(solution)/shard_map/convert_element_type | solution.py:243
  163.0 3.9 %all-to-all-start.4 = ((bf16[16,128,512]{2,1,0:T(8,128)(2,1)}), bf16[16,128,512]{2,1,0:T(8,128)(2,1)S(1)}, u32[]{:S(2)}, u32[]{:S(2)}) async-start(bf16[16,128,512]{2,1,0:T(8,128)(2,1)} %bitcast.81), calls=%async_computation.4 | async-start | bytes 4194304 | tf_op jit(solution)/shard_map/all_to_all | solution.py:38
  168.3 28.7 %shard_map.128 = bf16[128,8192]{1,0:T(8,128)(2,1)} custom-call(bf16[128,8192]{1,0:T(8,128)(2,1)} %bitcast.83, bf16[640,2048]{1,0:T(8,128)(2,1)} %constant_dynamic-update-slice_fusion.k_ref.v_ref, bf16[640,2048]{1,0:T(8,128)(2,1)} %constant_dynamic-update-slice_fusion.k_ref.v_ref, s32[128,1]{1,0:T(8,128)} %copy.88.iq_ref, s32[1,640]{1,0:T(1,128)} %reshape.154.ik_ref), custom_call_target="tpu_custom_call" | custom-call | tf_op jit(solution)/shard_map/pallas_call | solution.py:165
  (78 shorter events, 29.3 us)
Async XLA Ops:
  0.0 34.8 %copy-start = (f32[1,128]{1,0:T(1,128)S(1)}, f32[1,128]{1,0:T(1,128)}, u32[]{:S(2)}) copy-start(f32[1,128]{1,0:T(1,128)} %param.20) | copy-start | bytes 1540
  1.9 89.3 %collective-permute-start.3 = (bf16[128,2048]{1,0:T(8,128)(2,1)}, bf16[128,2048]{1,0:T(8,128)(2,1)}, u32[]{:S(2)}, u32[]{:S(2)}) collective-permute-start(bf16[128,2048]{1,0:T(8,128)(2,1)} %pad_maximum_fusion), channel_id=1, source_target_pairs={{0,1},{1,2},{2,3},{3,4},{4,5},{5,6},{6,7},{7,8},{8,9},{9,10},{10,1... | collective-permute-start | bytes 1572872 | tf_op jit(solution)/shard_map/ppermute | solution.py:24
  6.1 83.2 %collective-permute-start.2 = (bf16[128,2048]{1,0:T(8,128)(2,1)}, bf16[128,2048]{1,0:T(8,128)(2,1)}, u32[]{:S(2)}, u32[]{:S(2)}) collective-permute-start(bf16[128,2048]{1,0:T(8,128)(2,1)} %pad_maximum_fusion), channel_id=1, source_target_pairs={{0,2},{1,3},{2,4},{3,5},{4,6},{5,7},{6,8},{7,9},{8,10},{9,11},{10,... | collective-permute-start | bytes 1572872 | tf_op jit(solution)/shard_map/ppermute | solution.py:24
  10.7 76.7 %collective-permute-start.1 = (bf16[128,2048]{1,0:T(8,128)(2,1)}, bf16[128,2048]{1,0:T(8,128)(2,1)}, u32[]{:S(2)}, u32[]{:S(2)}) collective-permute-start(bf16[128,2048]{1,0:T(8,128)(2,1)} %pad_maximum_fusion), channel_id=1, source_target_pairs={{0,3},{1,4},{2,5},{3,6},{4,7},{5,8},{6,9},{7,10},{8,11},{9,12},{10... | collective-permute-start | bytes 1572872 | tf_op jit(solution)/shard_map/ppermute | solution.py:24
  15.1 70.4 %collective-permute-start = (bf16[128,2048]{1,0:T(8,128)(2,1)}, bf16[128,2048]{1,0:T(8,128)(2,1)}, u32[]{:S(2)}, u32[]{:S(2)}) collective-permute-start(bf16[128,2048]{1,0:T(8,128)(2,1)} %pad_maximum_fusion), channel_id=1, source_target_pairs={{0,4},{1,5},{2,6},{3,7},{4,8},{5,9},{6,10},{7,11},{8,12},{9,13},{1... | collective-permute-start | bytes 1572872 | tf_op jit(solution)/shard_map/ppermute | solution.py:24
  20.1 36.5 %all-to-all-start.2 = ((f32[16,128,8]{1,2,0:T(8,128)}), f32[16,128,8]{1,2,0:T(8,128)S(1)}, u32[]{:S(2)}, u32[]{:S(2)}) async-start(f32[16,128,8]{1,2,0:T(8,128)} %bitcast.9), calls=%async_computation.2 | async-start | bytes 131072 | tf_op jit(solution)/shard_map/all_to_all | solution.py:31
  23.6 37.7 %collective-permute-start.4 = (bf16[128,8192]{1,0:T(8,128)(2,1)}, bf16[128,8192]{1,0:T(8,128)(2,1)}, u32[]{:S(2)}, u32[]{:S(2)}) collective-permute-start(bf16[128,8192]{1,0:T(8,128)(2,1)} %bitcast.110), channel_id=1, source_target_pairs={{0,16},{16,32},{32,48},{48,64},{64,80},{80,96},{96,112},{1,17},{17... | collective-permute-start | bytes 6291464 | tf_op jit(solution)/shard_map/ppermute | solution.py:24
  30.4 2.9 %copy-start.7 = (s32[1,2048]{1,0:T(1,128)S(1)}, s32[1,2048]{1,0:T(1,128)}, u32[]{:S(2)}) copy-start(s32[1,2048]{1,0:T(1,128)} %param.25) | copy-start | bytes 24580
  31.0 3.7 %copy-start.9 = (f32[1,128]{1,0:T(1,128)S(1)}, f32[1,128]{1,0:T(1,128)}, u32[]{:S(2)}) copy-start(f32[1,128]{1,0:T(1,128)} %param.16) | copy-start | bytes 1540
  31.0 3.7 %copy-start.10 = (f32[1,128]{1,0:T(1,128)S(1)}, f32[1,128]{1,0:T(1,128)}, u32[]{:S(2)}) copy-start(f32[1,128]{1,0:T(1,128)} %param.17) | copy-start | bytes 1540
  33.3 28.0 %copy-start.3 = (bf16[128,8192]{1,0:T(8,128)(2,1)S(1)}, bf16[128,8192]{1,0:T(8,128)(2,1)}, u32[]{:S(2)}) copy-start(bf16[128,8192]{1,0:T(8,128)(2,1)} %param.14) | copy-start | bytes 6291460
  56.6 21.4 %all-to-all-start.1 = ((bf16[16,128,256]{2,1,0:T(8,128)(2,1)}), bf16[16,128,256]{2,1,0:T(8,128)(2,1)S(1)}, u32[]{:S(2)}, u32[]{:S(2)}) async-start(bf16[16,128,256]{2,1,0:T(8,128)(2,1)} %bitcast.5), calls=%async_computation.1 | async-start | bytes 2097152 | tf_op jit(solution)/shard_map/all_to_all | solution.py:31
  61.1 21.6 %copy-start.4 = (f32[16,128,8]{1,2,0:T(8,128)}, f32[16,128,8]{1,2,0:T(8,128)S(1)}, u32[]{:S(2)}) copy-start(f32[16,128,8]{1,2,0:T(8,128)S(1)} %get-tuple-element.14) | copy-start | bytes 196612
  78.0 34.0 %all-to-all-start = ((bf16[16,128,512]{2,1,0:T(8,128)(2,1)}), bf16[16,128,512]{2,1,0:T(8,128)(2,1)S(1)}, u32[]{:S(2)}, u32[]{:S(2)}) async-start(bf16[16,128,512]{2,1,0:T(8,128)(2,1)} %bitcast.80), calls=%async_computation | async-start | bytes 4194304 | tf_op jit(solution)/shard_map/all_to_all | solution.py:31
  84.1 9.0 %copy-start.5 = (bf16[1,128,1024]{2,1,0:T(8,128)(2,1)S(1)}, bf16[1,128,1024]{2,1,0:T(8,128)(2,1)}, u32[]{:S(2)}) copy-start(bf16[1,128,1024]{2,1,0:T(8,128)(2,1)} %param.24) | copy-start | bytes 786436
  85.4 7.7 %copy-start.6 = (bf16[1,128,1024]{2,1,0:T(8,128)(2,1)S(1)}, bf16[1,128,1024]{2,1,0:T(8,128)(2,1)}, u32[]{:S(2)}) copy-start(bf16[1,128,1024]{2,1,0:T(8,128)(2,1)} %param.23) | copy-start | bytes 786436
  112.0 1.3 copy-start.1
  146.6 11.5 %all-to-all-start.3 = ((f32[16,1,2048]{2,1,0:T(1,128)}), f32[16,1,2048]{2,1,0:T(1,128)S(1)}, u32[]{:S(2)}, u32[]{:S(2)}) async-start(f32[16,1,2048]{2,1,0:T(1,128)} %broadcast_in_dim.13), calls=%async_computation.3 | async-start | bytes 262144 | tf_op jit(solution)/shard_map/all_to_all | solution.py:236
  163.0 3.9 %copy-start.8 = (s32[1,2048]{1,0:T(1,128)S(1)}, s32[1,2048]{1,0:T(1,128)}, u32[]{:S(2)}) copy-start(s32[1,2048]{1,0:T(1,128)} %param.25) | copy-start | bytes 24580
  163.0 34.0 %all-to-all-start.4 = ((bf16[16,128,512]{2,1,0:T(8,128)(2,1)}), bf16[16,128,512]{2,1,0:T(8,128)(2,1)S(1)}, u32[]{:S(2)}, u32[]{:S(2)}) async-start(bf16[16,128,512]{2,1,0:T(8,128)(2,1)} %bitcast.81), calls=%async_computation.4 | async-start | bytes 4194304 | tf_op jit(solution)/shard_map/all_to_all | solution.py:38
  197.6 1.6 copy-start.2

commit v12 on v11

--- a/solution.py
+++ b/solution.py
@@ -208,13 +208,15 @@
     bc = jnp.stack(
         [b_in[0].reshape(tok_rows, GROUPS, STATE), c_in[0].reshape(tok_rows, GROUPS, STATE)], axis=2
     )
-    bc_h = to_heads(jnp.repeat(bc, rep, axis=1).reshape(tok_rows, nctx * 2 * STATE), nctx)
-    b_g, c_g = bc_h[:, :STATE], bc_h[:, STATE:]
+    bc_rows = jnp.repeat(bc, rep, axis=1).reshape(tok_rows, nctx, 2 * STATE)
     dt_h = to_heads(dt_raw[0], nctx)
 
     handed = shifted(previous[0], "section", 1)
     stream = jnp.where(lax.axis_index("section") == 0, fresh, handed)
-    x_h = to_heads(stream, nctx)
+    joined = jnp.concatenate([stream.reshape(tok_rows, nctx, part), bc_rows], axis=2)
+    moved = to_heads(joined.reshape(tok_rows, nctx * (part + 2 * STATE)), nctx)
+    x_h = moved[:, :part]
+    b_g, c_g = moved[:, part:part + STATE], moved[:, part + STATE:]
 
     halo = -(-MOST_DOC // tok_rows)
     kv_row = jnp.concatenate([keys[0], values[0]], axis=1)

time: 203 us -> 212 us (1.044)
  waiting for transfers between devices: 56.7 us -> 69 us
  starting transfers between devices: 36.8 us -> 34.3 us
    all_to_all x3 -> x2, waiting for transfers between devices: 49.5 us -> 61.7 us  [to_heads(): moved = lax.all_to_all(lead, 'ctx', split_axis=0, concat_axis=0, tiled=True)]
    all_to_all x3 -> x2, starting transfers between devices: 10.9 us -> 7.22 us  [to_heads(): moved = lax.all_to_all(lead, 'ctx', split_axis=0, concat_axis=0, tiled=True)]
    unnamed x32 -> x30, local copies, waits for them, and re-layouts: 13.1 us -> 12.5 us
  transfers between devices with their start and end apart: 10 -> 9, of which waited for: 4 -> 3; matrix products, arithmetic and copies ran while one was open for 16% -> 15% of each run, Pallas kernels for 14% -> 14%
where the time goes in v12:
time: 212 us; the launch traced here: 210 us
  waiting for transfers between devices  69 us (33%)
  Pallas kernels  59.7 us (28%)
  starting transfers between devices  34.3 us (16%)
  local copies, waits for them, and re-layouts  29.5 us (14%)
  other arithmetic  17.1 us (8%)
    all_to_all x2, waiting for transfers between devices, to_heads(): moved = lax.all_to_all(lead, 'ctx', split_axis=0, concat_axis=0, tiled=True)  61.7 us
    pallas_call x1, Pallas kernels, mixer_heads(): pl.pallas_call(kernel, grid=(nblk,), in_specs=[pl.BlockSpec((BLOCK, x_wid...  31 us
    pallas_call x1, Pallas kernels, attend_rows(): pl.pallas_call(kernel, grid=(kv_heads,), in_specs=[pl.BlockSpec((tok_rows...  28.7 us
    ppermute x5, starting transfers between devices, shifted(): return lax.ppermute(value, axis, pairs)  18.7 us
    unnamed x30, local copies, waits for them, and re-layouts  12.5 us
    all_to_all x1, waiting for transfers between devices, body(): lax.all_to_all(jnp.broadcast_to(sq_part[:, 0][None], (nctx, total)), 'ctx...  7.3 us
    all_to_all x2, starting transfers between devices, to_heads(): moved = lax.all_to_all(lead, 'ctx', split_axis=0, concat_axis=0, tiled=True)  7.22 us
    all_to_all x1, starting transfers between devices, body(): lax.all_to_all(jnp.broadcast_to(sq_part[:, 0][None], (nctx, total)), 'ctx...  4.47 us
  transfers between devices with their start and end apart: 9, of which 3 were waited for; matrix products, arithmetic and copies ran while one was open for 15% of the time, Pallas kernels for 14%

profile of v12, /device:TPU:32, one launch (start us, length us, event | category | flops | bytes accessed | tf_op | source)
XLA Modules:
  0.0 209.9 jit_solution(10850141975405855390)
XLA Ops:
  0.0 2.0 collective-permute-start.4
  2.1 1.9 pad_maximum_fusion
  3.9 4.2 %collective-permute-start.3 = (bf16[128,2048]{1,0:T(8,128)(2,1)}, bf16[128,2048]{1,0:T(8,128)(2,1)}, u32[]{:S(2)}, u32[]{:S(2)}) collective-permute-start(bf16[128,2048]{1,0:T(8,128)(2,1)} %pad_maximum_fusion), channel_id=1, source_target_pairs={{0,1},{1,2},{2,3},{3,4},{4,5},{5,6},{6,7},{7,8},{8,9},{9,10},{10,1... | collective-permute-start | bytes 1572872 | tf_op jit(solution)/shard_map/ppermute | solution.py:24
  8.1 4.6 %collective-permute-start.2 = (bf16[128,2048]{1,0:T(8,128)(2,1)}, bf16[128,2048]{1,0:T(8,128)(2,1)}, u32[]{:S(2)}, u32[]{:S(2)}) collective-permute-start(bf16[128,2048]{1,0:T(8,128)(2,1)} %pad_maximum_fusion), channel_id=1, source_target_pairs={{0,2},{1,3},{2,4},{3,5},{4,6},{5,7},{6,8},{7,9},{8,10},{9,11},{10,... | collective-permute-start | bytes 1572872 | tf_op jit(solution)/shard_map/ppermute | solution.py:24
  12.7 4.4 %collective-permute-start.1 = (bf16[128,2048]{1,0:T(8,128)(2,1)}, bf16[128,2048]{1,0:T(8,128)(2,1)}, u32[]{:S(2)}, u32[]{:S(2)}) collective-permute-start(bf16[128,2048]{1,0:T(8,128)(2,1)} %pad_maximum_fusion), channel_id=1, source_target_pairs={{0,3},{1,4},{2,5},{3,6},{4,7},{5,8},{6,9},{7,10},{8,11},{9,12},{10... | collective-permute-start | bytes 1572872 | tf_op jit(solution)/shard_map/ppermute | solution.py:24
  17.1 3.5 %collective-permute-start = (bf16[128,2048]{1,0:T(8,128)(2,1)}, bf16[128,2048]{1,0:T(8,128)(2,1)}, u32[]{:S(2)}, u32[]{:S(2)}) collective-permute-start(bf16[128,2048]{1,0:T(8,128)(2,1)} %pad_maximum_fusion), channel_id=1, source_target_pairs={{0,4},{1,5},{2,6},{3,7},{4,8},{5,9},{6,10},{7,11},{8,12},{9,13},{1... | collective-permute-start | bytes 1572872 | tf_op jit(solution)/shard_map/ppermute | solution.py:24
  22.2 3.5 %all-to-all-start.1 = ((f32[16,128,8]{1,2,0:T(8,128)}), f32[16,128,8]{1,2,0:T(8,128)S(1)}, u32[]{:S(2)}, u32[]{:S(2)}) async-start(f32[16,128,8]{1,2,0:T(8,128)} %bitcast.7), calls=%async_computation.1 | async-start | bytes 131072 | tf_op jit(solution)/shard_map/all_to_all | solution.py:31
  34.0 25.7 %all-to-all-done.1 = f32[16,128,8]{1,2,0:T(8,128)S(1)} async-done(((f32[16,128,8]{1,2,0:T(8,128)}), f32[16,128,8]{1,2,0:T(8,128)S(1)}, u32[]{:S(2)}, u32[]{:S(2)}) %all-to-all-start.1) | async-done | bytes 65568 | tf_op jit(solution)/shard_map/all_to_all | solution.py:31
  60.0 1.8 broadcast_select_fusion
  62.0 1.9 maximum_bitcast_fusion
  63.9 3.7 %all-to-all-start = ((bf16[16,128,768]{2,1,0:T(8,128)(2,1)}), bf16[16,128,768]{2,1,0:T(8,128)(2,1)S(1)}, u32[]{:S(2)}, u32[]{:S(2)}) async-start(bf16[16,128,768]{2,1,0:T(8,128)(2,1)} %maximum_bitcast_fusion), calls=%async_computation | async-start | bytes 6291456 | tf_op jit(solution)/shard_map/all_to_all | solution.py:31
  72.2 1.9 constant_dynamic-update-slice_fusion.4
  74.1 1.9 constant_dynamic-update-slice_fusion.3
  76.0 1.9 constant_dynamic-update-slice_fusion.2
  77.9 1.9 constant_dynamic-update-slice_fusion.1
  80.6 35.9 %all-to-all-done = bf16[16,128,768]{2,1,0:T(8,128)(2,1)S(1)} async-done(((bf16[16,128,768]{2,1,0:T(8,128)(2,1)}), bf16[16,128,768]{2,1,0:T(8,128)(2,1)S(1)}, u32[]{:S(2)}, u32[]{:S(2)}) %all-to-all-start) | async-done | bytes 3145760 | tf_op jit(solution)/shard_map/all_to_all | solution.py:31
  119.1 2.0 copy.82.b_ref
  121.8 31.0 %shard_map.127 = (f32[2048,512]{1,0:T(8,128)}, f32[2048,1]{1,0:T(8,128)}) custom-call(bf16[2048,512]{1,0:T(8,128)(2,1)} %slice.66.x_ref, bf16[128,2048]{1,0:T(8,128)(2,1)} %copy.82.b_ref, bf16[2048,128]{1,0:T(8,128)(2,1)} %get-tuple-element.15.c_ref, f32[16,128,8]{2,1,0:T(8,128)} %copy.83.lcc_ref, f32[16,8,128]{2,1,0:T(8,128)} %bitcast.80, ...), custom_call_target="tpu_custom_call" | custom-call | tf_op jit(solution)/shard_map/pallas_call | solution.py:106
  155.2 4.5 %all-to-all-start.2 = ((f32[16,1,2048]{2,1,0:T(1,128)}), f32[16,1,2048]{2,1,0:T(1,128)S(1)}, u32[]{:S(2)}, u32[]{:S(2)}) async-start(f32[16,1,2048]{2,1,0:T(1,128)} %broadcast_in_dim.13), calls=%async_computation.2 | async-start | bytes 262144 | tf_op jit(solution)/shard_map/all_to_all | solution.py:238
  160.4 7.3 %all-to-all-done.2 = f32[16,1,2048]{2,1,0:T(1,128)S(1)} async-done(((f32[16,1,2048]{2,1,0:T(1,128)}), f32[16,1,2048]{2,1,0:T(1,128)S(1)}, u32[]{:S(2)}, u32[]{:S(2)}) %all-to-all-start.2) | async-done | bytes 131104 | tf_op jit(solution)/shard_map/all_to_all | solution.py:238
  167.8 4.2 %add_convert_fusion.1 = bf16[2048,512]{1,0:T(8,128)(2,1)} fusion(f32[2048,512]{1,0:T(8,128)} %get-tuple-element.10, bf16[2048,512]{1,0:T(8,128)(2,1)S(1)} %copy-done.1, f32[512]{0:T(512)S(1)} %bitcast.103, f32[2048]{0:T(1024)S(1)} %add_rsqrt_fusion), kind=kLoop, calls=%fused_computation.2 | loop fusion | flops 5242880 | bytes 8398848 | tf_op jit(solution)/shard_map/convert_element_type | solution.py:245
  172.0 3.9 %all-to-all-start.3 = ((bf16[16,128,512]{2,1,0:T(8,128)(2,1)}), bf16[16,128,512]{2,1,0:T(8,128)(2,1)S(1)}, u32[]{:S(2)}, u32[]{:S(2)}) async-start(bf16[16,128,512]{2,1,0:T(8,128)(2,1)} %bitcast.78), calls=%async_computation.3 | async-start | bytes 4194304 | tf_op jit(solution)/shard_map/all_to_all | solution.py:38
  177.2 28.7 %shard_map.128 = bf16[128,8192]{1,0:T(8,128)(2,1)} custom-call(bf16[128,8192]{1,0:T(8,128)(2,1)} %bitcast.79, bf16[640,2048]{1,0:T(8,128)(2,1)} %constant_dynamic-update-slice_fusion.k_ref.v_ref, bf16[640,2048]{1,0:T(8,128)(2,1)} %constant_dynamic-update-slice_fusion.k_ref.v_ref, s32[128,1]{1,0:T(8,128)} %copy.88.iq_ref, s32[1,640]{1,0:T(1,128)} %reshape.150.ik_ref), custom_call_target="tpu_custom_call" | custom-call | tf_op jit(solution)/shard_map/pallas_call | solution.py:165
  208.1 1.8 fusion
  (76 shorter events, 25.4 us)
Async XLA Ops:
  0.0 33.4 %copy-start = (f32[1,128]{1,0:T(1,128)S(1)}, f32[1,128]{1,0:T(1,128)}, u32[]{:S(2)}) copy-start(f32[1,128]{1,0:T(1,128)} %param.20) | copy-start | bytes 1540
  0.0 60.0 %collective-permute-start.4 = (bf16[128,8192]{1,0:T(8,128)(2,1)}, bf16[128,8192]{1,0:T(8,128)(2,1)}, u32[]{:S(2)}, u32[]{:S(2)}) collective-permute-start(bf16[128,8192]{1,0:T(8,128)(2,1)} %bitcast.106), channel_id=1, source_target_pairs={{0,16},{16,32},{32,48},{48,64},{64,80},{80,96},{96,112},{1,17},{17... | collective-permute-start | bytes 6291464 | tf_op jit(solution)/shard_map/ppermute | solution.py:24
  3.9 74.0 %collective-permute-start.3 = (bf16[128,2048]{1,0:T(8,128)(2,1)}, bf16[128,2048]{1,0:T(8,128)(2,1)}, u32[]{:S(2)}, u32[]{:S(2)}) collective-permute-start(bf16[128,2048]{1,0:T(8,128)(2,1)} %pad_maximum_fusion), channel_id=1, source_target_pairs={{0,1},{1,2},{2,3},{3,4},{4,5},{5,6},{6,7},{7,8},{8,9},{9,10},{10,1... | collective-permute-start | bytes 1572872 | tf_op jit(solution)/shard_map/ppermute | solution.py:24
  8.1 67.9 %collective-permute-start.2 = (bf16[128,2048]{1,0:T(8,128)(2,1)}, bf16[128,2048]{1,0:T(8,128)(2,1)}, u32[]{:S(2)}, u32[]{:S(2)}) collective-permute-start(bf16[128,2048]{1,0:T(8,128)(2,1)} %pad_maximum_fusion), channel_id=1, source_target_pairs={{0,2},{1,3},{2,4},{3,5},{4,6},{5,7},{6,8},{7,9},{8,10},{9,11},{10,... | collective-permute-start | bytes 1572872 | tf_op jit(solution)/shard_map/ppermute | solution.py:24
  12.7 61.4 %collective-permute-start.1 = (bf16[128,2048]{1,0:T(8,128)(2,1)}, bf16[128,2048]{1,0:T(8,128)(2,1)}, u32[]{:S(2)}, u32[]{:S(2)}) collective-permute-start(bf16[128,2048]{1,0:T(8,128)(2,1)} %pad_maximum_fusion), channel_id=1, source_target_pairs={{0,3},{1,4},{2,5},{3,6},{4,7},{5,8},{6,9},{7,10},{8,11},{9,12},{10... | collective-permute-start | bytes 1572872 | tf_op jit(solution)/shard_map/ppermute | solution.py:24
  17.1 55.0 %collective-permute-start = (bf16[128,2048]{1,0:T(8,128)(2,1)}, bf16[128,2048]{1,0:T(8,128)(2,1)}, u32[]{:S(2)}, u32[]{:S(2)}) collective-permute-start(bf16[128,2048]{1,0:T(8,128)(2,1)} %pad_maximum_fusion), channel_id=1, source_target_pairs={{0,4},{1,5},{2,6},{3,7},{4,8},{5,9},{6,10},{7,11},{8,12},{9,13},{1... | collective-permute-start | bytes 1572872 | tf_op jit(solution)/shard_map/ppermute | solution.py:24
  22.2 37.5 %all-to-all-start.1 = ((f32[16,128,8]{1,2,0:T(8,128)}), f32[16,128,8]{1,2,0:T(8,128)S(1)}, u32[]{:S(2)}, u32[]{:S(2)}) async-start(f32[16,128,8]{1,2,0:T(8,128)} %bitcast.7), calls=%async_computation.1 | async-start | bytes 131072 | tf_op jit(solution)/shard_map/all_to_all | solution.py:31
  29.6 2.1 %copy-start.6 = (s32[1,2048]{1,0:T(1,128)S(1)}, s32[1,2048]{1,0:T(1,128)}, u32[]{:S(2)}) copy-start(s32[1,2048]{1,0:T(1,128)} %param.25) | copy-start | bytes 24580
  30.2 3.0 %copy-start.8 = (f32[1,128]{1,0:T(1,128)S(1)}, f32[1,128]{1,0:T(1,128)}, u32[]{:S(2)}) copy-start(f32[1,128]{1,0:T(1,128)} %param.16) | copy-start | bytes 1540
  30.2 3.0 %copy-start.9 = (f32[1,128]{1,0:T(1,128)S(1)}, f32[1,128]{1,0:T(1,128)}, u32[]{:S(2)}) copy-start(f32[1,128]{1,0:T(1,128)} %param.17) | copy-start | bytes 1540
  63.9 52.7 %all-to-all-start = ((bf16[16,128,768]{2,1,0:T(8,128)(2,1)}), bf16[16,128,768]{2,1,0:T(8,128)(2,1)S(1)}, u32[]{:S(2)}, u32[]{:S(2)}) async-start(bf16[16,128,768]{2,1,0:T(8,128)(2,1)} %maximum_bitcast_fusion), calls=%async_computation | async-start | bytes 6291456 | tf_op jit(solution)/shard_map/all_to_all | solution.py:31
  68.2 9.7 %copy-start.3 = (f32[16,128,8]{1,2,0:T(8,128)}, f32[16,128,8]{1,2,0:T(8,128)S(1)}, u32[]{:S(2)}) copy-start(f32[16,128,8]{1,2,0:T(8,128)S(1)} %get-tuple-element.14) | copy-start | bytes 196612
  70.9 8.9 %copy-start.4 = (bf16[1,128,1024]{2,1,0:T(8,128)(2,1)S(1)}, bf16[1,128,1024]{2,1,0:T(8,128)(2,1)}, u32[]{:S(2)}) copy-start(bf16[1,128,1024]{2,1,0:T(8,128)(2,1)} %param.24) | copy-start | bytes 786436
  72.2 7.6 %copy-start.5 = (bf16[1,128,1024]{2,1,0:T(8,128)(2,1)S(1)}, bf16[1,128,1024]{2,1,0:T(8,128)(2,1)}, u32[]{:S(2)}) copy-start(bf16[1,128,1024]{2,1,0:T(8,128)(2,1)} %param.23) | copy-start | bytes 786436
  121.8 45.9 %copy-start.1 = (bf16[2048,512]{1,0:T(8,128)(2,1)S(1)}, bf16[2048,512]{1,0:T(8,128)(2,1)}, u32[]{:S(2)}) copy-start(bf16[2048,512]{1,0:T(8,128)(2,1)} %slice.66.x_ref) | copy-start | bytes 6291460
  155.2 12.5 %all-to-all-start.2 = ((f32[16,1,2048]{2,1,0:T(1,128)}), f32[16,1,2048]{2,1,0:T(1,128)S(1)}, u32[]{:S(2)}, u32[]{:S(2)}) async-start(f32[16,1,2048]{2,1,0:T(1,128)} %broadcast_in_dim.13), calls=%async_computation.2 | async-start | bytes 262144 | tf_op jit(solution)/shard_map/all_to_all | solution.py:238
  172.0 3.9 %copy-start.7 = (s32[1,2048]{1,0:T(1,128)S(1)}, s32[1,2048]{1,0:T(1,128)}, u32[]{:S(2)}) copy-start(s32[1,2048]{1,0:T(1,128)} %param.25) | copy-start | bytes 24580
  172.0 34.0 %all-to-all-start.3 = ((bf16[16,128,512]{2,1,0:T(8,128)(2,1)}), bf16[16,128,512]{2,1,0:T(8,128)(2,1)S(1)}, u32[]{:S(2)}, u32[]{:S(2)}) async-start(bf16[16,128,512]{2,1,0:T(8,128)(2,1)} %bitcast.78), calls=%async_computation.3 | async-start | bytes 4194304 | tf_op jit(solution)/shard_map/all_to_all | solution.py:38
  206.5 1.6 copy-start.2

commit v13 on v11

--- a/solution.py
+++ b/solution.py
@@ -159,7 +159,8 @@
             logits = jnp.where(allowed, logits, -jnp.inf)
             row_max = jnp.max(logits, axis=1, keepdims=True)
             exp_terms = jnp.exp(logits - row_max)
-            probs = (exp_terms / jnp.sum(exp_terms, axis=1, keepdims=True)).astype(jnp.bfloat16)
+            inv_sum = 1.0 / jnp.sum(exp_terms, axis=1, keepdims=True)
+            probs = (exp_terms * inv_sum).astype(jnp.bfloat16)
             o_ref[:, cols] = jnp.dot(probs, vb, preferred_element_type=jnp.float32).astype(o_ref.dtype)
 
     return pl.pallas_call(

time: 203 us -> 203 us (level)
  no operation moved by 1% of the time
where the time goes in v13:
time: 203 us; the launch traced here: 201 us
  Pallas kernels  59.6 us (29%)
  waiting for transfers between devices  56.7 us (28%)
  starting transfers between devices  36.8 us (18%)
  local copies, waits for them, and re-layouts  30.8 us (15%)
  other arithmetic  16.7 us (8%)
    all_to_all x3, waiting for transfers between devices, to_heads(): moved = lax.all_to_all(lead, 'ctx', split_axis=0, concat_axis=0, tiled=True)  49.5 us
    pallas_call x1, Pallas kernels, mixer_heads(): pl.pallas_call(kernel, grid=(nblk,), in_specs=[pl.BlockSpec((BLOCK, x_wid...  30.9 us
    pallas_call x1, Pallas kernels, attend_rows(): pl.pallas_call(kernel, grid=(kv_heads,), in_specs=[pl.BlockSpec((tok_rows...  28.7 us
    ppermute x5, starting transfers between devices, shifted(): return lax.ppermute(value, axis, pairs)  18.6 us
    unnamed x32, local copies, waits for them, and re-layouts  13.1 us
    all_to_all x3, starting transfers between devices, to_heads(): moved = lax.all_to_all(lead, 'ctx', split_axis=0, concat_axis=0, tiled=True)  10.9 us
    all_to_all x1, waiting for transfers between devices, body(): lax.all_to_all(jnp.broadcast_to(sq_part[:, 0][None], (nctx, total)), 'ctx...  7.26 us
    convert_element_type x1, other arithmetic, body(): mixed = (x_h.astype(jnp.float32) + mixer_out * inv_rms * gain_h.astype(jn...  4.87 us
  transfers between devices with their start and end apart: 10, of which 4 were waited for; matrix products, arithmetic and copies ran while one was open for 16% of the time, Pallas kernels for 14%

profile of v13, /device:TPU:32, one launch (start us, length us, event | category | flops | bytes accessed | tf_op | source)
XLA Modules:
  0.0 201.0 jit_solution(1962175973834510149)
XLA Ops:
  0.0 1.9 pad_maximum_fusion
  1.9 4.2 %collective-permute-start.3 = (bf16[128,2048]{1,0:T(8,128)(2,1)}, bf16[128,2048]{1,0:T(8,128)(2,1)}, u32[]{:S(2)}, u32[]{:S(2)}) collective-permute-start(bf16[128,2048]{1,0:T(8,128)(2,1)} %pad_maximum_fusion), channel_id=1, source_target_pairs={{0,1},{1,2},{2,3},{3,4},{4,5},{5,6},{6,7},{7,8},{8,9},{9,10},{10,1... | collective-permute-start | bytes 1572872 | tf_op jit(solution)/shard_map/ppermute | solution.py:24
  6.1 4.7 %collective-permute-start.2 = (bf16[128,2048]{1,0:T(8,128)(2,1)}, bf16[128,2048]{1,0:T(8,128)(2,1)}, u32[]{:S(2)}, u32[]{:S(2)}) collective-permute-start(bf16[128,2048]{1,0:T(8,128)(2,1)} %pad_maximum_fusion), channel_id=1, source_target_pairs={{0,2},{1,3},{2,4},{3,5},{4,6},{5,7},{6,8},{7,9},{8,10},{9,11},{10,... | collective-permute-start | bytes 1572872 | tf_op jit(solution)/shard_map/ppermute | solution.py:24
  10.7 4.4 %collective-permute-start.1 = (bf16[128,2048]{1,0:T(8,128)(2,1)}, bf16[128,2048]{1,0:T(8,128)(2,1)}, u32[]{:S(2)}, u32[]{:S(2)}) collective-permute-start(bf16[128,2048]{1,0:T(8,128)(2,1)} %pad_maximum_fusion), channel_id=1, source_target_pairs={{0,3},{1,4},{2,5},{3,6},{4,7},{5,8},{6,9},{7,10},{8,11},{9,12},{10... | collective-permute-start | bytes 1572872 | tf_op jit(solution)/shard_map/ppermute | solution.py:24
  15.1 3.5 %collective-permute-start = (bf16[128,2048]{1,0:T(8,128)(2,1)}, bf16[128,2048]{1,0:T(8,128)(2,1)}, u32[]{:S(2)}, u32[]{:S(2)}) collective-permute-start(bf16[128,2048]{1,0:T(8,128)(2,1)} %pad_maximum_fusion), channel_id=1, source_target_pairs={{0,4},{1,5},{2,6},{3,7},{4,8},{5,9},{6,10},{7,11},{8,12},{9,13},{1... | collective-permute-start | bytes 1572872 | tf_op jit(solution)/shard_map/ppermute | solution.py:24
  20.1 3.5 %all-to-all-start.2 = ((f32[16,128,8]{1,2,0:T(8,128)}), f32[16,128,8]{1,2,0:T(8,128)S(1)}, u32[]{:S(2)}, u32[]{:S(2)}) async-start(f32[16,128,8]{1,2,0:T(8,128)} %bitcast.9), calls=%async_computation.2 | async-start | bytes 131072 | tf_op jit(solution)/shard_map/all_to_all | solution.py:31
  23.6 1.9 collective-permute-start.4
  35.4 21.2 %all-to-all-done.2 = f32[16,128,8]{1,2,0:T(8,128)S(1)} async-done(((f32[16,128,8]{1,2,0:T(8,128)}), f32[16,128,8]{1,2,0:T(8,128)S(1)}, u32[]{:S(2)}, u32[]{:S(2)}) %all-to-all-start.2) | async-done | bytes 65568 | tf_op jit(solution)/shard_map/all_to_all | solution.py:31
  56.6 3.7 %all-to-all-start.1 = ((bf16[16,128,256]{2,1,0:T(8,128)(2,1)}), bf16[16,128,256]{2,1,0:T(8,128)(2,1)S(1)}, u32[]{:S(2)}, u32[]{:S(2)}) async-start(bf16[16,128,256]{2,1,0:T(8,128)(2,1)} %bitcast.5), calls=%async_computation.1 | async-start | bytes 2097152 | tf_op jit(solution)/shard_map/all_to_all | solution.py:31
  61.3 1.8 broadcast_select_fusion
  64.7 13.3 %all-to-all-done.1 = bf16[16,128,256]{2,1,0:T(8,128)(2,1)S(1)} async-done(((bf16[16,128,256]{2,1,0:T(8,128)(2,1)}), bf16[16,128,256]{2,1,0:T(8,128)(2,1)S(1)}, u32[]{:S(2)}, u32[]{:S(2)}) %all-to-all-start.1) | async-done | bytes 1048608 | tf_op jit(solution)/shard_map/all_to_all | solution.py:31
  78.0 3.7 %all-to-all-start = ((bf16[16,128,512]{2,1,0:T(8,128)(2,1)}), bf16[16,128,512]{2,1,0:T(8,128)(2,1)S(1)}, u32[]{:S(2)}, u32[]{:S(2)}) async-start(bf16[16,128,512]{2,1,0:T(8,128)(2,1)} %bitcast.80), calls=%async_computation | async-start | bytes 4194304 | tf_op jit(solution)/shard_map/all_to_all | solution.py:31
  85.4 1.9 constant_dynamic-update-slice_fusion.4
  87.4 1.9 constant_dynamic-update-slice_fusion.3
  89.3 1.9 constant_dynamic-update-slice_fusion.2
  91.2 1.9 constant_dynamic-update-slice_fusion.1
  95.0 2.0 %copy.82.b_ref = bf16[128,2048]{1,0:T(8,128)(2,1)} copy(bf16[128,2048]{0,1:T(8,128)(2,1)} %get-tuple-element.16) | data formatting | bytes 1048576 | tf_op jit(solution)/shard_map/transpose | solution.py:69
  97.1 15.0 %all-to-all-done = bf16[16,128,512]{2,1,0:T(8,128)(2,1)S(1)} async-done(((bf16[16,128,512]{2,1,0:T(8,128)(2,1)}), bf16[16,128,512]{2,1,0:T(8,128)(2,1)S(1)}, u32[]{:S(2)}, u32[]{:S(2)}) %all-to-all-start) | async-done | bytes 2097184 | tf_op jit(solution)/shard_map/all_to_all | solution.py:31
  113.4 30.9 %shard_map.127 = (f32[2048,512]{1,0:T(8,128)}, f32[2048,1]{1,0:T(8,128)}) custom-call(bf16[2048,512]{1,0:T(8,128)(2,1)} %bitcast.76, bf16[128,2048]{1,0:T(8,128)(2,1)} %copy.82.b_ref, bf16[2048,128]{1,0:T(8,128)(2,1)} %get-tuple-element.15.c_ref, f32[16,128,8]{2,1,0:T(8,128)} %copy.83.lcc_ref, f32[16,8,128]{2,1,0:T(8,128)} %bitcast.84, ...), custom_call_target="tpu_custom_call" | custom-call | tf_op jit(solution)/shard_map/pallas_call | solution.py:106
  146.6 3.5 %all-to-all-start.3 = ((f32[16,1,2048]{2,1,0:T(1,128)}), f32[16,1,2048]{2,1,0:T(1,128)S(1)}, u32[]{:S(2)}, u32[]{:S(2)}) async-start(f32[16,1,2048]{2,1,0:T(1,128)} %broadcast_in_dim.13), calls=%async_computation.3 | async-start | bytes 262144 | tf_op jit(solution)/shard_map/all_to_all | solution.py:237
  150.8 7.3 %all-to-all-done.3 = f32[16,1,2048]{2,1,0:T(1,128)S(1)} async-done(((f32[16,1,2048]{2,1,0:T(1,128)}), f32[16,1,2048]{2,1,0:T(1,128)S(1)}, u32[]{:S(2)}, u32[]{:S(2)}) %all-to-all-start.3) | async-done | bytes 131104 | tf_op jit(solution)/shard_map/all_to_all | solution.py:237
  158.1 4.9 %add_convert_fusion.1 = bf16[2048,512]{1,0:T(8,128)(2,1)} fusion(f32[2048,512]{1,0:T(8,128)} %get-tuple-element.10, bf16[2048,512]{1,0:T(8,128)(2,1)} %bitcast.77, f32[512]{0:T(512)S(1)} %bitcast.107, f32[2048]{0:T(1024)S(1)} %add_rsqrt_fusion), kind=kLoop, calls=%fused_computation.2 | loop fusion | flops 5242880 | bytes 8398848 | tf_op jit(solution)/shard_map/convert_element_type | solution.py:244
  163.0 3.9 %all-to-all-start.4 = ((bf16[16,128,512]{2,1,0:T(8,128)(2,1)}), bf16[16,128,512]{2,1,0:T(8,128)(2,1)S(1)}, u32[]{:S(2)}, u32[]{:S(2)}) async-start(bf16[16,128,512]{2,1,0:T(8,128)(2,1)} %bitcast.81), calls=%async_computation.4 | async-start | bytes 4194304 | tf_op jit(solution)/shard_map/all_to_all | solution.py:38
  168.3 28.7 %shard_map.128 = bf16[128,8192]{1,0:T(8,128)(2,1)} custom-call(bf16[128,8192]{1,0:T(8,128)(2,1)} %bitcast.83, bf16[640,2048]{1,0:T(8,128)(2,1)} %constant_dynamic-update-slice_fusion.k_ref.v_ref, bf16[640,2048]{1,0:T(8,128)(2,1)} %constant_dynamic-update-slice_fusion.k_ref.v_ref, s32[128,1]{1,0:T(8,128)} %copy.88.iq_ref, s32[1,640]{1,0:T(1,128)} %reshape.154.ik_ref), custom_call_target="tpu_custom_call" | custom-call | tf_op jit(solution)/shard_map/pallas_call | solution.py:166
  (78 shorter events, 29.3 us)
Async XLA Ops:
  0.0 34.8 %copy-start = (f32[1,128]{1,0:T(1,128)S(1)}, f32[1,128]{1,0:T(1,128)}, u32[]{:S(2)}) copy-start(f32[1,128]{1,0:T(1,128)} %param.20) | copy-start | bytes 1540
  1.9 89.3 %collective-permute-start.3 = (bf16[128,2048]{1,0:T(8,128)(2,1)}, bf16[128,2048]{1,0:T(8,128)(2,1)}, u32[]{:S(2)}, u32[]{:S(2)}) collective-permute-start(bf16[128,2048]{1,0:T(8,128)(2,1)} %pad_maximum_fusion), channel_id=1, source_target_pairs={{0,1},{1,2},{2,3},{3,4},{4,5},{5,6},{6,7},{7,8},{8,9},{9,10},{10,1... | collective-permute-start | bytes 1572872 | tf_op jit(solution)/shard_map/ppermute | solution.py:24
  6.1 83.2 %collective-permute-start.2 = (bf16[128,2048]{1,0:T(8,128)(2,1)}, bf16[128,2048]{1,0:T(8,128)(2,1)}, u32[]{:S(2)}, u32[]{:S(2)}) collective-permute-start(bf16[128,2048]{1,0:T(8,128)(2,1)} %pad_maximum_fusion), channel_id=1, source_target_pairs={{0,2},{1,3},{2,4},{3,5},{4,6},{5,7},{6,8},{7,9},{8,10},{9,11},{10,... | collective-permute-start | bytes 1572872 | tf_op jit(solution)/shard_map/ppermute | solution.py:24
  10.7 76.7 %collective-permute-start.1 = (bf16[128,2048]{1,0:T(8,128)(2,1)}, bf16[128,2048]{1,0:T(8,128)(2,1)}, u32[]{:S(2)}, u32[]{:S(2)}) collective-permute-start(bf16[128,2048]{1,0:T(8,128)(2,1)} %pad_maximum_fusion), channel_id=1, source_target_pairs={{0,3},{1,4},{2,5},{3,6},{4,7},{5,8},{6,9},{7,10},{8,11},{9,12},{10... | collective-permute-start | bytes 1572872 | tf_op jit(solution)/shard_map/ppermute | solution.py:24
  15.1 70.4 %collective-permute-start = (bf16[128,2048]{1,0:T(8,128)(2,1)}, bf16[128,2048]{1,0:T(8,128)(2,1)}, u32[]{:S(2)}, u32[]{:S(2)}) collective-permute-start(bf16[128,2048]{1,0:T(8,128)(2,1)} %pad_maximum_fusion), channel_id=1, source_target_pairs={{0,4},{1,5},{2,6},{3,7},{4,8},{5,9},{6,10},{7,11},{8,12},{9,13},{1... | collective-permute-start | bytes 1572872 | tf_op jit(solution)/shard_map/ppermute | solution.py:24
  20.1 36.5 %all-to-all-start.2 = ((f32[16,128,8]{1,2,0:T(8,128)}), f32[16,128,8]{1,2,0:T(8,128)S(1)}, u32[]{:S(2)}, u32[]{:S(2)}) async-start(f32[16,128,8]{1,2,0:T(8,128)} %bitcast.9), calls=%async_computation.2 | async-start | bytes 131072 | tf_op jit(solution)/shard_map/all_to_all | solution.py:31
  23.6 37.7 %collective-permute-start.4 = (bf16[128,8192]{1,0:T(8,128)(2,1)}, bf16[128,8192]{1,0:T(8,128)(2,1)}, u32[]{:S(2)}, u32[]{:S(2)}) collective-permute-start(bf16[128,8192]{1,0:T(8,128)(2,1)} %bitcast.110), channel_id=1, source_target_pairs={{0,16},{16,32},{32,48},{48,64},{64,80},{80,96},{96,112},{1,17},{17... | collective-permute-start | bytes 6291464 | tf_op jit(solution)/shard_map/ppermute | solution.py:24
  30.4 2.9 %copy-start.7 = (s32[1,2048]{1,0:T(1,128)S(1)}, s32[1,2048]{1,0:T(1,128)}, u32[]{:S(2)}) copy-start(s32[1,2048]{1,0:T(1,128)} %param.25) | copy-start | bytes 24580
  31.0 3.7 %copy-start.9 = (f32[1,128]{1,0:T(1,128)S(1)}, f32[1,128]{1,0:T(1,128)}, u32[]{:S(2)}) copy-start(f32[1,128]{1,0:T(1,128)} %param.16) | copy-start | bytes 1540
  31.0 3.7 %copy-start.10 = (f32[1,128]{1,0:T(1,128)S(1)}, f32[1,128]{1,0:T(1,128)}, u32[]{:S(2)}) copy-start(f32[1,128]{1,0:T(1,128)} %param.17) | copy-start | bytes 1540
  33.3 28.0 %copy-start.3 = (bf16[128,8192]{1,0:T(8,128)(2,1)S(1)}, bf16[128,8192]{1,0:T(8,128)(2,1)}, u32[]{:S(2)}) copy-start(bf16[128,8192]{1,0:T(8,128)(2,1)} %param.14) | copy-start | bytes 6291460
  56.6 21.4 %all-to-all-start.1 = ((bf16[16,128,256]{2,1,0:T(8,128)(2,1)}), bf16[16,128,256]{2,1,0:T(8,128)(2,1)S(1)}, u32[]{:S(2)}, u32[]{:S(2)}) async-start(bf16[16,128,256]{2,1,0:T(8,128)(2,1)} %bitcast.5), calls=%async_computation.1 | async-start | bytes 2097152 | tf_op jit(solution)/shard_map/all_to_all | solution.py:31
  61.1 21.6 %copy-start.4 = (f32[16,128,8]{1,2,0:T(8,128)}, f32[16,128,8]{1,2,0:T(8,128)S(1)}, u32[]{:S(2)}) copy-start(f32[16,128,8]{1,2,0:T(8,128)S(1)} %get-tuple-element.14) | copy-start | bytes 196612
  78.0 34.0 %all-to-all-start = ((bf16[16,128,512]{2,1,0:T(8,128)(2,1)}), bf16[16,128,512]{2,1,0:T(8,128)(2,1)S(1)}, u32[]{:S(2)}, u32[]{:S(2)}) async-start(bf16[16,128,512]{2,1,0:T(8,128)(2,1)} %bitcast.80), calls=%async_computation | async-start | bytes 4194304 | tf_op jit(solution)/shard_map/all_to_all | solution.py:31
  84.1 9.0 %copy-start.5 = (bf16[1,128,1024]{2,1,0:T(8,128)(2,1)S(1)}, bf16[1,128,1024]{2,1,0:T(8,128)(2,1)}, u32[]{:S(2)}) copy-start(bf16[1,128,1024]{2,1,0:T(8,128)(2,1)} %param.24) | copy-start | bytes 786436
  85.4 7.7 %copy-start.6 = (bf16[1,128,1024]{2,1,0:T(8,128)(2,1)S(1)}, bf16[1,128,1024]{2,1,0:T(8,128)(2,1)}, u32[]{:S(2)}) copy-start(bf16[1,128,1024]{2,1,0:T(8,128)(2,1)} %param.23) | copy-start | bytes 786436
  112.0 1.3 copy-start.1
  146.6 11.5 %all-to-all-start.3 = ((f32[16,1,2048]{2,1,0:T(1,128)}), f32[16,1,2048]{2,1,0:T(1,128)S(1)}, u32[]{:S(2)}, u32[]{:S(2)}) async-start(f32[16,1,2048]{2,1,0:T(1,128)} %broadcast_in_dim.13), calls=%async_computation.3 | async-start | bytes 262144 | tf_op jit(solution)/shard_map/all_to_all | solution.py:237
  163.0 3.9 %copy-start.8 = (s32[1,2048]{1,0:T(1,128)S(1)}, s32[1,2048]{1,0:T(1,128)}, u32[]{:S(2)}) copy-start(s32[1,2048]{1,0:T(1,128)} %param.25) | copy-start | bytes 24580
  163.0 34.0 %all-to-all-start.4 = ((bf16[16,128,512]{2,1,0:T(8,128)(2,1)}), bf16[16,128,512]{2,1,0:T(8,128)(2,1)S(1)}, u32[]{:S(2)}, u32[]{:S(2)}) async-start(bf16[16,128,512]{2,1,0:T(8,128)(2,1)} %bitcast.81), calls=%async_computation.4 | async-start | bytes 4194304 | tf_op jit(solution)/shard_map/all_to_all | solution.py:38
  197.6 1.6 copy-start.2

commit v14 on v11

--- a/solution.py
+++ b/solution.py
@@ -69,60 +69,65 @@
     b_t = b_g.T
     st_rows = st.transpose(0, 2, 1)
 
+    sub = 2 if nblk % 2 == 0 else 1
+    span = sub * BLOCK
+
     def kernel(x_ref, b_ref, c_ref, lcc_ref, lcr_ref, str_ref, csc_ref, esc_ref, gain_ref,
                idc_ref, idr_ref, skip_ref, o_ref, sq_ref, carry_ref):
         @pl.when(pl.program_id(0) == 0)
         def _():
             carry_ref[...] = jnp.zeros(carry_ref.shape, carry_ref.dtype)
 
-        b_t_blk = b_ref[...]
-        c_blk = c_ref[...]
-        inner_cb = jnp.dot(c_blk, b_t_blk, preferred_element_type=jnp.float32)
         rows_at = lax.broadcasted_iota(jnp.int32, (BLOCK, BLOCK), 0)
         cols_at = lax.broadcasted_iota(jnp.int32, (BLOCK, BLOCK), 1)
-        same_doc = (idc_ref[...] == idr_ref[0]) & (rows_at >= cols_at)
-        b_t_f32 = b_t_blk.astype(jnp.float32)
-        sq = jnp.zeros((BLOCK, 1), jnp.float32)
-        for h in range(heads):
-            cols = slice(h * head_dim, (h + 1) * head_dim)
-            lc_c = lcc_ref[0, :, h:h + 1]
-            lc_r = lcr_ref[0, h:h + 1, :]
-            decay = jnp.where(same_doc, jnp.exp(lc_c - lc_r), 0.0)
-            intra_w = (decay * inner_cb * str_ref[0, h:h + 1, :]).astype(jnp.bfloat16)
-            xh = x_ref[:, cols]
-            local = jnp.dot(intra_w, xh, preferred_element_type=jnp.float32)
-            state_bf = carry_ref[h].astype(jnp.bfloat16)
-            carried = jnp.dot(c_blk, state_bf, preferred_element_type=jnp.float32)
-            carried = carried * csc_ref[0, :, h:h + 1]
-            out = local + carried + skip_ref[h] * xh.astype(jnp.float32)
-            o_ref[:, cols] = out
-            sq = sq + jnp.sum(out * out, axis=1, keepdims=True)
-            end_w_t = (esc_ref[0, h:h + 1, :] * b_t_f32).astype(jnp.bfloat16)
-            block_state = jnp.dot(end_w_t, xh, preferred_element_type=jnp.float32)
-            carry_ref[h] = gain_ref[0, h:h + 1, :] * carry_ref[h] + block_state
-        sq_ref[...] = sq
-
-    per_block = lambda shape: pl.BlockSpec((1,) + shape, lambda i: (i, 0, 0))
+        for s in range(sub):
+            rows = slice(s * BLOCK, (s + 1) * BLOCK)
+            b_t_blk = b_ref[:, rows]
+            c_blk = c_ref[rows, :]
+            inner_cb = jnp.dot(c_blk, b_t_blk, preferred_element_type=jnp.float32)
+            same_doc = (idc_ref[rows, :] == idr_ref[s]) & (rows_at >= cols_at)
+            b_t_f32 = b_t_blk.astype(jnp.float32)
+            sq = jnp.zeros((BLOCK, 1), jnp.float32)
+            for h in range(heads):
+                cols = slice(h * head_dim, (h + 1) * head_dim)
+                lc_c = lcc_ref[s, :, h:h + 1]
+                lc_r = lcr_ref[s, h:h + 1, :]
+                decay = jnp.where(same_doc, jnp.exp(lc_c - lc_r), 0.0)
+                intra_w = (decay * inner_cb * str_ref[s, h:h + 1, :]).astype(jnp.bfloat16)
+                xh = x_ref[rows, cols]
+                local = jnp.dot(intra_w, xh, preferred_element_type=jnp.float32)
+                state_bf = carry_ref[h].astype(jnp.bfloat16)
+                carried = jnp.dot(c_blk, state_bf, preferred_element_type=jnp.float32)
+                carried = carried * csc_ref[s, :, h:h + 1]
+                out = local + carried + skip_ref[h] * xh.astype(jnp.float32)
+                o_ref[rows, cols] = out
+                sq = sq + jnp.sum(out * out, axis=1, keepdims=True)
+                end_w_t = (esc_ref[s, h:h + 1, :] * b_t_f32).astype(jnp.bfloat16)
+                block_state = jnp.dot(end_w_t, xh, preferred_element_type=jnp.float32)
+                carry_ref[h] = gain_ref[s, h:h + 1, :] * carry_ref[h] + block_state
+            sq_ref[rows, :] = sq
+
+    per_block = lambda shape: pl.BlockSpec((sub,) + shape, lambda i: (i, 0, 0))
     return pl.pallas_call(
         kernel,
-        grid=(nblk,),
+        grid=(nblk // sub,),
         in_specs=[
-            pl.BlockSpec((BLOCK, x_width), lambda i: (i, 0)),
-            pl.BlockSpec((STATE, BLOCK), lambda i: (0, i)),
-            pl.BlockSpec((BLOCK, STATE), lambda i: (i, 0)),
+            pl.BlockSpec((span, x_width), lambda i: (i, 0)),
+            pl.BlockSpec((STATE, span), lambda i: (0, i)),
+            pl.BlockSpec((span, STATE), lambda i: (i, 0)),
             per_block((BLOCK, heads)),
             per_block((heads, BLOCK)),
             per_block((heads, BLOCK)),
             per_block((BLOCK, heads)),
             per_block((heads, BLOCK)),
             per_block((heads, head_dim)),
-            pl.BlockSpec((BLOCK, 1), lambda i: (i, 0)),
+            pl.BlockSpec((span, 1), lambda i: (i, 0)),
             per_block((1, BLOCK)),
             pl.BlockSpec(memory_space=pltpu.SMEM),
         ],
         out_specs=[
-            pl.BlockSpec((BLOCK, x_width), lambda i: (i, 0)),
-            pl.BlockSpec((BLOCK, 1), lambda i: (i, 0)),
+            pl.BlockSpec((span, x_width), lambda i: (i, 0)),
+            pl.BlockSpec((span, 1), lambda i: (i, 0)),
         ],
         out_shape=[
             jax.ShapeDtypeStruct((total, x_width), jnp.float32),

time: 203 us -> 206 us (1.015)
  Pallas kernels: 59.6 us -> 62.7 us
    pallas_call x1, Pallas kernels: 30.9 us -> 34 us  [mixer_heads(): pl.pallas_call(kernel, grid=(nblk // sub,), in_specs=[pl.BlockSpec((span,...]
where the time goes in v14:
time: 206 us; the launch traced here: 204 us
  Pallas kernels  62.7 us (30%)
  waiting for transfers between devices  56.7 us (28%)
  starting transfers between devices  37 us (18%)
  local copies, waits for them, and re-layouts  30.8 us (15%)
  other arithmetic  16.7 us (8%)
    all_to_all x3, waiting for transfers between devices, to_heads(): moved = lax.all_to_all(lead, 'ctx', split_axis=0, concat_axis=0, tiled=True)  49.5 us
    pallas_call x1, Pallas kernels, mixer_heads(): pl.pallas_call(kernel, grid=(nblk // sub,), in_specs=[pl.BlockSpec((span,...  34 us
    pallas_call x1, Pallas kernels, attend_rows(): pl.pallas_call(kernel, grid=(kv_heads,), in_specs=[pl.BlockSpec((tok_rows...  28.7 us
    ppermute x5, starting transfers between devices, shifted(): return lax.ppermute(value, axis, pairs)  18.6 us
    unnamed x32, local copies, waits for them, and re-layouts  13.1 us
    all_to_all x3, starting transfers between devices, to_heads(): moved = lax.all_to_all(lead, 'ctx', split_axis=0, concat_axis=0, tiled=True)  10.9 us
    all_to_all x1, waiting for transfers between devices, body(): lax.all_to_all(jnp.broadcast_to(sq_part[:, 0][None], (nctx, total)), 'ctx...  7.26 us
    convert_element_type x1, other arithmetic, body(): mixed = (x_h.astype(jnp.float32) + mixer_out * inv_rms * gain_h.astype(jn...  4.87 us
  transfers between devices with their start and end apart: 10, of which 4 were waited for; matrix products, arithmetic and copies ran while one was open for 16% of the time, Pallas kernels for 14%

profile of v14, /device:TPU:32, one launch (start us, length us, event | category | flops | bytes accessed | tf_op | source)
XLA Modules:
  0.0 204.3 jit_solution(1748789929729001911)
XLA Ops:
  0.0 1.9 pad_maximum_fusion
  1.9 4.2 %collective-permute-start.3 = (bf16[128,2048]{1,0:T(8,128)(2,1)}, bf16[128,2048]{1,0:T(8,128)(2,1)}, u32[]{:S(2)}, u32[]{:S(2)}) collective-permute-start(bf16[128,2048]{1,0:T(8,128)(2,1)} %pad_maximum_fusion), channel_id=1, source_target_pairs={{0,1},{1,2},{2,3},{3,4},{4,5},{5,6},{6,7},{7,8},{8,9},{9,10},{10,1... | collective-permute-start | bytes 1572872 | tf_op jit(solution)/shard_map/ppermute | solution.py:24
  6.1 4.7 %collective-permute-start.2 = (bf16[128,2048]{1,0:T(8,128)(2,1)}, bf16[128,2048]{1,0:T(8,128)(2,1)}, u32[]{:S(2)}, u32[]{:S(2)}) collective-permute-start(bf16[128,2048]{1,0:T(8,128)(2,1)} %pad_maximum_fusion), channel_id=1, source_target_pairs={{0,2},{1,3},{2,4},{3,5},{4,6},{5,7},{6,8},{7,9},{8,10},{9,11},{10,... | collective-permute-start | bytes 1572872 | tf_op jit(solution)/shard_map/ppermute | solution.py:24
  10.7 4.4 %collective-permute-start.1 = (bf16[128,2048]{1,0:T(8,128)(2,1)}, bf16[128,2048]{1,0:T(8,128)(2,1)}, u32[]{:S(2)}, u32[]{:S(2)}) collective-permute-start(bf16[128,2048]{1,0:T(8,128)(2,1)} %pad_maximum_fusion), channel_id=1, source_target_pairs={{0,3},{1,4},{2,5},{3,6},{4,7},{5,8},{6,9},{7,10},{8,11},{9,12},{10... | collective-permute-start | bytes 1572872 | tf_op jit(solution)/shard_map/ppermute | solution.py:24
  15.1 3.5 %collective-permute-start = (bf16[128,2048]{1,0:T(8,128)(2,1)}, bf16[128,2048]{1,0:T(8,128)(2,1)}, u32[]{:S(2)}, u32[]{:S(2)}) collective-permute-start(bf16[128,2048]{1,0:T(8,128)(2,1)} %pad_maximum_fusion), channel_id=1, source_target_pairs={{0,4},{1,5},{2,6},{3,7},{4,8},{5,9},{6,10},{7,11},{8,12},{9,13},{1... | collective-permute-start | bytes 1572872 | tf_op jit(solution)/shard_map/ppermute | solution.py:24
  20.1 3.5 %all-to-all-start.2 = ((f32[16,128,8]{1,2,0:T(8,128)}), f32[16,128,8]{1,2,0:T(8,128)S(1)}, u32[]{:S(2)}, u32[]{:S(2)}) async-start(f32[16,128,8]{1,2,0:T(8,128)} %bitcast.9), calls=%async_computation.2 | async-start | bytes 131072 | tf_op jit(solution)/shard_map/all_to_all | solution.py:31
  23.6 1.9 collective-permute-start.4
  35.4 21.2 %all-to-all-done.2 = f32[16,128,8]{1,2,0:T(8,128)S(1)} async-done(((f32[16,128,8]{1,2,0:T(8,128)}), f32[16,128,8]{1,2,0:T(8,128)S(1)}, u32[]{:S(2)}, u32[]{:S(2)}) %all-to-all-start.2) | async-done | bytes 65568 | tf_op jit(solution)/shard_map/all_to_all | solution.py:31
  56.6 3.7 %all-to-all-start.1 = ((bf16[16,128,256]{2,1,0:T(8,128)(2,1)}), bf16[16,128,256]{2,1,0:T(8,128)(2,1)S(1)}, u32[]{:S(2)}, u32[]{:S(2)}) async-start(bf16[16,128,256]{2,1,0:T(8,128)(2,1)} %bitcast.5), calls=%async_computation.1 | async-start | bytes 2097152 | tf_op jit(solution)/shard_map/all_to_all | solution.py:31
  61.3 1.8 broadcast_select_fusion
  64.7 13.3 %all-to-all-done.1 = bf16[16,128,256]{2,1,0:T(8,128)(2,1)S(1)} async-done(((bf16[16,128,256]{2,1,0:T(8,128)(2,1)}), bf16[16,128,256]{2,1,0:T(8,128)(2,1)S(1)}, u32[]{:S(2)}, u32[]{:S(2)}) %all-to-all-start.1) | async-done | bytes 1048608 | tf_op jit(solution)/shard_map/all_to_all | solution.py:31
  78.0 3.7 %all-to-all-start = ((bf16[16,128,512]{2,1,0:T(8,128)(2,1)}), bf16[16,128,512]{2,1,0:T(8,128)(2,1)S(1)}, u32[]{:S(2)}, u32[]{:S(2)}) async-start(bf16[16,128,512]{2,1,0:T(8,128)(2,1)} %bitcast.80), calls=%async_computation | async-start | bytes 4194304 | tf_op jit(solution)/shard_map/all_to_all | solution.py:31
  85.4 1.9 constant_dynamic-update-slice_fusion.4
  87.4 1.9 constant_dynamic-update-slice_fusion.3
  89.3 1.9 constant_dynamic-update-slice_fusion.2
  91.2 1.9 constant_dynamic-update-slice_fusion.1
  95.0 2.0 copy.82.b_ref
  97.1 15.0 %all-to-all-done = bf16[16,128,512]{2,1,0:T(8,128)(2,1)S(1)} async-done(((bf16[16,128,512]{2,1,0:T(8,128)(2,1)}), bf16[16,128,512]{2,1,0:T(8,128)(2,1)S(1)}, u32[]{:S(2)}, u32[]{:S(2)}) %all-to-all-start) | async-done | bytes 2097184 | tf_op jit(solution)/shard_map/all_to_all | solution.py:31
  113.4 34.0 %shard_map.127 = (f32[2048,512]{1,0:T(8,128)}, f32[2048,1]{1,0:T(8,128)}) custom-call(bf16[2048,512]{1,0:T(8,128)(2,1)} %bitcast.76, bf16[128,2048]{1,0:T(8,128)(2,1)} %copy.82.b_ref, bf16[2048,128]{1,0:T(8,128)(2,1)} %get-tuple-element.15.c_ref, f32[16,128,8]{2,1,0:T(8,128)} %copy.83.lcc_ref, f32[16,8,128]{2,1,0:T(8,128)} %bitcast.84, ...), custom_call_target="tpu_custom_call" | custom-call | tf_op jit(solution)/shard_map/pallas_call | solution.py:111
  149.7 3.5 %all-to-all-start.3 = ((f32[16,1,2048]{2,1,0:T(1,128)}), f32[16,1,2048]{2,1,0:T(1,128)S(1)}, u32[]{:S(2)}, u32[]{:S(2)}) async-start(f32[16,1,2048]{2,1,0:T(1,128)} %broadcast_in_dim.13), calls=%async_computation.3 | async-start | bytes 262144 | tf_op jit(solution)/shard_map/all_to_all | solution.py:241
  153.9 7.3 %all-to-all-done.3 = f32[16,1,2048]{2,1,0:T(1,128)S(1)} async-done(((f32[16,1,2048]{2,1,0:T(1,128)}), f32[16,1,2048]{2,1,0:T(1,128)S(1)}, u32[]{:S(2)}, u32[]{:S(2)}) %all-to-all-start.3) | async-done | bytes 131104 | tf_op jit(solution)/shard_map/all_to_all | solution.py:241
  161.3 4.9 %add_convert_fusion.1 = bf16[2048,512]{1,0:T(8,128)(2,1)} fusion(f32[2048,512]{1,0:T(8,128)} %get-tuple-element.10, bf16[2048,512]{1,0:T(8,128)(2,1)} %bitcast.77, f32[512]{0:T(512)S(1)} %bitcast.107, f32[2048]{0:T(1024)S(1)} %add_rsqrt_fusion), kind=kLoop, calls=%fused_computation.2 | loop fusion | flops 5242880 | bytes 8398848 | tf_op jit(solution)/shard_map/convert_element_type | solution.py:248
  166.2 4.0 %all-to-all-start.4 = ((bf16[16,128,512]{2,1,0:T(8,128)(2,1)}), bf16[16,128,512]{2,1,0:T(8,128)(2,1)S(1)}, u32[]{:S(2)}, u32[]{:S(2)}) async-start(bf16[16,128,512]{2,1,0:T(8,128)(2,1)} %bitcast.81), calls=%async_computation.4 | async-start | bytes 4194304 | tf_op jit(solution)/shard_map/all_to_all | solution.py:38
  171.6 28.7 %shard_map.128 = bf16[128,8192]{1,0:T(8,128)(2,1)} custom-call(bf16[128,8192]{1,0:T(8,128)(2,1)} %bitcast.83, bf16[640,2048]{1,0:T(8,128)(2,1)} %constant_dynamic-update-slice_fusion.k_ref.v_ref, bf16[640,2048]{1,0:T(8,128)(2,1)} %constant_dynamic-update-slice_fusion.k_ref.v_ref, s32[128,1]{1,0:T(8,128)} %copy.88.iq_ref, s32[1,640]{1,0:T(1,128)} %reshape.154.ik_ref), custom_call_target="tpu_custom_call" | custom-call | tf_op jit(solution)/shard_map/pallas_call | solution.py:170
  (78 shorter events, 29.3 us)
Async XLA Ops:
  0.0 34.8 %copy-start = (f32[1,128]{1,0:T(1,128)S(1)}, f32[1,128]{1,0:T(1,128)}, u32[]{:S(2)}) copy-start(f32[1,128]{1,0:T(1,128)} %param.20) | copy-start | bytes 1540
  1.9 89.3 %collective-permute-start.3 = (bf16[128,2048]{1,0:T(8,128)(2,1)}, bf16[128,2048]{1,0:T(8,128)(2,1)}, u32[]{:S(2)}, u32[]{:S(2)}) collective-permute-start(bf16[128,2048]{1,0:T(8,128)(2,1)} %pad_maximum_fusion), channel_id=1, source_target_pairs={{0,1},{1,2},{2,3},{3,4},{4,5},{5,6},{6,7},{7,8},{8,9},{9,10},{10,1... | collective-permute-start | bytes 1572872 | tf_op jit(solution)/shard_map/ppermute | solution.py:24
  6.1 83.2 %collective-permute-start.2 = (bf16[128,2048]{1,0:T(8,128)(2,1)}, bf16[128,2048]{1,0:T(8,128)(2,1)}, u32[]{:S(2)}, u32[]{:S(2)}) collective-permute-start(bf16[128,2048]{1,0:T(8,128)(2,1)} %pad_maximum_fusion), channel_id=1, source_target_pairs={{0,2},{1,3},{2,4},{3,5},{4,6},{5,7},{6,8},{7,9},{8,10},{9,11},{10,... | collective-permute-start | bytes 1572872 | tf_op jit(solution)/shard_map/ppermute | solution.py:24
  10.7 76.7 %collective-permute-start.1 = (bf16[128,2048]{1,0:T(8,128)(2,1)}, bf16[128,2048]{1,0:T(8,128)(2,1)}, u32[]{:S(2)}, u32[]{:S(2)}) collective-permute-start(bf16[128,2048]{1,0:T(8,128)(2,1)} %pad_maximum_fusion), channel_id=1, source_target_pairs={{0,3},{1,4},{2,5},{3,6},{4,7},{5,8},{6,9},{7,10},{8,11},{9,12},{10... | collective-permute-start | bytes 1572872 | tf_op jit(solution)/shard_map/ppermute | solution.py:24
  15.1 70.4 %collective-permute-start = (bf16[128,2048]{1,0:T(8,128)(2,1)}, bf16[128,2048]{1,0:T(8,128)(2,1)}, u32[]{:S(2)}, u32[]{:S(2)}) collective-permute-start(bf16[128,2048]{1,0:T(8,128)(2,1)} %pad_maximum_fusion), channel_id=1, source_target_pairs={{0,4},{1,5},{2,6},{3,7},{4,8},{5,9},{6,10},{7,11},{8,12},{9,13},{1... | collective-permute-start | bytes 1572872 | tf_op jit(solution)/shard_map/ppermute | solution.py:24
  20.1 36.5 %all-to-all-start.2 = ((f32[16,128,8]{1,2,0:T(8,128)}), f32[16,128,8]{1,2,0:T(8,128)S(1)}, u32[]{:S(2)}, u32[]{:S(2)}) async-start(f32[16,128,8]{1,2,0:T(8,128)} %bitcast.9), calls=%async_computation.2 | async-start | bytes 131072 | tf_op jit(solution)/shard_map/all_to_all | solution.py:31
  23.6 37.7 %collective-permute-start.4 = (bf16[128,8192]{1,0:T(8,128)(2,1)}, bf16[128,8192]{1,0:T(8,128)(2,1)}, u32[]{:S(2)}, u32[]{:S(2)}) collective-permute-start(bf16[128,8192]{1,0:T(8,128)(2,1)} %bitcast.110), channel_id=1, source_target_pairs={{0,16},{16,32},{32,48},{48,64},{64,80},{80,96},{96,112},{1,17},{17... | collective-permute-start | bytes 6291464 | tf_op jit(solution)/shard_map/ppermute | solution.py:24
  30.4 2.9 %copy-start.7 = (s32[1,2048]{1,0:T(1,128)S(1)}, s32[1,2048]{1,0:T(1,128)}, u32[]{:S(2)}) copy-start(s32[1,2048]{1,0:T(1,128)} %param.25) | copy-start | bytes 24580
  31.0 3.7 %copy-start.9 = (f32[1,128]{1,0:T(1,128)S(1)}, f32[1,128]{1,0:T(1,128)}, u32[]{:S(2)}) copy-start(f32[1,128]{1,0:T(1,128)} %param.16) | copy-start | bytes 1540
  31.0 3.7 %copy-start.10 = (f32[1,128]{1,0:T(1,128)S(1)}, f32[1,128]{1,0:T(1,128)}, u32[]{:S(2)}) copy-start(f32[1,128]{1,0:T(1,128)} %param.17) | copy-start | bytes 1540
  33.3 28.0 %copy-start.3 = (bf16[128,8192]{1,0:T(8,128)(2,1)S(1)}, bf16[128,8192]{1,0:T(8,128)(2,1)}, u32[]{:S(2)}) copy-start(bf16[128,8192]{1,0:T(8,128)(2,1)} %param.14) | copy-start | bytes 6291460
  56.6 21.4 %all-to-all-start.1 = ((bf16[16,128,256]{2,1,0:T(8,128)(2,1)}), bf16[16,128,256]{2,1,0:T(8,128)(2,1)S(1)}, u32[]{:S(2)}, u32[]{:S(2)}) async-start(bf16[16,128,256]{2,1,0:T(8,128)(2,1)} %bitcast.5), calls=%async_computation.1 | async-start | bytes 2097152 | tf_op jit(solution)/shard_map/all_to_all | solution.py:31
  61.1 21.6 %copy-start.4 = (f32[16,128,8]{1,2,0:T(8,128)}, f32[16,128,8]{1,2,0:T(8,128)S(1)}, u32[]{:S(2)}) copy-start(f32[16,128,8]{1,2,0:T(8,128)S(1)} %get-tuple-element.14) | copy-start | bytes 196612
  78.0 34.0 %all-to-all-start = ((bf16[16,128,512]{2,1,0:T(8,128)(2,1)}), bf16[16,128,512]{2,1,0:T(8,128)(2,1)S(1)}, u32[]{:S(2)}, u32[]{:S(2)}) async-start(bf16[16,128,512]{2,1,0:T(8,128)(2,1)} %bitcast.80), calls=%async_computation | async-start | bytes 4194304 | tf_op jit(solution)/shard_map/all_to_all | solution.py:31
  84.1 9.0 %copy-start.5 = (bf16[1,128,1024]{2,1,0:T(8,128)(2,1)S(1)}, bf16[1,128,1024]{2,1,0:T(8,128)(2,1)}, u32[]{:S(2)}) copy-start(bf16[1,128,1024]{2,1,0:T(8,128)(2,1)} %param.24) | copy-start | bytes 786436
  85.4 7.7 %copy-start.6 = (bf16[1,128,1024]{2,1,0:T(8,128)(2,1)S(1)}, bf16[1,128,1024]{2,1,0:T(8,128)(2,1)}, u32[]{:S(2)}) copy-start(bf16[1,128,1024]{2,1,0:T(8,128)(2,1)} %param.23) | copy-start | bytes 786436
  112.0 1.3 copy-start.1
  149.7 11.5 %all-to-all-start.3 = ((f32[16,1,2048]{2,1,0:T(1,128)}), f32[16,1,2048]{2,1,0:T(1,128)S(1)}, u32[]{:S(2)}, u32[]{:S(2)}) async-start(f32[16,1,2048]{2,1,0:T(1,128)} %broadcast_in_dim.13), calls=%async_computation.3 | async-start | bytes 262144 | tf_op jit(solution)/shard_map/all_to_all | solution.py:241
  166.2 4.0 %copy-start.8 = (s32[1,2048]{1,0:T(1,128)S(1)}, s32[1,2048]{1,0:T(1,128)}, u32[]{:S(2)}) copy-start(s32[1,2048]{1,0:T(1,128)} %param.25) | copy-start | bytes 24580
  166.2 34.2 %all-to-all-start.4 = ((bf16[16,128,512]{2,1,0:T(8,128)(2,1)}), bf16[16,128,512]{2,1,0:T(8,128)(2,1)S(1)}, u32[]{:S(2)}, u32[]{:S(2)}) async-start(bf16[16,128,512]{2,1,0:T(8,128)(2,1)} %bitcast.81), calls=%async_computation.4 | async-start | bytes 4194304 | tf_op jit(solution)/shard_map/all_to_all | solution.py:38
  200.9 1.6 copy-start.2

commit v15 on v11

--- a/solution.py
+++ b/solution.py
@@ -137,7 +137,7 @@
     )
 
 
-def attend_rows(q_row, kv_win, ids_q, ids_k, interpret=False):
+def attend_rows(q_row, kv_win, ids_q, ids_k, first, count, interpret=False):
     tok_rows, q_width = q_row.shape
     window = kv_win.shape[0]
     kv_heads = kv_win.shape[1] // (2 * HEAD_A)
@@ -164,16 +164,16 @@
 
     return pl.pallas_call(
         kernel,
-        grid=(kv_heads,),
+        grid=(count,),
         in_specs=[
-            pl.BlockSpec((tok_rows, group * HEAD_A), lambda i: (0, i)),
-            pl.BlockSpec((window, HEAD_A), lambda i: (0, i)),
-            pl.BlockSpec((window, HEAD_A), lambda i: (0, kv_heads + i)),
+            pl.BlockSpec((tok_rows, group * HEAD_A), lambda i: (0, first + i)),
+            pl.BlockSpec((window, HEAD_A), lambda i: (0, first + i)),
+            pl.BlockSpec((window, HEAD_A), lambda i: (0, kv_heads + first + i)),
             pl.BlockSpec((tok_rows, 1), lambda i: (0, 0)),
             pl.BlockSpec((1, window), lambda i: (0, 0)),
         ],
         out_specs=pl.BlockSpec((tok_rows, group * HEAD_A), lambda i: (0, i)),
-        out_shape=jax.ShapeDtypeStruct((tok_rows, q_width), jnp.bfloat16),
+        out_shape=jax.ShapeDtypeStruct((tok_rows, count * group * HEAD_A), jnp.bfloat16),
         interpret=interpret,
     )(q_row, kv_win, kv_win, ids_q, ids_k)
 
@@ -219,7 +219,6 @@
     halo = -(-MOST_DOC // tok_rows)
     kv_row = jnp.concatenate([keys[0], values[0]], axis=1)
     kv_win = jnp.concatenate([shifted(kv_row, "ctx", by) for by in range(halo, 0, -1)] + [kv_row], axis=0)
-    kv_win, x_h = lax.optimization_barrier((kv_win, x_h))
     all_ids = doc_ids[0]
     lead = halo * tok_rows
     padded_ids = jnp.concatenate([jnp.full((lead,), -1, all_ids.dtype), all_ids])
@@ -232,7 +231,10 @@
     gain_h = lax.dynamic_slice_in_dim(norm_gain[0], me * part, part)
 
     mixer_out, sq_part = mixer_heads(x_h, dt_h, bias_h, alog_h, b_g, c_g, skip_h, all_ids)
-    attended = attend_rows(queries[0], kv_win, ids_q.reshape(tok_rows, 1), ids_k.reshape(1, lead + tok_rows))
+    half = kv_heads // 2
+    ids_q2, ids_k2 = ids_q.reshape(tok_rows, 1), ids_k.reshape(1, lead + tok_rows)
+    att_a = attend_rows(queries[0], kv_win, ids_q2, ids_k2, 0, half)
+    att_a, x_h = lax.optimization_barrier((att_a, x_h))
     sq_all = lax.all_to_all(
         jnp.broadcast_to(sq_part[:, 0][None], (nctx, total)), "ctx", split_axis=0, concat_axis=0, tiled=True
     )
@@ -242,6 +244,8 @@
         x_h.astype(jnp.float32) + mixer_out * inv_rms * gain_h.astype(jnp.float32)[None, :]
     ).astype(jnp.bfloat16)
     mixed_rows = to_rows(mixed, nctx)
+    att_b = attend_rows(queries[0], kv_win, ids_q2, ids_k2, half, kv_heads - half)
+    attended = jnp.concatenate([att_a, att_b], axis=1)
     return (mixed_rows.astype(jnp.float32) + attended.astype(jnp.float32)).astype(jnp.bfloat16)[None]
 
 

time: 203 us -> 220 us (1.084)
  waiting for transfers between devices: 56.7 us -> 63.6 us
  local copies, waits for them, and re-layouts: 30.8 us -> 35.3 us
  starting transfers between devices: 36.8 us -> 40.5 us
    all_to_all x1, waiting for transfers between devices: 0.01 us -> 14.8 us  [to_rows(): lax.all_to_all(block.reshape(chunks, tok_rows, width), 'ctx', split_axis=...]
    convert_element_type x1 -> x2, local copies, waits for them, and re-layouts: 0.48 us -> 9.53 us  [body(): mixed_rows.astype(jnp.float32) + attended.astype(jnp.float32)]
    all_to_all x1, waiting for transfers between devices: 7.26 us -> 0.01 us  [body(): lax.all_to_all(jnp.broadcast_to(sq_part[:, 0][None], (nctx, total)), 'ctx...]
    convert_element_type x0 -> x2, other arithmetic: none -> 4.55 us  [the longest x1 3.99 us: body(): (mixed_rows.astype(jnp.float32) + attended.astype(jnp.float32)).astype(jn...]
    unnamed x32 -> x36, local copies, waits for them, and re-layouts: 13.1 us -> 9.77 us
    all_to_all x1, starting transfers between devices: 3.85 us -> 7.16 us  [to_rows(): lax.all_to_all(block.reshape(chunks, tok_rows, width), 'ctx', split_axis=...]
    pallas_call x1 -> x2, Pallas kernels: 28.7 us -> 30.5 us  [attend_rows(): pl.pallas_call(kernel, grid=(count,), in_specs=[pl.BlockSpec((tok_rows, g...]
  transfers between devices with their start and end apart: 10 -> 10, of which waited for: 4 -> 4; matrix products, arithmetic and copies ran while one was open for 16% -> 12% of each run, Pallas kernels for 14% -> 14%
where the time goes in v15:
time: 220 us; the launch traced here: 219 us
  waiting for transfers between devices  63.6 us (29%)
  Pallas kernels  61.5 us (28%)
  starting transfers between devices  40.5 us (18%)
  local copies, waits for them, and re-layouts  35.3 us (16%)
  other arithmetic  17.4 us (8%)
    all_to_all x3, waiting for transfers between devices, to_heads(): moved = lax.all_to_all(lead, 'ctx', split_axis=0, concat_axis=0, tiled=True)  48.8 us
    pallas_call x1, Pallas kernels, mixer_heads(): pl.pallas_call(kernel, grid=(nblk,), in_specs=[pl.BlockSpec((BLOCK, x_wid...  31 us
    pallas_call x2, Pallas kernels, attend_rows(): pl.pallas_call(kernel, grid=(count,), in_specs=[pl.BlockSpec((tok_rows, g...  30.5 us
    ppermute x5, starting transfers between devices, shifted(): return lax.ppermute(value, axis, pairs)  18.2 us
    all_to_all x1, waiting for transfers between devices, to_rows(): lax.all_to_all(block.reshape(chunks, tok_rows, width), 'ctx', split_axis=...  14.8 us
    all_to_all x3, starting transfers between devices, to_heads(): moved = lax.all_to_all(lead, 'ctx', split_axis=0, concat_axis=0, tiled=True)  11.6 us
    unnamed x36, local copies, waits for them, and re-layouts  9.77 us
    convert_element_type x2, local copies, waits for them, and re-layouts, body(): mixed_rows.astype(jnp.float32) + attended.astype(jnp.float32)  9.53 us
  transfers between devices with their start and end apart: 10, of which 4 were waited for; matrix products, arithmetic and copies ran while one was open for 12% of the time, Pallas kernels for 14%

profile of v15, /device:TPU:32, one launch (start us, length us, event | category | flops | bytes accessed | tf_op | source)
XLA Modules:
  0.0 218.5 jit_solution(11154287452036174823)
XLA Ops:
  0.0 1.9 pad_maximum_fusion
  1.9 4.3 %collective-permute-start = (bf16[128,2048]{1,0:T(8,128)(2,1)}, bf16[128,2048]{1,0:T(8,128)(2,1)}, u32[]{:S(2)}, u32[]{:S(2)}) collective-permute-start(bf16[128,2048]{1,0:T(8,128)(2,1)} %pad_maximum_fusion), channel_id=1, source_target_pairs={{0,4},{1,5},{2,6},{3,7},{4,8},{5,9},{6,10},{7,11},{8,12},{9,13},{1... | collective-permute-start | bytes 1572872 | tf_op jit(solution)/shard_map/ppermute | solution.py:24
  6.2 5.5 %collective-permute-start.1 = (bf16[128,2048]{1,0:T(8,128)(2,1)}, bf16[128,2048]{1,0:T(8,128)(2,1)}, u32[]{:S(2)}, u32[]{:S(2)}) collective-permute-start(bf16[128,2048]{1,0:T(8,128)(2,1)} %pad_maximum_fusion), channel_id=1, source_target_pairs={{0,3},{1,4},{2,5},{3,6},{4,7},{5,8},{6,9},{7,10},{8,11},{9,12},{10... | collective-permute-start | bytes 1572872 | tf_op jit(solution)/shard_map/ppermute | solution.py:24
  11.7 3.7 %collective-permute-start.2 = (bf16[128,2048]{1,0:T(8,128)(2,1)}, bf16[128,2048]{1,0:T(8,128)(2,1)}, u32[]{:S(2)}, u32[]{:S(2)}) collective-permute-start(bf16[128,2048]{1,0:T(8,128)(2,1)} %pad_maximum_fusion), channel_id=1, source_target_pairs={{0,2},{1,3},{2,4},{3,5},{4,6},{5,7},{6,8},{7,9},{8,10},{9,11},{10,... | collective-permute-start | bytes 1572872 | tf_op jit(solution)/shard_map/ppermute | solution.py:24
  15.4 2.8 %collective-permute-start.3 = (bf16[128,2048]{1,0:T(8,128)(2,1)}, bf16[128,2048]{1,0:T(8,128)(2,1)}, u32[]{:S(2)}, u32[]{:S(2)}) collective-permute-start(bf16[128,2048]{1,0:T(8,128)(2,1)} %pad_maximum_fusion), channel_id=1, source_target_pairs={{0,1},{1,2},{2,3},{3,4},{4,5},{5,6},{6,7},{7,8},{8,9},{9,10},{10,1... | collective-permute-start | bytes 1572872 | tf_op jit(solution)/shard_map/ppermute | solution.py:24
  18.2 1.6 copy.80
  19.8 3.5 %all-to-all-start.2 = ((f32[16,128,8]{1,2,0:T(8,128)}), f32[16,128,8]{1,2,0:T(8,128)S(1)}, u32[]{:S(2)}, u32[]{:S(2)}) async-start(f32[16,128,8]{1,2,0:T(8,128)} %bitcast.12), calls=%async_computation.2 | async-start | bytes 131072 | tf_op jit(solution)/shard_map/all_to_all | solution.py:31
  23.3 1.9 collective-permute-start.4
  36.5 18.0 %all-to-all-done.2 = f32[16,128,8]{1,2,0:T(8,128)S(1)} async-done(((f32[16,128,8]{1,2,0:T(8,128)}), f32[16,128,8]{1,2,0:T(8,128)S(1)}, u32[]{:S(2)}, u32[]{:S(2)}) %all-to-all-start.2) | async-done | bytes 65568 | tf_op jit(solution)/shard_map/all_to_all | solution.py:31
  54.5 3.7 %all-to-all-start.1 = ((bf16[16,128,256]{2,1,0:T(8,128)(2,1)}), bf16[16,128,256]{2,1,0:T(8,128)(2,1)S(1)}, u32[]{:S(2)}, u32[]{:S(2)}) async-start(bf16[16,128,256]{2,1,0:T(8,128)(2,1)} %bitcast.8), calls=%async_computation.1 | async-start | bytes 2097152 | tf_op jit(solution)/shard_map/all_to_all | solution.py:31
  58.9 1.8 broadcast_select_fusion
  62.3 12.4 %all-to-all-done.1 = bf16[16,128,256]{2,1,0:T(8,128)(2,1)S(1)} async-done(((bf16[16,128,256]{2,1,0:T(8,128)(2,1)}), bf16[16,128,256]{2,1,0:T(8,128)(2,1)S(1)}, u32[]{:S(2)}, u32[]{:S(2)}) %all-to-all-start.1) | async-done | bytes 1048608 | tf_op jit(solution)/shard_map/all_to_all | solution.py:31
  74.7 4.4 %all-to-all-start = ((bf16[16,128,512]{2,1,0:T(8,128)(2,1)}), bf16[16,128,512]{2,1,0:T(8,128)(2,1)}, u32[]{:S(2)}, u32[]{:S(2)}) async-start(bf16[16,128,512]{2,1,0:T(8,128)(2,1)} %bitcast.66), calls=%async_computation | async-start | bytes 4194304 | tf_op jit(solution)/shard_map/all_to_all | solution.py:31
  89.5 18.4 %all-to-all-done = bf16[16,128,512]{2,1,0:T(8,128)(2,1)} async-done(((bf16[16,128,512]{2,1,0:T(8,128)(2,1)}), bf16[16,128,512]{2,1,0:T(8,128)(2,1)}, u32[]{:S(2)}, u32[]{:S(2)}) %all-to-all-start) | async-done | bytes 2097184 | tf_op jit(solution)/shard_map/all_to_all | solution.py:31
  108.7 31.0 %shard_map.128 = (f32[2048,512]{1,0:T(8,128)}, f32[2048,1]{1,0:T(8,128)}) custom-call(bf16[2048,512]{1,0:T(8,128)(2,1)} %bitcast.7.x_ref, bf16[128,2048]{1,0:T(8,128)(2,1)} %copy.87.b_ref, bf16[2048,128]{1,0:T(8,128)(2,1)} %get-tuple-element.15.c_ref, f32[16,128,8]{2,1,0:T(8,128)} %copy.88.lcc_ref, f32[16,8,128]{2,1,0:T(8,128)} %bitcast.81, ...), custom_call_target="tpu_custom_call" | custom-call | tf_op jit(solution)/shard_map/pallas_call | solution.py:106
  141.9 3.5 %all-to-all-start.3 = ((f32[16,1,2048]{2,1,0:T(1,128)}), f32[16,1,2048]{2,1,0:T(1,128)S(1)}, u32[]{:S(2)}, u32[]{:S(2)}) async-start(f32[16,1,2048]{2,1,0:T(1,128)} %broadcast_in_dim.11), calls=%async_computation.3 | async-start | bytes 262144 | tf_op jit(solution)/shard_map/all_to_all | solution.py:238
  147.0 15.3 %shard_map.127 = bf16[128,4096]{1,0:T(8,128)(2,1)} custom-call(bf16[128,8192]{1,0:T(8,128)(2,1)} %bitcast.74, bf16[640,2048]{1,0:T(8,128)(2,1)} %copy-done.1, bf16[640,2048]{1,0:T(8,128)(2,1)} %copy-done.1, s32[128,1]{1,0:T(8,128)} %copy.77.iq_ref, s32[1,640]{1,0:T(1,128)} %reshape.195.ik_ref), custom_call_target="tpu_custom_call" | custom-call | tf_op jit(solution)/shard_map/pallas_call | solution.py:165
  162.4 4.9 %add_convert_fusion.1 = bf16[2048,512]{1,0:T(8,128)(2,1)} fusion(f32[2048,512]{1,0:T(8,128)} %get-tuple-element.10, bf16[2048,512]{1,0:T(8,128)(2,1)} %bitcast.7.x_ref, f32[512]{0:T(512)S(1)} %bitcast.104, f32[2048]{0:T(1024)S(1)} %add_rsqrt_fusion), kind=kLoop, calls=%fused_computation.2 | loop fusion | flops 5242880 | bytes 8398848 | tf_op jit(solution)/shard_map/convert_element_type | solution.py:245
  167.3 7.2 %all-to-all-start.4 = ((bf16[16,128,512]{2,1,0:T(8,128)(2,1)}), bf16[16,128,512]{2,1,0:T(8,128)(2,1)S(1)}, u32[]{:S(2)}, u32[]{:S(2)}) async-start(bf16[16,128,512]{2,1,0:T(8,128)(2,1)} %bitcast.77), calls=%async_computation.4 | async-start | bytes 4194304 | tf_op jit(solution)/shard_map/all_to_all | solution.py:38
  174.4 15.3 %shard_map.129 = bf16[128,4096]{1,0:T(8,128)(2,1)} custom-call(bf16[128,8192]{1,0:T(8,128)(2,1)} %bitcast.75, bf16[640,2048]{1,0:T(8,128)(2,1)} %copy-done.1, bf16[640,2048]{1,0:T(8,128)(2,1)} %copy-done.1, s32[128,1]{1,0:T(8,128)} %copy.77.iq_ref, s32[1,640]{1,0:T(1,128)} %reshape.195.ik_ref), custom_call_target="tpu_custom_call" | custom-call | tf_op jit(solution)/shard_map/pallas_call | solution.py:165
  189.7 14.8 %all-to-all-done.4 = bf16[16,128,512]{2,1,0:T(8,128)(2,1)S(1)} async-done(((bf16[16,128,512]{2,1,0:T(8,128)(2,1)}), bf16[16,128,512]{2,1,0:T(8,128)(2,1)S(1)}, u32[]{:S(2)}, u32[]{:S(2)}) %all-to-all-start.4) | async-done | bytes 2097184 | tf_op jit(solution)/shard_map/all_to_all | solution.py:38
  205.0 4.5 %copy.92 = f32[128,16,512]{2,1,0:T(8,128)} copy(f32[128,16,512]{2,0,1:T(8,128)S(1)} %convert_bitcast_fusion) | data formatting | bytes 8388608 | tf_op jit(solution)/shard_map/convert_element_type | solution.py:249
  209.5 5.1 %reshape.203 = f32[1,128,8192]{2,1,0:T(8,128)} reshape(f32[128,16,512]{2,1,0:T(8,128)} %copy.92) | data formatting | bytes 8388608 | tf_op jit(solution)/shard_map/convert_element_type | solution.py:249
  214.6 4.0 %add_convert_fusion = bf16[1,128,8192]{2,1,0:T(8,128)(2,1)} fusion(f32[1,128,8192]{2,1,0:T(8,128)} %reshape.203, bf16[1,128,4096]{2,1,0:T(8,128)(2,1)S(1)} %bitcast.80, bf16[1,128,4096]{2,1,0:T(8,128)(2,1)S(1)} %bitcast.79), kind=kLoop, calls=%fused_computation.1 | loop fusion | flops 6291456 | bytes 8388608 | tf_op jit(solution)/shard_map/convert_element_type | solution.py:249
  (84 shorter events, 28.9 us)
Async XLA Ops:
  0.0 35.8 %copy-start = (f32[1,128]{1,0:T(1,128)S(1)}, f32[1,128]{1,0:T(1,128)}, u32[]{:S(2)}) copy-start(f32[1,128]{1,0:T(1,128)} %param.20) | copy-start | bytes 1540
  1.9 81.2 %collective-permute-start = (bf16[128,2048]{1,0:T(8,128)(2,1)}, bf16[128,2048]{1,0:T(8,128)(2,1)}, u32[]{:S(2)}, u32[]{:S(2)}) collective-permute-start(bf16[128,2048]{1,0:T(8,128)(2,1)} %pad_maximum_fusion), channel_id=1, source_target_pairs={{0,4},{1,5},{2,6},{3,7},{4,8},{5,9},{6,10},{7,11},{8,12},{9,13},{1... | collective-permute-start | bytes 1572872 | tf_op jit(solution)/shard_map/ppermute | solution.py:24
  6.2 78.1 %collective-permute-start.1 = (bf16[128,2048]{1,0:T(8,128)(2,1)}, bf16[128,2048]{1,0:T(8,128)(2,1)}, u32[]{:S(2)}, u32[]{:S(2)}) collective-permute-start(bf16[128,2048]{1,0:T(8,128)(2,1)} %pad_maximum_fusion), channel_id=1, source_target_pairs={{0,3},{1,4},{2,5},{3,6},{4,7},{5,8},{6,9},{7,10},{8,11},{9,12},{10... | collective-permute-start | bytes 1572872 | tf_op jit(solution)/shard_map/ppermute | solution.py:24
  11.7 73.7 %collective-permute-start.2 = (bf16[128,2048]{1,0:T(8,128)(2,1)}, bf16[128,2048]{1,0:T(8,128)(2,1)}, u32[]{:S(2)}, u32[]{:S(2)}) collective-permute-start(bf16[128,2048]{1,0:T(8,128)(2,1)} %pad_maximum_fusion), channel_id=1, source_target_pairs={{0,2},{1,3},{2,4},{3,5},{4,6},{5,7},{6,8},{7,9},{8,10},{9,11},{10,... | collective-permute-start | bytes 1572872 | tf_op jit(solution)/shard_map/ppermute | solution.py:24
  15.4 71.1 %collective-permute-start.3 = (bf16[128,2048]{1,0:T(8,128)(2,1)}, bf16[128,2048]{1,0:T(8,128)(2,1)}, u32[]{:S(2)}, u32[]{:S(2)}) collective-permute-start(bf16[128,2048]{1,0:T(8,128)(2,1)} %pad_maximum_fusion), channel_id=1, source_target_pairs={{0,1},{1,2},{2,3},{3,4},{4,5},{5,6},{6,7},{7,8},{8,9},{9,10},{10,1... | collective-permute-start | bytes 1572872 | tf_op jit(solution)/shard_map/ppermute | solution.py:24
  19.8 34.7 %all-to-all-start.2 = ((f32[16,128,8]{1,2,0:T(8,128)}), f32[16,128,8]{1,2,0:T(8,128)S(1)}, u32[]{:S(2)}, u32[]{:S(2)}) async-start(f32[16,128,8]{1,2,0:T(8,128)} %bitcast.12), calls=%async_computation.2 | async-start | bytes 131072 | tf_op jit(solution)/shard_map/all_to_all | solution.py:31
  23.3 35.6 %collective-permute-start.4 = (bf16[128,8192]{1,0:T(8,128)(2,1)}, bf16[128,8192]{1,0:T(8,128)(2,1)}, u32[]{:S(2)}, u32[]{:S(2)}) collective-permute-start(bf16[128,8192]{1,0:T(8,128)(2,1)} %bitcast.107), channel_id=1, source_target_pairs={{0,16},{16,32},{32,48},{48,64},{64,80},{80,96},{96,112},{1,17},{17... | collective-permute-start | bytes 6291464 | tf_op jit(solution)/shard_map/ppermute | solution.py:24
  29.1 2.9 %copy-start.10 = (s32[1,2048]{1,0:T(1,128)S(1)}, s32[1,2048]{1,0:T(1,128)}, u32[]{:S(2)}) copy-start(s32[1,2048]{1,0:T(1,128)} %param.25) | copy-start | bytes 24580
  29.7 5.9 %copy-start.11 = (f32[1,128]{1,0:T(1,128)S(1)}, f32[1,128]{1,0:T(1,128)}, u32[]{:S(2)}) copy-start(f32[1,128]{1,0:T(1,128)} %param.16) | copy-start | bytes 1540
  29.7 5.9 %copy-start.12 = (f32[1,128]{1,0:T(1,128)S(1)}, f32[1,128]{1,0:T(1,128)}, u32[]{:S(2)}) copy-start(f32[1,128]{1,0:T(1,128)} %param.17) | copy-start | bytes 1540
  32.0 26.9 %copy-start.6 = (bf16[128,8192]{1,0:T(8,128)(2,1)S(1)}, bf16[128,8192]{1,0:T(8,128)(2,1)}, u32[]{:S(2)}) copy-start(bf16[128,8192]{1,0:T(8,128)(2,1)} %param.14) | copy-start | bytes 6291460
  54.5 20.1 %all-to-all-start.1 = ((bf16[16,128,256]{2,1,0:T(8,128)(2,1)}), bf16[16,128,256]{2,1,0:T(8,128)(2,1)S(1)}, u32[]{:S(2)}, u32[]{:S(2)}) async-start(bf16[16,128,256]{2,1,0:T(8,128)(2,1)} %bitcast.8), calls=%async_computation.1 | async-start | bytes 2097152 | tf_op jit(solution)/shard_map/all_to_all | solution.py:31
  74.6 7.1 %copy-start.2 = (bf16[16,128,256]{2,1,0:T(8,128)(2,1)}, bf16[16,128,256]{2,1,0:T(8,128)(2,1)S(1)}, u32[]{:S(2)}) copy-start(bf16[16,128,256]{2,1,0:T(8,128)(2,1)S(1)} %all-to-all-done.1) | copy-start | bytes 3145732
  74.7 33.3 %all-to-all-start = ((bf16[16,128,512]{2,1,0:T(8,128)(2,1)}), bf16[16,128,512]{2,1,0:T(8,128)(2,1)}, u32[]{:S(2)}, u32[]{:S(2)}) async-start(bf16[16,128,512]{2,1,0:T(8,128)(2,1)} %bitcast.66), calls=%async_computation | async-start | bytes 4194304 | tf_op jit(solution)/shard_map/all_to_all | solution.py:31
  79.2 7.3 %copy-start.7 = (f32[16,128,8]{1,2,0:T(8,128)}, f32[16,128,8]{1,2,0:T(8,128)S(1)}, u32[]{:S(2)}) copy-start(f32[16,128,8]{1,2,0:T(8,128)S(1)} %get-tuple-element.14) | copy-start | bytes 196612
  83.1 4.5 %copy-start.3 = (bf16[16,128,256]{2,1,0:T(8,128)(2,1)S(1)}, bf16[16,128,256]{2,1,0:T(8,128)(2,1)}, u32[]{:S(2)}) copy-start(bf16[16,128,256]{2,1,0:T(8,128)(2,1)} %copy-done.2) | copy-start | bytes 3145732
  108.7 36.8 %copy-start.8 = (bf16[1,128,1024]{2,1,0:T(8,128)(2,1)S(1)}, bf16[1,128,1024]{2,1,0:T(8,128)(2,1)}, u32[]{:S(2)}) copy-start(bf16[1,128,1024]{2,1,0:T(8,128)(2,1)} %param.24) | copy-start | bytes 786436
  108.7 36.8 %copy-start.9 = (bf16[1,128,1024]{2,1,0:T(8,128)(2,1)S(1)}, bf16[1,128,1024]{2,1,0:T(8,128)(2,1)}, u32[]{:S(2)}) copy-start(bf16[1,128,1024]{2,1,0:T(8,128)(2,1)} %param.23) | copy-start | bytes 786436
  141.9 20.4 %all-to-all-start.3 = ((f32[16,1,2048]{2,1,0:T(1,128)}), f32[16,1,2048]{2,1,0:T(1,128)S(1)}, u32[]{:S(2)}, u32[]{:S(2)}) async-start(f32[16,1,2048]{2,1,0:T(1,128)} %broadcast_in_dim.11), calls=%async_computation.3 | async-start | bytes 262144 | tf_op jit(solution)/shard_map/all_to_all | solution.py:238
  145.5 1.5 copy-start.1
  167.3 37.2 %all-to-all-start.4 = ((bf16[16,128,512]{2,1,0:T(8,128)(2,1)}), bf16[16,128,512]{2,1,0:T(8,128)(2,1)S(1)}, u32[]{:S(2)}, u32[]{:S(2)}) async-start(bf16[16,128,512]{2,1,0:T(8,128)(2,1)} %bitcast.77), calls=%async_computation.4 | async-start | bytes 4194304 | tf_op jit(solution)/shard_map/all_to_all | solution.py:38
  209.5 5.1 %copy-start.4 = (bf16[128,4096]{1,0:T(8,128)(2,1)S(1)}, bf16[128,4096]{1,0:T(8,128)(2,1)}, u32[]{:S(2)}) copy-start(bf16[128,4096]{1,0:T(8,128)(2,1)} %shard_map.127) | copy-start | bytes 3145732
  209.5 5.1 %copy-start.5 = (bf16[128,4096]{1,0:T(8,128)(2,1)S(1)}, bf16[128,4096]{1,0:T(8,128)(2,1)}, u32[]{:S(2)}) copy-start(bf16[128,4096]{1,0:T(8,128)(2,1)} %shard_map.129) | copy-start | bytes 3145732

commit v16 on v11

--- a/solution.py
+++ b/solution.py
@@ -208,9 +208,12 @@
     bc = jnp.stack(
         [b_in[0].reshape(tok_rows, GROUPS, STATE), c_in[0].reshape(tok_rows, GROUPS, STATE)], axis=2
     )
-    bc_h = to_heads(jnp.repeat(bc, rep, axis=1).reshape(tok_rows, nctx * 2 * STATE), nctx)
-    b_g, c_g = bc_h[:, :STATE], bc_h[:, STATE:]
-    dt_h = to_heads(dt_raw[0], nctx)
+    bc_rows = jnp.repeat(bc, rep, axis=1).reshape(tok_rows, nctx, 2 * STATE).astype(jnp.float32)
+    dt_rows = dt_raw[0].reshape(tok_rows, nctx, heads_dev)
+    side = to_heads(jnp.concatenate([bc_rows, dt_rows], axis=2).reshape(tok_rows, -1), nctx)
+    b_g = side[:, :STATE].astype(jnp.bfloat16)
+    c_g = side[:, STATE:2 * STATE].astype(jnp.bfloat16)
+    dt_h = side[:, 2 * STATE:]
 
     handed = shifted(previous[0], "section", 1)
     stream = jnp.where(lax.axis_index("section") == 0, fresh, handed)

time: 203 us -> 215 us (1.059)
  waiting for transfers between devices: 56.7 us -> 69.1 us
  other arithmetic: 16.7 us -> 20.9 us
  starting transfers between devices: 36.8 us -> 34.4 us
    ppermute x5, waiting for transfers between devices: 0.01 us -> 36.8 us  [shifted(): return lax.ppermute(value, axis, pairs)]
    all_to_all x3 -> x2, waiting for transfers between devices: 49.5 us -> 25 us  [to_heads(): moved = lax.all_to_all(lead, 'ctx', split_axis=0, concat_axis=0, tiled=True)]
    all_to_all x3 -> x2, starting transfers between devices: 10.9 us -> 8.43 us  [to_heads(): moved = lax.all_to_all(lead, 'ctx', split_axis=0, concat_axis=0, tiled=True)]
    mul x1, other arithmetic: 0.12 us -> 2.34 us  [mixer_heads(): log_rate = -step * jnp.exp(alog_h)[None, :]]
    all_to_all x0 -> x1, local copies, waits for them, and re-layouts: none -> 2.2 us  [to_heads(): moved = lax.all_to_all(lead, 'ctx', split_axis=0, concat_axis=0, tiled=True)]
    unnamed x32 -> x36, local copies, waits for them, and re-layouts: 13.1 us -> 11.4 us
  transfers between devices with their start and end apart: 10 -> 9, of which waited for: 4 -> 4; matrix products, arithmetic and copies ran while one was open for 16% -> 16% of each run, Pallas kernels for 14% -> 13%
where the time goes in v16:
time: 215 us; the launch traced here: 214 us
  waiting for transfers between devices  69.1 us (32%)
  Pallas kernels  59.6 us (28%)
  starting transfers between devices  34.4 us (16%)
  local copies, waits for them, and re-layouts  29.5 us (14%)
  other arithmetic  20.9 us (10%)
    ppermute x5, waiting for transfers between devices, shifted(): return lax.ppermute(value, axis, pairs)  36.8 us
    pallas_call x1, Pallas kernels, mixer_heads(): pl.pallas_call(kernel, grid=(nblk,), in_specs=[pl.BlockSpec((BLOCK, x_wid...  30.9 us
    pallas_call x1, Pallas kernels, attend_rows(): pl.pallas_call(kernel, grid=(kv_heads,), in_specs=[pl.BlockSpec((tok_rows...  28.7 us
    all_to_all x2, waiting for transfers between devices, to_heads(): moved = lax.all_to_all(lead, 'ctx', split_axis=0, concat_axis=0, tiled=True)  25 us
    ppermute x5, starting transfers between devices, shifted(): return lax.ppermute(value, axis, pairs)  18.6 us
    unnamed x36, local copies, waits for them, and re-layouts  11.4 us
    all_to_all x2, starting transfers between devices, to_heads(): moved = lax.all_to_all(lead, 'ctx', split_axis=0, concat_axis=0, tiled=True)  8.43 us
    all_to_all x1, waiting for transfers between devices, body(): lax.all_to_all(jnp.broadcast_to(sq_part[:, 0][None], (nctx, total)), 'ctx...  7.29 us
  transfers between devices with their start and end apart: 9, of which 4 were waited for; matrix products, arithmetic and copies ran while one was open for 16% of the time, Pallas kernels for 13%

profile of v16, /device:TPU:32, one launch (start us, length us, event | category | flops | bytes accessed | tf_op | source)
XLA Modules:
  0.0 213.8 jit_solution(9652768434914453574)
XLA Ops:
  1.1 3.4 %collective-permute-start.3 = (bf16[128,2048]{1,0:T(8,128)(2,1)S(1)}, bf16[128,2048]{1,0:T(8,128)(2,1)S(1)}, u32[]{:S(2)}, u32[]{:S(2)}) collective-permute-start(bf16[128,2048]{1,0:T(8,128)(2,1)S(1)} %pad_maximum_fusion), channel_id=1, source_target_pairs={{0,1},{1,2},{2,3},{3,4},{4,5},{5,6},{6,7},{7,8},{8,9},{9,10},{10,1... | collective-permute-start | bytes 1572872 | tf_op jit(solution)/shard_map/ppermute | solution.py:24
  4.5 5.4 %collective-permute-start.2 = (bf16[128,2048]{1,0:T(8,128)(2,1)S(1)}, bf16[128,2048]{1,0:T(8,128)(2,1)}, u32[]{:S(2)}, u32[]{:S(2)}) collective-permute-start(bf16[128,2048]{1,0:T(8,128)(2,1)S(1)} %pad_maximum_fusion), channel_id=1, source_target_pairs={{0,2},{1,3},{2,4},{3,5},{4,6},{5,7},{6,8},{7,9},{8,10},{9,11},{10,... | collective-permute-start | bytes 1572872 | tf_op jit(solution)/shard_map/ppermute | solution.py:24
  9.9 4.3 %collective-permute-start.1 = (bf16[128,2048]{1,0:T(8,128)(2,1)S(1)}, bf16[128,2048]{1,0:T(8,128)(2,1)}, u32[]{:S(2)}, u32[]{:S(2)}) collective-permute-start(bf16[128,2048]{1,0:T(8,128)(2,1)S(1)} %pad_maximum_fusion), channel_id=1, source_target_pairs={{0,3},{1,4},{2,5},{3,6},{4,7},{5,8},{6,9},{7,10},{8,11},{9,12},{10... | collective-permute-start | bytes 1572872 | tf_op jit(solution)/shard_map/ppermute | solution.py:24
  14.3 3.5 %collective-permute-start = (bf16[128,2048]{1,0:T(8,128)(2,1)S(1)}, bf16[128,2048]{1,0:T(8,128)(2,1)}, u32[]{:S(2)}, u32[]{:S(2)}) collective-permute-start(bf16[128,2048]{1,0:T(8,128)(2,1)S(1)} %pad_maximum_fusion), channel_id=1, source_target_pairs={{0,4},{1,5},{2,6},{3,7},{4,8},{5,9},{6,10},{7,11},{8,12},{9,13},{1... | collective-permute-start | bytes 1572872 | tf_op jit(solution)/shard_map/ppermute | solution.py:24
  23.0 4.6 %all-to-all-start.1 = ((f32[16,128,264]{1,2,0:T(8,128)}), f32[16,128,264]{1,2,0:T(8,128)}, u32[]{:S(2)}, u32[]{:S(2)}) async-start(f32[16,128,264]{1,2,0:T(8,128)} %maximum_bitcast_fusion), calls=%async_computation.1 | async-start | bytes 4325376 | tf_op jit(solution)/shard_map/all_to_all | solution.py:31
  27.6 1.9 collective-permute-start.4
  32.2 36.8 %collective-permute-done = bf16[128,2048]{1,0:T(8,128)(2,1)} collective-permute-done((bf16[128,2048]{1,0:T(8,128)(2,1)S(1)}, bf16[128,2048]{1,0:T(8,128)(2,1)}, u32[]{:S(2)}, u32[]{:S(2)}) %collective-permute-start) | collective-permute-done | bytes 524320 | tf_op jit(solution)/shard_map/ppermute | solution.py:24
  69.0 1.9 constant_dynamic-update-slice_fusion.4
  70.9 1.9 constant_dynamic-update-slice_fusion.3
  72.8 1.9 constant_dynamic-update-slice_fusion.2
  78.2 2.2 %copy.104 = f32[16,128,264]{2,1,0:T(8,128)S(1)} copy(f32[16,128,264]{1,2,0:T(8,128)} %all-to-all-done.1) | data formatting | bytes 4325376 | tf_op jit(solution)/shard_map/all_to_all | solution.py:31
  80.4 2.3 %negate_multiply_fusion = (f32[2048,8]{1,0:T(8,128)}, f32[2048,8]{1,0:T(8,128)}) fusion(f32[8]{0:T(128)S(1)} %get-tuple-element.26, f32[8]{0:T(128)S(1)} %get-tuple-element.25, f32[2048,264]{1,0:T(8,128)S(1)} %bitcast.87), kind=kLoop, calls=%fused_computation.9 | loop fusion | flops 147456 | bytes 196672 | tf_op jit(solution)/shard_map/mul | solution.py:48
  84.8 1.8 broadcast_select_fusion
  88.1 3.8 %all-to-all-start = ((bf16[16,128,512]{2,1,0:T(8,128)(2,1)}), bf16[16,128,512]{2,1,0:T(8,128)(2,1)S(1)}, u32[]{:S(2)}, u32[]{:S(2)}) async-start(bf16[16,128,512]{2,1,0:T(8,128)(2,1)} %bitcast.90), calls=%async_computation | async-start | bytes 4194304 | tf_op jit(solution)/shard_map/all_to_all | solution.py:31
  93.9 2.1 bitcast_convert_fusion
  97.1 2.1 copy.114.b_ref
  101.7 23.2 %all-to-all-done = bf16[16,128,512]{2,1,0:T(8,128)(2,1)S(1)} async-done(((bf16[16,128,512]{2,1,0:T(8,128)(2,1)}), bf16[16,128,512]{2,1,0:T(8,128)(2,1)S(1)}, u32[]{:S(2)}, u32[]{:S(2)}) %all-to-all-start) | async-done | bytes 2097184 | tf_op jit(solution)/shard_map/all_to_all | solution.py:31
  126.2 30.9 %shard_map.127 = (f32[2048,512]{1,0:T(8,128)}, f32[2048,1]{1,0:T(8,128)}) custom-call(bf16[2048,512]{1,0:T(8,128)(2,1)} %bitcast.85, bf16[128,2048]{1,0:T(8,128)(2,1)} %copy.114.b_ref, bf16[2048,128]{1,0:T(8,128)(2,1)} %get-tuple-element.17.c_ref, f32[16,128,8]{2,1,0:T(8,128)} %copy.115.lcc_ref, f32[16,8,128]{2,1,0:T(8,128)} %bitcast.96, ...), custom_call_target="tpu_custom_call" | custom-call | tf_op jit(solution)/shard_map/pallas_call | solution.py:106
  159.4 3.5 %all-to-all-start.2 = ((f32[16,1,2048]{2,1,0:T(1,128)}), f32[16,1,2048]{2,1,0:T(1,128)S(1)}, u32[]{:S(2)}, u32[]{:S(2)}) async-start(f32[16,1,2048]{2,1,0:T(1,128)} %broadcast_in_dim.13), calls=%async_computation.2 | async-start | bytes 262144 | tf_op jit(solution)/shard_map/all_to_all | solution.py:239
  163.6 7.3 %all-to-all-done.2 = f32[16,1,2048]{2,1,0:T(1,128)S(1)} async-done(((f32[16,1,2048]{2,1,0:T(1,128)}), f32[16,1,2048]{2,1,0:T(1,128)S(1)}, u32[]{:S(2)}, u32[]{:S(2)}) %all-to-all-start.2) | async-done | bytes 131104 | tf_op jit(solution)/shard_map/all_to_all | solution.py:239
  171.0 4.9 %add_convert_fusion.1 = bf16[2048,512]{1,0:T(8,128)(2,1)} fusion(f32[2048,512]{1,0:T(8,128)} %get-tuple-element.10, bf16[2048,512]{1,0:T(8,128)(2,1)} %bitcast.86, f32[512]{0:T(512)S(1)} %bitcast.120, f32[2048]{0:T(1024)S(1)} %add_rsqrt_fusion), kind=kLoop, calls=%fused_computation.2 | loop fusion | flops 5242880 | bytes 8398848 | tf_op jit(solution)/shard_map/convert_element_type | solution.py:246
  175.9 3.9 %all-to-all-start.3 = ((bf16[16,128,512]{2,1,0:T(8,128)(2,1)}), bf16[16,128,512]{2,1,0:T(8,128)(2,1)S(1)}, u32[]{:S(2)}, u32[]{:S(2)}) async-start(bf16[16,128,512]{2,1,0:T(8,128)(2,1)} %bitcast.92), calls=%async_computation.3 | async-start | bytes 4194304 | tf_op jit(solution)/shard_map/all_to_all | solution.py:38
  181.2 28.7 %shard_map.128 = bf16[128,8192]{1,0:T(8,128)(2,1)} custom-call(bf16[128,8192]{1,0:T(8,128)(2,1)} %bitcast.93, bf16[640,2048]{1,0:T(8,128)(2,1)} %constant_dynamic-update-slice_fusion.k_ref.v_ref, bf16[640,2048]{1,0:T(8,128)(2,1)} %constant_dynamic-update-slice_fusion.k_ref.v_ref, s32[128,1]{1,0:T(8,128)} %copy.120.iq_ref, s32[1,640]{1,0:T(1,128)} %reshape.145.ik_ref), custom_call_target="tpu_custom_call" | custom-call | tf_op jit(solution)/shard_map/pallas_call | solution.py:165
  212.0 1.8 fusion
  (84 shorter events, 29.4 us)
Async XLA Ops:
  0.0 30.2 %copy-start = (f32[1,128]{1,0:T(1,128)S(1)}, f32[1,128]{1,0:T(1,128)}, u32[]{:S(2)}) copy-start(f32[1,128]{1,0:T(1,128)} %param.20) | copy-start | bytes 1540
  1.1 73.6 %collective-permute-start.3 = (bf16[128,2048]{1,0:T(8,128)(2,1)S(1)}, bf16[128,2048]{1,0:T(8,128)(2,1)S(1)}, u32[]{:S(2)}, u32[]{:S(2)}) collective-permute-start(bf16[128,2048]{1,0:T(8,128)(2,1)S(1)} %pad_maximum_fusion), channel_id=1, source_target_pairs={{0,1},{1,2},{2,3},{3,4},{4,5},{5,6},{6,7},{7,8},{8,9},{9,10},{10,1... | collective-permute-start | bytes 1572872 | tf_op jit(solution)/shard_map/ppermute | solution.py:24
  4.5 68.3 %collective-permute-start.2 = (bf16[128,2048]{1,0:T(8,128)(2,1)S(1)}, bf16[128,2048]{1,0:T(8,128)(2,1)}, u32[]{:S(2)}, u32[]{:S(2)}) collective-permute-start(bf16[128,2048]{1,0:T(8,128)(2,1)S(1)} %pad_maximum_fusion), channel_id=1, source_target_pairs={{0,2},{1,3},{2,4},{3,5},{4,6},{5,7},{6,8},{7,9},{8,10},{9,11},{10,... | collective-permute-start | bytes 1572872 | tf_op jit(solution)/shard_map/ppermute | solution.py:24
  9.9 61.0 %collective-permute-start.1 = (bf16[128,2048]{1,0:T(8,128)(2,1)S(1)}, bf16[128,2048]{1,0:T(8,128)(2,1)}, u32[]{:S(2)}, u32[]{:S(2)}) collective-permute-start(bf16[128,2048]{1,0:T(8,128)(2,1)S(1)} %pad_maximum_fusion), channel_id=1, source_target_pairs={{0,3},{1,4},{2,5},{3,6},{4,7},{5,8},{6,9},{7,10},{8,11},{9,12},{10... | collective-permute-start | bytes 1572872 | tf_op jit(solution)/shard_map/ppermute | solution.py:24
  14.3 54.7 %collective-permute-start = (bf16[128,2048]{1,0:T(8,128)(2,1)S(1)}, bf16[128,2048]{1,0:T(8,128)(2,1)}, u32[]{:S(2)}, u32[]{:S(2)}) collective-permute-start(bf16[128,2048]{1,0:T(8,128)(2,1)S(1)} %pad_maximum_fusion), channel_id=1, source_target_pairs={{0,4},{1,5},{2,6},{3,7},{4,8},{5,9},{6,10},{7,11},{8,12},{9,13},{1... | collective-permute-start | bytes 1572872 | tf_op jit(solution)/shard_map/ppermute | solution.py:24
  23.0 6.5 %copy-start.9 = (s32[1,2048]{1,0:T(1,128)S(1)}, s32[1,2048]{1,0:T(1,128)}, u32[]{:S(2)}) copy-start(s32[1,2048]{1,0:T(1,128)} %param.25) | copy-start | bytes 24580
  23.0 7.0 %copy-start.11 = (f32[1,128]{1,0:T(1,128)S(1)}, f32[1,128]{1,0:T(1,128)}, u32[]{:S(2)}) copy-start(f32[1,128]{1,0:T(1,128)} %param.16) | copy-start | bytes 1540
  23.0 7.0 %copy-start.12 = (f32[1,128]{1,0:T(1,128)S(1)}, f32[1,128]{1,0:T(1,128)}, u32[]{:S(2)}) copy-start(f32[1,128]{1,0:T(1,128)} %param.17) | copy-start | bytes 1540
  23.0 55.2 %all-to-all-start.1 = ((f32[16,128,264]{1,2,0:T(8,128)}), f32[16,128,264]{1,2,0:T(8,128)}, u32[]{:S(2)}, u32[]{:S(2)}) async-start(f32[16,128,264]{1,2,0:T(8,128)} %maximum_bitcast_fusion), calls=%async_computation.1 | async-start | bytes 4325376 | tf_op jit(solution)/shard_map/all_to_all | solution.py:31
  27.6 57.2 %collective-permute-start.4 = (bf16[128,8192]{1,0:T(8,128)(2,1)}, bf16[128,8192]{1,0:T(8,128)(2,1)}, u32[]{:S(2)}, u32[]{:S(2)}) collective-permute-start(bf16[128,8192]{1,0:T(8,128)(2,1)} %bitcast.2), channel_id=1, source_target_pairs={{0,16},{16,32},{32,48},{48,64},{64,80},{80,96},{96,112},{1,17},{17... | collective-permute-start | bytes 6291464 | tf_op jit(solution)/shard_map/ppermute | solution.py:24
  30.9 44.7 %copy-start.6 = (bf16[1,128,1024]{2,1,0:T(8,128)(2,1)S(1)}, bf16[1,128,1024]{2,1,0:T(8,128)(2,1)}, u32[]{:S(2)}) copy-start(bf16[1,128,1024]{2,1,0:T(8,128)(2,1)} %param.24) | copy-start | bytes 786436
  30.9 44.7 %copy-start.7 = (bf16[1,128,1024]{2,1,0:T(8,128)(2,1)S(1)}, bf16[1,128,1024]{2,1,0:T(8,128)(2,1)}, u32[]{:S(2)}) copy-start(bf16[1,128,1024]{2,1,0:T(8,128)(2,1)} %param.23) | copy-start | bytes 786436
  80.4 4.4 %copy-start.2 = (f32[16,128,264]{2,1,0:T(8,128)}, f32[16,128,264]{2,1,0:T(8,128)S(1)}, u32[]{:S(2)}) copy-start(f32[16,128,264]{2,1,0:T(8,128)S(1)} %copy.104) | copy-start | bytes 6488068
  88.1 36.7 %all-to-all-start = ((bf16[16,128,512]{2,1,0:T(8,128)(2,1)}), bf16[16,128,512]{2,1,0:T(8,128)(2,1)S(1)}, u32[]{:S(2)}, u32[]{:S(2)}) async-start(bf16[16,128,512]{2,1,0:T(8,128)(2,1)} %bitcast.90), calls=%async_computation | async-start | bytes 4194304 | tf_op jit(solution)/shard_map/all_to_all | solution.py:31
  92.2 8.8 %copy-start.5 = (f32[16,128,8]{1,2,0:T(8,128)}, f32[16,128,8]{1,2,0:T(8,128)S(1)}, u32[]{:S(2)}) copy-start(f32[16,128,8]{1,2,0:T(8,128)S(1)} %get-tuple-element.14) | copy-start | bytes 196612
  96.0 3.2 %copy-start.4 = (f32[2048,8]{1,0:T(8,128)S(1)}, f32[2048,8]{1,0:T(8,128)}, u32[]{:S(2)}) copy-start(f32[2048,8]{1,0:T(8,128)} %get-tuple-element.16) | copy-start | bytes 196612
  99.4 26.2 %copy-start.8 = (f32[2048,8]{0,1:T(8,128)}, f32[2048,8]{0,1:T(8,128)S(1)}, u32[]{:S(2)}) copy-start(f32[2048,8]{0,1:T(8,128)S(1)} %copy.107) | copy-start | bytes 196612
  124.9 1.3 copy-start.1
  159.4 11.5 %all-to-all-start.2 = ((f32[16,1,2048]{2,1,0:T(1,128)}), f32[16,1,2048]{2,1,0:T(1,128)S(1)}, u32[]{:S(2)}, u32[]{:S(2)}) async-start(f32[16,1,2048]{2,1,0:T(1,128)} %broadcast_in_dim.13), calls=%async_computation.2 | async-start | bytes 262144 | tf_op jit(solution)/shard_map/all_to_all | solution.py:239
  175.9 3.9 %copy-start.10 = (s32[1,2048]{1,0:T(1,128)S(1)}, s32[1,2048]{1,0:T(1,128)}, u32[]{:S(2)}) copy-start(s32[1,2048]{1,0:T(1,128)} %param.25) | copy-start | bytes 24580
  175.9 34.0 %all-to-all-start.3 = ((bf16[16,128,512]{2,1,0:T(8,128)(2,1)}), bf16[16,128,512]{2,1,0:T(8,128)(2,1)S(1)}, u32[]{:S(2)}, u32[]{:S(2)}) async-start(bf16[16,128,512]{2,1,0:T(8,128)(2,1)} %bitcast.92), calls=%async_computation.3 | async-start | bytes 4194304 | tf_op jit(solution)/shard_map/all_to_all | solution.py:38
  210.5 1.6 copy-start.3

commit v17 on v11

--- a/solution.py
+++ b/solution.py
@@ -143,15 +143,17 @@
     kv_heads = kv_win.shape[1] // (2 * HEAD_A)
     group = q_width // HEAD_A // kv_heads
     lead = window - tok_rows
+    pair = 2 if kv_heads % 2 == 0 else 1
     inv_sqrt = 1.0 / math.sqrt(HEAD_A)
 
     def kernel(q_ref, k_ref, v_ref, iq_ref, ik_ref, o_ref):
         q_at = lead + lax.broadcasted_iota(jnp.int32, (tok_rows, window), 0)
         k_at = lax.broadcasted_iota(jnp.int32, (tok_rows, window), 1)
         allowed = (iq_ref[...] == ik_ref[...]) & (q_at >= k_at)
-        kb = k_ref[...]
-        vb = v_ref[...]
-        for g in range(group):
+        for g in range(pair * group):
+            kv_cols = slice((g // group) * HEAD_A, (g // group + 1) * HEAD_A)
+            kb = k_ref[:, kv_cols]
+            vb = v_ref[:, kv_cols]
             cols = slice(g * HEAD_A, (g + 1) * HEAD_A)
             logits = lax.dot_general(
                 q_ref[:, cols], kb, (((1,), (1,)), ((), ())), preferred_element_type=jnp.float32
@@ -164,15 +166,15 @@
 
     return pl.pallas_call(
         kernel,
-        grid=(kv_heads,),
+        grid=(kv_heads // pair,),
         in_specs=[
-            pl.BlockSpec((tok_rows, group * HEAD_A), lambda i: (0, i)),
-            pl.BlockSpec((window, HEAD_A), lambda i: (0, i)),
-            pl.BlockSpec((window, HEAD_A), lambda i: (0, kv_heads + i)),
+            pl.BlockSpec((tok_rows, pair * group * HEAD_A), lambda i: (0, i)),
+            pl.BlockSpec((window, pair * HEAD_A), lambda i: (0, i)),
+            pl.BlockSpec((window, pair * HEAD_A), lambda i: (0, kv_heads // pair + i)),
             pl.BlockSpec((tok_rows, 1), lambda i: (0, 0)),
             pl.BlockSpec((1, window), lambda i: (0, 0)),
         ],
-        out_specs=pl.BlockSpec((tok_rows, group * HEAD_A), lambda i: (0, i)),
+        out_specs=pl.BlockSpec((tok_rows, pair * group * HEAD_A), lambda i: (0, i)),
         out_shape=jax.ShapeDtypeStruct((tok_rows, q_width), jnp.bfloat16),
         interpret=interpret,
     )(q_row, kv_win, kv_win, ids_q, ids_k)

time: 203 us -> 202 us (level)
  transfers between devices with their start and end apart: 10 -> 10, of which waited for: 4 -> 4; matrix products, arithmetic and copies ran while one was open for 16% -> 17% of each run, Pallas kernels for 14% -> 14%
where the time goes in v17:
time: 202 us; the launch traced here: 200 us
  Pallas kernels  58.8 us (29%)
  waiting for transfers between devices  56.7 us (28%)
  starting transfers between devices  37 us (18%)
  local copies, waits for them, and re-layouts  30.8 us (15%)
  other arithmetic  16.7 us (8%)
    all_to_all x3, waiting for transfers between devices, to_heads(): moved = lax.all_to_all(lead, 'ctx', split_axis=0, concat_axis=0, tiled=True)  49.5 us
    pallas_call x1, Pallas kernels, mixer_heads(): pl.pallas_call(kernel, grid=(nblk,), in_specs=[pl.BlockSpec((BLOCK, x_wid...  30.9 us
    pallas_call x1, Pallas kernels, attend_rows(): pl.pallas_call(kernel, grid=(kv_heads // pair,), in_specs=[pl.BlockSpec((...  27.9 us
    ppermute x5, starting transfers between devices, shifted(): return lax.ppermute(value, axis, pairs)  18.6 us
    unnamed x32, local copies, waits for them, and re-layouts  13.1 us
    all_to_all x3, starting transfers between devices, to_heads(): moved = lax.all_to_all(lead, 'ctx', split_axis=0, concat_axis=0, tiled=True)  10.9 us
    all_to_all x1, waiting for transfers between devices, body(): lax.all_to_all(jnp.broadcast_to(sq_part[:, 0][None], (nctx, total)), 'ctx...  7.26 us
    convert_element_type x1, other arithmetic, body(): mixed = (x_h.astype(jnp.float32) + mixer_out * inv_rms * gain_h.astype(jn...  4.87 us
  transfers between devices with their start and end apart: 10, of which 4 were waited for; matrix products, arithmetic and copies ran while one was open for 17% of the time, Pallas kernels for 14%

profile of v17, /device:TPU:32, one launch (start us, length us, event | category | flops | bytes accessed | tf_op | source)
XLA Modules:
  0.0 200.4 jit_solution(13308921020342815459)
XLA Ops:
  0.0 1.9 pad_maximum_fusion
  1.9 4.2 %collective-permute-start.3 = (bf16[128,2048]{1,0:T(8,128)(2,1)}, bf16[128,2048]{1,0:T(8,128)(2,1)}, u32[]{:S(2)}, u32[]{:S(2)}) collective-permute-start(bf16[128,2048]{1,0:T(8,128)(2,1)} %pad_maximum_fusion), channel_id=1, source_target_pairs={{0,1},{1,2},{2,3},{3,4},{4,5},{5,6},{6,7},{7,8},{8,9},{9,10},{10,1... | collective-permute-start | bytes 1572872 | tf_op jit(solution)/shard_map/ppermute | solution.py:24
  6.1 4.7 %collective-permute-start.2 = (bf16[128,2048]{1,0:T(8,128)(2,1)}, bf16[128,2048]{1,0:T(8,128)(2,1)}, u32[]{:S(2)}, u32[]{:S(2)}) collective-permute-start(bf16[128,2048]{1,0:T(8,128)(2,1)} %pad_maximum_fusion), channel_id=1, source_target_pairs={{0,2},{1,3},{2,4},{3,5},{4,6},{5,7},{6,8},{7,9},{8,10},{9,11},{10,... | collective-permute-start | bytes 1572872 | tf_op jit(solution)/shard_map/ppermute | solution.py:24
  10.7 4.4 %collective-permute-start.1 = (bf16[128,2048]{1,0:T(8,128)(2,1)}, bf16[128,2048]{1,0:T(8,128)(2,1)}, u32[]{:S(2)}, u32[]{:S(2)}) collective-permute-start(bf16[128,2048]{1,0:T(8,128)(2,1)} %pad_maximum_fusion), channel_id=1, source_target_pairs={{0,3},{1,4},{2,5},{3,6},{4,7},{5,8},{6,9},{7,10},{8,11},{9,12},{10... | collective-permute-start | bytes 1572872 | tf_op jit(solution)/shard_map/ppermute | solution.py:24
  15.1 3.5 %collective-permute-start = (bf16[128,2048]{1,0:T(8,128)(2,1)}, bf16[128,2048]{1,0:T(8,128)(2,1)}, u32[]{:S(2)}, u32[]{:S(2)}) collective-permute-start(bf16[128,2048]{1,0:T(8,128)(2,1)} %pad_maximum_fusion), channel_id=1, source_target_pairs={{0,4},{1,5},{2,6},{3,7},{4,8},{5,9},{6,10},{7,11},{8,12},{9,13},{1... | collective-permute-start | bytes 1572872 | tf_op jit(solution)/shard_map/ppermute | solution.py:24
  20.1 3.5 %all-to-all-start.2 = ((f32[16,128,8]{1,2,0:T(8,128)}), f32[16,128,8]{1,2,0:T(8,128)S(1)}, u32[]{:S(2)}, u32[]{:S(2)}) async-start(f32[16,128,8]{1,2,0:T(8,128)} %bitcast.9), calls=%async_computation.2 | async-start | bytes 131072 | tf_op jit(solution)/shard_map/all_to_all | solution.py:31
  23.6 1.9 collective-permute-start.4
  35.4 21.2 %all-to-all-done.2 = f32[16,128,8]{1,2,0:T(8,128)S(1)} async-done(((f32[16,128,8]{1,2,0:T(8,128)}), f32[16,128,8]{1,2,0:T(8,128)S(1)}, u32[]{:S(2)}, u32[]{:S(2)}) %all-to-all-start.2) | async-done | bytes 65568 | tf_op jit(solution)/shard_map/all_to_all | solution.py:31
  56.6 3.7 %all-to-all-start.1 = ((bf16[16,128,256]{2,1,0:T(8,128)(2,1)}), bf16[16,128,256]{2,1,0:T(8,128)(2,1)S(1)}, u32[]{:S(2)}, u32[]{:S(2)}) async-start(bf16[16,128,256]{2,1,0:T(8,128)(2,1)} %bitcast.5), calls=%async_computation.1 | async-start | bytes 2097152 | tf_op jit(solution)/shard_map/all_to_all | solution.py:31
  61.3 1.8 broadcast_select_fusion
  64.7 13.3 %all-to-all-done.1 = bf16[16,128,256]{2,1,0:T(8,128)(2,1)S(1)} async-done(((bf16[16,128,256]{2,1,0:T(8,128)(2,1)}), bf16[16,128,256]{2,1,0:T(8,128)(2,1)S(1)}, u32[]{:S(2)}, u32[]{:S(2)}) %all-to-all-start.1) | async-done | bytes 1048608 | tf_op jit(solution)/shard_map/all_to_all | solution.py:31
  78.0 3.7 %all-to-all-start = ((bf16[16,128,512]{2,1,0:T(8,128)(2,1)}), bf16[16,128,512]{2,1,0:T(8,128)(2,1)S(1)}, u32[]{:S(2)}, u32[]{:S(2)}) async-start(bf16[16,128,512]{2,1,0:T(8,128)(2,1)} %bitcast.80), calls=%async_computation | async-start | bytes 4194304 | tf_op jit(solution)/shard_map/all_to_all | solution.py:31
  85.4 1.9 constant_dynamic-update-slice_fusion.4
  87.4 1.9 constant_dynamic-update-slice_fusion.3
  89.3 1.9 constant_dynamic-update-slice_fusion.2
  91.2 1.9 constant_dynamic-update-slice_fusion.1
  95.0 2.0 %copy.82.b_ref = bf16[128,2048]{1,0:T(8,128)(2,1)} copy(bf16[128,2048]{0,1:T(8,128)(2,1)} %get-tuple-element.16) | data formatting | bytes 1048576 | tf_op jit(solution)/shard_map/transpose | solution.py:69
  97.1 15.0 %all-to-all-done = bf16[16,128,512]{2,1,0:T(8,128)(2,1)S(1)} async-done(((bf16[16,128,512]{2,1,0:T(8,128)(2,1)}), bf16[16,128,512]{2,1,0:T(8,128)(2,1)S(1)}, u32[]{:S(2)}, u32[]{:S(2)}) %all-to-all-start) | async-done | bytes 2097184 | tf_op jit(solution)/shard_map/all_to_all | solution.py:31
  113.4 30.9 %shard_map.127 = (f32[2048,512]{1,0:T(8,128)}, f32[2048,1]{1,0:T(8,128)}) custom-call(bf16[2048,512]{1,0:T(8,128)(2,1)} %bitcast.76, bf16[128,2048]{1,0:T(8,128)(2,1)} %copy.82.b_ref, bf16[2048,128]{1,0:T(8,128)(2,1)} %get-tuple-element.15.c_ref, f32[16,128,8]{2,1,0:T(8,128)} %copy.83.lcc_ref, f32[16,8,128]{2,1,0:T(8,128)} %bitcast.84, ...), custom_call_target="tpu_custom_call" | custom-call | tf_op jit(solution)/shard_map/pallas_call | solution.py:106
  146.6 3.5 %all-to-all-start.3 = ((f32[16,1,2048]{2,1,0:T(1,128)}), f32[16,1,2048]{2,1,0:T(1,128)S(1)}, u32[]{:S(2)}, u32[]{:S(2)}) async-start(f32[16,1,2048]{2,1,0:T(1,128)} %broadcast_in_dim.13), calls=%async_computation.3 | async-start | bytes 262144 | tf_op jit(solution)/shard_map/all_to_all | solution.py:238
  150.8 7.3 %all-to-all-done.3 = f32[16,1,2048]{2,1,0:T(1,128)S(1)} async-done(((f32[16,1,2048]{2,1,0:T(1,128)}), f32[16,1,2048]{2,1,0:T(1,128)S(1)}, u32[]{:S(2)}, u32[]{:S(2)}) %all-to-all-start.3) | async-done | bytes 131104 | tf_op jit(solution)/shard_map/all_to_all | solution.py:238
  158.1 4.9 %add_convert_fusion.1 = bf16[2048,512]{1,0:T(8,128)(2,1)} fusion(f32[2048,512]{1,0:T(8,128)} %get-tuple-element.10, bf16[2048,512]{1,0:T(8,128)(2,1)} %bitcast.77, f32[512]{0:T(512)S(1)} %bitcast.107, f32[2048]{0:T(1024)S(1)} %add_rsqrt_fusion), kind=kLoop, calls=%fused_computation.2 | loop fusion | flops 5242880 | bytes 8398848 | tf_op jit(solution)/shard_map/convert_element_type | solution.py:245
  163.0 4.0 %all-to-all-start.4 = ((bf16[16,128,512]{2,1,0:T(8,128)(2,1)}), bf16[16,128,512]{2,1,0:T(8,128)(2,1)S(1)}, u32[]{:S(2)}, u32[]{:S(2)}) async-start(bf16[16,128,512]{2,1,0:T(8,128)(2,1)} %bitcast.81), calls=%async_computation.4 | async-start | bytes 4194304 | tf_op jit(solution)/shard_map/all_to_all | solution.py:38
  168.5 27.9 %shard_map.128 = bf16[128,8192]{1,0:T(8,128)(2,1)} custom-call(bf16[128,8192]{1,0:T(8,128)(2,1)} %bitcast.83, bf16[640,2048]{1,0:T(8,128)(2,1)} %constant_dynamic-update-slice_fusion.k_ref.v_ref, bf16[640,2048]{1,0:T(8,128)(2,1)} %constant_dynamic-update-slice_fusion.k_ref.v_ref, s32[128,1]{1,0:T(8,128)} %copy.88.iq_ref, s32[1,640]{1,0:T(1,128)} %reshape.154.ik_ref), custom_call_target="tpu_custom_call" | custom-call | tf_op jit(solution)/shard_map/pallas_call | solution.py:167
  (78 shorter events, 29.3 us)
Async XLA Ops:
  0.0 34.8 %copy-start = (f32[1,128]{1,0:T(1,128)S(1)}, f32[1,128]{1,0:T(1,128)}, u32[]{:S(2)}) copy-start(f32[1,128]{1,0:T(1,128)} %param.20) | copy-start | bytes 1540
  1.9 89.3 %collective-permute-start.3 = (bf16[128,2048]{1,0:T(8,128)(2,1)}, bf16[128,2048]{1,0:T(8,128)(2,1)}, u32[]{:S(2)}, u32[]{:S(2)}) collective-permute-start(bf16[128,2048]{1,0:T(8,128)(2,1)} %pad_maximum_fusion), channel_id=1, source_target_pairs={{0,1},{1,2},{2,3},{3,4},{4,5},{5,6},{6,7},{7,8},{8,9},{9,10},{10,1... | collective-permute-start | bytes 1572872 | tf_op jit(solution)/shard_map/ppermute | solution.py:24
  6.1 83.2 %collective-permute-start.2 = (bf16[128,2048]{1,0:T(8,128)(2,1)}, bf16[128,2048]{1,0:T(8,128)(2,1)}, u32[]{:S(2)}, u32[]{:S(2)}) collective-permute-start(bf16[128,2048]{1,0:T(8,128)(2,1)} %pad_maximum_fusion), channel_id=1, source_target_pairs={{0,2},{1,3},{2,4},{3,5},{4,6},{5,7},{6,8},{7,9},{8,10},{9,11},{10,... | collective-permute-start | bytes 1572872 | tf_op jit(solution)/shard_map/ppermute | solution.py:24
  10.7 76.7 %collective-permute-start.1 = (bf16[128,2048]{1,0:T(8,128)(2,1)}, bf16[128,2048]{1,0:T(8,128)(2,1)}, u32[]{:S(2)}, u32[]{:S(2)}) collective-permute-start(bf16[128,2048]{1,0:T(8,128)(2,1)} %pad_maximum_fusion), channel_id=1, source_target_pairs={{0,3},{1,4},{2,5},{3,6},{4,7},{5,8},{6,9},{7,10},{8,11},{9,12},{10... | collective-permute-start | bytes 1572872 | tf_op jit(solution)/shard_map/ppermute | solution.py:24
  15.1 70.4 %collective-permute-start = (bf16[128,2048]{1,0:T(8,128)(2,1)}, bf16[128,2048]{1,0:T(8,128)(2,1)}, u32[]{:S(2)}, u32[]{:S(2)}) collective-permute-start(bf16[128,2048]{1,0:T(8,128)(2,1)} %pad_maximum_fusion), channel_id=1, source_target_pairs={{0,4},{1,5},{2,6},{3,7},{4,8},{5,9},{6,10},{7,11},{8,12},{9,13},{1... | collective-permute-start | bytes 1572872 | tf_op jit(solution)/shard_map/ppermute | solution.py:24
  20.1 36.5 %all-to-all-start.2 = ((f32[16,128,8]{1,2,0:T(8,128)}), f32[16,128,8]{1,2,0:T(8,128)S(1)}, u32[]{:S(2)}, u32[]{:S(2)}) async-start(f32[16,128,8]{1,2,0:T(8,128)} %bitcast.9), calls=%async_computation.2 | async-start | bytes 131072 | tf_op jit(solution)/shard_map/all_to_all | solution.py:31
  23.6 37.7 %collective-permute-start.4 = (bf16[128,8192]{1,0:T(8,128)(2,1)}, bf16[128,8192]{1,0:T(8,128)(2,1)}, u32[]{:S(2)}, u32[]{:S(2)}) collective-permute-start(bf16[128,8192]{1,0:T(8,128)(2,1)} %bitcast.110), channel_id=1, source_target_pairs={{0,16},{16,32},{32,48},{48,64},{64,80},{80,96},{96,112},{1,17},{17... | collective-permute-start | bytes 6291464 | tf_op jit(solution)/shard_map/ppermute | solution.py:24
  30.4 2.9 %copy-start.7 = (s32[1,2048]{1,0:T(1,128)S(1)}, s32[1,2048]{1,0:T(1,128)}, u32[]{:S(2)}) copy-start(s32[1,2048]{1,0:T(1,128)} %param.25) | copy-start | bytes 24580
  31.0 3.7 %copy-start.9 = (f32[1,128]{1,0:T(1,128)S(1)}, f32[1,128]{1,0:T(1,128)}, u32[]{:S(2)}) copy-start(f32[1,128]{1,0:T(1,128)} %param.16) | copy-start | bytes 1540
  31.0 3.7 %copy-start.10 = (f32[1,128]{1,0:T(1,128)S(1)}, f32[1,128]{1,0:T(1,128)}, u32[]{:S(2)}) copy-start(f32[1,128]{1,0:T(1,128)} %param.17) | copy-start | bytes 1540
  33.3 28.0 %copy-start.3 = (bf16[128,8192]{1,0:T(8,128)(2,1)S(1)}, bf16[128,8192]{1,0:T(8,128)(2,1)}, u32[]{:S(2)}) copy-start(bf16[128,8192]{1,0:T(8,128)(2,1)} %param.14) | copy-start | bytes 6291460
  56.6 21.4 %all-to-all-start.1 = ((bf16[16,128,256]{2,1,0:T(8,128)(2,1)}), bf16[16,128,256]{2,1,0:T(8,128)(2,1)S(1)}, u32[]{:S(2)}, u32[]{:S(2)}) async-start(bf16[16,128,256]{2,1,0:T(8,128)(2,1)} %bitcast.5), calls=%async_computation.1 | async-start | bytes 2097152 | tf_op jit(solution)/shard_map/all_to_all | solution.py:31
  61.1 21.6 %copy-start.4 = (f32[16,128,8]{1,2,0:T(8,128)}, f32[16,128,8]{1,2,0:T(8,128)S(1)}, u32[]{:S(2)}) copy-start(f32[16,128,8]{1,2,0:T(8,128)S(1)} %get-tuple-element.14) | copy-start | bytes 196612
  78.0 34.0 %all-to-all-start = ((bf16[16,128,512]{2,1,0:T(8,128)(2,1)}), bf16[16,128,512]{2,1,0:T(8,128)(2,1)S(1)}, u32[]{:S(2)}, u32[]{:S(2)}) async-start(bf16[16,128,512]{2,1,0:T(8,128)(2,1)} %bitcast.80), calls=%async_computation | async-start | bytes 4194304 | tf_op jit(solution)/shard_map/all_to_all | solution.py:31
  84.1 9.0 %copy-start.5 = (bf16[1,128,1024]{2,1,0:T(8,128)(2,1)S(1)}, bf16[1,128,1024]{2,1,0:T(8,128)(2,1)}, u32[]{:S(2)}) copy-start(bf16[1,128,1024]{2,1,0:T(8,128)(2,1)} %param.24) | copy-start | bytes 786436
  85.4 7.7 %copy-start.6 = (bf16[1,128,1024]{2,1,0:T(8,128)(2,1)S(1)}, bf16[1,128,1024]{2,1,0:T(8,128)(2,1)}, u32[]{:S(2)}) copy-start(bf16[1,128,1024]{2,1,0:T(8,128)(2,1)} %param.23) | copy-start | bytes 786436
  112.0 1.3 copy-start.1
  146.6 11.5 %all-to-all-start.3 = ((f32[16,1,2048]{2,1,0:T(1,128)}), f32[16,1,2048]{2,1,0:T(1,128)S(1)}, u32[]{:S(2)}, u32[]{:S(2)}) async-start(f32[16,1,2048]{2,1,0:T(1,128)} %broadcast_in_dim.13), calls=%async_computation.3 | async-start | bytes 262144 | tf_op jit(solution)/shard_map/all_to_all | solution.py:238
  163.0 4.0 %copy-start.8 = (s32[1,2048]{1,0:T(1,128)S(1)}, s32[1,2048]{1,0:T(1,128)}, u32[]{:S(2)}) copy-start(s32[1,2048]{1,0:T(1,128)} %param.25) | copy-start | bytes 24580
  163.0 33.4 %all-to-all-start.4 = ((bf16[16,128,512]{2,1,0:T(8,128)(2,1)}), bf16[16,128,512]{2,1,0:T(8,128)(2,1)S(1)}, u32[]{:S(2)}, u32[]{:S(2)}) async-start(bf16[16,128,512]{2,1,0:T(8,128)(2,1)} %bitcast.81), calls=%async_computation.4 | async-start | bytes 4194304 | tf_op jit(solution)/shard_map/all_to_all | solution.py:38
  197.0 1.6 copy-start.2

commit v18 on v17

--- a/solution.py
+++ b/solution.py
@@ -82,7 +82,7 @@
         cols_at = lax.broadcasted_iota(jnp.int32, (BLOCK, BLOCK), 1)
         same_doc = (idc_ref[...] == idr_ref[0]) & (rows_at >= cols_at)
         b_t_f32 = b_t_blk.astype(jnp.float32)
-        sq = jnp.zeros((BLOCK, 1), jnp.float32)
+        sq = jnp.zeros((BLOCK, head_dim), jnp.float32)
         for h in range(heads):
             cols = slice(h * head_dim, (h + 1) * head_dim)
             lc_c = lcc_ref[0, :, h:h + 1]
@@ -96,11 +96,11 @@
             carried = carried * csc_ref[0, :, h:h + 1]
             out = local + carried + skip_ref[h] * xh.astype(jnp.float32)
             o_ref[:, cols] = out
-            sq = sq + jnp.sum(out * out, axis=1, keepdims=True)
+            sq = sq + out * out
             end_w_t = (esc_ref[0, h:h + 1, :] * b_t_f32).astype(jnp.bfloat16)
             block_state = jnp.dot(end_w_t, xh, preferred_element_type=jnp.float32)
             carry_ref[h] = gain_ref[0, h:h + 1, :] * carry_ref[h] + block_state
-        sq_ref[...] = sq
+        sq_ref[...] = jnp.sum(sq, axis=1, keepdims=True)
 
     per_block = lambda shape: pl.BlockSpec((1,) + shape, lambda i: (i, 0, 0))
     return pl.pallas_call(

time: 202 us -> 189 us (0.936)
  Pallas kernels: 58.8 us -> 45.4 us
    pallas_call x1, Pallas kernels: 30.9 us -> 17.5 us  [mixer_heads(): pl.pallas_call(kernel, grid=(nblk,), in_specs=[pl.BlockSpec((BLOCK, x_wid...]
  transfers between devices with their start and end apart: 10 -> 10, of which waited for: 4 -> 4; matrix products, arithmetic and copies ran while one was open for 17% -> 18% of each run, Pallas kernels for 14% -> 15%
where the time goes in v18:
time: 189 us; the launch traced here: 187 us
  waiting for transfers between devices  56.7 us (30%)
  Pallas kernels  45.4 us (24%)
  starting transfers between devices  37 us (20%)
  local copies, waits for them, and re-layouts  30.8 us (16%)
  other arithmetic  16.7 us (9%)
    all_to_all x3, waiting for transfers between devices, to_heads(): moved = lax.all_to_all(lead, 'ctx', split_axis=0, concat_axis=0, tiled=True)  49.5 us
    pallas_call x1, Pallas kernels, attend_rows(): pl.pallas_call(kernel, grid=(kv_heads // pair,), in_specs=[pl.BlockSpec((...  27.9 us
    ppermute x5, starting transfers between devices, shifted(): return lax.ppermute(value, axis, pairs)  18.6 us
    pallas_call x1, Pallas kernels, mixer_heads(): pl.pallas_call(kernel, grid=(nblk,), in_specs=[pl.BlockSpec((BLOCK, x_wid...  17.5 us
    unnamed x32, local copies, waits for them, and re-layouts  13.1 us
    all_to_all x3, starting transfers between devices, to_heads(): moved = lax.all_to_all(lead, 'ctx', split_axis=0, concat_axis=0, tiled=True)  10.9 us
    all_to_all x1, waiting for transfers between devices, body(): lax.all_to_all(jnp.broadcast_to(sq_part[:, 0][None], (nctx, total)), 'ctx...  7.26 us
    convert_element_type x1, other arithmetic, body(): mixed = (x_h.astype(jnp.float32) + mixer_out * inv_rms * gain_h.astype(jn...  4.87 us
  transfers between devices with their start and end apart: 10, of which 4 were waited for; matrix products, arithmetic and copies ran while one was open for 18% of the time, Pallas kernels for 15%

profile of v18, /device:TPU:32, one launch (start us, length us, event | category | flops | bytes accessed | tf_op | source)
XLA Modules:
  0.0 187.0 jit_solution(5731821150128063665)
XLA Ops:
  0.0 1.9 pad_maximum_fusion
  1.9 4.2 %collective-permute-start.3 = (bf16[128,2048]{1,0:T(8,128)(2,1)}, bf16[128,2048]{1,0:T(8,128)(2,1)}, u32[]{:S(2)}, u32[]{:S(2)}) collective-permute-start(bf16[128,2048]{1,0:T(8,128)(2,1)} %pad_maximum_fusion), channel_id=1, source_target_pairs={{0,1},{1,2},{2,3},{3,4},{4,5},{5,6},{6,7},{7,8},{8,9},{9,10},{10,1... | collective-permute-start | bytes 1572872 | tf_op jit(solution)/shard_map/ppermute | solution.py:24
  6.1 4.7 %collective-permute-start.2 = (bf16[128,2048]{1,0:T(8,128)(2,1)}, bf16[128,2048]{1,0:T(8,128)(2,1)}, u32[]{:S(2)}, u32[]{:S(2)}) collective-permute-start(bf16[128,2048]{1,0:T(8,128)(2,1)} %pad_maximum_fusion), channel_id=1, source_target_pairs={{0,2},{1,3},{2,4},{3,5},{4,6},{5,7},{6,8},{7,9},{8,10},{9,11},{10,... | collective-permute-start | bytes 1572872 | tf_op jit(solution)/shard_map/ppermute | solution.py:24
  10.7 4.4 %collective-permute-start.1 = (bf16[128,2048]{1,0:T(8,128)(2,1)}, bf16[128,2048]{1,0:T(8,128)(2,1)}, u32[]{:S(2)}, u32[]{:S(2)}) collective-permute-start(bf16[128,2048]{1,0:T(8,128)(2,1)} %pad_maximum_fusion), channel_id=1, source_target_pairs={{0,3},{1,4},{2,5},{3,6},{4,7},{5,8},{6,9},{7,10},{8,11},{9,12},{10... | collective-permute-start | bytes 1572872 | tf_op jit(solution)/shard_map/ppermute | solution.py:24
  15.1 3.5 %collective-permute-start = (bf16[128,2048]{1,0:T(8,128)(2,1)}, bf16[128,2048]{1,0:T(8,128)(2,1)}, u32[]{:S(2)}, u32[]{:S(2)}) collective-permute-start(bf16[128,2048]{1,0:T(8,128)(2,1)} %pad_maximum_fusion), channel_id=1, source_target_pairs={{0,4},{1,5},{2,6},{3,7},{4,8},{5,9},{6,10},{7,11},{8,12},{9,13},{1... | collective-permute-start | bytes 1572872 | tf_op jit(solution)/shard_map/ppermute | solution.py:24
  20.1 3.5 %all-to-all-start.2 = ((f32[16,128,8]{1,2,0:T(8,128)}), f32[16,128,8]{1,2,0:T(8,128)S(1)}, u32[]{:S(2)}, u32[]{:S(2)}) async-start(f32[16,128,8]{1,2,0:T(8,128)} %bitcast.9), calls=%async_computation.2 | async-start | bytes 131072 | tf_op jit(solution)/shard_map/all_to_all | solution.py:31
  23.6 1.9 %collective-permute-start.4 = (bf16[128,8192]{1,0:T(8,128)(2,1)}, bf16[128,8192]{1,0:T(8,128)(2,1)}, u32[]{:S(2)}, u32[]{:S(2)}) collective-permute-start(bf16[128,8192]{1,0:T(8,128)(2,1)} %bitcast.110), channel_id=1, source_target_pairs={{0,16},{16,32},{32,48},{48,64},{64,80},{80,96},{96,112},{1,17},{17... | collective-permute-start | bytes 6291464 | tf_op jit(solution)/shard_map/ppermute | solution.py:24
  35.4 21.2 %all-to-all-done.2 = f32[16,128,8]{1,2,0:T(8,128)S(1)} async-done(((f32[16,128,8]{1,2,0:T(8,128)}), f32[16,128,8]{1,2,0:T(8,128)S(1)}, u32[]{:S(2)}, u32[]{:S(2)}) %all-to-all-start.2) | async-done | bytes 65568 | tf_op jit(solution)/shard_map/all_to_all | solution.py:31
  56.6 3.7 %all-to-all-start.1 = ((bf16[16,128,256]{2,1,0:T(8,128)(2,1)}), bf16[16,128,256]{2,1,0:T(8,128)(2,1)S(1)}, u32[]{:S(2)}, u32[]{:S(2)}) async-start(bf16[16,128,256]{2,1,0:T(8,128)(2,1)} %bitcast.5), calls=%async_computation.1 | async-start | bytes 2097152 | tf_op jit(solution)/shard_map/all_to_all | solution.py:31
  61.3 1.8 broadcast_select_fusion
  64.7 13.3 %all-to-all-done.1 = bf16[16,128,256]{2,1,0:T(8,128)(2,1)S(1)} async-done(((bf16[16,128,256]{2,1,0:T(8,128)(2,1)}), bf16[16,128,256]{2,1,0:T(8,128)(2,1)S(1)}, u32[]{:S(2)}, u32[]{:S(2)}) %all-to-all-start.1) | async-done | bytes 1048608 | tf_op jit(solution)/shard_map/all_to_all | solution.py:31
  78.0 3.7 %all-to-all-start = ((bf16[16,128,512]{2,1,0:T(8,128)(2,1)}), bf16[16,128,512]{2,1,0:T(8,128)(2,1)S(1)}, u32[]{:S(2)}, u32[]{:S(2)}) async-start(bf16[16,128,512]{2,1,0:T(8,128)(2,1)} %bitcast.80), calls=%async_computation | async-start | bytes 4194304 | tf_op jit(solution)/shard_map/all_to_all | solution.py:31
  85.4 1.9 %constant_dynamic-update-slice_fusion.4 = bf16[640,2048]{1,0:T(8,128)(2,1)} fusion(bf16[128,2048]{1,0:T(8,128)(2,1)} %collective-permute-done), kind=kLoop, calls=%fused_computation.25 | loop fusion | bytes 1048576
  87.4 1.9 %constant_dynamic-update-slice_fusion.3 = bf16[640,2048]{1,0:T(8,128)(2,1)} fusion(bf16[640,2048]{1,0:T(8,128)(2,1)} %constant_dynamic-update-slice_fusion.4, bf16[128,2048]{1,0:T(8,128)(2,1)} %collective-permute-done.1), kind=kLoop, calls=%fused_computation.24 | loop fusion | bytes 1048576
  89.3 1.9 %constant_dynamic-update-slice_fusion.2 = bf16[640,2048]{1,0:T(8,128)(2,1)} fusion(bf16[640,2048]{1,0:T(8,128)(2,1)} %constant_dynamic-update-slice_fusion.3, bf16[128,2048]{1,0:T(8,128)(2,1)} %collective-permute-done.2), kind=kLoop, calls=%fused_computation.23 | loop fusion | bytes 1048576
  91.2 1.9 %constant_dynamic-update-slice_fusion.1 = bf16[640,2048]{1,0:T(8,128)(2,1)} fusion(bf16[640,2048]{1,0:T(8,128)(2,1)} %constant_dynamic-update-slice_fusion.2, bf16[128,2048]{1,0:T(8,128)(2,1)} %collective-permute-done.3), kind=kLoop, calls=%fused_computation.22 | loop fusion | bytes 1048576
  95.0 2.0 %copy.82.b_ref = bf16[128,2048]{1,0:T(8,128)(2,1)} copy(bf16[128,2048]{0,1:T(8,128)(2,1)} %get-tuple-element.16) | data formatting | bytes 1048576 | tf_op jit(solution)/shard_map/transpose | solution.py:69
  97.1 15.0 %all-to-all-done = bf16[16,128,512]{2,1,0:T(8,128)(2,1)S(1)} async-done(((bf16[16,128,512]{2,1,0:T(8,128)(2,1)}), bf16[16,128,512]{2,1,0:T(8,128)(2,1)S(1)}, u32[]{:S(2)}, u32[]{:S(2)}) %all-to-all-start) | async-done | bytes 2097184 | tf_op jit(solution)/shard_map/all_to_all | solution.py:31
  113.4 17.5 %shard_map.127 = (f32[2048,512]{1,0:T(8,128)}, f32[2048,1]{1,0:T(8,128)}) custom-call(bf16[2048,512]{1,0:T(8,128)(2,1)} %bitcast.76, bf16[128,2048]{1,0:T(8,128)(2,1)} %copy.82.b_ref, bf16[2048,128]{1,0:T(8,128)(2,1)} %get-tuple-element.15.c_ref, f32[16,128,8]{2,1,0:T(8,128)} %copy.83.lcc_ref, f32[16,8,128]{2,1,0:T(8,128)} %bitcast.84, ...), custom_call_target="tpu_custom_call" | custom-call | tf_op jit(solution)/shard_map/pallas_call | solution.py:106
  133.2 3.5 %all-to-all-start.3 = ((f32[16,1,2048]{2,1,0:T(1,128)}), f32[16,1,2048]{2,1,0:T(1,128)S(1)}, u32[]{:S(2)}, u32[]{:S(2)}) async-start(f32[16,1,2048]{2,1,0:T(1,128)} %broadcast_in_dim.13), calls=%async_computation.3 | async-start | bytes 262144 | tf_op jit(solution)/shard_map/all_to_all | solution.py:238
  137.4 7.3 %all-to-all-done.3 = f32[16,1,2048]{2,1,0:T(1,128)S(1)} async-done(((f32[16,1,2048]{2,1,0:T(1,128)}), f32[16,1,2048]{2,1,0:T(1,128)S(1)}, u32[]{:S(2)}, u32[]{:S(2)}) %all-to-all-start.3) | async-done | bytes 131104 | tf_op jit(solution)/shard_map/all_to_all | solution.py:238
  144.8 4.9 %add_convert_fusion.1 = bf16[2048,512]{1,0:T(8,128)(2,1)} fusion(f32[2048,512]{1,0:T(8,128)} %get-tuple-element.10, bf16[2048,512]{1,0:T(8,128)(2,1)} %bitcast.77, f32[512]{0:T(512)S(1)} %bitcast.107, f32[2048]{0:T(1024)S(1)} %add_rsqrt_fusion), kind=kLoop, calls=%fused_computation.2 | loop fusion | flops 5242880 | bytes 8398848 | tf_op jit(solution)/shard_map/convert_element_type | solution.py:245
  149.6 4.0 %all-to-all-start.4 = ((bf16[16,128,512]{2,1,0:T(8,128)(2,1)}), bf16[16,128,512]{2,1,0:T(8,128)(2,1)S(1)}, u32[]{:S(2)}, u32[]{:S(2)}) async-start(bf16[16,128,512]{2,1,0:T(8,128)(2,1)} %bitcast.81), calls=%async_computation.4 | async-start | bytes 4194304 | tf_op jit(solution)/shard_map/all_to_all | solution.py:38
  155.1 27.9 %shard_map.128 = bf16[128,8192]{1,0:T(8,128)(2,1)} custom-call(bf16[128,8192]{1,0:T(8,128)(2,1)} %bitcast.83, bf16[640,2048]{1,0:T(8,128)(2,1)} %constant_dynamic-update-slice_fusion.k_ref.v_ref, bf16[640,2048]{1,0:T(8,128)(2,1)} %constant_dynamic-update-slice_fusion.k_ref.v_ref, s32[128,1]{1,0:T(8,128)} %copy.88.iq_ref, s32[1,640]{1,0:T(1,128)} %reshape.154.ik_ref), custom_call_target="tpu_custom_call" | custom-call | tf_op jit(solution)/shard_map/pallas_call | solution.py:167
  (78 shorter events, 29.3 us)
Async XLA Ops:
  0.0 34.8 %copy-start = (f32[1,128]{1,0:T(1,128)S(1)}, f32[1,128]{1,0:T(1,128)}, u32[]{:S(2)}) copy-start(f32[1,128]{1,0:T(1,128)} %param.20) | copy-start | bytes 1540
  1.9 89.3 %collective-permute-start.3 = (bf16[128,2048]{1,0:T(8,128)(2,1)}, bf16[128,2048]{1,0:T(8,128)(2,1)}, u32[]{:S(2)}, u32[]{:S(2)}) collective-permute-start(bf16[128,2048]{1,0:T(8,128)(2,1)} %pad_maximum_fusion), channel_id=1, source_target_pairs={{0,1},{1,2},{2,3},{3,4},{4,5},{5,6},{6,7},{7,8},{8,9},{9,10},{10,1... | collective-permute-start | bytes 1572872 | tf_op jit(solution)/shard_map/ppermute | solution.py:24
  6.1 83.2 %collective-permute-start.2 = (bf16[128,2048]{1,0:T(8,128)(2,1)}, bf16[128,2048]{1,0:T(8,128)(2,1)}, u32[]{:S(2)}, u32[]{:S(2)}) collective-permute-start(bf16[128,2048]{1,0:T(8,128)(2,1)} %pad_maximum_fusion), channel_id=1, source_target_pairs={{0,2},{1,3},{2,4},{3,5},{4,6},{5,7},{6,8},{7,9},{8,10},{9,11},{10,... | collective-permute-start | bytes 1572872 | tf_op jit(solution)/shard_map/ppermute | solution.py:24
  10.7 76.7 %collective-permute-start.1 = (bf16[128,2048]{1,0:T(8,128)(2,1)}, bf16[128,2048]{1,0:T(8,128)(2,1)}, u32[]{:S(2)}, u32[]{:S(2)}) collective-permute-start(bf16[128,2048]{1,0:T(8,128)(2,1)} %pad_maximum_fusion), channel_id=1, source_target_pairs={{0,3},{1,4},{2,5},{3,6},{4,7},{5,8},{6,9},{7,10},{8,11},{9,12},{10... | collective-permute-start | bytes 1572872 | tf_op jit(solution)/shard_map/ppermute | solution.py:24
  15.1 70.4 %collective-permute-start = (bf16[128,2048]{1,0:T(8,128)(2,1)}, bf16[128,2048]{1,0:T(8,128)(2,1)}, u32[]{:S(2)}, u32[]{:S(2)}) collective-permute-start(bf16[128,2048]{1,0:T(8,128)(2,1)} %pad_maximum_fusion), channel_id=1, source_target_pairs={{0,4},{1,5},{2,6},{3,7},{4,8},{5,9},{6,10},{7,11},{8,12},{9,13},{1... | collective-permute-start | bytes 1572872 | tf_op jit(solution)/shard_map/ppermute | solution.py:24
  20.1 36.5 %all-to-all-start.2 = ((f32[16,128,8]{1,2,0:T(8,128)}), f32[16,128,8]{1,2,0:T(8,128)S(1)}, u32[]{:S(2)}, u32[]{:S(2)}) async-start(f32[16,128,8]{1,2,0:T(8,128)} %bitcast.9), calls=%async_computation.2 | async-start | bytes 131072 | tf_op jit(solution)/shard_map/all_to_all | solution.py:31
  23.6 37.7 %collective-permute-start.4 = (bf16[128,8192]{1,0:T(8,128)(2,1)}, bf16[128,8192]{1,0:T(8,128)(2,1)}, u32[]{:S(2)}, u32[]{:S(2)}) collective-permute-start(bf16[128,8192]{1,0:T(8,128)(2,1)} %bitcast.110), channel_id=1, source_target_pairs={{0,16},{16,32},{32,48},{48,64},{64,80},{80,96},{96,112},{1,17},{17... | collective-permute-start | bytes 6291464 | tf_op jit(solution)/shard_map/ppermute | solution.py:24
  30.4 2.9 %copy-start.7 = (s32[1,2048]{1,0:T(1,128)S(1)}, s32[1,2048]{1,0:T(1,128)}, u32[]{:S(2)}) copy-start(s32[1,2048]{1,0:T(1,128)} %param.25) | copy-start | bytes 24580
  31.0 3.7 %copy-start.9 = (f32[1,128]{1,0:T(1,128)S(1)}, f32[1,128]{1,0:T(1,128)}, u32[]{:S(2)}) copy-start(f32[1,128]{1,0:T(1,128)} %param.16) | copy-start | bytes 1540
  31.0 3.7 %copy-start.10 = (f32[1,128]{1,0:T(1,128)S(1)}, f32[1,128]{1,0:T(1,128)}, u32[]{:S(2)}) copy-start(f32[1,128]{1,0:T(1,128)} %param.17) | copy-start | bytes 1540
  33.3 28.0 %copy-start.3 = (bf16[128,8192]{1,0:T(8,128)(2,1)S(1)}, bf16[128,8192]{1,0:T(8,128)(2,1)}, u32[]{:S(2)}) copy-start(bf16[128,8192]{1,0:T(8,128)(2,1)} %param.14) | copy-start | bytes 6291460
  56.6 21.4 %all-to-all-start.1 = ((bf16[16,128,256]{2,1,0:T(8,128)(2,1)}), bf16[16,128,256]{2,1,0:T(8,128)(2,1)S(1)}, u32[]{:S(2)}, u32[]{:S(2)}) async-start(bf16[16,128,256]{2,1,0:T(8,128)(2,1)} %bitcast.5), calls=%async_computation.1 | async-start | bytes 2097152 | tf_op jit(solution)/shard_map/all_to_all | solution.py:31
  61.1 21.6 %copy-start.4 = (f32[16,128,8]{1,2,0:T(8,128)}, f32[16,128,8]{1,2,0:T(8,128)S(1)}, u32[]{:S(2)}) copy-start(f32[16,128,8]{1,2,0:T(8,128)S(1)} %get-tuple-element.14) | copy-start | bytes 196612
  78.0 34.0 %all-to-all-start = ((bf16[16,128,512]{2,1,0:T(8,128)(2,1)}), bf16[16,128,512]{2,1,0:T(8,128)(2,1)S(1)}, u32[]{:S(2)}, u32[]{:S(2)}) async-start(bf16[16,128,512]{2,1,0:T(8,128)(2,1)} %bitcast.80), calls=%async_computation | async-start | bytes 4194304 | tf_op jit(solution)/shard_map/all_to_all | solution.py:31
  84.1 9.0 %copy-start.5 = (bf16[1,128,1024]{2,1,0:T(8,128)(2,1)S(1)}, bf16[1,128,1024]{2,1,0:T(8,128)(2,1)}, u32[]{:S(2)}) copy-start(bf16[1,128,1024]{2,1,0:T(8,128)(2,1)} %param.24) | copy-start | bytes 786436
  85.4 7.7 %copy-start.6 = (bf16[1,128,1024]{2,1,0:T(8,128)(2,1)S(1)}, bf16[1,128,1024]{2,1,0:T(8,128)(2,1)}, u32[]{:S(2)}) copy-start(bf16[1,128,1024]{2,1,0:T(8,128)(2,1)} %param.23) | copy-start | bytes 786436
  112.0 1.3 copy-start.1
  133.2 11.5 %all-to-all-start.3 = ((f32[16,1,2048]{2,1,0:T(1,128)}), f32[16,1,2048]{2,1,0:T(1,128)S(1)}, u32[]{:S(2)}, u32[]{:S(2)}) async-start(f32[16,1,2048]{2,1,0:T(1,128)} %broadcast_in_dim.13), calls=%async_computation.3 | async-start | bytes 262144 | tf_op jit(solution)/shard_map/all_to_all | solution.py:238
  149.6 4.0 %copy-start.8 = (s32[1,2048]{1,0:T(1,128)S(1)}, s32[1,2048]{1,0:T(1,128)}, u32[]{:S(2)}) copy-start(s32[1,2048]{1,0:T(1,128)} %param.25) | copy-start | bytes 24580
  149.6 33.4 %all-to-all-start.4 = ((bf16[16,128,512]{2,1,0:T(8,128)(2,1)}), bf16[16,128,512]{2,1,0:T(8,128)(2,1)S(1)}, u32[]{:S(2)}, u32[]{:S(2)}) async-start(bf16[16,128,512]{2,1,0:T(8,128)(2,1)} %bitcast.81), calls=%async_computation.4 | async-start | bytes 4194304 | tf_op jit(solution)/shard_map/all_to_all | solution.py:38
  183.6 1.6 copy-start.2

commit v19 on v18

--- a/solution.py
+++ b/solution.py
@@ -143,7 +143,7 @@
     kv_heads = kv_win.shape[1] // (2 * HEAD_A)
     group = q_width // HEAD_A // kv_heads
     lead = window - tok_rows
-    pair = 2 if kv_heads % 2 == 0 else 1
+    pair = 4 if kv_heads % 4 == 0 else 1
     inv_sqrt = 1.0 / math.sqrt(HEAD_A)
 
     def kernel(q_ref, k_ref, v_ref, iq_ref, ik_ref, o_ref):

time: 189 us -> 189 us (level)
  no operation moved by 1% of the time
where the time goes in v19:
time: 189 us; the launch traced here: 187 us
  waiting for transfers between devices  56.7 us (30%)
  Pallas kernels  45.5 us (24%)
  starting transfers between devices  37 us (20%)
  local copies, waits for them, and re-layouts  30.8 us (16%)
  other arithmetic  16.7 us (9%)
    all_to_all x3, waiting for transfers between devices, to_heads(): moved = lax.all_to_all(lead, 'ctx', split_axis=0, concat_axis=0, tiled=True)  49.5 us
    pallas_call x1, Pallas kernels, attend_rows(): pl.pallas_call(kernel, grid=(kv_heads // pair,), in_specs=[pl.BlockSpec((...  28 us
    ppermute x5, starting transfers between devices, shifted(): return lax.ppermute(value, axis, pairs)  18.6 us
    pallas_call x1, Pallas kernels, mixer_heads(): pl.pallas_call(kernel, grid=(nblk,), in_specs=[pl.BlockSpec((BLOCK, x_wid...  17.5 us
    unnamed x32, local copies, waits for them, and re-layouts  13.1 us
    all_to_all x3, starting transfers between devices, to_heads(): moved = lax.all_to_all(lead, 'ctx', split_axis=0, concat_axis=0, tiled=True)  10.9 us
    all_to_all x1, waiting for transfers between devices, body(): lax.all_to_all(jnp.broadcast_to(sq_part[:, 0][None], (nctx, total)), 'ctx...  7.26 us
    convert_element_type x1, other arithmetic, body(): mixed = (x_h.astype(jnp.float32) + mixer_out * inv_rms * gain_h.astype(jn...  4.87 us
  transfers between devices with their start and end apart: 10, of which 4 were waited for; matrix products, arithmetic and copies ran while one was open for 18% of the time, Pallas kernels for 15%

profile of v19, /device:TPU:32, one launch (start us, length us, event | category | flops | bytes accessed | tf_op | source)
XLA Modules:
  0.0 187.1 jit_solution(15144101122605907697)
XLA Ops:
  0.0 1.9 pad_maximum_fusion
  1.9 4.2 %collective-permute-start.3 = (bf16[128,2048]{1,0:T(8,128)(2,1)}, bf16[128,2048]{1,0:T(8,128)(2,1)}, u32[]{:S(2)}, u32[]{:S(2)}) collective-permute-start(bf16[128,2048]{1,0:T(8,128)(2,1)} %pad_maximum_fusion), channel_id=1, source_target_pairs={{0,1},{1,2},{2,3},{3,4},{4,5},{5,6},{6,7},{7,8},{8,9},{9,10},{10,1... | collective-permute-start | bytes 1572872 | tf_op jit(solution)/shard_map/ppermute | solution.py:24
  6.1 4.7 %collective-permute-start.2 = (bf16[128,2048]{1,0:T(8,128)(2,1)}, bf16[128,2048]{1,0:T(8,128)(2,1)}, u32[]{:S(2)}, u32[]{:S(2)}) collective-permute-start(bf16[128,2048]{1,0:T(8,128)(2,1)} %pad_maximum_fusion), channel_id=1, source_target_pairs={{0,2},{1,3},{2,4},{3,5},{4,6},{5,7},{6,8},{7,9},{8,10},{9,11},{10,... | collective-permute-start | bytes 1572872 | tf_op jit(solution)/shard_map/ppermute | solution.py:24
  10.7 4.4 %collective-permute-start.1 = (bf16[128,2048]{1,0:T(8,128)(2,1)}, bf16[128,2048]{1,0:T(8,128)(2,1)}, u32[]{:S(2)}, u32[]{:S(2)}) collective-permute-start(bf16[128,2048]{1,0:T(8,128)(2,1)} %pad_maximum_fusion), channel_id=1, source_target_pairs={{0,3},{1,4},{2,5},{3,6},{4,7},{5,8},{6,9},{7,10},{8,11},{9,12},{10... | collective-permute-start | bytes 1572872 | tf_op jit(solution)/shard_map/ppermute | solution.py:24
  15.1 3.5 %collective-permute-start = (bf16[128,2048]{1,0:T(8,128)(2,1)}, bf16[128,2048]{1,0:T(8,128)(2,1)}, u32[]{:S(2)}, u32[]{:S(2)}) collective-permute-start(bf16[128,2048]{1,0:T(8,128)(2,1)} %pad_maximum_fusion), channel_id=1, source_target_pairs={{0,4},{1,5},{2,6},{3,7},{4,8},{5,9},{6,10},{7,11},{8,12},{9,13},{1... | collective-permute-start | bytes 1572872 | tf_op jit(solution)/shard_map/ppermute | solution.py:24
  20.1 3.5 %all-to-all-start.2 = ((f32[16,128,8]{1,2,0:T(8,128)}), f32[16,128,8]{1,2,0:T(8,128)S(1)}, u32[]{:S(2)}, u32[]{:S(2)}) async-start(f32[16,128,8]{1,2,0:T(8,128)} %bitcast.9), calls=%async_computation.2 | async-start | bytes 131072 | tf_op jit(solution)/shard_map/all_to_all | solution.py:31
  23.6 1.9 %collective-permute-start.4 = (bf16[128,8192]{1,0:T(8,128)(2,1)}, bf16[128,8192]{1,0:T(8,128)(2,1)}, u32[]{:S(2)}, u32[]{:S(2)}) collective-permute-start(bf16[128,8192]{1,0:T(8,128)(2,1)} %bitcast.110), channel_id=1, source_target_pairs={{0,16},{16,32},{32,48},{48,64},{64,80},{80,96},{96,112},{1,17},{17... | collective-permute-start | bytes 6291464 | tf_op jit(solution)/shard_map/ppermute | solution.py:24
  35.4 21.2 %all-to-all-done.2 = f32[16,128,8]{1,2,0:T(8,128)S(1)} async-done(((f32[16,128,8]{1,2,0:T(8,128)}), f32[16,128,8]{1,2,0:T(8,128)S(1)}, u32[]{:S(2)}, u32[]{:S(2)}) %all-to-all-start.2) | async-done | bytes 65568 | tf_op jit(solution)/shard_map/all_to_all | solution.py:31
  56.6 3.7 %all-to-all-start.1 = ((bf16[16,128,256]{2,1,0:T(8,128)(2,1)}), bf16[16,128,256]{2,1,0:T(8,128)(2,1)S(1)}, u32[]{:S(2)}, u32[]{:S(2)}) async-start(bf16[16,128,256]{2,1,0:T(8,128)(2,1)} %bitcast.5), calls=%async_computation.1 | async-start | bytes 2097152 | tf_op jit(solution)/shard_map/all_to_all | solution.py:31
  61.3 1.8 broadcast_select_fusion
  64.7 13.3 %all-to-all-done.1 = bf16[16,128,256]{2,1,0:T(8,128)(2,1)S(1)} async-done(((bf16[16,128,256]{2,1,0:T(8,128)(2,1)}), bf16[16,128,256]{2,1,0:T(8,128)(2,1)S(1)}, u32[]{:S(2)}, u32[]{:S(2)}) %all-to-all-start.1) | async-done | bytes 1048608 | tf_op jit(solution)/shard_map/all_to_all | solution.py:31
  78.0 3.7 %all-to-all-start = ((bf16[16,128,512]{2,1,0:T(8,128)(2,1)}), bf16[16,128,512]{2,1,0:T(8,128)(2,1)S(1)}, u32[]{:S(2)}, u32[]{:S(2)}) async-start(bf16[16,128,512]{2,1,0:T(8,128)(2,1)} %bitcast.80), calls=%async_computation | async-start | bytes 4194304 | tf_op jit(solution)/shard_map/all_to_all | solution.py:31
  85.4 1.9 %constant_dynamic-update-slice_fusion.4 = bf16[640,2048]{1,0:T(8,128)(2,1)} fusion(bf16[128,2048]{1,0:T(8,128)(2,1)} %collective-permute-done), kind=kLoop, calls=%fused_computation.25 | loop fusion | bytes 1048576
  87.4 1.9 %constant_dynamic-update-slice_fusion.3 = bf16[640,2048]{1,0:T(8,128)(2,1)} fusion(bf16[640,2048]{1,0:T(8,128)(2,1)} %constant_dynamic-update-slice_fusion.4, bf16[128,2048]{1,0:T(8,128)(2,1)} %collective-permute-done.1), kind=kLoop, calls=%fused_computation.24 | loop fusion | bytes 1048576
  89.3 1.9 %constant_dynamic-update-slice_fusion.2 = bf16[640,2048]{1,0:T(8,128)(2,1)} fusion(bf16[640,2048]{1,0:T(8,128)(2,1)} %constant_dynamic-update-slice_fusion.3, bf16[128,2048]{1,0:T(8,128)(2,1)} %collective-permute-done.2), kind=kLoop, calls=%fused_computation.23 | loop fusion | bytes 1048576
  91.2 1.9 %constant_dynamic-update-slice_fusion.1 = bf16[640,2048]{1,0:T(8,128)(2,1)} fusion(bf16[640,2048]{1,0:T(8,128)(2,1)} %constant_dynamic-update-slice_fusion.2, bf16[128,2048]{1,0:T(8,128)(2,1)} %collective-permute-done.3), kind=kLoop, calls=%fused_computation.22 | loop fusion | bytes 1048576
  95.0 2.0 %copy.82.b_ref = bf16[128,2048]{1,0:T(8,128)(2,1)} copy(bf16[128,2048]{0,1:T(8,128)(2,1)} %get-tuple-element.16) | data formatting | bytes 1048576 | tf_op jit(solution)/shard_map/transpose | solution.py:69
  97.1 15.0 %all-to-all-done = bf16[16,128,512]{2,1,0:T(8,128)(2,1)S(1)} async-done(((bf16[16,128,512]{2,1,0:T(8,128)(2,1)}), bf16[16,128,512]{2,1,0:T(8,128)(2,1)S(1)}, u32[]{:S(2)}, u32[]{:S(2)}) %all-to-all-start) | async-done | bytes 2097184 | tf_op jit(solution)/shard_map/all_to_all | solution.py:31
  113.4 17.5 %shard_map.127 = (f32[2048,512]{1,0:T(8,128)}, f32[2048,1]{1,0:T(8,128)}) custom-call(bf16[2048,512]{1,0:T(8,128)(2,1)} %bitcast.76, bf16[128,2048]{1,0:T(8,128)(2,1)} %copy.82.b_ref, bf16[2048,128]{1,0:T(8,128)(2,1)} %get-tuple-element.15.c_ref, f32[16,128,8]{2,1,0:T(8,128)} %copy.83.lcc_ref, f32[16,8,128]{2,1,0:T(8,128)} %bitcast.84, ...), custom_call_target="tpu_custom_call" | custom-call | tf_op jit(solution)/shard_map/pallas_call | solution.py:106
  133.2 3.5 %all-to-all-start.3 = ((f32[16,1,2048]{2,1,0:T(1,128)}), f32[16,1,2048]{2,1,0:T(1,128)S(1)}, u32[]{:S(2)}, u32[]{:S(2)}) async-start(f32[16,1,2048]{2,1,0:T(1,128)} %broadcast_in_dim.13), calls=%async_computation.3 | async-start | bytes 262144 | tf_op jit(solution)/shard_map/all_to_all | solution.py:238
  137.4 7.3 %all-to-all-done.3 = f32[16,1,2048]{2,1,0:T(1,128)S(1)} async-done(((f32[16,1,2048]{2,1,0:T(1,128)}), f32[16,1,2048]{2,1,0:T(1,128)S(1)}, u32[]{:S(2)}, u32[]{:S(2)}) %all-to-all-start.3) | async-done | bytes 131104 | tf_op jit(solution)/shard_map/all_to_all | solution.py:238
  144.8 4.9 %add_convert_fusion.1 = bf16[2048,512]{1,0:T(8,128)(2,1)} fusion(f32[2048,512]{1,0:T(8,128)} %get-tuple-element.10, bf16[2048,512]{1,0:T(8,128)(2,1)} %bitcast.77, f32[512]{0:T(512)S(1)} %bitcast.107, f32[2048]{0:T(1024)S(1)} %add_rsqrt_fusion), kind=kLoop, calls=%fused_computation.2 | loop fusion | flops 5242880 | bytes 8398848 | tf_op jit(solution)/shard_map/convert_element_type | solution.py:245
  149.6 4.0 %all-to-all-start.4 = ((bf16[16,128,512]{2,1,0:T(8,128)(2,1)}), bf16[16,128,512]{2,1,0:T(8,128)(2,1)S(1)}, u32[]{:S(2)}, u32[]{:S(2)}) async-start(bf16[16,128,512]{2,1,0:T(8,128)(2,1)} %bitcast.81), calls=%async_computation.4 | async-start | bytes 4194304 | tf_op jit(solution)/shard_map/all_to_all | solution.py:38
  155.1 28.0 %shard_map.128 = bf16[128,8192]{1,0:T(8,128)(2,1)} custom-call(bf16[128,8192]{1,0:T(8,128)(2,1)} %bitcast.83, bf16[640,2048]{1,0:T(8,128)(2,1)} %constant_dynamic-update-slice_fusion.k_ref.v_ref, bf16[640,2048]{1,0:T(8,128)(2,1)} %constant_dynamic-update-slice_fusion.k_ref.v_ref, s32[128,1]{1,0:T(8,128)} %copy.88.iq_ref, s32[1,640]{1,0:T(1,128)} %reshape.154.ik_ref), custom_call_target="tpu_custom_call" | custom-call | tf_op jit(solution)/shard_map/pallas_call | solution.py:167
  (78 shorter events, 29.3 us)
Async XLA Ops:
  0.0 34.8 %copy-start = (f32[1,128]{1,0:T(1,128)S(1)}, f32[1,128]{1,0:T(1,128)}, u32[]{:S(2)}) copy-start(f32[1,128]{1,0:T(1,128)} %param.20) | copy-start | bytes 1540
  1.9 89.3 %collective-permute-start.3 = (bf16[128,2048]{1,0:T(8,128)(2,1)}, bf16[128,2048]{1,0:T(8,128)(2,1)}, u32[]{:S(2)}, u32[]{:S(2)}) collective-permute-start(bf16[128,2048]{1,0:T(8,128)(2,1)} %pad_maximum_fusion), channel_id=1, source_target_pairs={{0,1},{1,2},{2,3},{3,4},{4,5},{5,6},{6,7},{7,8},{8,9},{9,10},{10,1... | collective-permute-start | bytes 1572872 | tf_op jit(solution)/shard_map/ppermute | solution.py:24
  6.1 83.2 %collective-permute-start.2 = (bf16[128,2048]{1,0:T(8,128)(2,1)}, bf16[128,2048]{1,0:T(8,128)(2,1)}, u32[]{:S(2)}, u32[]{:S(2)}) collective-permute-start(bf16[128,2048]{1,0:T(8,128)(2,1)} %pad_maximum_fusion), channel_id=1, source_target_pairs={{0,2},{1,3},{2,4},{3,5},{4,6},{5,7},{6,8},{7,9},{8,10},{9,11},{10,... | collective-permute-start | bytes 1572872 | tf_op jit(solution)/shard_map/ppermute | solution.py:24
  10.7 76.7 %collective-permute-start.1 = (bf16[128,2048]{1,0:T(8,128)(2,1)}, bf16[128,2048]{1,0:T(8,128)(2,1)}, u32[]{:S(2)}, u32[]{:S(2)}) collective-permute-start(bf16[128,2048]{1,0:T(8,128)(2,1)} %pad_maximum_fusion), channel_id=1, source_target_pairs={{0,3},{1,4},{2,5},{3,6},{4,7},{5,8},{6,9},{7,10},{8,11},{9,12},{10... | collective-permute-start | bytes 1572872 | tf_op jit(solution)/shard_map/ppermute | solution.py:24
  15.1 70.4 %collective-permute-start = (bf16[128,2048]{1,0:T(8,128)(2,1)}, bf16[128,2048]{1,0:T(8,128)(2,1)}, u32[]{:S(2)}, u32[]{:S(2)}) collective-permute-start(bf16[128,2048]{1,0:T(8,128)(2,1)} %pad_maximum_fusion), channel_id=1, source_target_pairs={{0,4},{1,5},{2,6},{3,7},{4,8},{5,9},{6,10},{7,11},{8,12},{9,13},{1... | collective-permute-start | bytes 1572872 | tf_op jit(solution)/shard_map/ppermute | solution.py:24
  20.1 36.5 %all-to-all-start.2 = ((f32[16,128,8]{1,2,0:T(8,128)}), f32[16,128,8]{1,2,0:T(8,128)S(1)}, u32[]{:S(2)}, u32[]{:S(2)}) async-start(f32[16,128,8]{1,2,0:T(8,128)} %bitcast.9), calls=%async_computation.2 | async-start | bytes 131072 | tf_op jit(solution)/shard_map/all_to_all | solution.py:31
  23.6 37.7 %collective-permute-start.4 = (bf16[128,8192]{1,0:T(8,128)(2,1)}, bf16[128,8192]{1,0:T(8,128)(2,1)}, u32[]{:S(2)}, u32[]{:S(2)}) collective-permute-start(bf16[128,8192]{1,0:T(8,128)(2,1)} %bitcast.110), channel_id=1, source_target_pairs={{0,16},{16,32},{32,48},{48,64},{64,80},{80,96},{96,112},{1,17},{17... | collective-permute-start | bytes 6291464 | tf_op jit(solution)/shard_map/ppermute | solution.py:24
  30.4 2.9 %copy-start.7 = (s32[1,2048]{1,0:T(1,128)S(1)}, s32[1,2048]{1,0:T(1,128)}, u32[]{:S(2)}) copy-start(s32[1,2048]{1,0:T(1,128)} %param.25) | copy-start | bytes 24580
  31.0 3.7 %copy-start.9 = (f32[1,128]{1,0:T(1,128)S(1)}, f32[1,128]{1,0:T(1,128)}, u32[]{:S(2)}) copy-start(f32[1,128]{1,0:T(1,128)} %param.16) | copy-start | bytes 1540
  31.0 3.7 %copy-start.10 = (f32[1,128]{1,0:T(1,128)S(1)}, f32[1,128]{1,0:T(1,128)}, u32[]{:S(2)}) copy-start(f32[1,128]{1,0:T(1,128)} %param.17) | copy-start | bytes 1540
  33.3 28.0 %copy-start.3 = (bf16[128,8192]{1,0:T(8,128)(2,1)S(1)}, bf16[128,8192]{1,0:T(8,128)(2,1)}, u32[]{:S(2)}) copy-start(bf16[128,8192]{1,0:T(8,128)(2,1)} %param.14) | copy-start | bytes 6291460
  56.6 21.4 %all-to-all-start.1 = ((bf16[16,128,256]{2,1,0:T(8,128)(2,1)}), bf16[16,128,256]{2,1,0:T(8,128)(2,1)S(1)}, u32[]{:S(2)}, u32[]{:S(2)}) async-start(bf16[16,128,256]{2,1,0:T(8,128)(2,1)} %bitcast.5), calls=%async_computation.1 | async-start | bytes 2097152 | tf_op jit(solution)/shard_map/all_to_all | solution.py:31
  61.1 21.6 %copy-start.4 = (f32[16,128,8]{1,2,0:T(8,128)}, f32[16,128,8]{1,2,0:T(8,128)S(1)}, u32[]{:S(2)}) copy-start(f32[16,128,8]{1,2,0:T(8,128)S(1)} %get-tuple-element.14) | copy-start | bytes 196612
  78.0 34.0 %all-to-all-start = ((bf16[16,128,512]{2,1,0:T(8,128)(2,1)}), bf16[16,128,512]{2,1,0:T(8,128)(2,1)S(1)}, u32[]{:S(2)}, u32[]{:S(2)}) async-start(bf16[16,128,512]{2,1,0:T(8,128)(2,1)} %bitcast.80), calls=%async_computation | async-start | bytes 4194304 | tf_op jit(solution)/shard_map/all_to_all | solution.py:31
  84.1 9.0 %copy-start.5 = (bf16[1,128,1024]{2,1,0:T(8,128)(2,1)S(1)}, bf16[1,128,1024]{2,1,0:T(8,128)(2,1)}, u32[]{:S(2)}) copy-start(bf16[1,128,1024]{2,1,0:T(8,128)(2,1)} %param.24) | copy-start | bytes 786436
  85.4 7.7 %copy-start.6 = (bf16[1,128,1024]{2,1,0:T(8,128)(2,1)S(1)}, bf16[1,128,1024]{2,1,0:T(8,128)(2,1)}, u32[]{:S(2)}) copy-start(bf16[1,128,1024]{2,1,0:T(8,128)(2,1)} %param.23) | copy-start | bytes 786436
  112.0 1.3 copy-start.1
  133.2 11.5 %all-to-all-start.3 = ((f32[16,1,2048]{2,1,0:T(1,128)}), f32[16,1,2048]{2,1,0:T(1,128)S(1)}, u32[]{:S(2)}, u32[]{:S(2)}) async-start(f32[16,1,2048]{2,1,0:T(1,128)} %broadcast_in_dim.13), calls=%async_computation.3 | async-start | bytes 262144 | tf_op jit(solution)/shard_map/all_to_all | solution.py:238
  149.6 4.0 %copy-start.8 = (s32[1,2048]{1,0:T(1,128)S(1)}, s32[1,2048]{1,0:T(1,128)}, u32[]{:S(2)}) copy-start(s32[1,2048]{1,0:T(1,128)} %param.25) | copy-start | bytes 24580
  149.6 33.5 %all-to-all-start.4 = ((bf16[16,128,512]{2,1,0:T(8,128)(2,1)}), bf16[16,128,512]{2,1,0:T(8,128)(2,1)S(1)}, u32[]{:S(2)}, u32[]{:S(2)}) async-start(bf16[16,128,512]{2,1,0:T(8,128)(2,1)} %bitcast.81), calls=%async_computation.4 | async-start | bytes 4194304 | tf_op jit(solution)/shard_map/all_to_all | solution.py:38
  183.7 1.6 copy-start.2

commit v20 on v18

--- a/solution.py
+++ b/solution.py
@@ -85,7 +85,7 @@
         sq = jnp.zeros((BLOCK, head_dim), jnp.float32)
         for h in range(heads):
             cols = slice(h * head_dim, (h + 1) * head_dim)
-            lc_c = lcc_ref[0, :, h:h + 1]
+            lc_c = lcc_ref[0, h]
             lc_r = lcr_ref[0, h:h + 1, :]
             decay = jnp.where(same_doc, jnp.exp(lc_c - lc_r), 0.0)
             intra_w = (decay * inner_cb * str_ref[0, h:h + 1, :]).astype(jnp.bfloat16)
@@ -110,7 +110,7 @@
             pl.BlockSpec((BLOCK, x_width), lambda i: (i, 0)),
             pl.BlockSpec((STATE, BLOCK), lambda i: (0, i)),
             pl.BlockSpec((BLOCK, STATE), lambda i: (i, 0)),
-            per_block((BLOCK, heads)),
+            pl.BlockSpec((1, heads, BLOCK, BLOCK), lambda i: (i, 0, 0, 0)),
             per_block((heads, BLOCK)),
             per_block((heads, BLOCK)),
             per_block((BLOCK, heads)),
@@ -132,7 +132,7 @@
         compiler_params=pltpu.CompilerParams(dimension_semantics=("arbitrary",)),
         interpret=interpret,
     )(
-        x_h, b_t, c_g, log_cum, lc_rows, st_rows, carry_scale, end_rows, gain_rows,
+        x_h, b_t, c_g, jnp.broadcast_to(lc_rows[:, :, :, None], (nblk, heads, BLOCK, BLOCK)), lc_rows, st_rows, carry_scale, end_rows, gain_rows,
         all_ids.reshape(total, 1), ids.reshape(nblk, 1, BLOCK), skip_h,
     )
 

time: 189 us -> 193 us (1.021)
  local copies, waits for them, and re-layouts: 30.8 us -> 33.7 us
    broadcast_in_dim x0 -> x1, local copies, waits for them, and re-layouts: none -> 4.59 us  [mixer_heads(): jnp.broadcast_to(lc_rows[:, :, :, None], (nblk, heads, BLOCK, BLOCK))]
  transfers between devices with their start and end apart: 10 -> 10, of which waited for: 4 -> 4; matrix products, arithmetic and copies ran while one was open for 18% -> 17% of each run, Pallas kernels for 15% -> 15%
where the time goes in v20:
time: 193 us; the launch traced here: 191 us
  waiting for transfers between devices  58 us (30%)
  Pallas kernels  45.5 us (24%)
  starting transfers between devices  37.1 us (19%)
  local copies, waits for them, and re-layouts  33.7 us (17%)
  other arithmetic  16.6 us (9%)
    all_to_all x3, waiting for transfers between devices, to_heads(): moved = lax.all_to_all(lead, 'ctx', split_axis=0, concat_axis=0, tiled=True)  50.7 us
    pallas_call x1, Pallas kernels, attend_rows(): pl.pallas_call(kernel, grid=(kv_heads // pair,), in_specs=[pl.BlockSpec((...  27.9 us
    ppermute x5, starting transfers between devices, shifted(): return lax.ppermute(value, axis, pairs)  18.6 us
    pallas_call x1, Pallas kernels, mixer_heads(): pl.pallas_call(kernel, grid=(nblk,), in_specs=[pl.BlockSpec((BLOCK, x_wid...  17.6 us
    unnamed x32, local copies, waits for them, and re-layouts  12.6 us
    all_to_all x3, starting transfers between devices, to_heads(): moved = lax.all_to_all(lead, 'ctx', split_axis=0, concat_axis=0, tiled=True)  10.9 us
    all_to_all x1, waiting for transfers between devices, body(): lax.all_to_all(jnp.broadcast_to(sq_part[:, 0][None], (nctx, total)), 'ctx...  7.26 us
    convert_element_type x1, other arithmetic, body(): mixed = (x_h.astype(jnp.float32) + mixer_out * inv_rms * gain_h.astype(jn...  4.87 us
  transfers between devices with their start and end apart: 10, of which 4 were waited for; matrix products, arithmetic and copies ran while one was open for 17% of the time, Pallas kernels for 15%

profile of v20, /device:TPU:32, one launch (start us, length us, event | category | flops | bytes accessed | tf_op | source)
XLA Modules:
  0.0 191.2 jit_solution(7082276956596073755)
XLA Ops:
  0.0 1.9 pad_maximum_fusion
  1.9 4.2 %collective-permute-start.3 = (bf16[128,2048]{1,0:T(8,128)(2,1)}, bf16[128,2048]{1,0:T(8,128)(2,1)}, u32[]{:S(2)}, u32[]{:S(2)}) collective-permute-start(bf16[128,2048]{1,0:T(8,128)(2,1)} %pad_maximum_fusion), channel_id=1, source_target_pairs={{0,1},{1,2},{2,3},{3,4},{4,5},{5,6},{6,7},{7,8},{8,9},{9,10},{10,1... | collective-permute-start | bytes 1572872 | tf_op jit(solution)/shard_map/ppermute | solution.py:24
  6.1 4.7 %collective-permute-start.2 = (bf16[128,2048]{1,0:T(8,128)(2,1)}, bf16[128,2048]{1,0:T(8,128)(2,1)}, u32[]{:S(2)}, u32[]{:S(2)}) collective-permute-start(bf16[128,2048]{1,0:T(8,128)(2,1)} %pad_maximum_fusion), channel_id=1, source_target_pairs={{0,2},{1,3},{2,4},{3,5},{4,6},{5,7},{6,8},{7,9},{8,10},{9,11},{10,... | collective-permute-start | bytes 1572872 | tf_op jit(solution)/shard_map/ppermute | solution.py:24
  10.7 4.3 %collective-permute-start.1 = (bf16[128,2048]{1,0:T(8,128)(2,1)}, bf16[128,2048]{1,0:T(8,128)(2,1)}, u32[]{:S(2)}, u32[]{:S(2)}) collective-permute-start(bf16[128,2048]{1,0:T(8,128)(2,1)} %pad_maximum_fusion), channel_id=1, source_target_pairs={{0,3},{1,4},{2,5},{3,6},{4,7},{5,8},{6,9},{7,10},{8,11},{9,12},{10... | collective-permute-start | bytes 1572872 | tf_op jit(solution)/shard_map/ppermute | solution.py:24
  15.1 3.5 %collective-permute-start = (bf16[128,2048]{1,0:T(8,128)(2,1)}, bf16[128,2048]{1,0:T(8,128)(2,1)}, u32[]{:S(2)}, u32[]{:S(2)}) collective-permute-start(bf16[128,2048]{1,0:T(8,128)(2,1)} %pad_maximum_fusion), channel_id=1, source_target_pairs={{0,4},{1,5},{2,6},{3,7},{4,8},{5,9},{6,10},{7,11},{8,12},{9,13},{1... | collective-permute-start | bytes 1572872 | tf_op jit(solution)/shard_map/ppermute | solution.py:24
  20.2 3.5 %all-to-all-start.2 = ((f32[16,128,8]{1,2,0:T(8,128)}), f32[16,128,8]{1,2,0:T(8,128)S(1)}, u32[]{:S(2)}, u32[]{:S(2)}) async-start(f32[16,128,8]{1,2,0:T(8,128)} %bitcast.9), calls=%async_computation.2 | async-start | bytes 131072 | tf_op jit(solution)/shard_map/all_to_all | solution.py:31
  23.7 1.9 %collective-permute-start.4 = (bf16[128,8192]{1,0:T(8,128)(2,1)}, bf16[128,8192]{1,0:T(8,128)(2,1)}, u32[]{:S(2)}, u32[]{:S(2)}) collective-permute-start(bf16[128,8192]{1,0:T(8,128)(2,1)} %bitcast.111), channel_id=1, source_target_pairs={{0,16},{16,32},{32,48},{48,64},{64,80},{80,96},{96,112},{1,17},{17... | collective-permute-start | bytes 6291464 | tf_op jit(solution)/shard_map/ppermute | solution.py:24
  35.5 21.1 %all-to-all-done.2 = f32[16,128,8]{1,2,0:T(8,128)S(1)} async-done(((f32[16,128,8]{1,2,0:T(8,128)}), f32[16,128,8]{1,2,0:T(8,128)S(1)}, u32[]{:S(2)}, u32[]{:S(2)}) %all-to-all-start.2) | async-done | bytes 65568 | tf_op jit(solution)/shard_map/all_to_all | solution.py:31
  56.6 3.7 %all-to-all-start.1 = ((bf16[16,128,256]{2,1,0:T(8,128)(2,1)}), bf16[16,128,256]{2,1,0:T(8,128)(2,1)S(1)}, u32[]{:S(2)}, u32[]{:S(2)}) async-start(bf16[16,128,256]{2,1,0:T(8,128)(2,1)} %bitcast.5), calls=%async_computation.1 | async-start | bytes 2097152 | tf_op jit(solution)/shard_map/all_to_all | solution.py:31
  64.7 13.3 %all-to-all-done.1 = bf16[16,128,256]{2,1,0:T(8,128)(2,1)S(1)} async-done(((bf16[16,128,256]{2,1,0:T(8,128)(2,1)}), bf16[16,128,256]{2,1,0:T(8,128)(2,1)S(1)}, u32[]{:S(2)}, u32[]{:S(2)}) %all-to-all-start.1) | async-done | bytes 1048608 | tf_op jit(solution)/shard_map/all_to_all | solution.py:31
  78.0 3.7 %all-to-all-start = ((bf16[16,128,512]{2,1,0:T(8,128)(2,1)}), bf16[16,128,512]{2,1,0:T(8,128)(2,1)S(1)}, u32[]{:S(2)}, u32[]{:S(2)}) async-start(bf16[16,128,512]{2,1,0:T(8,128)(2,1)} %bitcast.80), calls=%async_computation | async-start | bytes 4194304 | tf_op jit(solution)/shard_map/all_to_all | solution.py:31
  84.1 2.0 %constant_dynamic-update-slice_fusion.4 = bf16[640,2048]{1,0:T(8,128)(2,1)} fusion(bf16[128,2048]{1,0:T(8,128)(2,1)} %collective-permute-done), kind=kLoop, calls=%fused_computation.25 | loop fusion | bytes 1048576
  86.0 1.9 constant_dynamic-update-slice_fusion.3
  87.9 1.9 constant_dynamic-update-slice_fusion.2
  89.8 1.9 constant_dynamic-update-slice_fusion.1
  93.6 2.1 %copy.78.b_ref = bf16[128,2048]{1,0:T(8,128)(2,1)} copy(bf16[128,2048]{0,1:T(8,128)(2,1)} %get-tuple-element.16) | data formatting | bytes 1048576 | tf_op jit(solution)/shard_map/transpose | solution.py:69
  95.7 16.3 %all-to-all-done = bf16[16,128,512]{2,1,0:T(8,128)(2,1)S(1)} async-done(((bf16[16,128,512]{2,1,0:T(8,128)(2,1)}), bf16[16,128,512]{2,1,0:T(8,128)(2,1)S(1)}, u32[]{:S(2)}, u32[]{:S(2)}) %all-to-all-start) | async-done | bytes 2097184 | tf_op jit(solution)/shard_map/all_to_all | solution.py:31
  112.8 4.6 %broadcast_in_dim.13.lcc_ref = f32[16,8,128,128]{3,2,1,0:T(8,128)} broadcast(f32[16,8,128]{2,1,0:T(8,128)S(1)} %bitcast.84), dimensions={0,1,2} | broadcast | bytes 8454144 | tf_op jit(solution)/shard_map/broadcast_in_dim | solution.py:135
  117.4 17.6 %shard_map.127 = (f32[2048,512]{1,0:T(8,128)}, f32[2048,1]{1,0:T(8,128)}) custom-call(bf16[2048,512]{1,0:T(8,128)(2,1)} %bitcast.76, bf16[128,2048]{1,0:T(8,128)(2,1)} %copy.78.b_ref, bf16[2048,128]{1,0:T(8,128)(2,1)} %get-tuple-element.15.c_ref, f32[16,8,128,128]{3,2,1,0:T(8,128)} %broadcast_in_dim.13.lcc_ref, f32[16,8,128]{2,1,0:T(8,128)} %bitcast.85, ...), custom_call_target="tpu_custom_call" | custom-call | tf_op jit(solution)/shard_map/pallas_call | solution.py:106
  137.4 3.5 %all-to-all-start.3 = ((f32[16,1,2048]{2,1,0:T(1,128)}), f32[16,1,2048]{2,1,0:T(1,128)S(1)}, u32[]{:S(2)}, u32[]{:S(2)}) async-start(f32[16,1,2048]{2,1,0:T(1,128)} %broadcast_in_dim.16), calls=%async_computation.3 | async-start | bytes 262144 | tf_op jit(solution)/shard_map/all_to_all | solution.py:238
  141.6 7.3 %all-to-all-done.3 = f32[16,1,2048]{2,1,0:T(1,128)S(1)} async-done(((f32[16,1,2048]{2,1,0:T(1,128)}), f32[16,1,2048]{2,1,0:T(1,128)S(1)}, u32[]{:S(2)}, u32[]{:S(2)}) %all-to-all-start.3) | async-done | bytes 131104 | tf_op jit(solution)/shard_map/all_to_all | solution.py:238
  148.9 4.9 %add_convert_fusion.1 = bf16[2048,512]{1,0:T(8,128)(2,1)} fusion(f32[2048,512]{1,0:T(8,128)} %get-tuple-element.10, bf16[2048,512]{1,0:T(8,128)(2,1)} %bitcast.77, f32[512]{0:T(512)S(1)} %bitcast.108, f32[2048]{0:T(1024)S(1)} %add_rsqrt_fusion), kind=kLoop, calls=%fused_computation.2 | loop fusion | flops 5242880 | bytes 8398848 | tf_op jit(solution)/shard_map/convert_element_type | solution.py:245
  153.8 4.0 %all-to-all-start.4 = ((bf16[16,128,512]{2,1,0:T(8,128)(2,1)}), bf16[16,128,512]{2,1,0:T(8,128)(2,1)S(1)}, u32[]{:S(2)}, u32[]{:S(2)}) async-start(bf16[16,128,512]{2,1,0:T(8,128)(2,1)} %bitcast.81), calls=%async_computation.4 | async-start | bytes 4194304 | tf_op jit(solution)/shard_map/all_to_all | solution.py:38
  159.3 27.9 %shard_map.128 = bf16[128,8192]{1,0:T(8,128)(2,1)} custom-call(bf16[128,8192]{1,0:T(8,128)(2,1)} %bitcast.83, bf16[640,2048]{1,0:T(8,128)(2,1)} %constant_dynamic-update-slice_fusion.k_ref.v_ref, bf16[640,2048]{1,0:T(8,128)(2,1)} %constant_dynamic-update-slice_fusion.k_ref.v_ref, s32[128,1]{1,0:T(8,128)} %copy.83.iq_ref, s32[1,640]{1,0:T(1,128)} %reshape.155.ik_ref), custom_call_target="tpu_custom_call" | custom-call | tf_op jit(solution)/shard_map/pallas_call | solution.py:167
  (78 shorter events, 29.3 us)
Async XLA Ops:
  0.0 34.8 %copy-start = (f32[1,128]{1,0:T(1,128)S(1)}, f32[1,128]{1,0:T(1,128)}, u32[]{:S(2)}) copy-start(f32[1,128]{1,0:T(1,128)} %param.20) | copy-start | bytes 1540
  1.9 88.0 %collective-permute-start.3 = (bf16[128,2048]{1,0:T(8,128)(2,1)}, bf16[128,2048]{1,0:T(8,128)(2,1)}, u32[]{:S(2)}, u32[]{:S(2)}) collective-permute-start(bf16[128,2048]{1,0:T(8,128)(2,1)} %pad_maximum_fusion), channel_id=1, source_target_pairs={{0,1},{1,2},{2,3},{3,4},{4,5},{5,6},{6,7},{7,8},{8,9},{9,10},{10,1... | collective-permute-start | bytes 1572872 | tf_op jit(solution)/shard_map/ppermute | solution.py:24
  6.1 81.9 %collective-permute-start.2 = (bf16[128,2048]{1,0:T(8,128)(2,1)}, bf16[128,2048]{1,0:T(8,128)(2,1)}, u32[]{:S(2)}, u32[]{:S(2)}) collective-permute-start(bf16[128,2048]{1,0:T(8,128)(2,1)} %pad_maximum_fusion), channel_id=1, source_target_pairs={{0,2},{1,3},{2,4},{3,5},{4,6},{5,7},{6,8},{7,9},{8,10},{9,11},{10,... | collective-permute-start | bytes 1572872 | tf_op jit(solution)/shard_map/ppermute | solution.py:24
  10.7 75.3 %collective-permute-start.1 = (bf16[128,2048]{1,0:T(8,128)(2,1)}, bf16[128,2048]{1,0:T(8,128)(2,1)}, u32[]{:S(2)}, u32[]{:S(2)}) collective-permute-start(bf16[128,2048]{1,0:T(8,128)(2,1)} %pad_maximum_fusion), channel_id=1, source_target_pairs={{0,3},{1,4},{2,5},{3,6},{4,7},{5,8},{6,9},{7,10},{8,11},{9,12},{10... | collective-permute-start | bytes 1572872 | tf_op jit(solution)/shard_map/ppermute | solution.py:24
  15.1 69.0 %collective-permute-start = (bf16[128,2048]{1,0:T(8,128)(2,1)}, bf16[128,2048]{1,0:T(8,128)(2,1)}, u32[]{:S(2)}, u32[]{:S(2)}) collective-permute-start(bf16[128,2048]{1,0:T(8,128)(2,1)} %pad_maximum_fusion), channel_id=1, source_target_pairs={{0,4},{1,5},{2,6},{3,7},{4,8},{5,9},{6,10},{7,11},{8,12},{9,13},{1... | collective-permute-start | bytes 1572872 | tf_op jit(solution)/shard_map/ppermute | solution.py:24
  20.2 36.4 %all-to-all-start.2 = ((f32[16,128,8]{1,2,0:T(8,128)}), f32[16,128,8]{1,2,0:T(8,128)S(1)}, u32[]{:S(2)}, u32[]{:S(2)}) async-start(f32[16,128,8]{1,2,0:T(8,128)} %bitcast.9), calls=%async_computation.2 | async-start | bytes 131072 | tf_op jit(solution)/shard_map/all_to_all | solution.py:31
  23.7 37.6 %collective-permute-start.4 = (bf16[128,8192]{1,0:T(8,128)(2,1)}, bf16[128,8192]{1,0:T(8,128)(2,1)}, u32[]{:S(2)}, u32[]{:S(2)}) collective-permute-start(bf16[128,8192]{1,0:T(8,128)(2,1)} %bitcast.111), channel_id=1, source_target_pairs={{0,16},{16,32},{32,48},{48,64},{64,80},{80,96},{96,112},{1,17},{17... | collective-permute-start | bytes 6291464 | tf_op jit(solution)/shard_map/ppermute | solution.py:24
  30.4 2.9 %copy-start.7 = (s32[1,2048]{1,0:T(1,128)S(1)}, s32[1,2048]{1,0:T(1,128)}, u32[]{:S(2)}) copy-start(s32[1,2048]{1,0:T(1,128)} %param.25) | copy-start | bytes 24580
  31.0 3.7 %copy-start.9 = (f32[1,128]{1,0:T(1,128)S(1)}, f32[1,128]{1,0:T(1,128)}, u32[]{:S(2)}) copy-start(f32[1,128]{1,0:T(1,128)} %param.16) | copy-start | bytes 1540
  31.0 3.7 %copy-start.10 = (f32[1,128]{1,0:T(1,128)S(1)}, f32[1,128]{1,0:T(1,128)}, u32[]{:S(2)}) copy-start(f32[1,128]{1,0:T(1,128)} %param.17) | copy-start | bytes 1540
  33.4 28.0 %copy-start.3 = (bf16[128,8192]{1,0:T(8,128)(2,1)S(1)}, bf16[128,8192]{1,0:T(8,128)(2,1)}, u32[]{:S(2)}) copy-start(bf16[128,8192]{1,0:T(8,128)(2,1)} %param.14) | copy-start | bytes 6291460
  56.6 21.4 %all-to-all-start.1 = ((bf16[16,128,256]{2,1,0:T(8,128)(2,1)}), bf16[16,128,256]{2,1,0:T(8,128)(2,1)S(1)}, u32[]{:S(2)}, u32[]{:S(2)}) async-start(bf16[16,128,256]{2,1,0:T(8,128)(2,1)} %bitcast.5), calls=%async_computation.1 | async-start | bytes 2097152 | tf_op jit(solution)/shard_map/all_to_all | solution.py:31
  61.1 51.8 %copy-start.4 = (f32[16,128,8]{1,2,0:T(8,128)}, f32[16,128,8]{1,2,0:T(8,128)S(1)}, u32[]{:S(2)}) copy-start(f32[16,128,8]{1,2,0:T(8,128)S(1)} %get-tuple-element.14) | copy-start | bytes 196612
  78.0 34.0 %all-to-all-start = ((bf16[16,128,512]{2,1,0:T(8,128)(2,1)}), bf16[16,128,512]{2,1,0:T(8,128)(2,1)S(1)}, u32[]{:S(2)}, u32[]{:S(2)}) async-start(bf16[16,128,512]{2,1,0:T(8,128)(2,1)} %bitcast.80), calls=%async_computation | async-start | bytes 4194304 | tf_op jit(solution)/shard_map/all_to_all | solution.py:31
  82.7 9.0 %copy-start.5 = (bf16[1,128,1024]{2,1,0:T(8,128)(2,1)S(1)}, bf16[1,128,1024]{2,1,0:T(8,128)(2,1)}, u32[]{:S(2)}) copy-start(bf16[1,128,1024]{2,1,0:T(8,128)(2,1)} %param.24) | copy-start | bytes 786436
  84.0 7.7 %copy-start.6 = (bf16[1,128,1024]{2,1,0:T(8,128)(2,1)S(1)}, bf16[1,128,1024]{2,1,0:T(8,128)(2,1)}, u32[]{:S(2)}) copy-start(bf16[1,128,1024]{2,1,0:T(8,128)(2,1)} %param.23) | copy-start | bytes 786436
  112.0 5.4 %copy-start.1 = (bf16[16,128,512]{2,1,0:T(8,128)(2,1)}, bf16[16,128,512]{2,1,0:T(8,128)(2,1)S(1)}, u32[]{:S(2)}) copy-start(bf16[16,128,512]{2,1,0:T(8,128)(2,1)S(1)} %all-to-all-done) | copy-start | bytes 6291460
  137.4 11.5 %all-to-all-start.3 = ((f32[16,1,2048]{2,1,0:T(1,128)}), f32[16,1,2048]{2,1,0:T(1,128)S(1)}, u32[]{:S(2)}, u32[]{:S(2)}) async-start(f32[16,1,2048]{2,1,0:T(1,128)} %broadcast_in_dim.16), calls=%async_computation.3 | async-start | bytes 262144 | tf_op jit(solution)/shard_map/all_to_all | solution.py:238
  153.8 4.0 %copy-start.8 = (s32[1,2048]{1,0:T(1,128)S(1)}, s32[1,2048]{1,0:T(1,128)}, u32[]{:S(2)}) copy-start(s32[1,2048]{1,0:T(1,128)} %param.25) | copy-start | bytes 24580
  153.8 33.4 %all-to-all-start.4 = ((bf16[16,128,512]{2,1,0:T(8,128)(2,1)}), bf16[16,128,512]{2,1,0:T(8,128)(2,1)S(1)}, u32[]{:S(2)}, u32[]{:S(2)}) async-start(bf16[16,128,512]{2,1,0:T(8,128)(2,1)} %bitcast.81), calls=%async_computation.4 | async-start | bytes 4194304 | tf_op jit(solution)/shard_map/all_to_all | solution.py:38
  187.8 1.6 copy-start.2
